TPU v7x, 512 devices: a whole 4x8x8 slice. The times are simulated.
512 devices in a mesh: dp: 32 (over z, x_lo, core), tensor: 16 (over y, x_hi).
Axes of the slice: x: 4 (x_hi: 2, x_lo: 2; x = x_hi * 2 + x_lo), y: 8, z: 8, core: 2. Of those that a mesh axis runs over, the one named last changes fastest.
Arguments:
- features: bfloat16 [5120, 36864], P('tensor', 'dp'), may hold values from -24 to 24
- cotangents: bfloat16 [36864, 2048], P('dp', 'tensor'), may hold values from -24 to 24
- labels: int32 [36864], P('dp'), may hold values from 0 to 2
- diff_mask: int32 [36864], P('dp'), may hold values 0 or 1
- class_weight: float32 [3], replicated, may hold values from 0.25 to 2
- owners: int32 [16, 32], P('tensor'), may hold values from 0 to 31, each once within a row
- momentum: float32 [5120, 2048], P('dp', 'tensor'), may hold values from -3 to 3
Outputs:
- update: bfloat16 [5120, 2048], P(None, 'tensor')
- new_momentum: float32 [5120, 2048], P('dp', 'tensor')
Inputs may be any that keep to these rules, and one draw needn't show every extreme that they name: `owners`: each row names every dp index once.
All inputs are finite; a program needn't handle non-finite values. No bound on the sum of `diff_mask` on one device may be relied on, other than what follows from the above.
Results may differ from a plain program's by a relative error of at most 0.0065.
Values may be sent and summed in bfloat16 or wider, within the bound.
No kernel may reach another device: no remote copies, remote signals or barrier semaphores. Data moves between devices by JAX's collectives and lax.ppermute only.
A program may use at most 64 MiB of HBM per device.

v0:
```python
import math

import jax
import jax.numpy as jnp
from jax import lax
from jax.sharding import PartitionSpec as P

ITERS = 5


decay_rate = 0.95
quintic_first = 3.4445
quintic_second = -4.775
quintic_third = 2.0315
norm_epsilon = 1e-07


def weigh(cotangents, labels, diff_mask, class_weight, total_tokens):
    classes = jnp.arange(class_weight.shape[0], dtype=jnp.int32)
    picked = (labels[:, None] == classes[None, :]).astype(jnp.float32)
    token_weight = diff_mask.astype(jnp.float32) * jnp.sum(picked * class_weight[None, :], axis=1)
    factor = token_weight / math.sqrt(total_tokens)
    return (cotangents.astype(jnp.float32) * factor[:, None]).astype(jnp.bfloat16)


def invert(owners):
    number = owners.shape[1]
    candidates = jnp.arange(number, dtype=jnp.int32)
    matches = owners[:, None, :] == candidates[None, :, None]
    return jnp.sum(jnp.where(matches, candidates[None, None, :], 0), axis=2)


def reorder(blocks, lookup):
    return jnp.take_along_axis(blocks, jnp.transpose(lookup)[:, None, :, None], axis=0)


def orthogonalize(nesterov):
    frobenius = jnp.sqrt(jnp.sum(nesterov * nesterov, axis=(-3, -1), keepdims=True)) + norm_epsilon
    iterate = nesterov / frobenius
    for step in range(ITERS):
        gram_matrix = jnp.einsum(
            "...rhc,...rhd->...hcd", iterate, iterate, precision=lax.Precision.HIGHEST
        )
        poly_matrix = quintic_second * gram_matrix + quintic_third * jnp.einsum(
            "...hcd,...hde->...hce", gram_matrix, gram_matrix, precision=lax.Precision.HIGHEST
        )
        iterate = quintic_first * iterate + jnp.einsum(
            "...rhc,...hcd->...rhd", iterate, poly_matrix, precision=lax.Precision.HIGHEST
        )
    return iterate


def shards(features, cotangents, labels, diff_mask, class_weight, owners, momentum):
    dp_count = lax.axis_size("dp")
    tensor_count = lax.axis_size("tensor")
    local_tokens = cotangents.shape[0]
    scaled = weigh(cotangents, labels, diff_mask, class_weight, local_tokens * dp_count)
    heads_here = owners.shape[0]
    head_width = cotangents.shape[1] // heads_here
    block_rows = features.shape[0] * tensor_count // dp_count
    inverse = invert(owners)
    partial_grad = jnp.dot(
        lax.all_gather(features, "tensor", axis=0, tiled=True),
        scaled,
        preferred_element_type=jnp.float32,
    )
    summed = lax.psum(partial_grad, "dp")
    blocks = summed.reshape(dp_count, block_rows, heads_here, head_width)
    dp_position = lax.axis_index("dp")
    chosen = inverse[:, dp_position]
    selector = (jnp.arange(dp_count, dtype=jnp.int32)[:, None] == chosen[None, :]).astype(
        jnp.float32
    )
    own_block = jnp.sum(blocks * selector[:, None, :, None], axis=0)
    previous = momentum.reshape(block_rows, heads_here, head_width)
    new_momentum = decay_rate * previous + own_block
    nesterov = own_block + decay_rate * new_momentum
    ortho = orthogonalize(nesterov)
    own_update = (
        (ortho * math.sqrt(block_rows))
        .astype(jnp.bfloat16)
        .reshape(block_rows, heads_here * head_width)
    )
    gathered = lax.all_gather(own_update, "dp", axis=0, tiled=True)
    placed = reorder(gathered.reshape(dp_count, block_rows, heads_here, head_width), owners)
    return (
        placed.reshape(dp_count * block_rows, heads_here * head_width),
        new_momentum.reshape(block_rows, heads_here * head_width),
    )


def solution(mesh):
    in_specs = (
        P("tensor", "dp"),
        P("dp", "tensor"),
        P("dp"),
        P("dp"),
        P(),
        P("tensor", None),
        P("dp", "tensor"),
    )
    out_specs = (P(None, "tensor"), P("dp", "tensor"))
    return jax.shard_map(shards, mesh=mesh, in_specs=in_specs, out_specs=out_specs, check_vma=False)
```

profile of v0, /device:TPU:1, one launch (start us, length us, event | category | flops | bytes accessed | tf_op | source)
XLA Modules:
  0.0 528.0 jit_solution(8185749633837688364)
XLA Ops:
  7.2 0.0 all-gather.4.cloned.1.call-start
  7.2 0.7 all-gather.4.cloned.1.call-update
  7.9 0.0 all-reduce.2.cloned.1.call-start
  7.9 0.8 select_reduce_fusion
  8.7 0.7 multiply_multiply_fusion
  9.5 181.5 %all-gather.4.cloned.1.call-done = bf16[5120,1152]{1,0:T(8,128)(2,1)} async-done(((bf16[320,1152]{1,0:T(8,128)(2,1)}), bf16[5120,1152]{1,0:T(8,128)(2,1)}) %all-gather.4.cloned.1.call-update) | async-done | bytes 11796496 | tf_op jit(solution)/shard_map/all_gather | solution.py:63
  190.9 8.6 %convolution_bitcast_fusion = f32[5120,128]{0,1:T(8,128)S(1)} fusion(bf16[5120,1152]{1,0:T(8,128)(2,1)} %all-gather.4.cloned.1.call-done, bf16[1152,128]{1,0:T(8,128)(2,1)} %param.8, f32[1152]{0:T(1024)S(1)} %multiply_multiply_fusion), kind=kOutput, calls=%fused_computation.1 | convolution fusion | flops 1510391808 | bytes 14717440 | tf_op jit(solution)/shard_map/dot_general | solution.py:62
  199.5 2.1 copy.10
  201.7 0.0 copy-start.2
  201.7 0.0 copy-start
  201.7 0.0 all-reduce.2.cloned.1.call-update
  201.7 0.0 all-gather.6.cloned.1.call-start
  201.8 0.6 copy-done.2
  202.3 0.1 select_reduce_fusion.1
  202.4 0.6 dynamic-slice.3
  203.0 0.6 compare_convert_fusion
  203.7 237.3 %all-reduce.2.cloned.1.call-done = f32[32,160,1,128]{3,1,0,2:T(8,128)} async-done(((f32[32,160,1,128]{3,1,0,2:T(8,128)}), f32[32,160,1,128]{3,1,0,2:T(8,128)}) %all-reduce.2.cloned.1.call-update) | async-done | bytes 2621456 | tf_op jit(solution)/shard_map/psum | solution.py:67
  441.0 2.0 multiply_reduce_fusion
  443.0 0.0 copy-done
  443.0 0.6 multiply_reduce_fusion.1
  443.6 0.0 copy-start.1
  444.3 0.4 fusion.25
  444.8 0.2 fusion.10
  445.0 0.2 fusion
  445.2 0.4 fusion.23
  445.6 0.2 fusion.9
  445.9 0.2 fusion.1
  446.1 0.4 fusion.20
  446.5 0.2 fusion.8
  446.7 0.2 fusion.2
  447.0 0.4 fusion.17
  447.4 0.2 fusion.7
  447.6 0.2 fusion.3
  447.8 0.4 fusion.14
  448.3 0.2 fusion.6
  448.5 0.8 fusion.11
  449.3 0.0 all-gather.6.cloned.1.call-update
  449.4 0.1 broadcast_in_dim.34
  449.5 0.1 broadcast_in_dim.35
  449.6 66.3 %all-gather.6.cloned.1.call-done = bf16[5120,1,128]{2,0,1:T(8,128)(2,1)} async-done(((bf16[160,1,128]{2,0,1:T(8,128)(2,1)}), bf16[5120,1,128]{2,0,1:T(8,128)(2,1)}) %all-gather.6.cloned.1.call-update) | async-done | bytes 1310736 | tf_op jit(solution)/shard_map/all_gather | solution.py:84
  515.9 2.1 gather_fusion
  518.1 0.0 copy-done.1
  518.1 3.4 bitcast_select_fusion
  (3 shorter events, 0.0 us)
Async XLA Ops:
  7.2 183.7 %all-gather.4.cloned.1.call-start = ((), (), s32[]{:S(2)}) async-start(), calls=%async_computation | async-start | bytes 12533760 | tf_op jit(solution)/shard_map/all_gather | solution.py:63
  7.9 433.1 %all-reduce.2.cloned.1.call-start = ((), (), s32[]{:S(2)}) async-start(), calls=%async_computation.1 | async-start | bytes 5242880 | tf_op jit(solution)/shard_map/psum | solution.py:67
  201.7 0.7 copy-start.2
  201.7 241.3 %copy-start = (f32[160,128]{1,0:T(8,128)S(1)}, f32[160,128]{1,0:T(8,128)}, u32[]{:S(2)}) copy-start(f32[160,128]{1,0:T(8,128)} %param.13) | copy-start | bytes 245764
  201.7 314.2 %all-gather.6.cloned.1.call-start = ((), (), s32[]{:S(2)}) async-start(), calls=%async_computation.2 | async-start | bytes 1351680 | tf_op jit(solution)/shard_map/all_gather | solution.py:84
  443.6 74.4 %copy-start.1 = (f32[160,128]{1,0:T(8,128)}, f32[160,128]{1,0:T(8,128)S(1)}, u32[]{:S(2)}) copy-start(f32[160,128]{1,0:T(8,128)S(1)} %get-tuple-element.3) | copy-start | bytes 245764
Sparse Core Ops, SparseCore 0:
  11.1 179.7 all-gather.3
  201.8 239.1 all-reduce.1
  449.5 66.3 all-gather.5
where the time goes:
time: 528 us
  waiting for transfers between devices  486 us (92%)
  between operations  14.6 us (3%)
  matrix products  13.6 us (3%)
  other arithmetic  8.26 us (2%)
  local copies, waits for them, and re-layouts  5.59 us (1%)
    psum x1, waiting for transfers between devices, shards(): summed = lax.psum(partial_grad, 'dp')  237 us
    all_gather x1, waiting for transfers between devices, shards(): lax.all_gather(features, 'tensor', axis=0, tiled=True)  181 us
    all_gather x1, waiting for transfers between devices, shards(): gathered = lax.all_gather(own_update, 'dp', axis=0, tiled=True)  66.3 us
  transfers between devices with their start and end apart: 3, of which 3 were waited for; matrix products, arithmetic and copies ran while one was open for 1% of the time, Pallas kernels for 0%

commit v1 on v0

--- a/solution.py
+++ b/solution.py
@@ -64,14 +64,11 @@
         scaled,
         preferred_element_type=jnp.float32,
     )
-    summed = lax.psum(partial_grad, "dp")
-    blocks = summed.reshape(dp_count, block_rows, heads_here, head_width)
-    dp_position = lax.axis_index("dp")
-    chosen = inverse[:, dp_position]
-    selector = (jnp.arange(dp_count, dtype=jnp.int32)[:, None] == chosen[None, :]).astype(
-        jnp.float32
+    blocks = partial_grad.reshape(dp_count, block_rows, heads_here * head_width)
+    in_owner_order = jnp.take(blocks, inverse[0], axis=0).reshape(dp_count * block_rows, heads_here * head_width)
+    own_block = lax.psum_scatter(in_owner_order, "dp", scatter_dimension=0, tiled=True).reshape(
+        block_rows, heads_here, head_width
     )
-    own_block = jnp.sum(blocks * selector[:, None, :, None], axis=0)
     previous = momentum.reshape(block_rows, heads_here, head_width)
     new_momentum = decay_rate * previous + own_block
     nesterov = own_block + decay_rate * new_momentum

time: 528 us -> 417 us (0.79)
  waiting for transfers between devices: 486 us -> 369 us
    psum x1 -> x0, waiting for transfers between devices: 237 us -> none  [shards(): summed = lax.psum(partial_grad, 'dp')]
    reduce_scatter x0 -> x1, waiting for transfers between devices: none -> 120 us  [shards(): lax.psum_scatter(in_owner_order, 'dp', scatter_dimension=0, tiled=True)]
where the time goes in v1:
time: 417 us
  waiting for transfers between devices  369 us (88%)
  matrix products  15.5 us (4%)
  between operations  14.6 us (4%)
  other arithmetic  10.9 us (3%)
  local copies, waits for them, and re-layouts  7.04 us (2%)
    all_gather x1, waiting for transfers between devices, shards(): lax.all_gather(features, 'tensor', axis=0, tiled=True)  180 us
    reduce_scatter x1, waiting for transfers between devices, shards(): lax.psum_scatter(in_owner_order, 'dp', scatter_dimension=0, tiled=True)  120 us
    all_gather x1, waiting for transfers between devices, shards(): gathered = lax.all_gather(own_update, 'dp', axis=0, tiled=True)  67.8 us
    dot_general x1, matrix products, shards(): jnp.dot(lax.all_gather(features, 'tensor', axis=0, tiled=True), scaled, p...  8.64 us
  transfers between devices with their start and end apart: 3, of which 3 were waited for; matrix products, arithmetic and copies ran while one was open for 1% of the time, Pallas kernels for 0%

profile of v1, /device:TPU:1, one launch (start us, length us, event | category | flops | bytes accessed | tf_op | source)
XLA Modules:
  0.0 416.7 jit_solution(7471216906478547874)
XLA Ops:
  7.2 0.0 all-gather.4.cloned.1.call-start
  7.2 0.7 all-gather.4.cloned.1.call-update
  7.9 0.0 reduce-scatter.2.cloned.1.call-start
  7.9 0.8 select_reduce_fusion.1
  8.7 0.1 broadcast_in_dim.51
  8.8 0.1 broadcast_in_dim.52
  8.9 0.8 select_reduce_fusion
  9.7 0.7 multiply_multiply_fusion
  10.4 180.5 %all-gather.4.cloned.1.call-done = bf16[5120,1152]{1,0:T(8,128)(2,1)} async-done(((bf16[320,1152]{1,0:T(8,128)(2,1)}), bf16[5120,1152]{1,0:T(8,128)(2,1)}) %all-gather.4.cloned.1.call-update) | async-done | bytes 11796496 | tf_op jit(solution)/shard_map/all_gather | solution.py:63
  190.9 8.6 %convolution_bitcast_fusion = f32[5120,128]{0,1:T(8,128)S(1)} fusion(bf16[5120,1152]{1,0:T(8,128)(2,1)} %all-gather.4.cloned.1.call-done, bf16[1152,128]{1,0:T(8,128)(2,1)} %param.8, f32[1152]{0:T(1024)S(1)} %multiply_multiply_fusion), kind=kOutput, calls=%fused_computation.2 | convolution fusion | flops 1510391808 | bytes 14717440 | tf_op jit(solution)/shard_map/dot_general | solution.py:62
  199.5 2.1 copy.11
  201.7 2.5 gather_fusion
  204.1 3.7 bitcast_select_fusion
  207.8 0.0 copy-start
  207.8 0.0 copy-start.2
  207.8 0.0 reduce-scatter.2.cloned.1.call-update
  207.8 0.0 all-gather.6.cloned.1.call-start
  207.9 119.5 %reduce-scatter.2.cloned.1.call-done = f32[160,128]{1,0:T(8,128)} async-done(((f32[5120,128]{1,0:T(8,128)}), f32[160,128]{1,0:T(8,128)}) %reduce-scatter.2.cloned.1.call-update) | async-done | bytes 81936 | tf_op jit(solution)/shard_map/reduce_scatter | solution.py:69
  327.4 0.0 copy-done
  327.4 1.5 multiply_reduce_fusion
  329.0 0.0 copy-start.1
  329.6 1.4 fusion.25
  331.1 0.2 fusion.10
  331.3 1.2 fusion
  332.5 0.4 fusion.23
  332.9 0.2 fusion.9
  333.1 0.2 fusion.1
  333.3 0.4 fusion.20
  333.8 0.2 fusion.8
  334.0 0.2 fusion.2
  334.2 0.4 fusion.17
  334.7 0.2 fusion.7
  334.9 0.2 fusion.3
  335.1 0.4 fusion.14
  335.5 0.2 fusion.6
  335.7 0.8 fusion.11
  336.6 0.0 all-gather.6.cloned.1.call-update
  336.6 0.0 copy-done.2
  336.6 0.1 broadcast_in_dim.46
  336.7 0.1 broadcast_in_dim.47
  336.8 67.8 %all-gather.6.cloned.1.call-done = bf16[5120,1,128]{2,0,1:T(8,128)(2,1)} async-done(((bf16[160,1,128]{2,0,1:T(8,128)(2,1)}), bf16[5120,1,128]{2,0,1:T(8,128)(2,1)}) %all-gather.6.cloned.1.call-update) | async-done | bytes 1310736 | tf_op jit(solution)/shard_map/all_gather | solution.py:81
  404.6 2.1 gather_fusion.1
  406.8 0.0 copy-done.1
  406.8 3.4 bitcast_select_fusion.1
  (6 shorter events, 0.0 us)
Async XLA Ops:
  7.2 183.7 %all-gather.4.cloned.1.call-start = ((), (), s32[]{:S(2)}) async-start(), calls=%async_computation.1 | async-start | bytes 12533760 | tf_op jit(solution)/shard_map/all_gather | solution.py:63
  7.9 319.5 %reduce-scatter.2.cloned.1.call-start = ((), (), s32[]{:S(2)}) async-start(), calls=%async_computation.2 | async-start | bytes 2703360 | tf_op jit(solution)/shard_map/reduce_scatter | solution.py:69
  207.8 119.6 %copy-start = (f32[160,128]{1,0:T(8,128)S(1)}, f32[160,128]{1,0:T(8,128)}, u32[]{:S(2)}) copy-start(f32[160,128]{1,0:T(8,128)} %param.13) | copy-start | bytes 245764
  207.8 128.8 %copy-start.2 = (s32[1,32]{1,0:T(1,128)S(1)}, s32[1,32]{1,0:T(1,128)}, u32[]{:S(2)}) copy-start(s32[1,32]{1,0:T(1,128)} %param.12) | copy-start | bytes 388
  207.8 196.8 %all-gather.6.cloned.1.call-start = ((), (), s32[]{:S(2)}) async-start(), calls=%async_computation.3 | async-start | bytes 1351680 | tf_op jit(solution)/shard_map/all_gather | solution.py:81
  329.0 77.8 %copy-start.1 = (f32[160,128]{1,0:T(8,128)}, f32[160,128]{1,0:T(8,128)S(1)}, u32[]{:S(2)}) copy-start(f32[160,128]{1,0:T(8,128)S(1)} %get-tuple-element.3) | copy-start | bytes 245764
Sparse Core Ops, SparseCore 0:
  11.1 179.7 all-gather.3
  208.0 119.4 reduce-scatter.1
  336.7 67.8 all-gather.5

commit v2 on v1

--- a/solution.py
+++ b/solution.py
@@ -59,11 +59,15 @@
     head_width = cotangents.shape[1] // heads_here
     block_rows = features.shape[0] * tensor_count // dp_count
     inverse = invert(owners)
-    partial_grad = jnp.dot(
-        lax.all_gather(features, "tensor", axis=0, tiled=True),
-        scaled,
-        preferred_element_type=jnp.float32,
-    )
+    all_heads = lax.all_gather(scaled, "tensor", axis=1, tiled=True)
+    rows_all_heads = jnp.dot(features, all_heads, preferred_element_type=jnp.float32)
+    partial_grad = lax.all_to_all(
+        rows_all_heads.reshape(features.shape[0], tensor_count, head_width),
+        "tensor",
+        split_axis=1,
+        concat_axis=0,
+        tiled=True,
+    ).reshape(features.shape[0] * tensor_count, head_width)
     blocks = partial_grad.reshape(dp_count, block_rows, heads_here * head_width)
     in_owner_order = jnp.take(blocks, inverse[0], axis=0).reshape(dp_count * block_rows, heads_here * head_width)
     own_block = lax.psum_scatter(in_owner_order, "dp", scatter_dimension=0, tiled=True).reshape(

time: 417 us -> 417 us (level)
  matrix products: 15.5 us -> 11 us
    all_gather x1, waiting for transfers between devices: 180 us -> 118 us  [shards(): all_heads = lax.all_gather(scaled, 'tensor', axis=1, tiled=True)]
    all_to_all x0 -> x1, waiting for transfers between devices: none -> 59.7 us  [shards(): lax.all_to_all(rows_all_heads.reshape(features.shape[0], tensor_count, he...]
    dot_general x1, matrix products: 8.64 us -> 4.19 us  [shards(): jnp.dot(features, all_heads, preferred_element_type=jnp.float32)]
  transfers between devices with their start and end apart: 3 -> 4, of which waited for: 3 -> 4; matrix products, arithmetic and copies ran while one was open for 1% -> 0% of each run, Pallas kernels for 0% -> 0%
where the time goes in v2:
time: 417 us
  waiting for transfers between devices  367 us (88%)
  between operations  14.6 us (4%)
  other arithmetic  13.8 us (3%)
  matrix products  11 us (3%)
  local copies, waits for them, and re-layouts  6.46 us (2%)
    reduce_scatter x1, waiting for transfers between devices, shards(): lax.psum_scatter(in_owner_order, 'dp', scatter_dimension=0, tiled=True)  121 us
    all_gather x1, waiting for transfers between devices, shards(): all_heads = lax.all_gather(scaled, 'tensor', axis=1, tiled=True)  118 us
    all_gather x1, waiting for transfers between devices, shards(): gathered = lax.all_gather(own_update, 'dp', axis=0, tiled=True)  68 us
    all_to_all x1, waiting for transfers between devices, shards(): lax.all_to_all(rows_all_heads.reshape(features.shape[0], tensor_count, he...  59.7 us
  transfers between devices with their start and end apart: 4, of which 4 were waited for; matrix products, arithmetic and copies ran while one was open for 0% of the time, Pallas kernels for 0%

profile of v2, /device:TPU:1, one launch (start us, length us, event | category | flops | bytes accessed | tf_op | source)
XLA Modules:
  0.0 416.9 jit_solution(2855944453115864971)
XLA Ops:
  7.2 0.0 copy-start
  7.2 0.0 all-gather.4.cloned.1.call-start
  7.2 0.9 select_reduce_fusion
  8.1 0.7 multiply_multiply_fusion
  8.8 1.9 multiply_convert_fusion
  10.7 0.0 all-gather.4.cloned.1.call-update
  10.7 118.2 %all-gather.4.cloned.1.call-done = bf16[1152,2048]{1,0:T(8,128)(2,1)} async-done(((bf16[1152,128]{1,0:T(8,128)(2,1)}), bf16[1152,2048]{1,0:T(8,128)(2,1)}) %all-gather.4.cloned.1.call-update) | async-done | bytes 4718608 | tf_op jit(solution)/shard_map/all_gather | solution.py:62
  128.9 0.0 copy-done
  128.9 4.2 %convolution_bitcast_fusion = f32[40,16,8,128]{3,2,1,0:T(8,128)S(1)} fusion(bf16[320,1152]{1,0:T(8,128)(2,1)S(1)} %copy-done, bf16[1152,2048]{1,0:T(8,128)(2,1)} %all-gather.4.cloned.1.call-done), kind=kOutput, calls=%fused_computation.4 | convolution fusion | flops 1509949440 | bytes 8077312 | tf_op jit(solution)/shard_map/dot_general | solution.py:63
  133.1 1.8 copy.13
  134.9 0.0 copy-start.3
  134.9 3.9 all-to-all-start
  138.8 0.0 reduce-scatter.2.cloned.1.call-start
  138.8 0.0 copy-done.3
  138.8 0.1 select_reduce_fusion.1
  138.9 0.1 broadcast_in_dim.51
  139.0 0.1 broadcast_in_dim.52
  139.1 59.7 %all-to-all-done = f32[320,16,128]{2,0,1:T(8,128)S(1)} async-done(((f32[320,16,128]{2,0,1:T(8,128)}), f32[320,16,128]{2,0,1:T(8,128)S(1)}, u32[]{:S(2)}, u32[]{:S(2)}) %all-to-all-start) | async-done | bytes 2621472 | tf_op jit(solution)/shard_map/all_to_all | solution.py:64
  198.9 2.2 gather_fusion
  201.1 5.3 %bitcast_select_fusion = f32[5120,128]{1,0:T(8,128)} fusion(f32[32,160,128]{2,1,0:T(8,128)} %gather_fusion, pred[5120]{0:T(1024)(128)(4,1)S(1)} %broadcast_in_dim.52), kind=kLoop, calls=%fused_computation.3 | loop fusion | flops 655360 | bytes 5248000 | tf_op jit(solution)/shard_map/jit(_take)/select_n | solution.py:72
  206.3 0.0 copy-start.1
  206.3 0.0 reduce-scatter.2.cloned.1.call-update
  206.4 0.0 all-gather.6.cloned.1.call-start
  206.4 121.1 %reduce-scatter.2.cloned.1.call-done = f32[160,128]{1,0:T(8,128)} async-done(((f32[5120,128]{1,0:T(8,128)}), f32[160,128]{1,0:T(8,128)}) %reduce-scatter.2.cloned.1.call-update) | async-done | bytes 81936 | tf_op jit(solution)/shard_map/reduce_scatter | solution.py:73
  327.5 0.0 copy-done.1
  327.5 1.5 multiply_reduce_fusion
  329.0 0.0 copy-start.2
  329.7 1.4 fusion.24
  331.1 0.2 fusion.10
  331.3 1.2 fusion
  332.5 0.4 fusion.22
  332.9 0.2 fusion.9
  333.1 0.2 fusion.1
  333.4 0.4 fusion.19
  333.8 0.2 fusion.8
  334.0 0.2 fusion.2
  334.2 0.4 fusion.16
  334.7 0.2 fusion.7
  334.9 0.2 fusion.3
  335.1 0.4 fusion.13
  335.6 0.2 fusion.6
  335.8 0.8 fusion.11
  336.6 0.0 all-gather.6.cloned.1.call-update
  336.7 0.1 broadcast_in_dim.46
  336.7 0.1 broadcast_in_dim.47
  336.9 68.0 %all-gather.6.cloned.1.call-done = bf16[5120,1,128]{2,0,1:T(8,128)(2,1)} async-done(((bf16[160,1,128]{2,0,1:T(8,128)(2,1)}), bf16[5120,1,128]{2,0,1:T(8,128)(2,1)}) %all-gather.6.cloned.1.call-update) | async-done | bytes 1310736 | tf_op jit(solution)/shard_map/all_gather | solution.py:85
  404.9 2.1 gather_fusion.1
  407.0 0.0 copy-done.2
  407.0 3.4 bitcast_select_fusion.1
  (6 shorter events, 0.0 us)
Async XLA Ops:
  7.2 121.8 %copy-start = (bf16[320,1152]{1,0:T(8,128)(2,1)S(1)}, bf16[320,1152]{1,0:T(8,128)(2,1)}, u32[]{:S(2)}) copy-start(bf16[320,1152]{1,0:T(8,128)(2,1)} %param.7) | copy-start | bytes 2211844
  7.2 121.7 %all-gather.4.cloned.1.call-start = ((), (), s32[]{:S(2)}) async-start(), calls=%async_computation.2 | async-start | bytes 5013504 | tf_op jit(solution)/shard_map/all_gather | solution.py:62
  134.9 3.9 copy-start.3
  134.9 64.0 %all-to-all-start = ((f32[320,16,128]{2,0,1:T(8,128)}), f32[320,16,128]{2,0,1:T(8,128)S(1)}, u32[]{:S(2)}, u32[]{:S(2)}) async-start(f32[320,16,128]{2,0,1:T(8,128)} %bitcast.100), calls=%async_computation | async-start | bytes 5242880 | tf_op jit(solution)/shard_map/all_to_all | solution.py:64
  138.8 188.7 %reduce-scatter.2.cloned.1.call-start = ((), (), s32[]{:S(2)}) async-start(), calls=%async_computation.3 | async-start | bytes 2703360 | tf_op jit(solution)/shard_map/reduce_scatter | solution.py:73
  206.3 121.1 %copy-start.1 = (f32[160,128]{1,0:T(8,128)S(1)}, f32[160,128]{1,0:T(8,128)}, u32[]{:S(2)}) copy-start(f32[160,128]{1,0:T(8,128)} %param.13) | copy-start | bytes 245764
  206.4 198.6 %all-gather.6.cloned.1.call-start = ((), (), s32[]{:S(2)}) async-start(), calls=%async_computation.4 | async-start | bytes 1351680 | tf_op jit(solution)/shard_map/all_gather | solution.py:85
  329.0 78.1 %copy-start.2 = (f32[160,128]{1,0:T(8,128)}, f32[160,128]{1,0:T(8,128)S(1)}, u32[]{:S(2)}) copy-start(f32[160,128]{1,0:T(8,128)S(1)} %get-tuple-element.3) | copy-start | bytes 245764
Sparse Core Ops, SparseCore 0:
  11.6 117.2 all-gather.3
  206.5 120.9 reduce-scatter.1
  336.8 68.0 all-gather.5

commit v3 on v1

--- a/solution.py
+++ b/solution.py
@@ -1,9 +1,10 @@
 import math
 
 import jax
+import numpy as np
 import jax.numpy as jnp
 from jax import lax
-from jax.sharding import PartitionSpec as P
+from jax.sharding import Mesh, PartitionSpec as P
 
 ITERS = 5
 
@@ -50,23 +51,49 @@
     return iterate
 
 
+def staged_sum_scatter(blocks, axes):
+    for axis in axes:
+        blocks = lax.psum_scatter(blocks, axis, scatter_dimension=0, tiled=True)
+    return blocks
+
+
+def staged_gather(piece, axes):
+    for axis in axes:
+        piece = lax.all_gather(piece, axis, axis=0, tiled=True)
+    return piece
+
+
+def scatter_position(sizes, order):
+    count = int(np.prod(sizes))
+    coords = np.stack(np.unravel_index(np.arange(count), sizes), axis=1)
+    position = np.zeros(count, dtype=np.int64)
+    for axis in order:
+        position = position * sizes[axis] + coords[:, axis]
+    return position
+
+
 def shards(features, cotangents, labels, diff_mask, class_weight, owners, momentum):
-    dp_count = lax.axis_size("dp")
-    tensor_count = lax.axis_size("tensor")
+    dp_count = lax.axis_size(DP)
+    tensor_count = lax.axis_size(TP)
     local_tokens = cotangents.shape[0]
     scaled = weigh(cotangents, labels, diff_mask, class_weight, local_tokens * dp_count)
     heads_here = owners.shape[0]
     head_width = cotangents.shape[1] // heads_here
     block_rows = features.shape[0] * tensor_count // dp_count
     inverse = invert(owners)
+    dp_sizes = tuple(lax.axis_size(axis) for axis in DP)
     partial_grad = jnp.dot(
-        lax.all_gather(features, "tensor", axis=0, tiled=True),
+        staged_gather(features, ("xh", "y")),
         scaled,
         preferred_element_type=jnp.float32,
     )
     blocks = partial_grad.reshape(dp_count, block_rows, heads_here * head_width)
-    in_owner_order = jnp.take(blocks, inverse[0], axis=0).reshape(dp_count * block_rows, heads_here * head_width)
-    own_block = lax.psum_scatter(in_owner_order, "dp", scatter_dimension=0, tiled=True).reshape(
+    position = scatter_position(dp_sizes, (2, 1, 0))
+    owner_at = np.argsort(position)
+    in_owner_order = jnp.take(blocks, inverse[0][owner_at], axis=0).reshape(
+        dp_count * block_rows, heads_here * head_width
+    )
+    own_block = staged_sum_scatter(in_owner_order, ("c", "xl", "z")).reshape(
         block_rows, heads_here, head_width
     )
     previous = momentum.reshape(block_rows, heads_here, head_width)
@@ -78,23 +105,35 @@
         .astype(jnp.bfloat16)
         .reshape(block_rows, heads_here * head_width)
     )
-    gathered = lax.all_gather(own_update, "dp", axis=0, tiled=True)
-    placed = reorder(gathered.reshape(dp_count, block_rows, heads_here, head_width), owners)
+    gathered = staged_gather(own_update, ("z", "xl", "c"))
+    gather_at = jnp.asarray(scatter_position(dp_sizes, (2, 1, 0)), dtype=jnp.int32)
+    placed = reorder(
+        gathered.reshape(dp_count, block_rows, heads_here, head_width), gather_at[owners]
+    )
     return (
         placed.reshape(dp_count * block_rows, heads_here * head_width),
         new_momentum.reshape(block_rows, heads_here * head_width),
     )
 
 
+DP = ("z", "xl", "c")
+TP = ("y", "xh")
+
+
 def solution(mesh):
+    dp_size, tp_size = mesh.shape["dp"], mesh.shape["tensor"]
+    fine = Mesh(
+        mesh.devices.reshape(dp_size // 4, 2, 2, tp_size // 2, 2),
+        DP + TP,
+    )
     in_specs = (
-        P("tensor", "dp"),
-        P("dp", "tensor"),
-        P("dp"),
-        P("dp"),
+        P(TP, DP),
+        P(DP, TP),
+        P(DP),
+        P(DP),
         P(),
-        P("tensor", None),
-        P("dp", "tensor"),
+        P(TP, None),
+        P(DP, TP),
     )
-    out_specs = (P(None, "tensor"), P("dp", "tensor"))
-    return jax.shard_map(shards, mesh=mesh, in_specs=in_specs, out_specs=out_specs, check_vma=False)
+    out_specs = (P(None, TP), P(DP, TP))
+    return jax.shard_map(shards, mesh=fine, in_specs=in_specs, out_specs=out_specs, check_vma=False)

time: 417 us -> 367 us (0.88)
  waiting for transfers between devices: 369 us -> 293 us
  blocking collectives: 0 us -> 25.2 us
    all_gather x2 -> x3, waiting for transfers between devices: 248 us -> 199 us  [staged_gather(): piece = lax.all_gather(piece, axis, axis=0, tiled=True)]
    reduce_scatter x1 -> x3, waiting for transfers between devices: 120 us -> 93.3 us  [staged_sum_scatter(): blocks = lax.psum_scatter(blocks, axis, scatter_dimension=0, tiled=True)]
    all_gather x0 -> x2, blocking collectives: none -> 25.2 us  [staged_gather(): piece = lax.all_gather(piece, axis, axis=0, tiled=True)]
  transfers between devices with their start and end apart: 3 -> 6, of which waited for: 3 -> 6; matrix products, arithmetic and copies ran while one was open for 1% -> 1% of each run, Pallas kernels for 0% -> 0%
where the time goes in v3:
time: 367 us
  waiting for transfers between devices  293 us (80%)
  blocking collectives  25.2 us (7%)
  between operations  15.1 us (4%)
  matrix products  14.8 us (4%)
  other arithmetic  10.2 us (3%)
  local copies, waits for them, and re-layouts  8.47 us (2%)
    all_gather x3, waiting for transfers between devices, staged_gather(): piece = lax.all_gather(piece, axis, axis=0, tiled=True)  199 us
    reduce_scatter x3, waiting for transfers between devices, staged_sum_scatter(): blocks = lax.psum_scatter(blocks, axis, scatter_dimension=0, tiled=True)  93.3 us
    all_gather x2, blocking collectives, staged_gather(): piece = lax.all_gather(piece, axis, axis=0, tiled=True)  25.2 us
    dot_general x1, matrix products, shards(): jnp.dot(staged_gather(features, ('xh', 'y')), scaled, preferred_element_t...  8.52 us
  transfers between devices with their start and end apart: 6, of which 6 were waited for; matrix products, arithmetic and copies ran while one was open for 1% of the time, Pallas kernels for 0%

profile of v3, /device:TPU:1, one launch (start us, length us, event | category | flops | bytes accessed | tf_op | source)
XLA Modules:
  0.0 367.1 jit_solution(9558253937401800869)
XLA Ops:
  7.2 0.0 copy-start.6
  7.2 0.0 copy-start.5
  7.2 0.0 copy-start.4
  7.2 0.0 copy-start.1
  7.2 0.0 all-gather.7.cloned.1.call-start
  7.2 0.7 all-gather.7.cloned.1.call-update
  7.9 0.0 all-gather.9.cloned.1.call-start
  8.0 42.9 %all-gather.7.cloned.1.call-done = bf16[640,1152]{1,0:T(8,128)(2,1)} async-done(((bf16[320,1152]{1,0:T(8,128)(2,1)}), bf16[640,1152]{1,0:T(8,128)(2,1)}) %all-gather.7.cloned.1.call-update) | async-done | bytes 1474576 | tf_op jit(solution)/shard_map/all_gather | solution.py:62
  50.9 0.0 all-gather.9.cloned.1.call-update
  50.9 0.0 reduce-scatter.4.cloned.1.call-start
  51.0 0.7 pad_clamp_fusion.2
  51.6 0.8 select_reduce_fusion.1
  52.4 0.7 gather_fusion.1
  53.1 0.1 broadcast_in_dim.59
  53.2 0.1 broadcast_in_dim.60
  53.3 0.0 copy-done.6
  53.3 0.0 copy-done.5
  53.3 0.1 select_reduce_fusion
  53.4 0.0 copy-done.4
  53.5 127.4 %all-gather.9.cloned.1.call-done = bf16[5120,1152]{1,0:T(8,128)(2,1)} async-done(((bf16[640,1152]{1,0:T(8,128)(2,1)}), bf16[5120,1152]{1,0:T(8,128)(2,1)}) %all-gather.9.cloned.1.call-update) | async-done | bytes 11796496 | tf_op jit(solution)/shard_map/all_gather | solution.py:62
  180.8 0.0 copy-done.1
  180.8 8.5 %convolution_bitcast_fusion = f32[5120,128]{0,1:T(8,128)S(1)} fusion(bf16[5120,1152]{1,0:T(8,128)(2,1)} %all-gather.9.cloned.1.call-done, bf16[1152,128]{1,0:T(8,128)(2,1)S(1)} %copy-done.1, f32[1152]{0:T(1024)S(1)} %multiply_multiply_fusion), kind=kOutput, calls=%fused_computation.4 | convolution fusion | flops 1510391808 | bytes 14717440 | tf_op jit(solution)/shard_map/dot_general | solution.py:85
  189.4 2.1 copy.14
  191.5 2.5 gather_fusion.2
  193.9 3.7 %bitcast_select_fusion = f32[5120,128]{1,0:T(8,128)} fusion(f32[32,160,128]{2,1,0:T(8,128)S(1)} %gather_fusion.2, pred[5120]{0:T(1024)(128)(4,1)S(1)} %broadcast_in_dim.60), kind=kLoop, calls=%fused_computation.5 | loop fusion | flops 655360 | bytes 5248000 | tf_op jit(solution)/shard_map/jit(_take)/select_n | solution.py:93
  197.6 0.0 reduce-scatter.4.cloned.1.call-update
  197.7 0.0 reduce-scatter.6.cloned.1.call-start
  197.7 18.7 %reduce-scatter.4.cloned.1.call-done = f32[2560,128]{1,0:T(8,128)} async-done(((f32[5120,128]{1,0:T(8,128)}), f32[2560,128]{1,0:T(8,128)}) %reduce-scatter.4.cloned.1.call-update) | async-done | bytes 1310736 | tf_op jit(solution)/shard_map/reduce_scatter | solution.py:56
  216.4 0.0 reduce-scatter.6.cloned.1.call-update
  216.4 0.0 reduce-scatter.8.cloned.1.call-start
  216.4 34.3 %reduce-scatter.6.cloned.1.call-done = f32[1280,128]{1,0:T(8,128)} async-done(((f32[2560,128]{1,0:T(8,128)}), f32[1280,128]{1,0:T(8,128)}) %reduce-scatter.6.cloned.1.call-update) | async-done | bytes 655376 | tf_op jit(solution)/shard_map/reduce_scatter | solution.py:56
  250.7 0.0 reduce-scatter.8.cloned.1.call-update
  250.7 0.0 all-gather.11.cloned.1.call-start
  250.8 40.4 %reduce-scatter.8.cloned.1.call-done = f32[160,128]{1,0:T(8,128)} async-done(((f32[1280,128]{1,0:T(8,128)}), f32[160,128]{1,0:T(8,128)}) %reduce-scatter.8.cloned.1.call-update) | async-done | bytes 81936 | tf_op jit(solution)/shard_map/reduce_scatter | solution.py:56
  291.2 0.0 copy-done.2
  291.2 1.5 multiply_reduce_fusion
  293.4 1.4 fusion.25
  294.8 0.0 copy-start.7
  294.8 0.0 copy-start
  294.8 0.2 fusion.10
  295.0 1.2 fusion
  296.2 0.4 fusion.23
  296.7 0.2 fusion.9
  296.9 0.2 fusion.1
  297.1 0.4 fusion.20
  297.6 0.2 fusion.8
  297.8 0.2 fusion.2
  298.0 0.4 fusion.17
  298.4 0.2 fusion.7
  298.6 0.2 fusion.3
  298.9 0.4 fusion.14
  299.3 0.2 fusion.6
  299.5 0.2 fusion.11
  299.8 18.5 %all-gather = bf16[1280,1,128]{2,0,1:T(8,128)(2,1)S(1)} all-gather(bf16[160,1,128]{2,0,1:T(8,128)(2,1)S(1)} %fusion.11), channel_id=2, replica_groups=mesh['z'=8,'xl'=2,'c'=2,'y'=8,'xh'=2] {'z'}, dimensions={0}, use_global_device_ids=true | all-gather | bytes 368640 | tf_op jit(solution)/shard_map/all_gather | solution.py:62
  318.3 6.7 %all-gather.1 = bf16[2560,1,128]{2,0,1:T(8,128)(2,1)} all-gather(bf16[1280,1,128]{2,0,1:T(8,128)(2,1)S(1)} %all-gather), channel_id=3, replica_groups=mesh['z'=8,'xl'=2,'c'=2,'y'=8,'xh'=2] {'xl'}, dimensions={0}, use_global_device_ids=true | all-gather | bytes 983040 | tf_op jit(solution)/shard_map/all_gather | solution.py:62
  325.0 0.0 all-gather.11.cloned.1.call-update
  325.0 0.0 copy-done.3
  325.1 0.0 copy-done
  325.1 0.7 gather_fusion
  325.8 0.1 broadcast_in_dim.53
  325.9 0.1 broadcast_in_dim.54
  326.0 28.7 %all-gather.11.cloned.1.call-done = bf16[5120,1,128]{2,0,1:T(8,128)(2,1)} async-done(((bf16[2560,1,128]{2,0,1:T(8,128)(2,1)}), bf16[5120,1,128]{2,0,1:T(8,128)(2,1)}) %all-gather.11.cloned.1.call-update) | async-done | bytes 1310736 | tf_op jit(solution)/shard_map/all_gather | solution.py:62
  354.7 2.1 gather_fusion.3
  356.8 3.4 bitcast_select_fusion.1
  (12 shorter events, 0.1 us)
Async XLA Ops:
  7.2 46.2 %copy-start.6 = (f32[3]{0:T(128)S(1)}, f32[3]{0:T(128)}, u32[]{:S(2)}) copy-start(f32[3]{0:T(128)} %param.14) | copy-start | bytes 40
  7.2 46.2 %copy-start.5 = (s32[1152]{0:T(1024)S(1)}, s32[1152]{0:T(1024)}, u32[]{:S(2)}) copy-start(s32[1152]{0:T(1024)} %param.12) | copy-start | bytes 13828
  7.2 46.2 %copy-start.4 = (s32[1152]{0:T(1024)S(1)}, s32[1152]{0:T(1024)}, u32[]{:S(2)}) copy-start(s32[1152]{0:T(1024)} %param.13) | copy-start | bytes 13828
  7.2 173.6 %copy-start.1 = (bf16[1152,128]{1,0:T(8,128)(2,1)S(1)}, bf16[1152,128]{1,0:T(8,128)(2,1)}, u32[]{:S(2)}) copy-start(bf16[1152,128]{1,0:T(8,128)(2,1)} %param.11) | copy-start | bytes 884740
  7.2 43.7 %all-gather.7.cloned.1.call-start = ((), (), s32[]{:S(2)}) async-start(), calls=%async_computation.3 | async-start | bytes 2211840 | tf_op jit(solution)/shard_map/all_gather | solution.py:62
  7.9 172.9 %all-gather.9.cloned.1.call-start = ((), (), s32[]{:S(2)}) async-start(), calls=%async_computation.4 | async-start | bytes 13271040 | tf_op jit(solution)/shard_map/all_gather | solution.py:62
  50.9 165.4 %reduce-scatter.4.cloned.1.call-start = ((), (), s32[]{:S(2)}) async-start(), calls=%async_computation.5 | async-start | bytes 3932160 | tf_op jit(solution)/shard_map/reduce_scatter | solution.py:56
  197.6 93.5 %copy-start.2 = (f32[160,128]{1,0:T(8,128)S(1)}, f32[160,128]{1,0:T(8,128)}, u32[]{:S(2)}) copy-start(f32[160,128]{1,0:T(8,128)} %param.16) | copy-start | bytes 245764
  197.7 53.1 %reduce-scatter.6.cloned.1.call-start = ((), (), s32[]{:S(2)}) async-start(), calls=%async_computation.6 | async-start | bytes 1966080 | tf_op jit(solution)/shard_map/reduce_scatter | solution.py:56
  216.4 74.8 %reduce-scatter.8.cloned.1.call-start = ((), (), s32[]{:S(2)}) async-start(), calls=%async_computation.7 | async-start | bytes 737280 | tf_op jit(solution)/shard_map/reduce_scatter | solution.py:56
  250.7 104.0 %all-gather.11.cloned.1.call-start = ((), (), s32[]{:S(2)}) async-start(), calls=%async_computation.8 | async-start | bytes 1966080 | tf_op jit(solution)/shard_map/all_gather | solution.py:62
  292.7 32.3 %copy-start.3 = (f32[160,128]{1,0:T(8,128)}, f32[160,128]{1,0:T(8,128)S(1)}, u32[]{:S(2)}) copy-start(f32[160,128]{1,0:T(8,128)S(1)} %get-tuple-element.3) | copy-start | bytes 245764
  294.8 30.2 %copy-start.7 = (s32[1,32]{1,0:T(1,128)S(1)}, s32[1,32]{1,0:T(1,128)}, u32[]{:S(2)}) copy-start(s32[1,32]{1,0:T(1,128)} %param.15) | copy-start | bytes 388
  294.8 30.2 %copy-start = (s32[32]{0:T(128)S(1)}, s32[32]{0:T(128)}, u32[]{:S(2)}) copy-start(s32[32]{0:T(128)} %constant.60.clone) | copy-start | bytes 388
Sparse Core Ops, SparseCore 0:
  10.1 40.7 all-gather.6
  53.0 127.8 all-gather.8
  197.8 18.5 reduce-scatter.3
  219.0 31.6 reduce-scatter.5
  253.4 37.7 reduce-scatter.7
  325.1 29.5 all-gather.10

commit v4 on v1

--- a/solution.py
+++ b/solution.py
@@ -3,7 +3,7 @@
 import jax
 import jax.numpy as jnp
 from jax import lax
-from jax.sharding import PartitionSpec as P
+from jax.sharding import Mesh, PartitionSpec as P
 
 ITERS = 5
 
@@ -13,6 +13,10 @@
 quintic_second = -4.775
 quintic_third = 2.0315
 norm_epsilon = 1e-07
+
+DP = ("z", "xl", "c")
+TP = ("y", "xh")
+SWAP = [(0, 1), (1, 0)]
 
 
 def weigh(cotangents, labels, diff_mask, class_weight, total_tokens):
@@ -50,25 +54,54 @@
     return iterate
 
 
+def pair_sum_scatter(blocks, axis):
+    half = blocks.shape[0] // 2
+    return blocks[:half] + lax.ppermute(blocks[half:], axis, SWAP)
+
+
+def pair_gather(piece, axis):
+    return jnp.concatenate([piece, lax.ppermute(piece, axis, SWAP)], axis=0)
+
+
 def shards(features, cotangents, labels, diff_mask, class_weight, owners, momentum):
-    dp_count = lax.axis_size("dp")
-    tensor_count = lax.axis_size("tensor")
+    dp_count = lax.axis_size(DP)
+    z_count = lax.axis_size("z")
+    tensor_count = lax.axis_size(TP)
     local_tokens = cotangents.shape[0]
     scaled = weigh(cotangents, labels, diff_mask, class_weight, local_tokens * dp_count)
     heads_here = owners.shape[0]
     head_width = cotangents.shape[1] // heads_here
-    block_rows = features.shape[0] * tensor_count // dp_count
+    feature_rows = features.shape[0]
+    block_rows = feature_rows * tensor_count // dp_count
+    sub_blocks = feature_rows // block_rows
     inverse = invert(owners)
-    partial_grad = jnp.dot(
-        lax.all_gather(features, "tensor", axis=0, tiled=True),
-        scaled,
-        preferred_element_type=jnp.float32,
-    )
+    z = lax.axis_index("z")
+    xl = lax.axis_index("xl")
+    c = lax.axis_index("c")
+    xh = lax.axis_index("xh")
+
+    pair_rows = pair_gather(features, "xh")
+    all_rows = lax.all_gather(pair_rows, "y", axis=0, tiled=True)
+    partial_grad = jnp.dot(all_rows, scaled, preferred_element_type=jnp.float32)
+    k = sub_blocks
+    b = jnp.arange(dp_count, dtype=jnp.int32)
+    pair_slot = jnp.where((b // k) % 2 == xh, 0, 1)
+    block_position = (b // (2 * k)) * (2 * k) + pair_slot * k + b % k
+
+    p = jnp.arange(dp_count, dtype=jnp.int32)
+    half, quarter = dp_count // 2, dp_count // 4
+    owner_c = jnp.where(p < half, c, 1 - c)
+    owner_xl = jnp.where(p % half < quarter, xl, 1 - xl)
+    owner_z = p % quarter
+    owner = owner_z * 4 + owner_xl * 2 + owner_c
     blocks = partial_grad.reshape(dp_count, block_rows, heads_here * head_width)
-    in_owner_order = jnp.take(blocks, inverse[0], axis=0).reshape(dp_count * block_rows, heads_here * head_width)
-    own_block = lax.psum_scatter(in_owner_order, "dp", scatter_dimension=0, tiled=True).reshape(
-        block_rows, heads_here, head_width
-    )
+    in_scatter_order = jnp.take(blocks, block_position[inverse[0][owner]], axis=0)
+    kept = pair_sum_scatter(in_scatter_order, "c")
+    kept = pair_sum_scatter(kept, "xl")
+    own_block = lax.psum_scatter(
+        kept.reshape(z_count * block_rows, heads_here * head_width), "z", scatter_dimension=0, tiled=True
+    ).reshape(block_rows, heads_here, head_width)
+
     previous = momentum.reshape(block_rows, heads_here, head_width)
     new_momentum = decay_rate * previous + own_block
     nesterov = own_block + decay_rate * new_momentum
@@ -78,8 +111,16 @@
         .astype(jnp.bfloat16)
         .reshape(block_rows, heads_here * head_width)
     )
-    gathered = lax.all_gather(own_update, "dp", axis=0, tiled=True)
-    placed = reorder(gathered.reshape(dp_count, block_rows, heads_here, head_width), owners)
+    gathered = lax.all_gather(own_update, "z", axis=0, tiled=True)
+    gathered = pair_gather(gathered, "xl")
+    gathered = pair_gather(gathered, "c")
+    d = jnp.arange(dp_count, dtype=jnp.int32)
+    update_position = (
+        jnp.where(d % 2 == c, 0, half) + jnp.where((d // 2) % 2 == xl, 0, quarter) + d // 4
+    )
+    placed = reorder(
+        gathered.reshape(dp_count, block_rows, heads_here, head_width), update_position[owners]
+    )
     return (
         placed.reshape(dp_count * block_rows, heads_here * head_width),
         new_momentum.reshape(block_rows, heads_here * head_width),
@@ -87,14 +128,16 @@
 
 
 def solution(mesh):
+    dp_size, tp_size = mesh.shape["dp"], mesh.shape["tensor"]
+    fine = Mesh(mesh.devices.reshape(dp_size // 4, 2, 2, tp_size // 2, 2), DP + TP)
     in_specs = (
-        P("tensor", "dp"),
-        P("dp", "tensor"),
-        P("dp"),
-        P("dp"),
+        P(TP, DP),
+        P(DP, TP),
+        P(DP),
+        P(DP),
         P(),
-        P("tensor", None),
-        P("dp", "tensor"),
+        P(TP, None),
+        P(DP, TP),
     )
-    out_specs = (P(None, "tensor"), P("dp", "tensor"))
-    return jax.shard_map(shards, mesh=mesh, in_specs=in_specs, out_specs=out_specs, check_vma=False)
+    out_specs = (P(None, TP), P(DP, TP))
+    return jax.shard_map(shards, mesh=fine, in_specs=in_specs, out_specs=out_specs, check_vma=False)

time: 417 us -> 300 us (0.72)
  waiting for transfers between devices: 369 us -> 207 us
  starting transfers between devices: 0.12 us -> 29.5 us
  blocking collectives: 0 us -> 18.5 us
    all_gather x2 -> x1, waiting for transfers between devices: 248 us -> 135 us  [shards(): all_rows = lax.all_gather(pair_rows, 'y', axis=0, tiled=True)]
    reduce_scatter x1, waiting for transfers between devices: 120 us -> 36.3 us  [shards(): lax.psum_scatter(kept.reshape(z_count * block_rows, heads_here * head_wid...]
    ppermute x0 -> x5, waiting for transfers between devices: none -> 36.1 us  [the longest x3 18.8 us: pair_gather(): return jnp.concatenate([piece, lax.ppermute(piece, axis, SWAP)], axis=0)]
    ppermute x0 -> x5, starting transfers between devices: none -> 29.4 us  [the longest x3 23.4 us: pair_gather(): return jnp.concatenate([piece, lax.ppermute(piece, axis, SWAP)], axis=0)]
    all_gather x0 -> x1, blocking collectives: none -> 18.5 us  [shards(): gathered = lax.all_gather(own_update, 'z', axis=0, tiled=True)]
  transfers between devices with their start and end apart: 3 -> 7, of which waited for: 3 -> 7; matrix products, arithmetic and copies ran while one was open for 1% -> 1% of each run, Pallas kernels for 0% -> 0%
where the time goes in v4:
time: 300 us
  waiting for transfers between devices  207 us (69%)
  starting transfers between devices  29.5 us (10%)
  blocking collectives  18.5 us (6%)
  between operations  15.1 us (5%)
  matrix products  12.6 us (4%)
  other arithmetic  10.9 us (4%)
  local copies, waits for them, and re-layouts  5.99 us (2%)
    all_gather x1, waiting for transfers between devices, shards(): all_rows = lax.all_gather(pair_rows, 'y', axis=0, tiled=True)  135 us
    reduce_scatter x1, waiting for transfers between devices, shards(): lax.psum_scatter(kept.reshape(z_count * block_rows, heads_here * head_wid...  36.3 us
    ppermute x3, starting transfers between devices, pair_gather(): return jnp.concatenate([piece, lax.ppermute(piece, axis, SWAP)], axis=0)  23.4 us
    ppermute x3, waiting for transfers between devices, pair_gather(): return jnp.concatenate([piece, lax.ppermute(piece, axis, SWAP)], axis=0)  18.8 us
    all_gather x1, blocking collectives, shards(): gathered = lax.all_gather(own_update, 'z', axis=0, tiled=True)  18.5 us
    ppermute x2, waiting for transfers between devices, pair_sum_scatter(): return blocks[:half] + lax.ppermute(blocks[half:], axis, SWAP)  17.3 us
    dot_general x1, matrix products, shards(): partial_grad = jnp.dot(all_rows, scaled, preferred_element_type=jnp.float32)  6.32 us
  transfers between devices with their start and end apart: 7, of which 7 were waited for; matrix products, arithmetic and copies ran while one was open for 1% of the time, Pallas kernels for 0%

profile of v4, /device:TPU:1, one launch (start us, length us, event | category | flops | bytes accessed | tf_op | source)
XLA Modules:
  0.0 299.7 jit_solution(10720275515969730181)
XLA Ops:
  7.2 0.0 all-gather.3.cloned.1.call-start
  7.2 5.5 %collective-permute-start = (bf16[320,1152]{1,0:T(8,128)(2,1)}, bf16[320,1152]{1,0:T(8,128)(2,1)S(1)}, u32[]{:S(2)}, u32[]{:S(2)}) collective-permute-start(bf16[320,1152]{1,0:T(8,128)(2,1)} %param.7), channel_id=1, source_target_pairs={{0,1},{1,0},{2,3},{3,2},{4,5},{5,4},{6,7},{7,6},{8,9},{9,8},{10,11... | collective-permute-start | bytes 2211848 | tf_op jit(solution)/shard_map/ppermute | solution.py:63
  12.7 13.1 %collective-permute-done = bf16[320,1152]{1,0:T(8,128)(2,1)S(1)} collective-permute-done((bf16[320,1152]{1,0:T(8,128)(2,1)}, bf16[320,1152]{1,0:T(8,128)(2,1)S(1)}, u32[]{:S(2)}, u32[]{:S(2)}) %collective-permute-start) | collective-permute-done | bytes 737312 | tf_op jit(solution)/shard_map/ppermute | solution.py:63
  25.8 2.4 pad_maximum_fusion
  28.2 0.0 copy-start.6
  28.2 0.0 copy-start.4
  28.2 0.0 copy-start.5
  28.2 0.0 copy-start.3
  28.2 0.0 copy-start
  28.3 0.0 all-gather.3.cloned.1.call-update
  28.3 0.0 reduce-scatter.2.cloned.1.call-start
  28.4 0.5 copy-done.6
  28.9 0.1 select_reduce_fusion.1
  29.0 0.7 gather_fusion.1
  29.7 0.7 gather_fusion.2
  30.5 0.0 copy-done.4
  30.5 0.0 copy-done.5
  30.5 0.1 select_reduce_fusion
  30.6 0.0 copy-done.3
  30.6 134.7 %all-gather.3.cloned.1.call-done = bf16[5120,1152]{1,0:T(8,128)(2,1)} async-done(((bf16[640,1152]{1,0:T(8,128)(2,1)}), bf16[5120,1152]{1,0:T(8,128)(2,1)}) %all-gather.3.cloned.1.call-update) | async-done | bytes 11796496 | tf_op jit(solution)/shard_map/all_gather | solution.py:84
  165.3 0.0 copy-done
  165.3 6.3 %fusion.12 = f32[5120,128]{1,0:T(8,128)S(1)} fusion(bf16[5120,1152]{1,0:T(8,128)(2,1)} %all-gather.3.cloned.1.call-done, bf16[1152,128]{1,0:T(8,128)(2,1)S(1)} %copy-done, f32[1152]{0:T(1024)S(1)} %multiply_multiply_fusion), kind=kOutput, calls=%fused_computation.35 | convolution fusion | flops 1510391808 | bytes 14717440 | tf_op jit(solution)/shard_map/dot_general | solution.py:85
  171.7 2.2 gather_fusion.3
  173.9 2.0 broadcast_select_fusion
  175.9 0.1 slice.27
  176.0 2.7 collective-permute-start.1
  178.7 2.6 collective-permute-done.1
  181.4 0.2 slice_add_fusion
  181.6 0.0 copy-start.1
  181.6 3.2 %collective-permute-start.2 = (f32[8,160,128]{2,1,0:T(8,128)S(1)}, f32[8,160,128]{2,1,0:T(8,128)S(1)}, u32[]{:S(2)}, u32[]{:S(2)}) collective-permute-start(f32[8,160,128]{2,1,0:T(8,128)S(1)} %slice.29), channel_id=1, source_target_pairs={{0,32},{32,0},{1,33},{33,1},{2,34},{34,2},{3,35},{35,3},{4,36},{36... | collective-permute-start | bytes 1966088 | tf_op jit(solution)/shard_map/ppermute | solution.py:59
  184.9 14.7 %collective-permute-done.2 = f32[8,160,128]{2,1,0:T(8,128)S(1)} collective-permute-done((f32[8,160,128]{2,1,0:T(8,128)S(1)}, f32[8,160,128]{2,1,0:T(8,128)S(1)}, u32[]{:S(2)}, u32[]{:S(2)}) %collective-permute-start.2) | collective-permute-done | bytes 655392 | tf_op jit(solution)/shard_map/ppermute | solution.py:59
  199.6 0.9 slice_add_fusion.1
  200.5 0.0 reduce-scatter.2.cloned.1.call-update
  200.5 36.3 %reduce-scatter.2.cloned.1.call-done = f32[160,128]{1,0:T(8,128)} async-done(((f32[1280,128]{1,0:T(8,128)}), f32[160,128]{1,0:T(8,128)}) %reduce-scatter.2.cloned.1.call-update) | async-done | bytes 81936 | tf_op jit(solution)/shard_map/reduce_scatter | solution.py:101
  236.9 0.0 copy-done.1
  236.9 1.5 multiply_reduce_fusion
  238.4 0.0 copy-start.2
  239.1 1.4 fusion.26
  240.5 0.2 fusion.10
  240.7 1.2 fusion
  241.9 0.4 fusion.24
  242.3 0.2 fusion.9
  242.5 0.2 fusion.1
  242.8 0.4 fusion.21
  243.2 0.2 fusion.8
  243.4 0.2 fusion.2
  243.6 0.4 fusion.18
  244.1 0.2 fusion.7
  244.3 0.2 fusion.3
  244.5 0.4 fusion.15
  245.0 0.0 copy-done.2
  245.0 0.2 fusion.6
  245.2 0.2 fusion.11
  245.4 18.5 %all-gather = bf16[1280,1,128]{2,0,1:T(8,128)(2,1)S(1)} all-gather(bf16[160,1,128]{2,0,1:T(8,128)(2,1)S(1)} %fusion.11), channel_id=2, replica_groups=mesh['z'=8,'xl'=2,'c'=2,'y'=8,'xh'=2] {'z'}, dimensions={0}, use_global_device_ids=true | all-gather | bytes 368640 | tf_op jit(solution)/shard_map/all_gather | solution.py:114
  264.0 3.1 %collective-permute-start.3 = (bf16[1280,128]{1,0:T(8,128)(2,1)S(1)}, bf16[1280,128]{1,0:T(8,128)(2,1)S(1)}, u32[]{:S(2)}, u32[]{:S(2)}) collective-permute-start(bf16[1280,128]{1,0:T(8,128)(2,1)S(1)} %bitcast.97), channel_id=1, source_target_pairs={{0,32},{32,0},{1,33},{33,1},{2,34},{34,2},{3,35},{35,3},{4,36},{36... | collective-permute-start | bytes 983048 | tf_op jit(solution)/shard_map/ppermute | solution.py:63
  267.1 4.9 %collective-permute-done.3 = bf16[1280,128]{1,0:T(8,128)(2,1)S(1)} collective-permute-done((bf16[1280,128]{1,0:T(8,128)(2,1)S(1)}, bf16[1280,128]{1,0:T(8,128)(2,1)S(1)}, u32[]{:S(2)}, u32[]{:S(2)}) %collective-permute-start.3) | collective-permute-done | bytes 327712 | tf_op jit(solution)/shard_map/ppermute | solution.py:63
  272.0 14.9 %collective-permute-start.4 = (bf16[2560,128]{1,0:T(8,128)(2,1)S(1)}, bf16[2560,128]{1,0:T(8,128)(2,1)S(1)}, u32[]{:S(2)}, u32[]{:S(2)}) collective-permute-start(bf16[2560,128]{1,0:T(8,128)(2,1)S(1)} %pad_maximum_fusion.2), channel_id=1, source_target_pairs={{0,16},{16,0},{1,17},{17,1},{2,18},{18,2},{3,19},{19,3},{4,20},{20... | collective-permute-start | bytes 1966088 | tf_op jit(solution)/shard_map/ppermute | solution.py:63
  286.9 0.7 gather_fusion
  287.6 0.1 broadcast_in_dim.72
  287.7 0.1 broadcast_in_dim.73
  287.8 0.8 collective-permute-done.4
  288.6 0.1 pad_maximum_fusion.1
  288.7 0.8 gather_fusion.4
  289.5 3.4 %bitcast_select_fusion = bf16[5120,128]{1,0:T(8,128)(2,1)} fusion(bf16[32,160,128]{2,1,0:T(8,128)(2,1)S(1)} %gather_fusion.4, pred[5120]{0:T(1024)(128)(4,1)S(1)} %broadcast_in_dim.73), kind=kLoop, calls=%fused_computation.8 | loop fusion | flops 655360 | bytes 2626560 | tf_op jit(solution)/shard_map/jit(take_along_axis)/select_n | solution.py:38
  (17 shorter events, 0.2 us)
Async XLA Ops:
  7.2 158.2 %all-gather.3.cloned.1.call-start = ((), (), s32[]{:S(2)}) async-start(), calls=%async_computation.1 | async-start | bytes 13271040 | tf_op jit(solution)/shard_map/all_gather | solution.py:84
  7.2 18.6 %collective-permute-start = (bf16[320,1152]{1,0:T(8,128)(2,1)}, bf16[320,1152]{1,0:T(8,128)(2,1)S(1)}, u32[]{:S(2)}, u32[]{:S(2)}) collective-permute-start(bf16[320,1152]{1,0:T(8,128)(2,1)} %param.7), channel_id=1, source_target_pairs={{0,1},{1,0},{2,3},{3,2},{4,5},{5,4},{6,7},{7,6},{8,9},{9,8},{10,11... | collective-permute-start | bytes 2211848 | tf_op jit(solution)/shard_map/ppermute | solution.py:63
  28.2 0.7 copy-start.6
  28.2 2.2 copy-start.4
  28.2 2.2 copy-start.5
  28.2 2.3 copy-start.3
  28.2 137.1 %copy-start = (bf16[1152,128]{1,0:T(8,128)(2,1)S(1)}, bf16[1152,128]{1,0:T(8,128)(2,1)}, u32[]{:S(2)}) copy-start(bf16[1152,128]{1,0:T(8,128)(2,1)} %param.8) | copy-start | bytes 884740
  28.3 208.6 %reduce-scatter.2.cloned.1.call-start = ((), (), s32[]{:S(2)}) async-start(), calls=%async_computation.2 | async-start | bytes 737280 | tf_op jit(solution)/shard_map/reduce_scatter | solution.py:101
  176.0 5.4 %collective-permute-start.1 = (f32[16,160,128]{2,1,0:T(8,128)S(1)}, f32[16,160,128]{2,1,0:T(8,128)S(1)}, u32[]{:S(2)}, u32[]{:S(2)}) collective-permute-start(f32[16,160,128]{2,1,0:T(8,128)S(1)} %slice.27), channel_id=1, source_target_pairs={{0,16},{16,0},{1,17},{17,1},{2,18},{18,2},{3,19},{19,3},{4,20},{20... | collective-permute-start | bytes 3932168 | tf_op jit(solution)/shard_map/ppermute | solution.py:59
  181.6 55.2 %copy-start.1 = (f32[160,128]{1,0:T(8,128)S(1)}, f32[160,128]{1,0:T(8,128)}, u32[]{:S(2)}) copy-start(f32[160,128]{1,0:T(8,128)} %param.13) | copy-start | bytes 245764
  181.6 17.9 %collective-permute-start.2 = (f32[8,160,128]{2,1,0:T(8,128)S(1)}, f32[8,160,128]{2,1,0:T(8,128)S(1)}, u32[]{:S(2)}, u32[]{:S(2)}) collective-permute-start(f32[8,160,128]{2,1,0:T(8,128)S(1)} %slice.29), channel_id=1, source_target_pairs={{0,32},{32,0},{1,33},{33,1},{2,34},{34,2},{3,35},{35,3},{4,36},{36... | collective-permute-start | bytes 1966088 | tf_op jit(solution)/shard_map/ppermute | solution.py:59
  238.4 6.6 %copy-start.2 = (f32[160,128]{1,0:T(8,128)}, f32[160,128]{1,0:T(8,128)S(1)}, u32[]{:S(2)}) copy-start(f32[160,128]{1,0:T(8,128)S(1)} %get-tuple-element.3) | copy-start | bytes 245764
  264.0 8.0 %collective-permute-start.3 = (bf16[1280,128]{1,0:T(8,128)(2,1)S(1)}, bf16[1280,128]{1,0:T(8,128)(2,1)S(1)}, u32[]{:S(2)}, u32[]{:S(2)}) collective-permute-start(bf16[1280,128]{1,0:T(8,128)(2,1)S(1)} %bitcast.97), channel_id=1, source_target_pairs={{0,32},{32,0},{1,33},{33,1},{2,34},{34,2},{3,35},{35,3},{4,36},{36... | collective-permute-start | bytes 983048 | tf_op jit(solution)/shard_map/ppermute | solution.py:63
  272.0 16.6 %collective-permute-start.4 = (bf16[2560,128]{1,0:T(8,128)(2,1)S(1)}, bf16[2560,128]{1,0:T(8,128)(2,1)S(1)}, u32[]{:S(2)}, u32[]{:S(2)}) collective-permute-start(bf16[2560,128]{1,0:T(8,128)(2,1)S(1)} %pad_maximum_fusion.2), channel_id=1, source_target_pairs={{0,16},{16,0},{1,17},{17,1},{2,18},{18,2},{3,19},{19,3},{4,20},{20... | collective-permute-start | bytes 1966088 | tf_op jit(solution)/shard_map/ppermute | solution.py:63
Sparse Core Ops, SparseCore 0:
  28.4 136.8 all-gather.2
  200.7 36.1 reduce-scatter.1

commit v5 on v4

--- a/solution.py
+++ b/solution.py
@@ -80,26 +80,38 @@
     c = lax.axis_index("c")
     xh = lax.axis_index("xh")
 
+    y_count = lax.axis_size("y")
+    half, quarter = dp_count // 2, dp_count // 4
+    quarter_rows = block_rows // 4
     pair_rows = pair_gather(features, "xh")
-    all_rows = lax.all_gather(pair_rows, "y", axis=0, tiled=True)
-    partial_grad = jnp.dot(all_rows, scaled, preferred_element_type=jnp.float32)
-    k = sub_blocks
-    b = jnp.arange(dp_count, dtype=jnp.int32)
-    pair_slot = jnp.where((b // k) % 2 == xh, 0, 1)
-    block_position = (b // (2 * k)) * (2 * k) + pair_slot * k + b % k
-
-    p = jnp.arange(dp_count, dtype=jnp.int32)
-    half, quarter = dp_count // 2, dp_count // 4
-    owner_c = jnp.where(p < half, c, 1 - c)
-    owner_xl = jnp.where(p % half < quarter, xl, 1 - xl)
-    owner_z = p % quarter
-    owner = owner_z * 4 + owner_xl * 2 + owner_c
-    blocks = partial_grad.reshape(dp_count, block_rows, heads_here * head_width)
-    in_scatter_order = jnp.take(blocks, block_position[inverse[0][owner]], axis=0)
-    kept = pair_sum_scatter(in_scatter_order, "c")
+    heads_y = lax.all_gather(scaled, "y", axis=1, tiled=True)
+    pair_blocks = 2 * sub_blocks
+    group_rows = pair_blocks * quarter_rows
+    position = jnp.arange(2 * feature_rows, dtype=jnp.int32)
+    group = position // group_rows
+    within = position % group_rows
+    j = within // quarter_rows
+    r = within % quarter_rows
+    quarter_xl = jnp.where(group % 2 == 0, xl, 1 - xl)
+    quarter_c = jnp.where(group < 2, c, 1 - c)
+    u = 2 * quarter_xl + quarter_c
+    shard_slot = jnp.where(j // sub_blocks == xh, 0, 1)
+    source_row = shard_slot * feature_rows + (j % sub_blocks) * block_rows + u * quarter_rows + r
+    arranged = jnp.take(pair_rows, source_row, axis=0)
+    partial = jnp.dot(arranged, heads_y, preferred_element_type=jnp.float32).reshape(
+        2 * feature_rows, y_count, head_width
+    )
+    kept = pair_sum_scatter(partial, "c")
     kept = pair_sum_scatter(kept, "xl")
-    own_block = lax.psum_scatter(
-        kept.reshape(z_count * block_rows, heads_here * head_width), "z", scatter_dimension=0, tiled=True
+    quarters = lax.all_to_all(kept, "y", split_axis=1, concat_axis=0, tiled=True).reshape(
+        dp_count, quarter_rows, head_width
+    )
+    in_owner_order = jnp.take(quarters, inverse[0], axis=0).reshape(
+        dp_count * quarter_rows, head_width
+    )
+    local_owners = lax.psum_scatter(in_owner_order, "z", scatter_dimension=0, tiled=True)
+    own_block = lax.all_to_all(
+        local_owners, ("xl", "c"), split_axis=0, concat_axis=0, tiled=True
     ).reshape(block_rows, heads_here, head_width)
 
     previous = momentum.reshape(block_rows, heads_here, head_width)

time: 300 us -> 225 us (0.75)
  waiting for transfers between devices: 207 us -> 122 us
  blocking collectives: 18.5 us -> 31 us
  matrix products: 12.6 us -> 7.91 us
    all_gather x1, waiting for transfers between devices: 135 us -> 31.4 us  [shards(): heads_y = lax.all_gather(scaled, 'y', axis=1, tiled=True)]
    all_to_all x0 -> x1, waiting for transfers between devices: none -> 20.3 us  [shards(): lax.all_to_all(kept, 'y', split_axis=1, concat_axis=0, tiled=True)]
    all_to_all x0 -> x1, blocking collectives: none -> 12.2 us  [shards(): lax.all_to_all(local_owners, ('xl', 'c'), split_axis=0, concat_axis=0, ti...]
    ppermute x3, starting transfers between devices: 23.4 us -> 17.8 us  [pair_gather(): return jnp.concatenate([piece, lax.ppermute(piece, axis, SWAP)], axis=0)]
    ppermute x2, starting transfers between devices: 5.98 us -> 10.3 us  [pair_sum_scatter(): return blocks[:half] + lax.ppermute(blocks[half:], axis, SWAP)]
    reduce_scatter x1, waiting for transfers between devices: 36.3 us -> 32.6 us  [shards(): lax.psum_scatter(in_owner_order, 'z', scatter_dimension=0, tiled=True)]
    all_to_all x0 -> x1, starting transfers between devices: none -> 3.54 us  [shards(): lax.all_to_all(kept, 'y', split_axis=1, concat_axis=0, tiled=True)]
  transfers between devices with their start and end apart: 7 -> 8, of which waited for: 7 -> 8; matrix products, arithmetic and copies ran while one was open for 1% -> 2% of each run, Pallas kernels for 0% -> 0%
where the time goes in v5:
time: 225 us
  waiting for transfers between devices  122 us (54%)
  starting transfers between devices  31.8 us (14%)
  blocking collectives  31 us (14%)
  between operations  15 us (7%)
  other arithmetic  10.8 us (5%)
  matrix products  7.91 us (4%)
  local copies, waits for them, and re-layouts  5.96 us (3%)
    reduce_scatter x1, waiting for transfers between devices, shards(): lax.psum_scatter(in_owner_order, 'z', scatter_dimension=0, tiled=True)  32.6 us
    all_gather x1, waiting for transfers between devices, shards(): heads_y = lax.all_gather(scaled, 'y', axis=1, tiled=True)  31.4 us
    all_to_all x1, waiting for transfers between devices, shards(): lax.all_to_all(kept, 'y', split_axis=1, concat_axis=0, tiled=True)  20.3 us
    ppermute x3, waiting for transfers between devices, pair_gather(): return jnp.concatenate([piece, lax.ppermute(piece, axis, SWAP)], axis=0)  19.3 us
    all_gather x1, blocking collectives, shards(): gathered = lax.all_gather(own_update, 'z', axis=0, tiled=True)  18.9 us
    ppermute x2, waiting for transfers between devices, pair_sum_scatter(): return blocks[:half] + lax.ppermute(blocks[half:], axis, SWAP)  18.5 us
    ppermute x3, starting transfers between devices, pair_gather(): return jnp.concatenate([piece, lax.ppermute(piece, axis, SWAP)], axis=0)  17.8 us
    all_to_all x1, blocking collectives, shards(): lax.all_to_all(local_owners, ('xl', 'c'), split_axis=0, concat_axis=0, ti...  12.2 us
  transfers between devices with their start and end apart: 8, of which 8 were waited for; matrix products, arithmetic and copies ran while one was open for 2% of the time, Pallas kernels for 0%

profile of v5, /device:TPU:1, one launch (start us, length us, event | category | flops | bytes accessed | tf_op | source)
XLA Modules:
  0.0 224.7 jit_solution(15164028894208010712)
XLA Ops:
  7.2 0.0 copy-start
  7.2 0.0 all-gather.3.cloned.1.call-start
  7.2 0.9 select_reduce_fusion
  8.1 0.7 multiply_multiply_fusion
  8.8 1.9 multiply_convert_fusion
  10.7 0.0 all-gather.3.cloned.1.call-update
  10.7 5.5 %collective-permute-start = (bf16[320,1152]{1,0:T(8,128)(2,1)}, bf16[320,1152]{1,0:T(8,128)(2,1)S(1)}, u32[]{:S(2)}, u32[]{:S(2)}) collective-permute-start(bf16[320,1152]{1,0:T(8,128)(2,1)} %param.7), channel_id=1, source_target_pairs={{0,1},{1,0},{2,3},{3,2},{4,5},{5,4},{6,7},{7,6},{8,9},{9,8},{10,11... | collective-permute-start | bytes 2211848 | tf_op jit(solution)/shard_map/ppermute | solution.py:63
  16.2 0.1 fusion.50
  16.3 13.0 %collective-permute-done = bf16[320,1152]{1,0:T(8,128)(2,1)S(1)} collective-permute-done((bf16[320,1152]{1,0:T(8,128)(2,1)}, bf16[320,1152]{1,0:T(8,128)(2,1)S(1)}, u32[]{:S(2)}, u32[]{:S(2)}) %collective-permute-start) | collective-permute-done | bytes 737312 | tf_op jit(solution)/shard_map/ppermute | solution.py:63
  29.3 0.0 copy-done
  29.3 0.1 pad_maximum_fusion
  29.4 3.0 %gather_fusion.1 = bf16[640,1152]{1,0:T(8,128)(2,1)S(1)} fusion(bf16[640,1152]{1,0:T(8,128)(2,1)S(1)} %pad_maximum_fusion, s32[1024]{0:T(1024)S(1)} %pad_clamp_fusion.2), kind=kCustom, calls=%fused_computation.1 | custom fusion | bytes 2951680 | tf_op jit(solution)/shard_map/jit(_take)/gather | solution.py:100
  32.5 31.4 %all-gather.3.cloned.1.call-done = bf16[1152,1024]{1,0:T(8,128)(2,1)} async-done(((bf16[1152,128]{1,0:T(8,128)(2,1)}), bf16[1152,1024]{1,0:T(8,128)(2,1)}) %all-gather.3.cloned.1.call-update) | async-done | bytes 2359312 | tf_op jit(solution)/shard_map/all_gather | solution.py:87
  63.9 3.6 %fusion = f32[640,1024]{1,0:T(8,128)S(1)} fusion(bf16[1152,1024]{1,0:T(8,128)(2,1)} %all-gather.3.cloned.1.call-done, bf16[640,1152]{1,0:T(8,128)(2,1)S(1)} %gather_fusion.1, pred[640]{0:T(1024)(128)(4,1)S(1)} %compare_and_fusion), kind=kOutput, calls=%fused_computation.5 | convolution fusion | flops 1510686720 | bytes 6455936 | tf_op jit(solution)/shard_map/dot_general | solution.py:101
  67.5 0.3 slice_bitcast_fusion.1
  67.9 0.1 copy.17
  67.9 8.4 %collective-permute-start.1 = (f32[320,8,128]{2,0,1:T(8,128)S(1)}, f32[320,8,128]{2,0,1:T(8,128)S(1)}, u32[]{:S(2)}, u32[]{:S(2)}) collective-permute-start(f32[320,8,128]{2,0,1:T(8,128)S(1)} %bitcast.114), channel_id=1, source_target_pairs={{0,16},{16,0},{1,17},{17,1},{2,18},{18,2},{3,19},{19,3},{4,20},{20... | collective-permute-start | bytes 3932168 | tf_op jit(solution)/shard_map/ppermute | solution.py:59
  76.4 2.6 %collective-permute-done.1 = f32[320,8,128]{2,0,1:T(8,128)S(1)} collective-permute-done((f32[320,8,128]{2,0,1:T(8,128)S(1)}, f32[320,8,128]{2,0,1:T(8,128)S(1)}, u32[]{:S(2)}, u32[]{:S(2)}) %collective-permute-start.1) | collective-permute-done | bytes 1310752 | tf_op jit(solution)/shard_map/ppermute | solution.py:59
  79.0 0.2 bitcast_add_fusion
  79.3 0.0 copy-start.2
  79.3 1.9 collective-permute-start.2
  81.2 15.9 %collective-permute-done.2 = f32[160,8,128]{2,0,1:T(8,128)S(1)} collective-permute-done((f32[160,8,128]{2,0,1:T(8,128)S(1)}, f32[160,8,128]{2,0,1:T(8,128)S(1)}, u32[]{:S(2)}, u32[]{:S(2)}) %collective-permute-start.2) | collective-permute-done | bytes 655392 | tf_op jit(solution)/shard_map/ppermute | solution.py:59
  97.1 0.9 slice_add_fusion
  98.0 3.5 %all-to-all-start = ((f32[160,8,128]{2,0,1:T(8,128)}), f32[160,8,128]{2,0,1:T(8,128)S(1)}, u32[]{:S(2)}, u32[]{:S(2)}) async-start(f32[160,8,128]{2,0,1:T(8,128)} %slice_add_fusion), calls=%async_computation | async-start | bytes 1310720 | tf_op jit(solution)/shard_map/all_to_all | solution.py:106
  101.6 0.0 reduce-scatter.2.cloned.1.call-start
  101.6 0.0 copy-done.2
  101.6 0.1 select_reduce_fusion.1
  101.7 0.1 broadcast_in_dim.103
  101.8 0.1 broadcast_in_dim.104
  102.0 20.3 %all-to-all-done = f32[160,8,128]{2,0,1:T(8,128)S(1)} async-done(((f32[160,8,128]{2,0,1:T(8,128)}), f32[160,8,128]{2,0,1:T(8,128)S(1)}, u32[]{:S(2)}, u32[]{:S(2)}) %all-to-all-start) | async-done | bytes 655392 | tf_op jit(solution)/shard_map/all_to_all | solution.py:106
  122.2 0.0 copy-start.1
  122.2 0.6 gather_fusion.2
  122.8 1.1 bitcast_select_fusion.1
  123.9 0.0 reduce-scatter.2.cloned.1.call-update
  123.9 32.6 %reduce-scatter.2.cloned.1.call-done = f32[160,128]{1,0:T(8,128)} async-done(((f32[1280,128]{1,0:T(8,128)}), f32[160,128]{1,0:T(8,128)}) %reduce-scatter.2.cloned.1.call-update) | async-done | bytes 81936 | tf_op jit(solution)/shard_map/reduce_scatter | solution.py:112
  156.6 12.2 %all_to_all.27 = f32[4,40,128]{2,1,0:T(8,128)S(1)} all-to-all(f32[4,40,128]{2,1,0:T(8,128)} %bitcast.115), channel_id=1, replica_groups=mesh['z'=8,'xl'=2,'c'=2,'y'=8,'xh'=2] {'xl','c'}, dimensions={0} | all-to-all | bytes 163840 | tf_op jit(solution)/shard_map/all_to_all | solution.py:113
  168.7 0.0 copy-done.1
  168.7 1.3 multiply_reduce_fusion
  170.7 0.4 fusion.28
  171.1 0.2 fusion.13
  171.3 0.2 fusion.3
  171.6 0.4 fusion.26
  172.0 0.2 fusion.12
  172.2 0.2 fusion.4
  172.4 0.4 fusion.23
  172.9 0.2 fusion.11
  173.1 0.2 fusion.5
  173.3 0.4 fusion.20
  173.7 0.2 fusion.10
  174.0 0.2 fusion.6
  174.2 0.4 fusion.17
  174.6 0.2 fusion.9
  174.8 0.2 fusion.14
  175.1 18.9 %all-gather = bf16[1280,1,128]{2,0,1:T(8,128)(2,1)S(1)} all-gather(bf16[160,1,128]{2,0,1:T(8,128)(2,1)S(1)} %fusion.14), channel_id=2, replica_groups=mesh['z'=8,'xl'=2,'c'=2,'y'=8,'xh'=2] {'z'}, dimensions={0}, use_global_device_ids=true | all-gather | bytes 368640 | tf_op jit(solution)/shard_map/all_gather | solution.py:126
  193.9 2.3 %collective-permute-start.3 = (bf16[1280,128]{1,0:T(8,128)(2,1)S(1)}, bf16[1280,128]{1,0:T(8,128)(2,1)S(1)}, u32[]{:S(2)}, u32[]{:S(2)}) collective-permute-start(bf16[1280,128]{1,0:T(8,128)(2,1)S(1)} %bitcast.110), channel_id=1, source_target_pairs={{0,32},{32,0},{1,33},{33,1},{2,34},{34,2},{3,35},{35,3},{4,36},{36... | collective-permute-start | bytes 983048 | tf_op jit(solution)/shard_map/ppermute | solution.py:63
  196.2 5.5 %collective-permute-done.3 = bf16[1280,128]{1,0:T(8,128)(2,1)S(1)} collective-permute-done((bf16[1280,128]{1,0:T(8,128)(2,1)S(1)}, bf16[1280,128]{1,0:T(8,128)(2,1)S(1)}, u32[]{:S(2)}, u32[]{:S(2)}) %collective-permute-start.3) | collective-permute-done | bytes 327712 | tf_op jit(solution)/shard_map/ppermute | solution.py:63
  201.8 10.1 %collective-permute-start.4 = (bf16[2560,128]{1,0:T(8,128)(2,1)S(1)}, bf16[2560,128]{1,0:T(8,128)(2,1)S(1)}, u32[]{:S(2)}, u32[]{:S(2)}) collective-permute-start(bf16[2560,128]{1,0:T(8,128)(2,1)S(1)} %pad_maximum_fusion.2), channel_id=1, source_target_pairs={{0,16},{16,0},{1,17},{17,1},{2,18},{18,2},{3,19},{19,3},{4,20},{20... | collective-permute-start | bytes 1966088 | tf_op jit(solution)/shard_map/ppermute | solution.py:63
  211.9 0.7 gather_fusion
  212.6 0.1 broadcast_in_dim.98
  212.7 0.1 broadcast_in_dim.99
  212.8 0.8 collective-permute-done.4
  213.6 0.1 pad_maximum_fusion.1
  213.7 0.8 gather_fusion.3
  214.5 3.4 %bitcast_select_fusion = bf16[5120,128]{1,0:T(8,128)(2,1)} fusion(bf16[32,160,128]{2,1,0:T(8,128)(2,1)S(1)} %gather_fusion.3, pred[5120]{0:T(1024)(128)(4,1)S(1)} %broadcast_in_dim.99), kind=kLoop, calls=%fused_computation.13 | loop fusion | flops 655360 | bytes 2626560 | tf_op jit(solution)/shard_map/jit(take_along_axis)/select_n | solution.py:38
  (13 shorter events, 0.2 us)
Async XLA Ops:
  7.2 22.2 %copy-start = (bf16[320,1152]{1,0:T(8,128)(2,1)S(1)}, bf16[320,1152]{1,0:T(8,128)(2,1)}, u32[]{:S(2)}) copy-start(bf16[320,1152]{1,0:T(8,128)(2,1)} %param.7) | copy-start | bytes 2211844
  7.2 56.8 %all-gather.3.cloned.1.call-start = ((), (), s32[]{:S(2)}) async-start(), calls=%async_computation.3 | async-start | bytes 2654208 | tf_op jit(solution)/shard_map/all_gather | solution.py:87
  10.7 18.6 %collective-permute-start = (bf16[320,1152]{1,0:T(8,128)(2,1)}, bf16[320,1152]{1,0:T(8,128)(2,1)S(1)}, u32[]{:S(2)}, u32[]{:S(2)}) collective-permute-start(bf16[320,1152]{1,0:T(8,128)(2,1)} %param.7), channel_id=1, source_target_pairs={{0,1},{1,0},{2,3},{3,2},{4,5},{5,4},{6,7},{7,6},{8,9},{9,8},{10,11... | collective-permute-start | bytes 2211848 | tf_op jit(solution)/shard_map/ppermute | solution.py:63
  67.9 11.1 %collective-permute-start.1 = (f32[320,8,128]{2,0,1:T(8,128)S(1)}, f32[320,8,128]{2,0,1:T(8,128)S(1)}, u32[]{:S(2)}, u32[]{:S(2)}) collective-permute-start(f32[320,8,128]{2,0,1:T(8,128)S(1)} %bitcast.114), channel_id=1, source_target_pairs={{0,16},{16,0},{1,17},{17,1},{2,18},{18,2},{3,19},{19,3},{4,20},{20... | collective-permute-start | bytes 3932168 | tf_op jit(solution)/shard_map/ppermute | solution.py:59
  79.3 22.4 %copy-start.2 = (s32[1,32]{1,0:T(1,128)S(1)}, s32[1,32]{1,0:T(1,128)}, u32[]{:S(2)}) copy-start(s32[1,32]{1,0:T(1,128)} %param.12) | copy-start | bytes 388
  79.3 17.8 %collective-permute-start.2 = (f32[160,8,128]{2,0,1:T(8,128)S(1)}, f32[160,8,128]{2,0,1:T(8,128)S(1)}, u32[]{:S(2)}, u32[]{:S(2)}) collective-permute-start(f32[160,8,128]{2,0,1:T(8,128)S(1)} %slice.35), channel_id=1, source_target_pairs={{0,32},{32,0},{1,33},{33,1},{2,34},{34,2},{3,35},{35,3},{4,36},{36... | collective-permute-start | bytes 1966088 | tf_op jit(solution)/shard_map/ppermute | solution.py:59
  98.0 24.2 %all-to-all-start = ((f32[160,8,128]{2,0,1:T(8,128)}), f32[160,8,128]{2,0,1:T(8,128)S(1)}, u32[]{:S(2)}, u32[]{:S(2)}) async-start(f32[160,8,128]{2,0,1:T(8,128)} %slice_add_fusion), calls=%async_computation | async-start | bytes 1310720 | tf_op jit(solution)/shard_map/all_to_all | solution.py:106
  101.6 55.0 %reduce-scatter.2.cloned.1.call-start = ((), (), s32[]{:S(2)}) async-start(), calls=%async_computation.4 | async-start | bytes 737280 | tf_op jit(solution)/shard_map/reduce_scatter | solution.py:112
  122.2 46.5 %copy-start.1 = (f32[160,128]{1,0:T(8,128)S(1)}, f32[160,128]{1,0:T(8,128)}, u32[]{:S(2)}) copy-start(f32[160,128]{1,0:T(8,128)} %param.13) | copy-start | bytes 245764
  193.9 7.8 %collective-permute-start.3 = (bf16[1280,128]{1,0:T(8,128)(2,1)S(1)}, bf16[1280,128]{1,0:T(8,128)(2,1)S(1)}, u32[]{:S(2)}, u32[]{:S(2)}) collective-permute-start(bf16[1280,128]{1,0:T(8,128)(2,1)S(1)} %bitcast.110), channel_id=1, source_target_pairs={{0,32},{32,0},{1,33},{33,1},{2,34},{34,2},{3,35},{35,3},{4,36},{36... | collective-permute-start | bytes 983048 | tf_op jit(solution)/shard_map/ppermute | solution.py:63
  201.8 11.8 %collective-permute-start.4 = (bf16[2560,128]{1,0:T(8,128)(2,1)S(1)}, bf16[2560,128]{1,0:T(8,128)(2,1)S(1)}, u32[]{:S(2)}, u32[]{:S(2)}) collective-permute-start(bf16[2560,128]{1,0:T(8,128)(2,1)S(1)} %pad_maximum_fusion.2), channel_id=1, source_target_pairs={{0,16},{16,0},{1,17},{17,1},{2,18},{18,2},{3,19},{19,3},{4,20},{20... | collective-permute-start | bytes 1966088 | tf_op jit(solution)/shard_map/ppermute | solution.py:63
Sparse Core Ops, SparseCore 0:
  10.8 53.0 all-gather.2
  124.1 32.4 reduce-scatter.1

commit v6 on v5

--- a/solution.py
+++ b/solution.py
@@ -59,6 +59,34 @@
     return blocks[:half] + lax.ppermute(blocks[half:], axis, SWAP)
 
 
+def xor_sum_scatter(blocks, axis, distance):
+    half = blocks.shape[0] // 2
+    count = lax.axis_size(axis)
+    perm = [(i, i ^ distance) for i in range(count)]
+    return blocks[:half] + lax.ppermute(blocks[half:], axis, perm)
+
+
+def xor_gather(piece, axis, distance):
+    count = lax.axis_size(axis)
+    perm = [(i, i ^ distance) for i in range(count)]
+    return jnp.concatenate([piece, lax.ppermute(piece, axis, perm)], axis=0)
+
+
+def ring_gather(piece, axis):
+    count = lax.axis_size(axis)
+    to_right = [(i, (i + 1) % count) for i in range(count)]
+    to_left = [(i, (i - 1) % count) for i in range(count)]
+    pieces = [piece]
+    from_left = from_right = piece
+    for step in range(1, count // 2 + 1):
+        from_left = lax.ppermute(from_left, axis, to_right)
+        pieces.append(from_left)
+        if 2 * step < count:
+            from_right = lax.ppermute(from_right, axis, to_left)
+            pieces.append(from_right)
+    return jnp.stack(pieces)
+
+
 def pair_gather(piece, axis):
     return jnp.concatenate([piece, lax.ppermute(piece, axis, SWAP)], axis=0)
 
@@ -84,7 +112,15 @@
     half, quarter = dp_count // 2, dp_count // 4
     quarter_rows = block_rows // 4
     pair_rows = pair_gather(features, "xh")
-    heads_y = lax.all_gather(scaled, "y", axis=1, tiled=True)
+    y = lax.axis_index("y")
+    ring_pieces = ring_gather(scaled, "y")
+    head = jnp.arange(y_count, dtype=jnp.int32)
+    ahead = (head - y) % y_count
+    behind = (y - head) % y_count
+    slot = jnp.where(ahead == 0, 0, jnp.where(ahead < behind, 2 * ahead, 2 * behind - 1))
+    heads_y = jnp.transpose(jnp.take(ring_pieces, slot, axis=0), (1, 0, 2)).reshape(
+        local_tokens, y_count * head_width
+    )
     pair_blocks = 2 * sub_blocks
     group_rows = pair_blocks * quarter_rows
     position = jnp.arange(2 * feature_rows, dtype=jnp.int32)
@@ -106,10 +142,15 @@
     quarters = lax.all_to_all(kept, "y", split_axis=1, concat_axis=0, tiled=True).reshape(
         dp_count, quarter_rows, head_width
     )
-    in_owner_order = jnp.take(quarters, inverse[0], axis=0).reshape(
-        dp_count * quarter_rows, head_width
-    )
-    local_owners = lax.psum_scatter(in_owner_order, "z", scatter_dimension=0, tiled=True)
+    p = jnp.arange(dp_count, dtype=jnp.int32)
+    per_z = dp_count // z_count
+    flips = (p // half) % 2 + 2 * ((p // quarter) % 2) + 4 * ((p // (quarter // 2)) % 2)
+    owner = per_z * (z ^ flips) + p % per_z
+    in_owner_order = jnp.take(quarters, inverse[0][owner], axis=0)
+    kept = in_owner_order
+    for distance in (1, 2, 4):
+        kept = xor_sum_scatter(kept, "z", distance)
+    local_owners = kept.reshape(per_z * quarter_rows, head_width)
     own_block = lax.all_to_all(
         local_owners, ("xl", "c"), split_axis=0, concat_axis=0, tiled=True
     ).reshape(block_rows, heads_here, head_width)
@@ -123,12 +164,14 @@
         .astype(jnp.bfloat16)
         .reshape(block_rows, heads_here * head_width)
     )
-    gathered = lax.all_gather(own_update, "z", axis=0, tiled=True)
+    gathered = own_update
+    for distance in (1, 2, 4):
+        gathered = xor_gather(gathered, "z", distance)
     gathered = pair_gather(gathered, "xl")
     gathered = pair_gather(gathered, "c")
     d = jnp.arange(dp_count, dtype=jnp.int32)
     update_position = (
-        jnp.where(d % 2 == c, 0, half) + jnp.where((d // 2) % 2 == xl, 0, quarter) + d // 4
+        jnp.where(d % 2 == c, 0, half) + jnp.where((d // 2) % 2 == xl, 0, quarter) + ((d // 4) ^ z)
     )
     placed = reorder(
         gathered.reshape(dp_count, block_rows, heads_here, head_width), update_position[owners]

time: 225 us -> 212 us (0.942)
  starting transfers between devices: 31.8 us -> 83.4 us
  waiting for transfers between devices: 122 us -> 75.4 us
  blocking collectives: 31 us -> 8.82 us
  local copies, waits for them, and re-layouts: 5.96 us -> 21.7 us
  between operations: 15 us -> 1.86 us
    ppermute x0 -> x13, starting transfers between devices: none -> 53.1 us  [the longest x3 18 us: xor_sum_scatter(): return blocks[:half] + lax.ppermute(blocks[half:], axis, perm)]
    reduce_scatter x1 -> x0, waiting for transfers between devices: 32.6 us -> none  [shards(): lax.psum_scatter(in_owner_order, 'z', scatter_dimension=0, tiled=True)]
    all_gather x1 -> x0, waiting for transfers between devices: 31.4 us -> none  [shards(): heads_y = lax.all_gather(scaled, 'y', axis=1, tiled=True)]
    ppermute x0 -> x13, waiting for transfers between devices: none -> 31 us  [the longest x3 16.5 us: xor_sum_scatter(): return blocks[:half] + lax.ppermute(blocks[half:], axis, perm)]
    all_gather x1 -> x0, blocking collectives: 18.9 us -> none  [shards(): gathered = lax.all_gather(own_update, 'z', axis=0, tiled=True)]
    ppermute x3, waiting for transfers between devices: 19.3 us -> 6.26 us  [pair_gather(): return jnp.concatenate([piece, lax.ppermute(piece, axis, SWAP)], axis=0)]
    unnamed x7 -> x18, local copies, waits for them, and re-layouts: 0.34 us -> 8.35 us
    gather x1 -> x3, local copies, waits for them, and re-layouts: 0.59 us -> 3.96 us  [the longest x1 2.66 us: shards(): jnp.take(ring_pieces, slot, axis=0)]
  transfers between devices with their start and end apart: 8 -> 19, of which waited for: 8 -> 14; matrix products, arithmetic and copies ran while one was open for 2% -> 6% of each run, Pallas kernels for 0% -> 0%
where the time goes in v6:
time: 212 us; the launch traced here: 211 us
  starting transfers between devices  83.4 us (39%)
  waiting for transfers between devices  75.4 us (36%)
  local copies, waits for them, and re-layouts  21.7 us (10%)
  other arithmetic  12 us (6%)
  blocking collectives  8.82 us (4%)
  matrix products  7.65 us (4%)
    all_to_all x1, waiting for transfers between devices, shards(): lax.all_to_all(kept, 'y', split_axis=1, concat_axis=0, tiled=True)  19.7 us
    ppermute x2, waiting for transfers between devices, pair_sum_scatter(): return blocks[:half] + lax.ppermute(blocks[half:], axis, SWAP)  18.5 us
    ppermute x3, starting transfers between devices, xor_sum_scatter(): return blocks[:half] + lax.ppermute(blocks[half:], axis, perm)  18 us
    ppermute x3, waiting for transfers between devices, xor_sum_scatter(): return blocks[:half] + lax.ppermute(blocks[half:], axis, perm)  16.5 us
    ppermute x3, starting transfers between devices, pair_gather(): return jnp.concatenate([piece, lax.ppermute(piece, axis, SWAP)], axis=0)  15.3 us
    ppermute x3, starting transfers between devices, ring_gather(): from_right = lax.ppermute(from_right, axis, to_left)  13.7 us
    ppermute x3, starting transfers between devices, xor_gather(): return jnp.concatenate([piece, lax.ppermute(piece, axis, perm)], axis=0)  11.7 us
    ppermute x2, starting transfers between devices, pair_sum_scatter(): return blocks[:half] + lax.ppermute(blocks[half:], axis, SWAP)  10.3 us
  transfers between devices with their start and end apart: 19, of which 14 were waited for; matrix products, arithmetic and copies ran while one was open for 6% of the time, Pallas kernels for 0%

profile of v6, /device:TPU:1, one launch (start us, length us, event | category | flops | bytes accessed | tf_op | source)
XLA Modules:
  0.0 210.8 jit_solution(18183082276022897492)
XLA Ops:
  0.6 0.8 select_reduce_fusion
  1.4 0.7 multiply_multiply_fusion
  2.1 1.2 bitcast_dynamic-update-slice_fusion.7
  3.4 4.0 %collective-permute-start.1 = (bf16[1152,128]{1,0:T(8,128)(2,1)S(1)}, bf16[1152,128]{1,0:T(8,128)(2,1)}, u32[]{:S(2)}, u32[]{:S(2)}) collective-permute-start(bf16[1152,128]{1,0:T(8,128)(2,1)S(1)} %get-tuple-element.6), channel_id=1, source_target_pairs={{0,2},{2,4},{4,6},{6,8},{8,10},{10,12},{12,14},{14,0},{1,3},{3,5},... | collective-permute-start | bytes 884744 | tf_op jit(solution)/shard_map/ppermute | solution.py:82
  7.4 3.8 %collective-permute-start.2 = (bf16[1152,128]{1,0:T(8,128)(2,1)S(1)}, bf16[1152,128]{1,0:T(8,128)(2,1)}, u32[]{:S(2)}, u32[]{:S(2)}) collective-permute-start(bf16[1152,128]{1,0:T(8,128)(2,1)S(1)} %get-tuple-element.6), channel_id=1, source_target_pairs={{0,14},{2,0},{4,2},{6,4},{8,6},{10,8},{12,10},{14,12},{1,15},{3,1}... | collective-permute-start | bytes 884744 | tf_op jit(solution)/shard_map/ppermute | solution.py:85
  11.2 4.7 %collective-permute-start = (bf16[320,1152]{1,0:T(8,128)(2,1)}, bf16[320,1152]{1,0:T(8,128)(2,1)}, u32[]{:S(2)}, u32[]{:S(2)}) collective-permute-start(bf16[320,1152]{1,0:T(8,128)(2,1)} %param.7), channel_id=1, source_target_pairs={{0,1},{1,0},{2,3},{3,2},{4,5},{5,4},{6,7},{7,6},{8,9},{9,8},{10,11... | collective-permute-start | bytes 2211848 | tf_op jit(solution)/shard_map/ppermute | solution.py:91
  16.1 1.9 collective-permute-start.3
  18.1 1.0 bitcast_dynamic-update-slice_fusion.6
  19.1 4.6 %collective-permute-start.4 = (bf16[1152,128]{1,0:T(8,128)(2,1)}, bf16[1152,128]{1,0:T(8,128)(2,1)S(1)}, u32[]{:S(2)}, u32[]{:S(2)}) collective-permute-start(bf16[1152,128]{1,0:T(8,128)(2,1)} %collective-permute-done.2), channel_id=1, source_target_pairs={{0,14},{2,0},{4,2},{6,4},{8,6},{10,8},{12,10},{14,12},{1,15},{3,1}... | collective-permute-start | bytes 884744 | tf_op jit(solution)/shard_map/ppermute | solution.py:85
  23.7 1.0 bitcast_dynamic-update-slice_fusion.5
  24.7 0.7 collective-permute-done.3
  25.4 1.9 collective-permute-start.5
  27.3 0.3 collective-permute-done.4
  27.6 5.3 %collective-permute-start.6 = (bf16[1152,128]{1,0:T(8,128)(2,1)S(1)}, bf16[1152,128]{1,0:T(8,128)(2,1)}, u32[]{:S(2)}, u32[]{:S(2)}) collective-permute-start(bf16[1152,128]{1,0:T(8,128)(2,1)S(1)} %collective-permute-done.4), channel_id=1, source_target_pairs={{0,14},{2,0},{4,2},{6,4},{8,6},{10,8},{12,10},{14,12},{1,15},{3,1}... | collective-permute-start | bytes 884744 | tf_op jit(solution)/shard_map/ppermute | solution.py:85
  32.9 1.0 bitcast_dynamic-update-slice_fusion.4
  34.0 1.4 copy-done
  35.4 1.2 pad_maximum_fusion
  36.7 3.6 %gather_fusion.2 = bf16[640,1152]{1,0:T(8,128)(2,1)} fusion(bf16[640,1152]{1,0:T(8,128)(2,1)S(1)} %pad_maximum_fusion, s32[1024]{0:T(1024)S(1)} %pad_clamp_fusion.3), kind=kCustom, calls=%fused_computation.2 | custom fusion | bytes 2951680 | tf_op jit(solution)/shard_map/jit(_take)/gather | solution.py:136
  40.2 1.9 collective-permute-start.7
  42.2 1.7 bitcast_dynamic-update-slice_fusion.2
  43.9 1.7 bitcast_dynamic-update-slice_fusion.1
  45.6 3.5 %collective-permute-done.7 = bf16[1152,128]{1,0:T(8,128)(2,1)S(1)} collective-permute-done((bf16[1152,128]{1,0:T(8,128)(2,1)}, bf16[1152,128]{1,0:T(8,128)(2,1)S(1)}, u32[]{:S(2)}, u32[]{:S(2)}) %collective-permute-start.7) | collective-permute-done | bytes 294944 | tf_op jit(solution)/shard_map/ppermute | solution.py:82
  49.1 0.7 bitcast_dynamic-update-slice_fusion
  49.9 2.7 %gather_fusion.3 = bf16[8,1152,128]{2,1,0:T(8,128)(2,1)S(1)} fusion(bf16[8,1152,128]{2,1,0:T(8,128)(2,1)} %bitcast_dynamic-update-slice_fusion, s32[1024]{0:T(1024)S(1)} %pad_clamp_fusion.2), kind=kCustom, calls=%fused_computation.3 | custom fusion | bytes 4718624 | tf_op jit(solution)/shard_map/jit(_take)/gather | solution.py:121
  52.5 1.7 select_bitcast_fusion
  54.3 3.0 %copy.14 = bf16[1152,8,128]{0,2,1:T(8,128)(2,1)S(1)} copy(bf16[1152,8,128]{2,0,1:T(8,128)(2,1)} %select_bitcast_fusion) | data formatting | bytes 4718592 | tf_op jit(solution)/shard_map/jit(_take)/select_n | solution.py:121
  57.3 3.3 %fusion = f32[640,1024]{1,0:T(8,128)S(1)} fusion(bf16[1152,1024]{0,1:T(8,128)(2,1)S(1)} %bitcast.135, bf16[640,1152]{1,0:T(8,128)(2,1)} %gather_fusion.2, pred[640]{0:T(1024)(128)(4,1)S(1)} %compare_and_fusion), kind=kOutput, calls=%fused_computation.8 | convolution fusion | flops 1510686720 | bytes 6455936 | tf_op jit(solution)/shard_map/dot_general | solution.py:137
  60.6 0.3 slice_bitcast_fusion.1
  61.0 8.4 %collective-permute-start.8 = (f32[320,8,128]{2,0,1:T(8,128)S(1)}, f32[320,8,128]{2,0,1:T(8,128)S(1)}, u32[]{:S(2)}, u32[]{:S(2)}) collective-permute-start(f32[320,8,128]{2,0,1:T(8,128)S(1)} %bitcast.137), channel_id=1, source_target_pairs={{0,16},{16,0},{1,17},{17,1},{2,18},{18,2},{3,19},{19,3},{4,20},{20... | collective-permute-start | bytes 3932168 | tf_op jit(solution)/shard_map/ppermute | solution.py:59
  69.4 2.6 %collective-permute-done.8 = f32[320,8,128]{2,0,1:T(8,128)S(1)} collective-permute-done((f32[320,8,128]{2,0,1:T(8,128)S(1)}, f32[320,8,128]{2,0,1:T(8,128)S(1)}, u32[]{:S(2)}, u32[]{:S(2)}) %collective-permute-start.8) | collective-permute-done | bytes 1310752 | tf_op jit(solution)/shard_map/ppermute | solution.py:59
  72.3 1.9 collective-permute-start.9
  74.2 15.9 %collective-permute-done.9 = f32[160,8,128]{2,0,1:T(8,128)S(1)} collective-permute-done((f32[160,8,128]{2,0,1:T(8,128)S(1)}, f32[160,8,128]{2,0,1:T(8,128)S(1)}, u32[]{:S(2)}, u32[]{:S(2)}) %collective-permute-start.9) | collective-permute-done | bytes 655392 | tf_op jit(solution)/shard_map/ppermute | solution.py:59
  90.1 0.9 slice_add_fusion
  91.0 4.7 %all-to-all-start = ((f32[160,8,128]{2,0,1:T(8,128)}), f32[160,8,128]{2,0,1:T(8,128)S(1)}, u32[]{:S(2)}, u32[]{:S(2)}) async-start(f32[160,8,128]{2,0,1:T(8,128)} %slice_add_fusion), calls=%async_computation | async-start | bytes 1310720 | tf_op jit(solution)/shard_map/all_to_all | solution.py:142
  95.9 0.7 gather_fusion.1
  96.6 19.7 %all-to-all-done = f32[160,8,128]{2,0,1:T(8,128)S(1)} async-done(((f32[160,8,128]{2,0,1:T(8,128)}), f32[160,8,128]{2,0,1:T(8,128)S(1)}, u32[]{:S(2)}, u32[]{:S(2)}) %all-to-all-start) | async-done | bytes 655392 | tf_op jit(solution)/shard_map/all_to_all | solution.py:142
  116.3 0.6 gather_fusion.4
  117.1 4.0 %collective-permute-start.10 = (f32[16,40,128]{2,1,0:T(8,128)S(1)}, f32[16,40,128]{2,1,0:T(8,128)S(1)}, u32[]{:S(2)}, u32[]{:S(2)}) collective-permute-start(f32[16,40,128]{2,1,0:T(8,128)S(1)} %slice.65), channel_id=1, source_target_pairs={{0,64},{64,0},{128,192},{192,128},{256,320},{320,256},{384,448},{4... | collective-permute-start | bytes 983048 | tf_op jit(solution)/shard_map/ppermute | solution.py:66
  121.1 7.4 %collective-permute-done.10 = f32[16,40,128]{2,1,0:T(8,128)S(1)} collective-permute-done((f32[16,40,128]{2,1,0:T(8,128)S(1)}, f32[16,40,128]{2,1,0:T(8,128)S(1)}, u32[]{:S(2)}, u32[]{:S(2)}) %collective-permute-start.10) | collective-permute-done | bytes 327712 | tf_op jit(solution)/shard_map/ppermute | solution.py:66
  128.6 5.8 %collective-permute-start.11 = (f32[8,40,128]{2,1,0:T(8,128)S(1)}, f32[8,40,128]{2,1,0:T(8,128)S(1)}, u32[]{:S(2)}, u32[]{:S(2)}) collective-permute-start(f32[8,40,128]{2,1,0:T(8,128)S(1)} %slice.67), channel_id=1, source_target_pairs={{0,128},{64,192},{128,0},{192,64},{256,384},{320,448},{384,256},{4... | collective-permute-start | bytes 491528 | tf_op jit(solution)/shard_map/ppermute | solution.py:66
  134.4 7.3 %collective-permute-done.11 = f32[8,40,128]{2,1,0:T(8,128)S(1)} collective-permute-done((f32[8,40,128]{2,1,0:T(8,128)S(1)}, f32[8,40,128]{2,1,0:T(8,128)S(1)}, u32[]{:S(2)}, u32[]{:S(2)}) %collective-permute-start.11) | collective-permute-done | bytes 163872 | tf_op jit(solution)/shard_map/ppermute | solution.py:66
  141.7 8.2 %collective-permute-start.12 = (f32[4,40,128]{2,1,0:T(8,128)S(1)}, f32[4,40,128]{2,1,0:T(8,128)S(1)}, u32[]{:S(2)}, u32[]{:S(2)}) collective-permute-start(f32[4,40,128]{2,1,0:T(8,128)S(1)} %slice.69), channel_id=1, source_target_pairs={{0,256},{64,320},{128,384},{192,448},{256,0},{320,64},{384,128},{4... | collective-permute-start | bytes 245768 | tf_op jit(solution)/shard_map/ppermute | solution.py:66
  149.8 1.8 collective-permute-done.12
  151.7 8.8 %all_to_all.24 = f32[4,40,128]{2,1,0:T(8,128)S(1)} all-to-all(f32[4,40,128]{2,1,0:T(8,128)S(1)} %slice_add_fusion.3), channel_id=1, replica_groups=mesh['z'=8,'xl'=2,'c'=2,'y'=8,'xh'=2] {'xl','c'}, dimensions={0} | all-to-all | bytes 163840 | tf_op jit(solution)/shard_map/all_to_all | solution.py:154
  160.5 1.2 multiply_reduce_fusion
  162.4 0.4 fusion.29
  163.1 0.2 fusion.3
  163.3 0.4 fusion.27
  164.2 0.4 fusion.24
  165.1 0.4 fusion.21
  166.0 0.4 fusion.18
  166.9 1.9 collective-permute-start.13
  168.8 2.8 %collective-permute-done.13 = bf16[160,128]{1,0:T(8,128)(2,1)S(1)} collective-permute-done((bf16[160,128]{1,0:T(8,128)(2,1)S(1)}, bf16[160,128]{1,0:T(8,128)(2,1)S(1)}, u32[]{:S(2)}, u32[]{:S(2)}) %collective-permute-start.13) | collective-permute-done | bytes 40992 | tf_op jit(solution)/shard_map/ppermute | solution.py:72
  171.6 2.9 %collective-permute-start.14 = (bf16[320,128]{1,0:T(8,128)(2,1)S(1)}, bf16[320,128]{1,0:T(8,128)(2,1)S(1)}, u32[]{:S(2)}, u32[]{:S(2)}) collective-permute-start(bf16[320,128]{1,0:T(8,128)(2,1)S(1)} %pad_maximum_fusion.3), channel_id=1, source_target_pairs={{0,128},{64,192},{128,0},{192,64},{256,384},{320,448},{384,256},{4... | collective-permute-start | bytes 245768 | tf_op jit(solution)/shard_map/ppermute | solution.py:72
  174.5 3.9 %collective-permute-done.14 = bf16[320,128]{1,0:T(8,128)(2,1)S(1)} collective-permute-done((bf16[320,128]{1,0:T(8,128)(2,1)S(1)}, bf16[320,128]{1,0:T(8,128)(2,1)S(1)}, u32[]{:S(2)}, u32[]{:S(2)}) %collective-permute-start.14) | collective-permute-done | bytes 81952 | tf_op jit(solution)/shard_map/ppermute | solution.py:72
  178.4 6.8 %collective-permute-start.15 = (bf16[640,128]{1,0:T(8,128)(2,1)S(1)}, bf16[640,128]{1,0:T(8,128)(2,1)S(1)}, u32[]{:S(2)}, u32[]{:S(2)}) collective-permute-start(bf16[640,128]{1,0:T(8,128)(2,1)S(1)} %pad_maximum_fusion.2), channel_id=1, source_target_pairs={{0,256},{64,320},{128,384},{192,448},{256,0},{320,64},{384,128},{4... | collective-permute-start | bytes 491528 | tf_op jit(solution)/shard_map/ppermute | solution.py:72
  185.3 3.2 %collective-permute-done.15 = bf16[640,128]{1,0:T(8,128)(2,1)S(1)} collective-permute-done((bf16[640,128]{1,0:T(8,128)(2,1)S(1)}, bf16[640,128]{1,0:T(8,128)(2,1)S(1)}, u32[]{:S(2)}, u32[]{:S(2)}) %collective-permute-start.15) | collective-permute-done | bytes 163872 | tf_op jit(solution)/shard_map/ppermute | solution.py:72
  188.5 2.2 %collective-permute-start.16 = (bf16[1280,128]{1,0:T(8,128)(2,1)S(1)}, bf16[1280,128]{1,0:T(8,128)(2,1)S(1)}, u32[]{:S(2)}, u32[]{:S(2)}) collective-permute-start(bf16[1280,128]{1,0:T(8,128)(2,1)S(1)} %pad_maximum_fusion.1), channel_id=1, source_target_pairs={{0,32},{32,0},{1,33},{33,1},{2,34},{34,2},{3,35},{35,3},{4,36},{36... | collective-permute-start | bytes 983048 | tf_op jit(solution)/shard_map/ppermute | solution.py:91
  190.8 5.5 %collective-permute-done.16 = bf16[1280,128]{1,0:T(8,128)(2,1)S(1)} collective-permute-done((bf16[1280,128]{1,0:T(8,128)(2,1)S(1)}, bf16[1280,128]{1,0:T(8,128)(2,1)S(1)}, u32[]{:S(2)}, u32[]{:S(2)}) %collective-permute-start.16) | collective-permute-done | bytes 327712 | tf_op jit(solution)/shard_map/ppermute | solution.py:91
  196.4 8.4 %collective-permute-start.17 = (bf16[2560,128]{1,0:T(8,128)(2,1)S(1)}, bf16[2560,128]{1,0:T(8,128)(2,1)S(1)}, u32[]{:S(2)}, u32[]{:S(2)}) collective-permute-start(bf16[2560,128]{1,0:T(8,128)(2,1)S(1)} %get-tuple-element.9), channel_id=1, source_target_pairs={{0,16},{16,0},{1,17},{17,1},{2,18},{18,2},{3,19},{19,3},{4,20},{20... | collective-permute-start | bytes 1966088 | tf_op jit(solution)/shard_map/ppermute | solution.py:91
  204.9 0.7 gather_fusion
  205.8 0.8 collective-permute-done.17
  206.6 0.8 gather_fusion.5
  207.5 3.4 %bitcast_select_fusion = bf16[5120,128]{1,0:T(8,128)(2,1)} fusion(bf16[32,160,128]{2,1,0:T(8,128)(2,1)S(1)} %gather_fusion.5, pred[5120]{0:T(1024)(128)(4,1)S(1)} %broadcast_in_dim.108), kind=kLoop, calls=%fused_computation.15 | loop fusion | flops 655360 | bytes 2626560 | tf_op jit(solution)/shard_map/jit(take_along_axis)/select_n | solution.py:38
  (59 shorter events, 3.4 us)
Async XLA Ops:
  2.1 33.3 %copy-start.1 = (bf16[320,1152]{1,0:T(8,128)(2,1)S(1)}, bf16[320,1152]{1,0:T(8,128)(2,1)}, u32[]{:S(2)}) copy-start(bf16[320,1152]{1,0:T(8,128)(2,1)} %param.7) | copy-start | bytes 2211844
  3.4 12.7 %collective-permute-start.1 = (bf16[1152,128]{1,0:T(8,128)(2,1)S(1)}, bf16[1152,128]{1,0:T(8,128)(2,1)}, u32[]{:S(2)}, u32[]{:S(2)}) collective-permute-start(bf16[1152,128]{1,0:T(8,128)(2,1)S(1)} %get-tuple-element.6), channel_id=1, source_target_pairs={{0,2},{2,4},{4,6},{6,8},{8,10},{10,12},{12,14},{14,0},{1,3},{3,5},... | collective-permute-start | bytes 884744 | tf_op jit(solution)/shard_map/ppermute | solution.py:82
  7.4 11.7 %collective-permute-start.2 = (bf16[1152,128]{1,0:T(8,128)(2,1)S(1)}, bf16[1152,128]{1,0:T(8,128)(2,1)}, u32[]{:S(2)}, u32[]{:S(2)}) collective-permute-start(bf16[1152,128]{1,0:T(8,128)(2,1)S(1)} %get-tuple-element.6), channel_id=1, source_target_pairs={{0,14},{2,0},{4,2},{6,4},{8,6},{10,8},{12,10},{14,12},{1,15},{3,1}... | collective-permute-start | bytes 884744 | tf_op jit(solution)/shard_map/ppermute | solution.py:85
  11.2 24.2 %collective-permute-start = (bf16[320,1152]{1,0:T(8,128)(2,1)}, bf16[320,1152]{1,0:T(8,128)(2,1)}, u32[]{:S(2)}, u32[]{:S(2)}) collective-permute-start(bf16[320,1152]{1,0:T(8,128)(2,1)} %param.7), channel_id=1, source_target_pairs={{0,1},{1,0},{2,3},{3,2},{4,5},{5,4},{6,7},{7,6},{8,9},{9,8},{10,11... | collective-permute-start | bytes 2211848 | tf_op jit(solution)/shard_map/ppermute | solution.py:91
  16.1 9.3 %collective-permute-start.3 = (bf16[1152,128]{1,0:T(8,128)(2,1)}, bf16[1152,128]{1,0:T(8,128)(2,1)}, u32[]{:S(2)}, u32[]{:S(2)}) collective-permute-start(bf16[1152,128]{1,0:T(8,128)(2,1)} %collective-permute-done.1), channel_id=1, source_target_pairs={{0,2},{2,4},{4,6},{6,8},{8,10},{10,12},{12,14},{14,0},{1,3},{3,5},... | collective-permute-start | bytes 884744 | tf_op jit(solution)/shard_map/ppermute | solution.py:82
  19.1 8.5 %collective-permute-start.4 = (bf16[1152,128]{1,0:T(8,128)(2,1)}, bf16[1152,128]{1,0:T(8,128)(2,1)S(1)}, u32[]{:S(2)}, u32[]{:S(2)}) collective-permute-start(bf16[1152,128]{1,0:T(8,128)(2,1)} %collective-permute-done.2), channel_id=1, source_target_pairs={{0,14},{2,0},{4,2},{6,4},{8,6},{10,8},{12,10},{14,12},{1,15},{3,1}... | collective-permute-start | bytes 884744 | tf_op jit(solution)/shard_map/ppermute | solution.py:85
  25.4 14.8 %collective-permute-start.5 = (bf16[1152,128]{1,0:T(8,128)(2,1)}, bf16[1152,128]{1,0:T(8,128)(2,1)}, u32[]{:S(2)}, u32[]{:S(2)}) collective-permute-start(bf16[1152,128]{1,0:T(8,128)(2,1)} %collective-permute-done.3), channel_id=1, source_target_pairs={{0,2},{2,4},{4,6},{6,8},{8,10},{10,12},{12,14},{14,0},{1,3},{3,5},... | collective-permute-start | bytes 884744 | tf_op jit(solution)/shard_map/ppermute | solution.py:82
  27.6 16.2 %collective-permute-start.6 = (bf16[1152,128]{1,0:T(8,128)(2,1)S(1)}, bf16[1152,128]{1,0:T(8,128)(2,1)}, u32[]{:S(2)}, u32[]{:S(2)}) collective-permute-start(bf16[1152,128]{1,0:T(8,128)(2,1)S(1)} %collective-permute-done.4), channel_id=1, source_target_pairs={{0,14},{2,0},{4,2},{6,4},{8,6},{10,8},{12,10},{14,12},{1,15},{3,1}... | collective-permute-start | bytes 884744 | tf_op jit(solution)/shard_map/ppermute | solution.py:85
  34.0 1.4 copy-start
  40.2 8.9 %collective-permute-start.7 = (bf16[1152,128]{1,0:T(8,128)(2,1)}, bf16[1152,128]{1,0:T(8,128)(2,1)S(1)}, u32[]{:S(2)}, u32[]{:S(2)}) collective-permute-start(bf16[1152,128]{1,0:T(8,128)(2,1)} %collective-permute-done.5), channel_id=1, source_target_pairs={{0,2},{2,4},{4,6},{6,8},{8,10},{10,12},{12,14},{14,0},{1,3},{3,5},... | collective-permute-start | bytes 884744 | tf_op jit(solution)/shard_map/ppermute | solution.py:82
  61.0 11.0 %collective-permute-start.8 = (f32[320,8,128]{2,0,1:T(8,128)S(1)}, f32[320,8,128]{2,0,1:T(8,128)S(1)}, u32[]{:S(2)}, u32[]{:S(2)}) collective-permute-start(f32[320,8,128]{2,0,1:T(8,128)S(1)} %bitcast.137), channel_id=1, source_target_pairs={{0,16},{16,0},{1,17},{17,1},{2,18},{18,2},{3,19},{19,3},{4,20},{20... | collective-permute-start | bytes 3932168 | tf_op jit(solution)/shard_map/ppermute | solution.py:59
  72.3 23.5 %copy-start.3 = (s32[1,32]{1,0:T(1,128)S(1)}, s32[1,32]{1,0:T(1,128)}, u32[]{:S(2)}) copy-start(s32[1,32]{1,0:T(1,128)} %param.12) | copy-start | bytes 388
  72.3 17.8 %collective-permute-start.9 = (f32[160,8,128]{2,0,1:T(8,128)S(1)}, f32[160,8,128]{2,0,1:T(8,128)S(1)}, u32[]{:S(2)}, u32[]{:S(2)}) collective-permute-start(f32[160,8,128]{2,0,1:T(8,128)S(1)} %slice.63), channel_id=1, source_target_pairs={{0,32},{32,0},{1,33},{33,1},{2,34},{34,2},{3,35},{35,3},{4,36},{36... | collective-permute-start | bytes 1966088 | tf_op jit(solution)/shard_map/ppermute | solution.py:59
  91.0 25.3 %all-to-all-start = ((f32[160,8,128]{2,0,1:T(8,128)}), f32[160,8,128]{2,0,1:T(8,128)S(1)}, u32[]{:S(2)}, u32[]{:S(2)}) async-start(f32[160,8,128]{2,0,1:T(8,128)} %slice_add_fusion), calls=%async_computation | async-start | bytes 1310720 | tf_op jit(solution)/shard_map/all_to_all | solution.py:142
  117.0 43.5 %copy-start.2 = (f32[160,128]{1,0:T(8,128)S(1)}, f32[160,128]{1,0:T(8,128)}, u32[]{:S(2)}) copy-start(f32[160,128]{1,0:T(8,128)} %param.13) | copy-start | bytes 245764
  117.1 11.4 %collective-permute-start.10 = (f32[16,40,128]{2,1,0:T(8,128)S(1)}, f32[16,40,128]{2,1,0:T(8,128)S(1)}, u32[]{:S(2)}, u32[]{:S(2)}) collective-permute-start(f32[16,40,128]{2,1,0:T(8,128)S(1)} %slice.65), channel_id=1, source_target_pairs={{0,64},{64,0},{128,192},{192,128},{256,320},{320,256},{384,448},{4... | collective-permute-start | bytes 983048 | tf_op jit(solution)/shard_map/ppermute | solution.py:66
  128.6 13.1 %collective-permute-start.11 = (f32[8,40,128]{2,1,0:T(8,128)S(1)}, f32[8,40,128]{2,1,0:T(8,128)S(1)}, u32[]{:S(2)}, u32[]{:S(2)}) collective-permute-start(f32[8,40,128]{2,1,0:T(8,128)S(1)} %slice.67), channel_id=1, source_target_pairs={{0,128},{64,192},{128,0},{192,64},{256,384},{320,448},{384,256},{4... | collective-permute-start | bytes 491528 | tf_op jit(solution)/shard_map/ppermute | solution.py:66
  141.7 10.0 %collective-permute-start.12 = (f32[4,40,128]{2,1,0:T(8,128)S(1)}, f32[4,40,128]{2,1,0:T(8,128)S(1)}, u32[]{:S(2)}, u32[]{:S(2)}) collective-permute-start(f32[4,40,128]{2,1,0:T(8,128)S(1)} %slice.69), channel_id=1, source_target_pairs={{0,256},{64,320},{128,384},{192,448},{256,0},{320,64},{384,128},{4... | collective-permute-start | bytes 245768 | tf_op jit(solution)/shard_map/ppermute | solution.py:66
  166.9 4.7 %collective-permute-start.13 = (bf16[160,128]{1,0:T(8,128)(2,1)S(1)}, bf16[160,128]{1,0:T(8,128)(2,1)S(1)}, u32[]{:S(2)}, u32[]{:S(2)}) collective-permute-start(bf16[160,128]{1,0:T(8,128)(2,1)S(1)} %get-tuple-element.19), channel_id=1, source_target_pairs={{0,64},{64,0},{128,192},{192,128},{256,320},{320,256},{384,448},{4... | collective-permute-start | bytes 122888 | tf_op jit(solution)/shard_map/ppermute | solution.py:72
  171.6 6.8 %collective-permute-start.14 = (bf16[320,128]{1,0:T(8,128)(2,1)S(1)}, bf16[320,128]{1,0:T(8,128)(2,1)S(1)}, u32[]{:S(2)}, u32[]{:S(2)}) collective-permute-start(bf16[320,128]{1,0:T(8,128)(2,1)S(1)} %pad_maximum_fusion.3), channel_id=1, source_target_pairs={{0,128},{64,192},{128,0},{192,64},{256,384},{320,448},{384,256},{4... | collective-permute-start | bytes 245768 | tf_op jit(solution)/shard_map/ppermute | solution.py:72
  178.4 10.1 %collective-permute-start.15 = (bf16[640,128]{1,0:T(8,128)(2,1)S(1)}, bf16[640,128]{1,0:T(8,128)(2,1)S(1)}, u32[]{:S(2)}, u32[]{:S(2)}) collective-permute-start(bf16[640,128]{1,0:T(8,128)(2,1)S(1)} %pad_maximum_fusion.2), channel_id=1, source_target_pairs={{0,256},{64,320},{128,384},{192,448},{256,0},{320,64},{384,128},{4... | collective-permute-start | bytes 491528 | tf_op jit(solution)/shard_map/ppermute | solution.py:72
  188.5 7.8 %collective-permute-start.16 = (bf16[1280,128]{1,0:T(8,128)(2,1)S(1)}, bf16[1280,128]{1,0:T(8,128)(2,1)S(1)}, u32[]{:S(2)}, u32[]{:S(2)}) collective-permute-start(bf16[1280,128]{1,0:T(8,128)(2,1)S(1)} %pad_maximum_fusion.1), channel_id=1, source_target_pairs={{0,32},{32,0},{1,33},{33,1},{2,34},{34,2},{3,35},{35,3},{4,36},{36... | collective-permute-start | bytes 983048 | tf_op jit(solution)/shard_map/ppermute | solution.py:91
  196.4 10.1 %collective-permute-start.17 = (bf16[2560,128]{1,0:T(8,128)(2,1)S(1)}, bf16[2560,128]{1,0:T(8,128)(2,1)S(1)}, u32[]{:S(2)}, u32[]{:S(2)}) collective-permute-start(bf16[2560,128]{1,0:T(8,128)(2,1)S(1)} %get-tuple-element.9), channel_id=1, source_target_pairs={{0,16},{16,0},{1,17},{17,1},{2,18},{18,2},{3,19},{19,3},{4,20},{20... | collective-permute-start | bytes 1966088 | tf_op jit(solution)/shard_map/ppermute | solution.py:91

commit v7 on v6

--- a/solution.py
+++ b/solution.py
@@ -142,17 +142,10 @@
     quarters = lax.all_to_all(kept, "y", split_axis=1, concat_axis=0, tiled=True).reshape(
         dp_count, quarter_rows, head_width
     )
-    p = jnp.arange(dp_count, dtype=jnp.int32)
-    per_z = dp_count // z_count
-    flips = (p // half) % 2 + 2 * ((p // quarter) % 2) + 4 * ((p // (quarter // 2)) % 2)
-    owner = per_z * (z ^ flips) + p % per_z
-    in_owner_order = jnp.take(quarters, inverse[0][owner], axis=0)
-    kept = in_owner_order
-    for distance in (1, 2, 4):
-        kept = xor_sum_scatter(kept, "z", distance)
-    local_owners = kept.reshape(per_z * quarter_rows, head_width)
-    own_block = lax.all_to_all(
-        local_owners, ("xl", "c"), split_axis=0, concat_axis=0, tiled=True
+    in_owner_order = jnp.take(quarters, inverse[0], axis=0)
+    from_all = lax.all_to_all(in_owner_order, DP, split_axis=0, concat_axis=0, tiled=True)
+    own_block = jnp.sum(
+        from_all.reshape(z_count, dp_count // z_count, quarter_rows, head_width), axis=0
     ).reshape(block_rows, heads_here, head_width)
 
     previous = momentum.reshape(block_rows, heads_here, head_width)
@@ -164,18 +157,14 @@
         .astype(jnp.bfloat16)
         .reshape(block_rows, heads_here * head_width)
     )
-    gathered = own_update
-    for distance in (1, 2, 4):
-        gathered = xor_gather(gathered, "z", distance)
-    gathered = pair_gather(gathered, "xl")
-    gathered = pair_gather(gathered, "c")
-    d = jnp.arange(dp_count, dtype=jnp.int32)
-    update_position = (
-        jnp.where(d % 2 == c, 0, half) + jnp.where((d // 2) % 2 == xl, 0, quarter) + ((d // 4) ^ z)
+    gathered = lax.all_to_all(
+        jnp.broadcast_to(own_update[None], (dp_count,) + own_update.shape),
+        DP,
+        split_axis=0,
+        concat_axis=0,
+        tiled=True,
     )
-    placed = reorder(
-        gathered.reshape(dp_count, block_rows, heads_here, head_width), update_position[owners]
-    )
+    placed = reorder(gathered.reshape(dp_count, block_rows, heads_here, head_width), owners)
     return (
         placed.reshape(dp_count * block_rows, heads_here * head_width),
         new_momentum.reshape(block_rows, heads_here * head_width),

time: 212 us -> 200 us (0.943)
  starting transfers between devices: 83.4 us -> 48.1 us
  blocking collectives: 8.82 us -> 31.1 us
    all_to_all x0 -> x1, waiting for transfers between devices: none -> 33.3 us  [shards(): lax.all_to_all(jnp.broadcast_to(own_update[None], (dp_count,) + own_updat...]
    ppermute x6 -> x0, starting transfers between devices: 29.6 us -> none  [the longest x3 18 us: xor_sum_scatter(): return blocks[:half] + lax.ppermute(blocks[half:], axis, perm)]
    ppermute x6 -> x0, waiting for transfers between devices: 26.4 us -> none  [the longest x3 16.5 us: xor_sum_scatter(): return blocks[:half] + lax.ppermute(blocks[half:], axis, perm)]
    all_to_all x1, blocking collectives: 8.82 us -> 31.1 us  [shards(): lax.all_to_all(in_owner_order, DP, split_axis=0, concat_axis=0, tiled=True)]
    ppermute x3 -> x1, starting transfers between devices: 15.3 us -> 4.66 us  [pair_gather(): return jnp.concatenate([piece, lax.ppermute(piece, axis, SWAP)], axis=0)]
    ppermute x3 -> x1, waiting for transfers between devices: 6.26 us -> 0.01 us  [pair_gather(): return jnp.concatenate([piece, lax.ppermute(piece, axis, SWAP)], axis=0)]
    all_to_all x0 -> x1, starting transfers between devices: none -> 4.95 us  [shards(): lax.all_to_all(jnp.broadcast_to(own_update[None], (dp_count,) + own_updat...]
    unnamed x18 -> x15, local copies, waits for them, and re-layouts: 8.35 us -> 8.18 us
  transfers between devices with their start and end apart: 19 -> 12, of which waited for: 14 -> 7; matrix products, arithmetic and copies ran while one was open for 6% -> 6% of each run, Pallas kernels for 0% -> 0%
where the time goes in v7:
time: 200 us; the launch traced here: 198 us
  waiting for transfers between devices  76.9 us (38%)
  starting transfers between devices  48.1 us (24%)
  blocking collectives  31.1 us (16%)
  local copies, waits for them, and re-layouts  21.1 us (11%)
  other arithmetic  11.9 us (6%)
  matrix products  7.61 us (4%)
    all_to_all x1, waiting for transfers between devices, shards(): lax.all_to_all(jnp.broadcast_to(own_update[None], (dp_count,) + own_updat...  33.3 us
    all_to_all x1, blocking collectives, shards(): lax.all_to_all(in_owner_order, DP, split_axis=0, concat_axis=0, tiled=True)  31.1 us
    all_to_all x1, waiting for transfers between devices, shards(): lax.all_to_all(kept, 'y', split_axis=1, concat_axis=0, tiled=True)  20.4 us
    ppermute x2, waiting for transfers between devices, pair_sum_scatter(): return blocks[:half] + lax.ppermute(blocks[half:], axis, SWAP)  18.5 us
    ppermute x3, starting transfers between devices, ring_gather(): from_right = lax.ppermute(from_right, axis, to_left)  13.7 us
    ppermute x2, starting transfers between devices, pair_sum_scatter(): return blocks[:half] + lax.ppermute(blocks[half:], axis, SWAP)  10.3 us
    ppermute x4, starting transfers between devices, ring_gather(): from_left = lax.ppermute(from_left, axis, to_right)  9.76 us
    unnamed x15, local copies, waits for them, and re-layouts  8.18 us
  transfers between devices with their start and end apart: 12, of which 7 were waited for; matrix products, arithmetic and copies ran while one was open for 6% of the time, Pallas kernels for 0%

profile of v7, /device:TPU:1, one launch (start us, length us, event | category | flops | bytes accessed | tf_op | source)
XLA Modules:
  0.0 198.4 jit_solution(12754986405989517198)
XLA Ops:
  0.6 0.9 select_reduce_fusion
  1.5 0.7 multiply_multiply_fusion
  2.2 1.2 bitcast_dynamic-update-slice_fusion.7
  3.4 4.0 %collective-permute-start.1 = (bf16[1152,128]{1,0:T(8,128)(2,1)S(1)}, bf16[1152,128]{1,0:T(8,128)(2,1)}, u32[]{:S(2)}, u32[]{:S(2)}) collective-permute-start(bf16[1152,128]{1,0:T(8,128)(2,1)S(1)} %get-tuple-element.6), channel_id=1, source_target_pairs={{0,2},{2,4},{4,6},{6,8},{8,10},{10,12},{12,14},{14,0},{1,3},{3,5},... | collective-permute-start | bytes 884744 | tf_op jit(solution)/shard_map/ppermute | solution.py:82
  7.4 3.8 %collective-permute-start.2 = (bf16[1152,128]{1,0:T(8,128)(2,1)S(1)}, bf16[1152,128]{1,0:T(8,128)(2,1)}, u32[]{:S(2)}, u32[]{:S(2)}) collective-permute-start(bf16[1152,128]{1,0:T(8,128)(2,1)S(1)} %get-tuple-element.6), channel_id=1, source_target_pairs={{0,14},{2,0},{4,2},{6,4},{8,6},{10,8},{12,10},{14,12},{1,15},{3,1}... | collective-permute-start | bytes 884744 | tf_op jit(solution)/shard_map/ppermute | solution.py:85
  11.3 4.7 %collective-permute-start = (bf16[320,1152]{1,0:T(8,128)(2,1)}, bf16[320,1152]{1,0:T(8,128)(2,1)}, u32[]{:S(2)}, u32[]{:S(2)}) collective-permute-start(bf16[320,1152]{1,0:T(8,128)(2,1)} %param.7), channel_id=1, source_target_pairs={{0,1},{1,0},{2,3},{3,2},{4,5},{5,4},{6,7},{7,6},{8,9},{9,8},{10,11... | collective-permute-start | bytes 2211848 | tf_op jit(solution)/shard_map/ppermute | solution.py:91
  15.9 0.1 fusion.51
  16.1 1.9 collective-permute-start.3
  18.1 1.0 bitcast_dynamic-update-slice_fusion.6
  19.1 4.6 %collective-permute-start.4 = (bf16[1152,128]{1,0:T(8,128)(2,1)}, bf16[1152,128]{1,0:T(8,128)(2,1)S(1)}, u32[]{:S(2)}, u32[]{:S(2)}) collective-permute-start(bf16[1152,128]{1,0:T(8,128)(2,1)} %collective-permute-done.2), channel_id=1, source_target_pairs={{0,14},{2,0},{4,2},{6,4},{8,6},{10,8},{12,10},{14,12},{1,15},{3,1}... | collective-permute-start | bytes 884744 | tf_op jit(solution)/shard_map/ppermute | solution.py:85
  23.7 1.0 bitcast_dynamic-update-slice_fusion.5
  24.7 0.7 collective-permute-done.3
  25.4 1.9 collective-permute-start.5
  27.3 0.3 collective-permute-done.4
  27.6 5.3 %collective-permute-start.6 = (bf16[1152,128]{1,0:T(8,128)(2,1)S(1)}, bf16[1152,128]{1,0:T(8,128)(2,1)}, u32[]{:S(2)}, u32[]{:S(2)}) collective-permute-start(bf16[1152,128]{1,0:T(8,128)(2,1)S(1)} %collective-permute-done.4), channel_id=1, source_target_pairs={{0,14},{2,0},{4,2},{6,4},{8,6},{10,8},{12,10},{14,12},{1,15},{3,1}... | collective-permute-start | bytes 884744 | tf_op jit(solution)/shard_map/ppermute | solution.py:85
  33.0 1.0 bitcast_dynamic-update-slice_fusion.4
  34.0 1.4 copy-done
  35.4 1.2 pad_maximum_fusion
  36.7 3.5 %gather_fusion = bf16[640,1152]{1,0:T(8,128)(2,1)} fusion(bf16[640,1152]{1,0:T(8,128)(2,1)S(1)} %pad_maximum_fusion, s32[1024]{0:T(1024)S(1)} %pad_clamp_fusion.3), kind=kCustom, calls=%fused_computation | custom fusion | bytes 2951680 | tf_op jit(solution)/shard_map/jit(_take)/gather | solution.py:136
  40.2 1.9 collective-permute-start.7
  42.1 1.7 bitcast_dynamic-update-slice_fusion.2
  43.8 1.7 bitcast_dynamic-update-slice_fusion.1
  45.5 3.6 %collective-permute-done.7 = bf16[1152,128]{1,0:T(8,128)(2,1)S(1)} collective-permute-done((bf16[1152,128]{1,0:T(8,128)(2,1)}, bf16[1152,128]{1,0:T(8,128)(2,1)S(1)}, u32[]{:S(2)}, u32[]{:S(2)}) %collective-permute-start.7) | collective-permute-done | bytes 294944 | tf_op jit(solution)/shard_map/ppermute | solution.py:82
  49.1 0.7 bitcast_dynamic-update-slice_fusion
  49.8 2.7 %gather_fusion.1 = bf16[8,1152,128]{2,1,0:T(8,128)(2,1)S(1)} fusion(bf16[8,1152,128]{2,1,0:T(8,128)(2,1)} %bitcast_dynamic-update-slice_fusion, s32[1024]{0:T(1024)S(1)} %pad_clamp_fusion.2), kind=kCustom, calls=%fused_computation.1 | custom fusion | bytes 4718624 | tf_op jit(solution)/shard_map/jit(_take)/gather | solution.py:121
  52.5 1.7 select_bitcast_fusion
  54.2 3.0 %copy.14 = bf16[1152,8,128]{0,2,1:T(8,128)(2,1)S(1)} copy(bf16[1152,8,128]{2,0,1:T(8,128)(2,1)} %select_bitcast_fusion) | data formatting | bytes 4718592 | tf_op jit(solution)/shard_map/jit(_take)/select_n | solution.py:121
  57.2 3.3 %fusion = f32[640,1024]{1,0:T(8,128)S(1)} fusion(bf16[1152,1024]{0,1:T(8,128)(2,1)S(1)} %bitcast.131, bf16[640,1152]{1,0:T(8,128)(2,1)} %gather_fusion, pred[640]{0:T(1024)(128)(4,1)S(1)} %compare_and_fusion), kind=kOutput, calls=%fused_computation.6 | convolution fusion | flops 1510686720 | bytes 6455936 | tf_op jit(solution)/shard_map/dot_general | solution.py:137
  60.5 0.3 slice_bitcast_fusion.1
  60.8 0.1 copy.21
  60.9 8.4 %collective-permute-start.8 = (f32[320,8,128]{2,0,1:T(8,128)S(1)}, f32[320,8,128]{2,0,1:T(8,128)S(1)}, u32[]{:S(2)}, u32[]{:S(2)}) collective-permute-start(f32[320,8,128]{2,0,1:T(8,128)S(1)} %bitcast.132), channel_id=1, source_target_pairs={{0,16},{16,0},{1,17},{17,1},{2,18},{18,2},{3,19},{19,3},{4,20},{20... | collective-permute-start | bytes 3932168 | tf_op jit(solution)/shard_map/ppermute | solution.py:59
  69.3 2.6 %collective-permute-done.8 = f32[320,8,128]{2,0,1:T(8,128)S(1)} collective-permute-done((f32[320,8,128]{2,0,1:T(8,128)S(1)}, f32[320,8,128]{2,0,1:T(8,128)S(1)}, u32[]{:S(2)}, u32[]{:S(2)}) %collective-permute-start.8) | collective-permute-done | bytes 1310752 | tf_op jit(solution)/shard_map/ppermute | solution.py:59
  72.0 0.2 bitcast_add_fusion
  72.2 1.9 collective-permute-start.9
  74.1 15.9 %collective-permute-done.9 = f32[160,8,128]{2,0,1:T(8,128)S(1)} collective-permute-done((f32[160,8,128]{2,0,1:T(8,128)S(1)}, f32[160,8,128]{2,0,1:T(8,128)S(1)}, u32[]{:S(2)}, u32[]{:S(2)}) %collective-permute-start.9) | collective-permute-done | bytes 655392 | tf_op jit(solution)/shard_map/ppermute | solution.py:59
  90.0 0.9 slice_add_fusion
  91.0 4.7 %all-to-all-start = ((f32[160,8,128]{2,0,1:T(8,128)}), f32[160,8,128]{2,0,1:T(8,128)S(1)}, u32[]{:S(2)}, u32[]{:S(2)}) async-start(f32[160,8,128]{2,0,1:T(8,128)} %slice_add_fusion), calls=%async_computation | async-start | bytes 1310720 | tf_op jit(solution)/shard_map/all_to_all | solution.py:142
  95.7 0.1 select_reduce_fusion.1
  95.8 20.4 %all-to-all-done = f32[160,8,128]{2,0,1:T(8,128)S(1)} async-done(((f32[160,8,128]{2,0,1:T(8,128)}), f32[160,8,128]{2,0,1:T(8,128)S(1)}, u32[]{:S(2)}, u32[]{:S(2)}) %all-to-all-start) | async-done | bytes 655392 | tf_op jit(solution)/shard_map/all_to_all | solution.py:142
  116.3 0.6 gather_fusion.2
  116.8 0.1 broadcast_select_fusion
  117.0 31.1 %all_to_all.25 = f32[32,40,128]{2,1,0:T(8,128)S(1)} all-to-all(f32[32,40,128]{2,1,0:T(8,128)S(1)} %broadcast_select_fusion), channel_id=1, replica_groups=mesh['z'=8,'xl'=2,'c'=2,'y'=8,'xh'=2] {'z','xl','c'}, dimensions={0} | all-to-all | bytes 1310720 | tf_op jit(solution)/shard_map/all_to_all | solution.py:146
  148.1 1.3 multiply_reduce_fusion
  150.1 0.4 fusion.29
  150.5 0.2 fusion.13
  150.7 0.2 fusion.3
  150.9 0.4 fusion.27
  151.4 0.2 fusion.12
  151.6 0.2 fusion.4
  151.8 0.4 fusion.24
  152.3 0.2 fusion.11
  152.5 0.2 fusion.5
  152.7 0.4 fusion.21
  153.1 0.2 fusion.10
  153.3 0.2 fusion.6
  153.6 0.4 fusion.18
  154.0 0.2 fusion.9
  154.2 0.2 fusion.15
  154.5 1.2 broadcast_in_dim.117
  155.7 5.0 %all-to-all-start.2 = ((bf16[32,160,128]{2,1,0:T(8,128)(2,1)}), bf16[32,160,128]{2,1,0:T(8,128)(2,1)S(1)}, u32[]{:S(2)}, u32[]{:S(2)}) async-start(bf16[32,160,128]{2,1,0:T(8,128)(2,1)} %broadcast_in_dim.117), calls=%async_computation.2 | async-start | bytes 2621440 | tf_op jit(solution)/shard_map/all_to_all | solution.py:160
  160.7 0.1 broadcast_in_dim.98
  160.9 33.3 %all-to-all-done.2 = bf16[32,160,128]{2,1,0:T(8,128)(2,1)S(1)} async-done(((bf16[32,160,128]{2,1,0:T(8,128)(2,1)}), bf16[32,160,128]{2,1,0:T(8,128)(2,1)S(1)}, u32[]{:S(2)}, u32[]{:S(2)}) %all-to-all-start.2) | async-done | bytes 1310752 | tf_op jit(solution)/shard_map/all_to_all | solution.py:160
  194.2 0.8 gather_fusion.3
  195.0 3.4 %bitcast_select_fusion = bf16[5120,128]{1,0:T(8,128)(2,1)} fusion(bf16[32,160,128]{2,1,0:T(8,128)(2,1)S(1)} %gather_fusion.3, pred[5120]{0:T(1024)(128)(4,1)S(1)} %broadcast_in_dim.98), kind=kLoop, calls=%fused_computation.13 | loop fusion | flops 655360 | bytes 2626560 | tf_op jit(solution)/shard_map/jit(take_along_axis)/select_n | solution.py:38
  (27 shorter events, 0.4 us)
Async XLA Ops:
  0.6 34.8 %copy-start.1 = (bf16[320,1152]{1,0:T(8,128)(2,1)S(1)}, bf16[320,1152]{1,0:T(8,128)(2,1)}, u32[]{:S(2)}) copy-start(bf16[320,1152]{1,0:T(8,128)(2,1)} %param.7) | copy-start | bytes 2211844
  3.4 12.7 %collective-permute-start.1 = (bf16[1152,128]{1,0:T(8,128)(2,1)S(1)}, bf16[1152,128]{1,0:T(8,128)(2,1)}, u32[]{:S(2)}, u32[]{:S(2)}) collective-permute-start(bf16[1152,128]{1,0:T(8,128)(2,1)S(1)} %get-tuple-element.6), channel_id=1, source_target_pairs={{0,2},{2,4},{4,6},{6,8},{8,10},{10,12},{12,14},{14,0},{1,3},{3,5},... | collective-permute-start | bytes 884744 | tf_op jit(solution)/shard_map/ppermute | solution.py:82
  7.4 11.7 %collective-permute-start.2 = (bf16[1152,128]{1,0:T(8,128)(2,1)S(1)}, bf16[1152,128]{1,0:T(8,128)(2,1)}, u32[]{:S(2)}, u32[]{:S(2)}) collective-permute-start(bf16[1152,128]{1,0:T(8,128)(2,1)S(1)} %get-tuple-element.6), channel_id=1, source_target_pairs={{0,14},{2,0},{4,2},{6,4},{8,6},{10,8},{12,10},{14,12},{1,15},{3,1}... | collective-permute-start | bytes 884744 | tf_op jit(solution)/shard_map/ppermute | solution.py:85
  11.3 24.2 %collective-permute-start = (bf16[320,1152]{1,0:T(8,128)(2,1)}, bf16[320,1152]{1,0:T(8,128)(2,1)}, u32[]{:S(2)}, u32[]{:S(2)}) collective-permute-start(bf16[320,1152]{1,0:T(8,128)(2,1)} %param.7), channel_id=1, source_target_pairs={{0,1},{1,0},{2,3},{3,2},{4,5},{5,4},{6,7},{7,6},{8,9},{9,8},{10,11... | collective-permute-start | bytes 2211848 | tf_op jit(solution)/shard_map/ppermute | solution.py:91
  16.1 9.3 %collective-permute-start.3 = (bf16[1152,128]{1,0:T(8,128)(2,1)}, bf16[1152,128]{1,0:T(8,128)(2,1)}, u32[]{:S(2)}, u32[]{:S(2)}) collective-permute-start(bf16[1152,128]{1,0:T(8,128)(2,1)} %collective-permute-done.1), channel_id=1, source_target_pairs={{0,2},{2,4},{4,6},{6,8},{8,10},{10,12},{12,14},{14,0},{1,3},{3,5},... | collective-permute-start | bytes 884744 | tf_op jit(solution)/shard_map/ppermute | solution.py:82
  19.1 8.5 %collective-permute-start.4 = (bf16[1152,128]{1,0:T(8,128)(2,1)}, bf16[1152,128]{1,0:T(8,128)(2,1)S(1)}, u32[]{:S(2)}, u32[]{:S(2)}) collective-permute-start(bf16[1152,128]{1,0:T(8,128)(2,1)} %collective-permute-done.2), channel_id=1, source_target_pairs={{0,14},{2,0},{4,2},{6,4},{8,6},{10,8},{12,10},{14,12},{1,15},{3,1}... | collective-permute-start | bytes 884744 | tf_op jit(solution)/shard_map/ppermute | solution.py:85
  25.4 14.8 %collective-permute-start.5 = (bf16[1152,128]{1,0:T(8,128)(2,1)}, bf16[1152,128]{1,0:T(8,128)(2,1)}, u32[]{:S(2)}, u32[]{:S(2)}) collective-permute-start(bf16[1152,128]{1,0:T(8,128)(2,1)} %collective-permute-done.3), channel_id=1, source_target_pairs={{0,2},{2,4},{4,6},{6,8},{8,10},{10,12},{12,14},{14,0},{1,3},{3,5},... | collective-permute-start | bytes 884744 | tf_op jit(solution)/shard_map/ppermute | solution.py:82
  27.6 16.2 %collective-permute-start.6 = (bf16[1152,128]{1,0:T(8,128)(2,1)S(1)}, bf16[1152,128]{1,0:T(8,128)(2,1)}, u32[]{:S(2)}, u32[]{:S(2)}) collective-permute-start(bf16[1152,128]{1,0:T(8,128)(2,1)S(1)} %collective-permute-done.4), channel_id=1, source_target_pairs={{0,14},{2,0},{4,2},{6,4},{8,6},{10,8},{12,10},{14,12},{1,15},{3,1}... | collective-permute-start | bytes 884744 | tf_op jit(solution)/shard_map/ppermute | solution.py:85
  34.0 1.4 copy-start
  40.2 8.9 %collective-permute-start.7 = (bf16[1152,128]{1,0:T(8,128)(2,1)}, bf16[1152,128]{1,0:T(8,128)(2,1)S(1)}, u32[]{:S(2)}, u32[]{:S(2)}) collective-permute-start(bf16[1152,128]{1,0:T(8,128)(2,1)} %collective-permute-done.5), channel_id=1, source_target_pairs={{0,2},{2,4},{4,6},{6,8},{8,10},{10,12},{12,14},{14,0},{1,3},{3,5},... | collective-permute-start | bytes 884744 | tf_op jit(solution)/shard_map/ppermute | solution.py:82
  60.9 11.0 %collective-permute-start.8 = (f32[320,8,128]{2,0,1:T(8,128)S(1)}, f32[320,8,128]{2,0,1:T(8,128)S(1)}, u32[]{:S(2)}, u32[]{:S(2)}) collective-permute-start(f32[320,8,128]{2,0,1:T(8,128)S(1)} %bitcast.132), channel_id=1, source_target_pairs={{0,16},{16,0},{1,17},{17,1},{2,18},{18,2},{3,19},{19,3},{4,20},{20... | collective-permute-start | bytes 3932168 | tf_op jit(solution)/shard_map/ppermute | solution.py:59
  72.1 23.5 %copy-start.3 = (s32[1,32]{1,0:T(1,128)S(1)}, s32[1,32]{1,0:T(1,128)}, u32[]{:S(2)}) copy-start(s32[1,32]{1,0:T(1,128)} %param.12) | copy-start | bytes 388
  72.2 17.8 %collective-permute-start.9 = (f32[160,8,128]{2,0,1:T(8,128)S(1)}, f32[160,8,128]{2,0,1:T(8,128)S(1)}, u32[]{:S(2)}, u32[]{:S(2)}) collective-permute-start(f32[160,8,128]{2,0,1:T(8,128)S(1)} %slice.35), channel_id=1, source_target_pairs={{0,32},{32,0},{1,33},{33,1},{2,34},{34,2},{3,35},{35,3},{4,36},{36... | collective-permute-start | bytes 1966088 | tf_op jit(solution)/shard_map/ppermute | solution.py:59
  91.0 25.3 %all-to-all-start = ((f32[160,8,128]{2,0,1:T(8,128)}), f32[160,8,128]{2,0,1:T(8,128)S(1)}, u32[]{:S(2)}, u32[]{:S(2)}) async-start(f32[160,8,128]{2,0,1:T(8,128)} %slice_add_fusion), calls=%async_computation | async-start | bytes 1310720 | tf_op jit(solution)/shard_map/all_to_all | solution.py:142
  95.7 52.5 %copy-start.2 = (f32[160,128]{1,0:T(8,128)S(1)}, f32[160,128]{1,0:T(8,128)}, u32[]{:S(2)}) copy-start(f32[160,128]{1,0:T(8,128)} %param.13) | copy-start | bytes 245764
  155.7 38.5 %all-to-all-start.2 = ((bf16[32,160,128]{2,1,0:T(8,128)(2,1)}), bf16[32,160,128]{2,1,0:T(8,128)(2,1)S(1)}, u32[]{:S(2)}, u32[]{:S(2)}) async-start(bf16[32,160,128]{2,1,0:T(8,128)(2,1)} %broadcast_in_dim.117), calls=%async_computation.2 | async-start | bytes 2621440 | tf_op jit(solution)/shard_map/all_to_all | solution.py:160

commit v8 on v7

--- a/solution.py
+++ b/solution.py
@@ -142,10 +142,14 @@
     quarters = lax.all_to_all(kept, "y", split_axis=1, concat_axis=0, tiled=True).reshape(
         dp_count, quarter_rows, head_width
     )
+    per_z = dp_count // z_count
     in_owner_order = jnp.take(quarters, inverse[0], axis=0)
-    from_all = lax.all_to_all(in_owner_order, DP, split_axis=0, concat_axis=0, tiled=True)
-    own_block = jnp.sum(
-        from_all.reshape(z_count, dp_count // z_count, quarter_rows, head_width), axis=0
+    from_z = lax.all_to_all(in_owner_order, "z", split_axis=0, concat_axis=0, tiled=True)
+    local_owners = jnp.sum(
+        from_z.reshape(z_count, per_z * quarter_rows, head_width), axis=0
+    )
+    own_block = lax.all_to_all(
+        local_owners, ("xl", "c"), split_axis=0, concat_axis=0, tiled=True
     ).reshape(block_rows, heads_here, head_width)
 
     previous = momentum.reshape(block_rows, heads_here, head_width)
@@ -158,13 +162,21 @@
         .reshape(block_rows, heads_here * head_width)
     )
     gathered = lax.all_to_all(
-        jnp.broadcast_to(own_update[None], (dp_count,) + own_update.shape),
-        DP,
+        jnp.broadcast_to(own_update[None], (z_count,) + own_update.shape),
+        "z",
         split_axis=0,
         concat_axis=0,
         tiled=True,
+    ).reshape(z_count * block_rows, heads_here * head_width)
+    gathered = pair_gather(gathered, "xl")
+    gathered = pair_gather(gathered, "c")
+    d = jnp.arange(dp_count, dtype=jnp.int32)
+    update_position = (
+        jnp.where(d % 2 == c, 0, half) + jnp.where((d // 2) % 2 == xl, 0, quarter) + d // 4
     )
-    placed = reorder(gathered.reshape(dp_count, block_rows, heads_here, head_width), owners)
+    placed = reorder(
+        gathered.reshape(dp_count, block_rows, heads_here, head_width), update_position[owners]
+    )
     return (
         placed.reshape(dp_count * block_rows, heads_here * head_width),
         new_momentum.reshape(block_rows, heads_here * head_width),

time: 200 us -> 196 us (0.980)
  waiting for transfers between devices: 76.9 us -> 50.7 us
  blocking collectives: 31.1 us -> 51.4 us
  starting transfers between devices: 48.1 us -> 50.6 us
    all_to_all x1 -> x0, waiting for transfers between devices: 33.3 us -> none  [shards(): lax.all_to_all(jnp.broadcast_to(own_update[None], (dp_count,) + own_updat...]
    all_to_all x1 -> x3, blocking collectives: 31.1 us -> 51.4 us  [the longest x1 29 us: shards(): lax.all_to_all(in_owner_order, 'z', split_axis=0, concat_axis=0, tiled=True)]
    ppermute x1 -> x3, starting transfers between devices: 4.66 us -> 12.2 us  [pair_gather(): return jnp.concatenate([piece, lax.ppermute(piece, axis, SWAP)], axis=0)]
    ppermute x1 -> x3, waiting for transfers between devices: 0.01 us -> 7.13 us  [pair_gather(): return jnp.concatenate([piece, lax.ppermute(piece, axis, SWAP)], axis=0)]
    all_to_all x1 -> x0, starting transfers between devices: 4.95 us -> none  [shards(): lax.all_to_all(jnp.broadcast_to(own_update[None], (dp_count,) + own_updat...]
  transfers between devices with their start and end apart: 12 -> 13, of which waited for: 7 -> 8; matrix products, arithmetic and copies ran while one was open for 6% -> 6% of each run, Pallas kernels for 0% -> 0%
where the time goes in v8:
time: 196 us; the launch traced here: 195 us
  blocking collectives  51.4 us (26%)
  waiting for transfers between devices  50.7 us (26%)
  starting transfers between devices  50.6 us (26%)
  local copies, waits for them, and re-layouts  20.6 us (11%)
  other arithmetic  12.1 us (6%)
  matrix products  7.61 us (4%)
    all_to_all x1, blocking collectives, shards(): lax.all_to_all(in_owner_order, 'z', split_axis=0, concat_axis=0, tiled=True)  29 us
    all_to_all x1, waiting for transfers between devices, shards(): lax.all_to_all(kept, 'y', split_axis=1, concat_axis=0, tiled=True)  20.4 us
    ppermute x2, waiting for transfers between devices, pair_sum_scatter(): return blocks[:half] + lax.ppermute(blocks[half:], axis, SWAP)  18.5 us
    all_to_all x1, blocking collectives, shards(): lax.all_to_all(jnp.broadcast_to(own_update[None], (z_count,) + own_update...  14.6 us
    ppermute x3, starting transfers between devices, ring_gather(): from_right = lax.ppermute(from_right, axis, to_left)  13.7 us
    ppermute x3, starting transfers between devices, pair_gather(): return jnp.concatenate([piece, lax.ppermute(piece, axis, SWAP)], axis=0)  12.2 us
    ppermute x2, starting transfers between devices, pair_sum_scatter(): return blocks[:half] + lax.ppermute(blocks[half:], axis, SWAP)  10.3 us
    ppermute x4, starting transfers between devices, ring_gather(): from_left = lax.ppermute(from_left, axis, to_right)  9.76 us
  transfers between devices with their start and end apart: 13, of which 8 were waited for; matrix products, arithmetic and copies ran while one was open for 6% of the time, Pallas kernels for 0%

profile of v8, /device:TPU:1, one launch (start us, length us, event | category | flops | bytes accessed | tf_op | source)
XLA Modules:
  0.0 194.7 jit_solution(15236862396616945664)
XLA Ops:
  0.6 0.9 select_reduce_fusion
  1.5 0.7 multiply_multiply_fusion
  2.2 1.2 bitcast_dynamic-update-slice_fusion.7
  3.4 4.0 %collective-permute-start.1 = (bf16[1152,128]{1,0:T(8,128)(2,1)S(1)}, bf16[1152,128]{1,0:T(8,128)(2,1)}, u32[]{:S(2)}, u32[]{:S(2)}) collective-permute-start(bf16[1152,128]{1,0:T(8,128)(2,1)S(1)} %get-tuple-element.6), channel_id=1, source_target_pairs={{0,2},{2,4},{4,6},{6,8},{8,10},{10,12},{12,14},{14,0},{1,3},{3,5},... | collective-permute-start | bytes 884744 | tf_op jit(solution)/shard_map/ppermute | solution.py:82
  7.4 3.8 %collective-permute-start.2 = (bf16[1152,128]{1,0:T(8,128)(2,1)S(1)}, bf16[1152,128]{1,0:T(8,128)(2,1)}, u32[]{:S(2)}, u32[]{:S(2)}) collective-permute-start(bf16[1152,128]{1,0:T(8,128)(2,1)S(1)} %get-tuple-element.6), channel_id=1, source_target_pairs={{0,14},{2,0},{4,2},{6,4},{8,6},{10,8},{12,10},{14,12},{1,15},{3,1}... | collective-permute-start | bytes 884744 | tf_op jit(solution)/shard_map/ppermute | solution.py:85
  11.3 4.7 %collective-permute-start = (bf16[320,1152]{1,0:T(8,128)(2,1)}, bf16[320,1152]{1,0:T(8,128)(2,1)}, u32[]{:S(2)}, u32[]{:S(2)}) collective-permute-start(bf16[320,1152]{1,0:T(8,128)(2,1)} %param.7), channel_id=1, source_target_pairs={{0,1},{1,0},{2,3},{3,2},{4,5},{5,4},{6,7},{7,6},{8,9},{9,8},{10,11... | collective-permute-start | bytes 2211848 | tf_op jit(solution)/shard_map/ppermute | solution.py:91
  16.1 1.9 collective-permute-start.3
  18.1 1.0 bitcast_dynamic-update-slice_fusion.6
  19.1 4.6 %collective-permute-start.4 = (bf16[1152,128]{1,0:T(8,128)(2,1)}, bf16[1152,128]{1,0:T(8,128)(2,1)S(1)}, u32[]{:S(2)}, u32[]{:S(2)}) collective-permute-start(bf16[1152,128]{1,0:T(8,128)(2,1)} %collective-permute-done.2), channel_id=1, source_target_pairs={{0,14},{2,0},{4,2},{6,4},{8,6},{10,8},{12,10},{14,12},{1,15},{3,1}... | collective-permute-start | bytes 884744 | tf_op jit(solution)/shard_map/ppermute | solution.py:85
  23.7 1.0 bitcast_dynamic-update-slice_fusion.5
  24.7 0.7 collective-permute-done.3
  25.4 1.9 collective-permute-start.5
  27.3 0.3 collective-permute-done.4
  27.6 5.3 %collective-permute-start.6 = (bf16[1152,128]{1,0:T(8,128)(2,1)S(1)}, bf16[1152,128]{1,0:T(8,128)(2,1)}, u32[]{:S(2)}, u32[]{:S(2)}) collective-permute-start(bf16[1152,128]{1,0:T(8,128)(2,1)S(1)} %collective-permute-done.4), channel_id=1, source_target_pairs={{0,14},{2,0},{4,2},{6,4},{8,6},{10,8},{12,10},{14,12},{1,15},{3,1}... | collective-permute-start | bytes 884744 | tf_op jit(solution)/shard_map/ppermute | solution.py:85
  33.0 1.0 bitcast_dynamic-update-slice_fusion.4
  34.0 1.4 copy-done
  35.4 1.2 pad_maximum_fusion
  36.7 3.5 %gather_fusion.1 = bf16[640,1152]{1,0:T(8,128)(2,1)} fusion(bf16[640,1152]{1,0:T(8,128)(2,1)S(1)} %pad_maximum_fusion, s32[1024]{0:T(1024)S(1)} %pad_clamp_fusion.3), kind=kCustom, calls=%fused_computation.1 | custom fusion | bytes 2951680 | tf_op jit(solution)/shard_map/jit(_take)/gather | solution.py:136
  40.2 1.9 collective-permute-start.7
  42.1 1.7 bitcast_dynamic-update-slice_fusion.2
  43.8 1.7 bitcast_dynamic-update-slice_fusion.1
  45.5 3.6 %collective-permute-done.7 = bf16[1152,128]{1,0:T(8,128)(2,1)S(1)} collective-permute-done((bf16[1152,128]{1,0:T(8,128)(2,1)}, bf16[1152,128]{1,0:T(8,128)(2,1)S(1)}, u32[]{:S(2)}, u32[]{:S(2)}) %collective-permute-start.7) | collective-permute-done | bytes 294944 | tf_op jit(solution)/shard_map/ppermute | solution.py:82
  49.1 0.7 bitcast_dynamic-update-slice_fusion
  49.8 2.7 %gather_fusion.2 = bf16[8,1152,128]{2,1,0:T(8,128)(2,1)S(1)} fusion(bf16[8,1152,128]{2,1,0:T(8,128)(2,1)} %bitcast_dynamic-update-slice_fusion, s32[1024]{0:T(1024)S(1)} %pad_clamp_fusion.2), kind=kCustom, calls=%fused_computation.2 | custom fusion | bytes 4718624 | tf_op jit(solution)/shard_map/jit(_take)/gather | solution.py:121
  52.5 1.7 select_bitcast_fusion
  54.2 3.0 %copy.14 = bf16[1152,8,128]{0,2,1:T(8,128)(2,1)S(1)} copy(bf16[1152,8,128]{2,0,1:T(8,128)(2,1)} %select_bitcast_fusion) | data formatting | bytes 4718592 | tf_op jit(solution)/shard_map/jit(_take)/select_n | solution.py:121
  57.2 3.3 %fusion = f32[640,1024]{1,0:T(8,128)S(1)} fusion(bf16[1152,1024]{0,1:T(8,128)(2,1)S(1)} %bitcast.141, bf16[640,1152]{1,0:T(8,128)(2,1)} %gather_fusion.1, pred[640]{0:T(1024)(128)(4,1)S(1)} %compare_and_fusion), kind=kOutput, calls=%fused_computation.7 | convolution fusion | flops 1510686720 | bytes 6455936 | tf_op jit(solution)/shard_map/dot_general | solution.py:137
  60.5 0.3 slice_bitcast_fusion.1
  60.9 8.4 %collective-permute-start.8 = (f32[320,8,128]{2,0,1:T(8,128)S(1)}, f32[320,8,128]{2,0,1:T(8,128)S(1)}, u32[]{:S(2)}, u32[]{:S(2)}) collective-permute-start(f32[320,8,128]{2,0,1:T(8,128)S(1)} %bitcast.142), channel_id=1, source_target_pairs={{0,16},{16,0},{1,17},{17,1},{2,18},{18,2},{3,19},{19,3},{4,20},{20... | collective-permute-start | bytes 3932168 | tf_op jit(solution)/shard_map/ppermute | solution.py:59
  69.3 2.6 %collective-permute-done.8 = f32[320,8,128]{2,0,1:T(8,128)S(1)} collective-permute-done((f32[320,8,128]{2,0,1:T(8,128)S(1)}, f32[320,8,128]{2,0,1:T(8,128)S(1)}, u32[]{:S(2)}, u32[]{:S(2)}) %collective-permute-start.8) | collective-permute-done | bytes 1310752 | tf_op jit(solution)/shard_map/ppermute | solution.py:59
  72.0 0.2 bitcast_add_fusion
  72.2 1.9 collective-permute-start.9
  74.1 15.9 %collective-permute-done.9 = f32[160,8,128]{2,0,1:T(8,128)S(1)} collective-permute-done((f32[160,8,128]{2,0,1:T(8,128)S(1)}, f32[160,8,128]{2,0,1:T(8,128)S(1)}, u32[]{:S(2)}, u32[]{:S(2)}) %collective-permute-start.9) | collective-permute-done | bytes 655392 | tf_op jit(solution)/shard_map/ppermute | solution.py:59
  90.0 0.9 slice_add_fusion
  91.0 4.7 %all-to-all-start = ((f32[160,8,128]{2,0,1:T(8,128)}), f32[160,8,128]{2,0,1:T(8,128)S(1)}, u32[]{:S(2)}, u32[]{:S(2)}) async-start(f32[160,8,128]{2,0,1:T(8,128)} %slice_add_fusion), calls=%async_computation | async-start | bytes 1310720 | tf_op jit(solution)/shard_map/all_to_all | solution.py:142
  95.7 0.1 select_reduce_fusion.1
  95.8 20.4 %all-to-all-done = f32[160,8,128]{2,0,1:T(8,128)S(1)} async-done(((f32[160,8,128]{2,0,1:T(8,128)}), f32[160,8,128]{2,0,1:T(8,128)S(1)}, u32[]{:S(2)}, u32[]{:S(2)}) %all-to-all-start) | async-done | bytes 655392 | tf_op jit(solution)/shard_map/all_to_all | solution.py:142
  116.3 0.6 gather_fusion.3
  117.0 29.0 %all_to_all.37 = f32[32,40,128]{2,1,0:T(8,128)S(1)} all-to-all(f32[32,40,128]{2,1,0:T(8,128)S(1)} %broadcast_select_fusion), channel_id=1, replica_groups=mesh['z'=8,'xl'=2,'c'=2,'y'=8,'xh'=2] {'z'}, dimensions={0} | all-to-all | bytes 1310720 | tf_op jit(solution)/shard_map/all_to_all | solution.py:147
  146.0 7.7 %all_to_all.38 = f32[4,40,128]{2,1,0:T(8,128)S(1)} all-to-all(f32[4,40,128]{2,1,0:T(8,128)S(1)} %bitcast.143), channel_id=1, replica_groups=mesh['z'=8,'xl'=2,'c'=2,'y'=8,'xh'=2] {'xl','c'}, dimensions={0} | all-to-all | bytes 163840 | tf_op jit(solution)/shard_map/all_to_all | solution.py:151
  153.8 1.3 multiply_reduce_fusion
  155.7 0.4 fusion.29
  156.2 0.2 fusion.13
  156.4 0.2 fusion.3
  156.6 0.4 fusion.27
  157.0 0.2 fusion.12
  157.2 0.2 fusion.4
  157.5 0.4 fusion.24
  157.9 0.2 fusion.11
  158.1 0.2 fusion.5
  158.4 0.4 fusion.21
  158.8 0.2 fusion.10
  159.0 0.2 fusion.6
  159.2 0.4 fusion.18
  159.7 0.2 fusion.9
  159.9 0.2 fusion.15
  160.2 14.6 %all_to_all.39 = bf16[8,160,128]{2,1,0:T(8,128)(2,1)S(1)} all-to-all(bf16[8,160,128]{2,1,0:T(8,128)(2,1)S(1)} %broadcast_in_dim.133), channel_id=1, replica_groups=mesh['z'=8,'xl'=2,'c'=2,'y'=8,'xh'=2] {'z'}, dimensions={0} | all-to-all | bytes 655360 | tf_op jit(solution)/shard_map/all_to_all | solution.py:164
  174.8 2.8 %collective-permute-start.10 = (bf16[1280,128]{1,0:T(8,128)(2,1)S(1)}, bf16[1280,128]{1,0:T(8,128)(2,1)S(1)}, u32[]{:S(2)}, u32[]{:S(2)}) collective-permute-start(bf16[1280,128]{1,0:T(8,128)(2,1)S(1)} %bitcast.136), channel_id=1, source_target_pairs={{0,32},{32,0},{1,33},{33,1},{2,34},{34,2},{3,35},{35,3},{4,36},{36... | collective-permute-start | bytes 983048 | tf_op jit(solution)/shard_map/ppermute | solution.py:91
  177.6 6.4 %collective-permute-done.10 = bf16[1280,128]{1,0:T(8,128)(2,1)S(1)} collective-permute-done((bf16[1280,128]{1,0:T(8,128)(2,1)S(1)}, bf16[1280,128]{1,0:T(8,128)(2,1)S(1)}, u32[]{:S(2)}, u32[]{:S(2)}) %collective-permute-start.10) | collective-permute-done | bytes 327712 | tf_op jit(solution)/shard_map/ppermute | solution.py:91
  184.0 4.8 %collective-permute-start.11 = (bf16[2560,128]{1,0:T(8,128)(2,1)S(1)}, bf16[2560,128]{1,0:T(8,128)(2,1)S(1)}, u32[]{:S(2)}, u32[]{:S(2)}) collective-permute-start(bf16[2560,128]{1,0:T(8,128)(2,1)S(1)} %pad_maximum_fusion.2), channel_id=1, source_target_pairs={{0,16},{16,0},{1,17},{17,1},{2,18},{18,2},{3,19},{19,3},{4,20},{20... | collective-permute-start | bytes 1966088 | tf_op jit(solution)/shard_map/ppermute | solution.py:91
  188.8 0.7 gather_fusion
  189.7 0.8 collective-permute-done.11
  190.5 0.8 gather_fusion.4
  191.4 3.4 %bitcast_select_fusion = bf16[5120,128]{1,0:T(8,128)(2,1)} fusion(bf16[32,160,128]{2,1,0:T(8,128)(2,1)S(1)} %gather_fusion.4, pred[5120]{0:T(1024)(128)(4,1)S(1)} %broadcast_in_dim.114), kind=kLoop, calls=%fused_computation.15 | loop fusion | flops 655360 | bytes 2626560 | tf_op jit(solution)/shard_map/jit(take_along_axis)/select_n | solution.py:38
  (37 shorter events, 0.9 us)
Async XLA Ops:
  0.6 34.8 %copy-start.1 = (bf16[320,1152]{1,0:T(8,128)(2,1)S(1)}, bf16[320,1152]{1,0:T(8,128)(2,1)}, u32[]{:S(2)}) copy-start(bf16[320,1152]{1,0:T(8,128)(2,1)} %param.7) | copy-start | bytes 2211844
  3.4 12.7 %collective-permute-start.1 = (bf16[1152,128]{1,0:T(8,128)(2,1)S(1)}, bf16[1152,128]{1,0:T(8,128)(2,1)}, u32[]{:S(2)}, u32[]{:S(2)}) collective-permute-start(bf16[1152,128]{1,0:T(8,128)(2,1)S(1)} %get-tuple-element.6), channel_id=1, source_target_pairs={{0,2},{2,4},{4,6},{6,8},{8,10},{10,12},{12,14},{14,0},{1,3},{3,5},... | collective-permute-start | bytes 884744 | tf_op jit(solution)/shard_map/ppermute | solution.py:82
  7.4 11.7 %collective-permute-start.2 = (bf16[1152,128]{1,0:T(8,128)(2,1)S(1)}, bf16[1152,128]{1,0:T(8,128)(2,1)}, u32[]{:S(2)}, u32[]{:S(2)}) collective-permute-start(bf16[1152,128]{1,0:T(8,128)(2,1)S(1)} %get-tuple-element.6), channel_id=1, source_target_pairs={{0,14},{2,0},{4,2},{6,4},{8,6},{10,8},{12,10},{14,12},{1,15},{3,1}... | collective-permute-start | bytes 884744 | tf_op jit(solution)/shard_map/ppermute | solution.py:85
  11.3 24.2 %collective-permute-start = (bf16[320,1152]{1,0:T(8,128)(2,1)}, bf16[320,1152]{1,0:T(8,128)(2,1)}, u32[]{:S(2)}, u32[]{:S(2)}) collective-permute-start(bf16[320,1152]{1,0:T(8,128)(2,1)} %param.7), channel_id=1, source_target_pairs={{0,1},{1,0},{2,3},{3,2},{4,5},{5,4},{6,7},{7,6},{8,9},{9,8},{10,11... | collective-permute-start | bytes 2211848 | tf_op jit(solution)/shard_map/ppermute | solution.py:91
  16.1 9.3 %collective-permute-start.3 = (bf16[1152,128]{1,0:T(8,128)(2,1)}, bf16[1152,128]{1,0:T(8,128)(2,1)}, u32[]{:S(2)}, u32[]{:S(2)}) collective-permute-start(bf16[1152,128]{1,0:T(8,128)(2,1)} %collective-permute-done.1), channel_id=1, source_target_pairs={{0,2},{2,4},{4,6},{6,8},{8,10},{10,12},{12,14},{14,0},{1,3},{3,5},... | collective-permute-start | bytes 884744 | tf_op jit(solution)/shard_map/ppermute | solution.py:82
  19.1 8.5 %collective-permute-start.4 = (bf16[1152,128]{1,0:T(8,128)(2,1)}, bf16[1152,128]{1,0:T(8,128)(2,1)S(1)}, u32[]{:S(2)}, u32[]{:S(2)}) collective-permute-start(bf16[1152,128]{1,0:T(8,128)(2,1)} %collective-permute-done.2), channel_id=1, source_target_pairs={{0,14},{2,0},{4,2},{6,4},{8,6},{10,8},{12,10},{14,12},{1,15},{3,1}... | collective-permute-start | bytes 884744 | tf_op jit(solution)/shard_map/ppermute | solution.py:85
  25.4 14.8 %collective-permute-start.5 = (bf16[1152,128]{1,0:T(8,128)(2,1)}, bf16[1152,128]{1,0:T(8,128)(2,1)}, u32[]{:S(2)}, u32[]{:S(2)}) collective-permute-start(bf16[1152,128]{1,0:T(8,128)(2,1)} %collective-permute-done.3), channel_id=1, source_target_pairs={{0,2},{2,4},{4,6},{6,8},{8,10},{10,12},{12,14},{14,0},{1,3},{3,5},... | collective-permute-start | bytes 884744 | tf_op jit(solution)/shard_map/ppermute | solution.py:82
  27.6 16.2 %collective-permute-start.6 = (bf16[1152,128]{1,0:T(8,128)(2,1)S(1)}, bf16[1152,128]{1,0:T(8,128)(2,1)}, u32[]{:S(2)}, u32[]{:S(2)}) collective-permute-start(bf16[1152,128]{1,0:T(8,128)(2,1)S(1)} %collective-permute-done.4), channel_id=1, source_target_pairs={{0,14},{2,0},{4,2},{6,4},{8,6},{10,8},{12,10},{14,12},{1,15},{3,1}... | collective-permute-start | bytes 884744 | tf_op jit(solution)/shard_map/ppermute | solution.py:85
  34.0 1.4 copy-start
  40.2 8.9 %collective-permute-start.7 = (bf16[1152,128]{1,0:T(8,128)(2,1)}, bf16[1152,128]{1,0:T(8,128)(2,1)S(1)}, u32[]{:S(2)}, u32[]{:S(2)}) collective-permute-start(bf16[1152,128]{1,0:T(8,128)(2,1)} %collective-permute-done.5), channel_id=1, source_target_pairs={{0,2},{2,4},{4,6},{6,8},{8,10},{10,12},{12,14},{14,0},{1,3},{3,5},... | collective-permute-start | bytes 884744 | tf_op jit(solution)/shard_map/ppermute | solution.py:82
  60.9 11.0 %collective-permute-start.8 = (f32[320,8,128]{2,0,1:T(8,128)S(1)}, f32[320,8,128]{2,0,1:T(8,128)S(1)}, u32[]{:S(2)}, u32[]{:S(2)}) collective-permute-start(f32[320,8,128]{2,0,1:T(8,128)S(1)} %bitcast.142), channel_id=1, source_target_pairs={{0,16},{16,0},{1,17},{17,1},{2,18},{18,2},{3,19},{19,3},{4,20},{20... | collective-permute-start | bytes 3932168 | tf_op jit(solution)/shard_map/ppermute | solution.py:59
  72.1 23.5 %copy-start.3 = (s32[1,32]{1,0:T(1,128)S(1)}, s32[1,32]{1,0:T(1,128)}, u32[]{:S(2)}) copy-start(s32[1,32]{1,0:T(1,128)} %param.12) | copy-start | bytes 388
  72.2 17.8 %collective-permute-start.9 = (f32[160,8,128]{2,0,1:T(8,128)S(1)}, f32[160,8,128]{2,0,1:T(8,128)S(1)}, u32[]{:S(2)}, u32[]{:S(2)}) collective-permute-start(f32[160,8,128]{2,0,1:T(8,128)S(1)} %slice.37), channel_id=1, source_target_pairs={{0,32},{32,0},{1,33},{33,1},{2,34},{34,2},{3,35},{35,3},{4,36},{36... | collective-permute-start | bytes 1966088 | tf_op jit(solution)/shard_map/ppermute | solution.py:59
  91.0 25.3 %all-to-all-start = ((f32[160,8,128]{2,0,1:T(8,128)}), f32[160,8,128]{2,0,1:T(8,128)S(1)}, u32[]{:S(2)}, u32[]{:S(2)}) async-start(f32[160,8,128]{2,0,1:T(8,128)} %slice_add_fusion), calls=%async_computation | async-start | bytes 1310720 | tf_op jit(solution)/shard_map/all_to_all | solution.py:142
  116.3 37.5 %copy-start.2 = (f32[160,128]{1,0:T(8,128)S(1)}, f32[160,128]{1,0:T(8,128)}, u32[]{:S(2)}) copy-start(f32[160,128]{1,0:T(8,128)} %param.13) | copy-start | bytes 245764
  174.8 9.1 %collective-permute-start.10 = (bf16[1280,128]{1,0:T(8,128)(2,1)S(1)}, bf16[1280,128]{1,0:T(8,128)(2,1)S(1)}, u32[]{:S(2)}, u32[]{:S(2)}) collective-permute-start(bf16[1280,128]{1,0:T(8,128)(2,1)S(1)} %bitcast.136), channel_id=1, source_target_pairs={{0,32},{32,0},{1,33},{33,1},{2,34},{34,2},{3,35},{35,3},{4,36},{36... | collective-permute-start | bytes 983048 | tf_op jit(solution)/shard_map/ppermute | solution.py:91
  184.0 6.5 %collective-permute-start.11 = (bf16[2560,128]{1,0:T(8,128)(2,1)S(1)}, bf16[2560,128]{1,0:T(8,128)(2,1)S(1)}, u32[]{:S(2)}, u32[]{:S(2)}) collective-permute-start(bf16[2560,128]{1,0:T(8,128)(2,1)S(1)} %pad_maximum_fusion.2), channel_id=1, source_target_pairs={{0,16},{16,0},{1,17},{17,1},{2,18},{18,2},{3,19},{19,3},{4,20},{20... | collective-permute-start | bytes 1966088 | tf_op jit(solution)/shard_map/ppermute | solution.py:91

commit v9 on v8

--- a/solution.py
+++ b/solution.py
@@ -142,14 +142,10 @@
     quarters = lax.all_to_all(kept, "y", split_axis=1, concat_axis=0, tiled=True).reshape(
         dp_count, quarter_rows, head_width
     )
-    per_z = dp_count // z_count
     in_owner_order = jnp.take(quarters, inverse[0], axis=0)
-    from_z = lax.all_to_all(in_owner_order, "z", split_axis=0, concat_axis=0, tiled=True)
-    local_owners = jnp.sum(
-        from_z.reshape(z_count, per_z * quarter_rows, head_width), axis=0
-    )
-    own_block = lax.all_to_all(
-        local_owners, ("xl", "c"), split_axis=0, concat_axis=0, tiled=True
+    from_all = lax.all_to_all(in_owner_order, DP, split_axis=0, concat_axis=0, tiled=True)
+    own_block = jnp.sum(
+        from_all.reshape(z_count, dp_count // z_count, quarter_rows, head_width), axis=0
     ).reshape(block_rows, heads_here, head_width)
 
     previous = momentum.reshape(block_rows, heads_here, head_width)

time: 196 us -> 191 us (0.974)
  blocking collectives: 51.4 us -> 47 us
    all_to_all x2 -> x1, blocking collectives: 36.8 us -> 31.1 us  [shards(): lax.all_to_all(in_owner_order, DP, split_axis=0, concat_axis=0, tiled=True)]
  transfers between devices with their start and end apart: 13 -> 13, of which waited for: 8 -> 8; matrix products, arithmetic and copies ran while one was open for 6% -> 7% of each run, Pallas kernels for 0% -> 0%
where the time goes in v9:
time: 191 us; the launch traced here: 190 us
  waiting for transfers between devices  51.6 us (27%)
  starting transfers between devices  49.7 us (26%)
  blocking collectives  47 us (25%)
  local copies, waits for them, and re-layouts  20.6 us (11%)
  other arithmetic  12.1 us (6%)
  matrix products  7.61 us (4%)
    all_to_all x1, blocking collectives, shards(): lax.all_to_all(in_owner_order, DP, split_axis=0, concat_axis=0, tiled=True)  31.1 us
    all_to_all x1, waiting for transfers between devices, shards(): lax.all_to_all(kept, 'y', split_axis=1, concat_axis=0, tiled=True)  20.4 us
    ppermute x2, waiting for transfers between devices, pair_sum_scatter(): return blocks[:half] + lax.ppermute(blocks[half:], axis, SWAP)  18.5 us
    all_to_all x1, blocking collectives, shards(): lax.all_to_all(jnp.broadcast_to(own_update[None], (z_count,) + own_update...  15.9 us
    ppermute x3, starting transfers between devices, ring_gather(): from_right = lax.ppermute(from_right, axis, to_left)  13.7 us
    ppermute x3, starting transfers between devices, pair_gather(): return jnp.concatenate([piece, lax.ppermute(piece, axis, SWAP)], axis=0)  11.3 us
    ppermute x2, starting transfers between devices, pair_sum_scatter(): return blocks[:half] + lax.ppermute(blocks[half:], axis, SWAP)  10.3 us
    ppermute x4, starting transfers between devices, ring_gather(): from_left = lax.ppermute(from_left, axis, to_right)  9.76 us
  transfers between devices with their start and end apart: 13, of which 8 were waited for; matrix products, arithmetic and copies ran while one was open for 7% of the time, Pallas kernels for 0%

profile of v9, /device:TPU:1, one launch (start us, length us, event | category | flops | bytes accessed | tf_op | source)
XLA Modules:
  0.0 190.3 jit_solution(8419213764395164080)
XLA Ops:
  0.6 0.9 select_reduce_fusion
  1.5 0.7 multiply_multiply_fusion
  2.2 1.2 bitcast_dynamic-update-slice_fusion.7
  3.4 4.0 %collective-permute-start.1 = (bf16[1152,128]{1,0:T(8,128)(2,1)S(1)}, bf16[1152,128]{1,0:T(8,128)(2,1)}, u32[]{:S(2)}, u32[]{:S(2)}) collective-permute-start(bf16[1152,128]{1,0:T(8,128)(2,1)S(1)} %get-tuple-element.6), channel_id=1, source_target_pairs={{0,2},{2,4},{4,6},{6,8},{8,10},{10,12},{12,14},{14,0},{1,3},{3,5},... | collective-permute-start | bytes 884744 | tf_op jit(solution)/shard_map/ppermute | solution.py:82
  7.4 3.8 %collective-permute-start.2 = (bf16[1152,128]{1,0:T(8,128)(2,1)S(1)}, bf16[1152,128]{1,0:T(8,128)(2,1)}, u32[]{:S(2)}, u32[]{:S(2)}) collective-permute-start(bf16[1152,128]{1,0:T(8,128)(2,1)S(1)} %get-tuple-element.6), channel_id=1, source_target_pairs={{0,14},{2,0},{4,2},{6,4},{8,6},{10,8},{12,10},{14,12},{1,15},{3,1}... | collective-permute-start | bytes 884744 | tf_op jit(solution)/shard_map/ppermute | solution.py:85
  11.3 4.7 %collective-permute-start = (bf16[320,1152]{1,0:T(8,128)(2,1)}, bf16[320,1152]{1,0:T(8,128)(2,1)}, u32[]{:S(2)}, u32[]{:S(2)}) collective-permute-start(bf16[320,1152]{1,0:T(8,128)(2,1)} %param.7), channel_id=1, source_target_pairs={{0,1},{1,0},{2,3},{3,2},{4,5},{5,4},{6,7},{7,6},{8,9},{9,8},{10,11... | collective-permute-start | bytes 2211848 | tf_op jit(solution)/shard_map/ppermute | solution.py:91
  16.1 1.9 %collective-permute-start.3 = (bf16[1152,128]{1,0:T(8,128)(2,1)}, bf16[1152,128]{1,0:T(8,128)(2,1)}, u32[]{:S(2)}, u32[]{:S(2)}) collective-permute-start(bf16[1152,128]{1,0:T(8,128)(2,1)} %collective-permute-done.1), channel_id=1, source_target_pairs={{0,2},{2,4},{4,6},{6,8},{8,10},{10,12},{12,14},{14,0},{1,3},{3,5},... | collective-permute-start | bytes 884744 | tf_op jit(solution)/shard_map/ppermute | solution.py:82
  18.1 1.0 bitcast_dynamic-update-slice_fusion.6
  19.1 4.6 %collective-permute-start.4 = (bf16[1152,128]{1,0:T(8,128)(2,1)}, bf16[1152,128]{1,0:T(8,128)(2,1)S(1)}, u32[]{:S(2)}, u32[]{:S(2)}) collective-permute-start(bf16[1152,128]{1,0:T(8,128)(2,1)} %collective-permute-done.2), channel_id=1, source_target_pairs={{0,14},{2,0},{4,2},{6,4},{8,6},{10,8},{12,10},{14,12},{1,15},{3,1}... | collective-permute-start | bytes 884744 | tf_op jit(solution)/shard_map/ppermute | solution.py:85
  23.7 1.0 bitcast_dynamic-update-slice_fusion.5
  24.7 0.7 collective-permute-done.3
  25.4 1.9 %collective-permute-start.5 = (bf16[1152,128]{1,0:T(8,128)(2,1)}, bf16[1152,128]{1,0:T(8,128)(2,1)}, u32[]{:S(2)}, u32[]{:S(2)}) collective-permute-start(bf16[1152,128]{1,0:T(8,128)(2,1)} %collective-permute-done.3), channel_id=1, source_target_pairs={{0,2},{2,4},{4,6},{6,8},{8,10},{10,12},{12,14},{14,0},{1,3},{3,5},... | collective-permute-start | bytes 884744 | tf_op jit(solution)/shard_map/ppermute | solution.py:82
  27.3 0.3 collective-permute-done.4
  27.6 5.3 %collective-permute-start.6 = (bf16[1152,128]{1,0:T(8,128)(2,1)S(1)}, bf16[1152,128]{1,0:T(8,128)(2,1)}, u32[]{:S(2)}, u32[]{:S(2)}) collective-permute-start(bf16[1152,128]{1,0:T(8,128)(2,1)S(1)} %collective-permute-done.4), channel_id=1, source_target_pairs={{0,14},{2,0},{4,2},{6,4},{8,6},{10,8},{12,10},{14,12},{1,15},{3,1}... | collective-permute-start | bytes 884744 | tf_op jit(solution)/shard_map/ppermute | solution.py:85
  33.0 1.0 bitcast_dynamic-update-slice_fusion.4
  34.0 1.4 copy-done
  35.4 1.2 pad_maximum_fusion
  36.7 3.5 %gather_fusion.1 = bf16[640,1152]{1,0:T(8,128)(2,1)} fusion(bf16[640,1152]{1,0:T(8,128)(2,1)S(1)} %pad_maximum_fusion, s32[1024]{0:T(1024)S(1)} %pad_clamp_fusion.3), kind=kCustom, calls=%fused_computation.1 | custom fusion | bytes 2951680 | tf_op jit(solution)/shard_map/jit(_take)/gather | solution.py:136
  40.2 1.9 %collective-permute-start.7 = (bf16[1152,128]{1,0:T(8,128)(2,1)}, bf16[1152,128]{1,0:T(8,128)(2,1)S(1)}, u32[]{:S(2)}, u32[]{:S(2)}) collective-permute-start(bf16[1152,128]{1,0:T(8,128)(2,1)} %collective-permute-done.5), channel_id=1, source_target_pairs={{0,2},{2,4},{4,6},{6,8},{8,10},{10,12},{12,14},{14,0},{1,3},{3,5},... | collective-permute-start | bytes 884744 | tf_op jit(solution)/shard_map/ppermute | solution.py:82
  42.1 1.7 bitcast_dynamic-update-slice_fusion.2
  43.8 1.7 bitcast_dynamic-update-slice_fusion.1
  45.5 3.6 %collective-permute-done.7 = bf16[1152,128]{1,0:T(8,128)(2,1)S(1)} collective-permute-done((bf16[1152,128]{1,0:T(8,128)(2,1)}, bf16[1152,128]{1,0:T(8,128)(2,1)S(1)}, u32[]{:S(2)}, u32[]{:S(2)}) %collective-permute-start.7) | collective-permute-done | bytes 294944 | tf_op jit(solution)/shard_map/ppermute | solution.py:82
  49.1 0.7 bitcast_dynamic-update-slice_fusion
  49.8 2.7 %gather_fusion.2 = bf16[8,1152,128]{2,1,0:T(8,128)(2,1)S(1)} fusion(bf16[8,1152,128]{2,1,0:T(8,128)(2,1)} %bitcast_dynamic-update-slice_fusion, s32[1024]{0:T(1024)S(1)} %pad_clamp_fusion.2), kind=kCustom, calls=%fused_computation.2 | custom fusion | bytes 4718624 | tf_op jit(solution)/shard_map/jit(_take)/gather | solution.py:121
  52.5 1.7 select_bitcast_fusion
  54.2 3.0 %copy.14 = bf16[1152,8,128]{0,2,1:T(8,128)(2,1)S(1)} copy(bf16[1152,8,128]{2,0,1:T(8,128)(2,1)} %select_bitcast_fusion) | data formatting | bytes 4718592 | tf_op jit(solution)/shard_map/jit(_take)/select_n | solution.py:121
  57.2 3.3 %fusion = f32[640,1024]{1,0:T(8,128)S(1)} fusion(bf16[1152,1024]{0,1:T(8,128)(2,1)S(1)} %bitcast.138, bf16[640,1152]{1,0:T(8,128)(2,1)} %gather_fusion.1, pred[640]{0:T(1024)(128)(4,1)S(1)} %compare_and_fusion), kind=kOutput, calls=%fused_computation.7 | convolution fusion | flops 1510686720 | bytes 6455936 | tf_op jit(solution)/shard_map/dot_general | solution.py:137
  60.5 0.3 slice_bitcast_fusion.1
  60.9 8.4 %collective-permute-start.8 = (f32[320,8,128]{2,0,1:T(8,128)S(1)}, f32[320,8,128]{2,0,1:T(8,128)S(1)}, u32[]{:S(2)}, u32[]{:S(2)}) collective-permute-start(f32[320,8,128]{2,0,1:T(8,128)S(1)} %bitcast.139), channel_id=1, source_target_pairs={{0,16},{16,0},{1,17},{17,1},{2,18},{18,2},{3,19},{19,3},{4,20},{20... | collective-permute-start | bytes 3932168 | tf_op jit(solution)/shard_map/ppermute | solution.py:59
  69.3 2.6 %collective-permute-done.8 = f32[320,8,128]{2,0,1:T(8,128)S(1)} collective-permute-done((f32[320,8,128]{2,0,1:T(8,128)S(1)}, f32[320,8,128]{2,0,1:T(8,128)S(1)}, u32[]{:S(2)}, u32[]{:S(2)}) %collective-permute-start.8) | collective-permute-done | bytes 1310752 | tf_op jit(solution)/shard_map/ppermute | solution.py:59
  72.0 0.2 bitcast_add_fusion
  72.2 1.9 %collective-permute-start.9 = (f32[160,8,128]{2,0,1:T(8,128)S(1)}, f32[160,8,128]{2,0,1:T(8,128)S(1)}, u32[]{:S(2)}, u32[]{:S(2)}) collective-permute-start(f32[160,8,128]{2,0,1:T(8,128)S(1)} %slice.37), channel_id=1, source_target_pairs={{0,32},{32,0},{1,33},{33,1},{2,34},{34,2},{3,35},{35,3},{4,36},{36... | collective-permute-start | bytes 1966088 | tf_op jit(solution)/shard_map/ppermute | solution.py:59
  74.1 15.9 %collective-permute-done.9 = f32[160,8,128]{2,0,1:T(8,128)S(1)} collective-permute-done((f32[160,8,128]{2,0,1:T(8,128)S(1)}, f32[160,8,128]{2,0,1:T(8,128)S(1)}, u32[]{:S(2)}, u32[]{:S(2)}) %collective-permute-start.9) | collective-permute-done | bytes 655392 | tf_op jit(solution)/shard_map/ppermute | solution.py:59
  90.0 0.9 slice_add_fusion
  91.0 4.7 %all-to-all-start = ((f32[160,8,128]{2,0,1:T(8,128)}), f32[160,8,128]{2,0,1:T(8,128)S(1)}, u32[]{:S(2)}, u32[]{:S(2)}) async-start(f32[160,8,128]{2,0,1:T(8,128)} %slice_add_fusion), calls=%async_computation | async-start | bytes 1310720 | tf_op jit(solution)/shard_map/all_to_all | solution.py:142
  95.7 0.1 select_reduce_fusion.1
  95.8 20.4 %all-to-all-done = f32[160,8,128]{2,0,1:T(8,128)S(1)} async-done(((f32[160,8,128]{2,0,1:T(8,128)}), f32[160,8,128]{2,0,1:T(8,128)S(1)}, u32[]{:S(2)}, u32[]{:S(2)}) %all-to-all-start) | async-done | bytes 655392 | tf_op jit(solution)/shard_map/all_to_all | solution.py:142
  116.3 0.6 gather_fusion.3
  116.8 0.1 broadcast_select_fusion
  117.0 31.1 %all_to_all.25 = f32[32,40,128]{2,1,0:T(8,128)S(1)} all-to-all(f32[32,40,128]{2,1,0:T(8,128)S(1)} %broadcast_select_fusion), channel_id=1, replica_groups=mesh['z'=8,'xl'=2,'c'=2,'y'=8,'xh'=2] {'z','xl','c'}, dimensions={0} | all-to-all | bytes 1310720 | tf_op jit(solution)/shard_map/all_to_all | solution.py:146
  148.1 1.3 multiply_reduce_fusion
  150.1 0.4 fusion.29
  150.5 0.2 fusion.13
  150.7 0.2 fusion.3
  150.9 0.4 fusion.27
  151.4 0.2 fusion.12
  151.6 0.2 fusion.4
  151.8 0.4 fusion.24
  152.3 0.2 fusion.11
  152.5 0.2 fusion.5
  152.7 0.4 fusion.21
  153.1 0.2 fusion.10
  153.3 0.2 fusion.6
  153.6 0.4 fusion.18
  154.0 0.2 fusion.9
  154.2 0.2 fusion.15
  154.5 15.9 %all_to_all.26 = bf16[8,160,128]{2,1,0:T(8,128)(2,1)S(1)} all-to-all(bf16[8,160,128]{2,1,0:T(8,128)(2,1)S(1)} %broadcast_in_dim.133), channel_id=1, replica_groups=mesh['z'=8,'xl'=2,'c'=2,'y'=8,'xh'=2] {'z'}, dimensions={0} | all-to-all | bytes 655360 | tf_op jit(solution)/shard_map/all_to_all | solution.py:160
  170.4 2.4 %collective-permute-start.10 = (bf16[1280,128]{1,0:T(8,128)(2,1)S(1)}, bf16[1280,128]{1,0:T(8,128)(2,1)S(1)}, u32[]{:S(2)}, u32[]{:S(2)}) collective-permute-start(bf16[1280,128]{1,0:T(8,128)(2,1)S(1)} %bitcast.133), channel_id=1, source_target_pairs={{0,32},{32,0},{1,33},{33,1},{2,34},{34,2},{3,35},{35,3},{4,36},{36... | collective-permute-start | bytes 983048 | tf_op jit(solution)/shard_map/ppermute | solution.py:91
  172.8 7.3 %collective-permute-done.10 = bf16[1280,128]{1,0:T(8,128)(2,1)S(1)} collective-permute-done((bf16[1280,128]{1,0:T(8,128)(2,1)S(1)}, bf16[1280,128]{1,0:T(8,128)(2,1)S(1)}, u32[]{:S(2)}, u32[]{:S(2)}) %collective-permute-start.10) | collective-permute-done | bytes 327712 | tf_op jit(solution)/shard_map/ppermute | solution.py:91
  180.1 4.2 %collective-permute-start.11 = (bf16[2560,128]{1,0:T(8,128)(2,1)S(1)}, bf16[2560,128]{1,0:T(8,128)(2,1)S(1)}, u32[]{:S(2)}, u32[]{:S(2)}) collective-permute-start(bf16[2560,128]{1,0:T(8,128)(2,1)S(1)} %pad_maximum_fusion.2), channel_id=1, source_target_pairs={{0,16},{16,0},{1,17},{17,1},{2,18},{18,2},{3,19},{19,3},{4,20},{20... | collective-permute-start | bytes 1966088 | tf_op jit(solution)/shard_map/ppermute | solution.py:91
  184.4 0.7 gather_fusion
  185.3 0.8 collective-permute-done.11
  186.1 0.8 gather_fusion.4
  186.9 3.4 %bitcast_select_fusion = bf16[5120,128]{1,0:T(8,128)(2,1)} fusion(bf16[32,160,128]{2,1,0:T(8,128)(2,1)S(1)} %gather_fusion.4, pred[5120]{0:T(1024)(128)(4,1)S(1)} %broadcast_in_dim.114), kind=kLoop, calls=%fused_computation.15 | loop fusion | flops 655360 | bytes 2626560 | tf_op jit(solution)/shard_map/jit(take_along_axis)/select_n | solution.py:38
  (36 shorter events, 0.8 us)
Async XLA Ops:
  0.6 34.8 %copy-start.1 = (bf16[320,1152]{1,0:T(8,128)(2,1)S(1)}, bf16[320,1152]{1,0:T(8,128)(2,1)}, u32[]{:S(2)}) copy-start(bf16[320,1152]{1,0:T(8,128)(2,1)} %param.7) | copy-start | bytes 2211844
  3.4 12.7 %collective-permute-start.1 = (bf16[1152,128]{1,0:T(8,128)(2,1)S(1)}, bf16[1152,128]{1,0:T(8,128)(2,1)}, u32[]{:S(2)}, u32[]{:S(2)}) collective-permute-start(bf16[1152,128]{1,0:T(8,128)(2,1)S(1)} %get-tuple-element.6), channel_id=1, source_target_pairs={{0,2},{2,4},{4,6},{6,8},{8,10},{10,12},{12,14},{14,0},{1,3},{3,5},... | collective-permute-start | bytes 884744 | tf_op jit(solution)/shard_map/ppermute | solution.py:82
  7.4 11.7 %collective-permute-start.2 = (bf16[1152,128]{1,0:T(8,128)(2,1)S(1)}, bf16[1152,128]{1,0:T(8,128)(2,1)}, u32[]{:S(2)}, u32[]{:S(2)}) collective-permute-start(bf16[1152,128]{1,0:T(8,128)(2,1)S(1)} %get-tuple-element.6), channel_id=1, source_target_pairs={{0,14},{2,0},{4,2},{6,4},{8,6},{10,8},{12,10},{14,12},{1,15},{3,1}... | collective-permute-start | bytes 884744 | tf_op jit(solution)/shard_map/ppermute | solution.py:85
  11.3 24.2 %collective-permute-start = (bf16[320,1152]{1,0:T(8,128)(2,1)}, bf16[320,1152]{1,0:T(8,128)(2,1)}, u32[]{:S(2)}, u32[]{:S(2)}) collective-permute-start(bf16[320,1152]{1,0:T(8,128)(2,1)} %param.7), channel_id=1, source_target_pairs={{0,1},{1,0},{2,3},{3,2},{4,5},{5,4},{6,7},{7,6},{8,9},{9,8},{10,11... | collective-permute-start | bytes 2211848 | tf_op jit(solution)/shard_map/ppermute | solution.py:91
  16.1 9.3 %collective-permute-start.3 = (bf16[1152,128]{1,0:T(8,128)(2,1)}, bf16[1152,128]{1,0:T(8,128)(2,1)}, u32[]{:S(2)}, u32[]{:S(2)}) collective-permute-start(bf16[1152,128]{1,0:T(8,128)(2,1)} %collective-permute-done.1), channel_id=1, source_target_pairs={{0,2},{2,4},{4,6},{6,8},{8,10},{10,12},{12,14},{14,0},{1,3},{3,5},... | collective-permute-start | bytes 884744 | tf_op jit(solution)/shard_map/ppermute | solution.py:82
  19.1 8.5 %collective-permute-start.4 = (bf16[1152,128]{1,0:T(8,128)(2,1)}, bf16[1152,128]{1,0:T(8,128)(2,1)S(1)}, u32[]{:S(2)}, u32[]{:S(2)}) collective-permute-start(bf16[1152,128]{1,0:T(8,128)(2,1)} %collective-permute-done.2), channel_id=1, source_target_pairs={{0,14},{2,0},{4,2},{6,4},{8,6},{10,8},{12,10},{14,12},{1,15},{3,1}... | collective-permute-start | bytes 884744 | tf_op jit(solution)/shard_map/ppermute | solution.py:85
  25.4 14.8 %collective-permute-start.5 = (bf16[1152,128]{1,0:T(8,128)(2,1)}, bf16[1152,128]{1,0:T(8,128)(2,1)}, u32[]{:S(2)}, u32[]{:S(2)}) collective-permute-start(bf16[1152,128]{1,0:T(8,128)(2,1)} %collective-permute-done.3), channel_id=1, source_target_pairs={{0,2},{2,4},{4,6},{6,8},{8,10},{10,12},{12,14},{14,0},{1,3},{3,5},... | collective-permute-start | bytes 884744 | tf_op jit(solution)/shard_map/ppermute | solution.py:82
  27.6 16.2 %collective-permute-start.6 = (bf16[1152,128]{1,0:T(8,128)(2,1)S(1)}, bf16[1152,128]{1,0:T(8,128)(2,1)}, u32[]{:S(2)}, u32[]{:S(2)}) collective-permute-start(bf16[1152,128]{1,0:T(8,128)(2,1)S(1)} %collective-permute-done.4), channel_id=1, source_target_pairs={{0,14},{2,0},{4,2},{6,4},{8,6},{10,8},{12,10},{14,12},{1,15},{3,1}... | collective-permute-start | bytes 884744 | tf_op jit(solution)/shard_map/ppermute | solution.py:85
  34.0 1.4 copy-start
  40.2 8.9 %collective-permute-start.7 = (bf16[1152,128]{1,0:T(8,128)(2,1)}, bf16[1152,128]{1,0:T(8,128)(2,1)S(1)}, u32[]{:S(2)}, u32[]{:S(2)}) collective-permute-start(bf16[1152,128]{1,0:T(8,128)(2,1)} %collective-permute-done.5), channel_id=1, source_target_pairs={{0,2},{2,4},{4,6},{6,8},{8,10},{10,12},{12,14},{14,0},{1,3},{3,5},... | collective-permute-start | bytes 884744 | tf_op jit(solution)/shard_map/ppermute | solution.py:82
  60.9 11.0 %collective-permute-start.8 = (f32[320,8,128]{2,0,1:T(8,128)S(1)}, f32[320,8,128]{2,0,1:T(8,128)S(1)}, u32[]{:S(2)}, u32[]{:S(2)}) collective-permute-start(f32[320,8,128]{2,0,1:T(8,128)S(1)} %bitcast.139), channel_id=1, source_target_pairs={{0,16},{16,0},{1,17},{17,1},{2,18},{18,2},{3,19},{19,3},{4,20},{20... | collective-permute-start | bytes 3932168 | tf_op jit(solution)/shard_map/ppermute | solution.py:59
  72.1 23.5 %copy-start.3 = (s32[1,32]{1,0:T(1,128)S(1)}, s32[1,32]{1,0:T(1,128)}, u32[]{:S(2)}) copy-start(s32[1,32]{1,0:T(1,128)} %param.12) | copy-start | bytes 388
  72.2 17.8 %collective-permute-start.9 = (f32[160,8,128]{2,0,1:T(8,128)S(1)}, f32[160,8,128]{2,0,1:T(8,128)S(1)}, u32[]{:S(2)}, u32[]{:S(2)}) collective-permute-start(f32[160,8,128]{2,0,1:T(8,128)S(1)} %slice.37), channel_id=1, source_target_pairs={{0,32},{32,0},{1,33},{33,1},{2,34},{34,2},{3,35},{35,3},{4,36},{36... | collective-permute-start | bytes 1966088 | tf_op jit(solution)/shard_map/ppermute | solution.py:59
  91.0 25.3 %all-to-all-start = ((f32[160,8,128]{2,0,1:T(8,128)}), f32[160,8,128]{2,0,1:T(8,128)S(1)}, u32[]{:S(2)}, u32[]{:S(2)}) async-start(f32[160,8,128]{2,0,1:T(8,128)} %slice_add_fusion), calls=%async_computation | async-start | bytes 1310720 | tf_op jit(solution)/shard_map/all_to_all | solution.py:142
  95.7 52.5 %copy-start.2 = (f32[160,128]{1,0:T(8,128)S(1)}, f32[160,128]{1,0:T(8,128)}, u32[]{:S(2)}) copy-start(f32[160,128]{1,0:T(8,128)} %param.13) | copy-start | bytes 245764
  170.4 9.7 %collective-permute-start.10 = (bf16[1280,128]{1,0:T(8,128)(2,1)S(1)}, bf16[1280,128]{1,0:T(8,128)(2,1)S(1)}, u32[]{:S(2)}, u32[]{:S(2)}) collective-permute-start(bf16[1280,128]{1,0:T(8,128)(2,1)S(1)} %bitcast.133), channel_id=1, source_target_pairs={{0,32},{32,0},{1,33},{33,1},{2,34},{34,2},{3,35},{35,3},{4,36},{36... | collective-permute-start | bytes 983048 | tf_op jit(solution)/shard_map/ppermute | solution.py:91
  180.1 5.9 %collective-permute-start.11 = (bf16[2560,128]{1,0:T(8,128)(2,1)S(1)}, bf16[2560,128]{1,0:T(8,128)(2,1)S(1)}, u32[]{:S(2)}, u32[]{:S(2)}) collective-permute-start(bf16[2560,128]{1,0:T(8,128)(2,1)S(1)} %pad_maximum_fusion.2), channel_id=1, source_target_pairs={{0,16},{16,0},{1,17},{17,1},{2,18},{18,2},{3,19},{19,3},{4,20},{20... | collective-permute-start | bytes 1966088 | tf_op jit(solution)/shard_map/ppermute | solution.py:91

commit v10 on v9

--- a/solution.py
+++ b/solution.py
@@ -84,7 +84,7 @@
         if 2 * step < count:
             from_right = lax.ppermute(from_right, axis, to_left)
             pieces.append(from_right)
-    return jnp.stack(pieces)
+    return pieces
 
 
 def pair_gather(piece, axis):
@@ -114,13 +114,6 @@
     pair_rows = pair_gather(features, "xh")
     y = lax.axis_index("y")
     ring_pieces = ring_gather(scaled, "y")
-    head = jnp.arange(y_count, dtype=jnp.int32)
-    ahead = (head - y) % y_count
-    behind = (y - head) % y_count
-    slot = jnp.where(ahead == 0, 0, jnp.where(ahead < behind, 2 * ahead, 2 * behind - 1))
-    heads_y = jnp.transpose(jnp.take(ring_pieces, slot, axis=0), (1, 0, 2)).reshape(
-        local_tokens, y_count * head_width
-    )
     pair_blocks = 2 * sub_blocks
     group_rows = pair_blocks * quarter_rows
     position = jnp.arange(2 * feature_rows, dtype=jnp.int32)
@@ -134,11 +127,23 @@
     shard_slot = jnp.where(j // sub_blocks == xh, 0, 1)
     source_row = shard_slot * feature_rows + (j % sub_blocks) * block_rows + u * quarter_rows + r
     arranged = jnp.take(pair_rows, source_row, axis=0)
-    partial = jnp.dot(arranged, heads_y, preferred_element_type=jnp.float32).reshape(
-        2 * feature_rows, y_count, head_width
-    )
-    kept = pair_sum_scatter(partial, "c")
-    kept = pair_sum_scatter(kept, "xl")
+
+    def reduced_heads(pieces):
+        partial = jnp.dot(
+            arranged, jnp.concatenate(pieces, axis=1), preferred_element_type=jnp.float32
+        ).reshape(2 * feature_rows, len(pieces), head_width)
+        kept = pair_sum_scatter(partial, "c")
+        return pair_sum_scatter(kept, "xl")
+
+    early = 2 * 2 + 1
+    kept_ring_order = jnp.concatenate(
+        [reduced_heads(ring_pieces[:early]), reduced_heads(ring_pieces[early:])], axis=1
+    )
+    head = jnp.arange(y_count, dtype=jnp.int32)
+    ahead = (head - y) % y_count
+    behind = (y - head) % y_count
+    slot = jnp.where(ahead == 0, 0, jnp.where(ahead < behind, 2 * ahead, 2 * behind - 1))
+    kept = jnp.take(kept_ring_order, slot, axis=1)
     quarters = lax.all_to_all(kept, "y", split_axis=1, concat_axis=0, tiled=True).reshape(
         dp_count, quarter_rows, head_width
     )

time: 191 us -> 183 us (0.958)
  waiting for transfers between devices: 51.6 us -> 42.4 us
  local copies, waits for them, and re-layouts: 20.6 us -> 14.7 us
  starting transfers between devices: 49.7 us -> 55.4 us
    ppermute x2 -> x4, starting transfers between devices: 10.3 us -> 16.3 us  [pair_sum_scatter(): return blocks[:half] + lax.ppermute(blocks[half:], axis, SWAP)]
    unnamed x15 -> x13, local copies, waits for them, and re-layouts: 8.18 us -> 2.26 us
    ppermute x2 -> x4, waiting for transfers between devices: 18.5 us -> 13.2 us  [pair_sum_scatter(): return blocks[:half] + lax.ppermute(blocks[half:], axis, SWAP)]
    slice x2 -> x12, local copies, waits for them, and re-layouts: 0.13 us -> 4.78 us  [pair_sum_scatter(): return blocks[:half] + lax.ppermute(blocks[half:], axis, SWAP)]
    ppermute x4, waiting for transfers between devices: 4.31 us -> 0.97 us  [ring_gather(): from_left = lax.ppermute(from_left, axis, to_right)]
    select_n x1 -> x0, local copies, waits for them, and re-layouts: 3.01 us -> none  [shards(): jnp.take(ring_pieces, slot, axis=0)]
    gather x1, local copies, waits for them, and re-layouts: 2.66 us -> 0.59 us  [shards(): kept = jnp.take(kept_ring_order, slot, axis=1)]
    dot_general x1 -> x2, matrix products: 3.3 us -> 5 us  [reduced_heads(): jnp.dot(arranged, jnp.concatenate(pieces, axis=1), preferred_element_type...]
  transfers between devices with their start and end apart: 13 -> 15, of which waited for: 8 -> 7; matrix products, arithmetic and copies ran while one was open for 7% -> 11% of each run, Pallas kernels for 0% -> 0%
where the time goes in v10:
time: 183 us; the launch traced here: 182 us
  starting transfers between devices  55.4 us (30%)
  blocking collectives  46.9 us (26%)
  waiting for transfers between devices  42.4 us (23%)
  local copies, waits for them, and re-layouts  14.7 us (8%)
  other arithmetic  11.1 us (6%)
  matrix products  9.31 us (5%)
  between operations  1.88 us (1%)
    all_to_all x1, blocking collectives, shards(): lax.all_to_all(in_owner_order, DP, split_axis=0, concat_axis=0, tiled=True)  31.1 us
    all_to_all x1, waiting for transfers between devices, shards(): lax.all_to_all(kept, 'y', split_axis=1, concat_axis=0, tiled=True)  20.4 us
    ppermute x4, starting transfers between devices, pair_sum_scatter(): return blocks[:half] + lax.ppermute(blocks[half:], axis, SWAP)  16.3 us
    all_to_all x1, blocking collectives, shards(): lax.all_to_all(jnp.broadcast_to(own_update[None], (z_count,) + own_update...  15.8 us
    ppermute x4, waiting for transfers between devices, pair_sum_scatter(): return blocks[:half] + lax.ppermute(blocks[half:], axis, SWAP)  13.2 us
    ppermute x3, starting transfers between devices, ring_gather(): from_right = lax.ppermute(from_right, axis, to_left)  13 us
    ppermute x3, starting transfers between devices, pair_gather(): return jnp.concatenate([piece, lax.ppermute(piece, axis, SWAP)], axis=0)  11.5 us
    ppermute x4, starting transfers between devices, ring_gather(): from_left = lax.ppermute(from_left, axis, to_right)  9.76 us
  transfers between devices with their start and end apart: 15, of which 7 were waited for; matrix products, arithmetic and copies ran while one was open for 11% of the time, Pallas kernels for 0%

profile of v10, /device:TPU:1, one launch (start us, length us, event | category | flops | bytes accessed | tf_op | source)
XLA Modules:
  0.0 181.8 jit_solution(13466174675564229540)
XLA Ops:
  0.6 0.8 select_reduce_fusion
  1.4 0.7 multiply_multiply_fusion
  2.1 2.0 %constant_dynamic-update-slice_fusion.4 = (bf16[1152,640]{1,0:T(8,128)(2,1)}, bf16[1152,128]{1,0:T(8,128)(2,1)S(1)}) fusion(f32[1152]{0:T(1024)S(1)} %multiply_multiply_fusion, bf16[1152,128]{1,0:T(8,128)(2,1)} %param.8), kind=kLoop, calls=%fused_computation.75 | loop fusion | flops 442367 | bytes 889344
  4.1 4.0 %collective-permute-start.1 = (bf16[1152,128]{1,0:T(8,128)(2,1)S(1)}, bf16[1152,128]{1,0:T(8,128)(2,1)S(1)}, u32[]{:S(2)}, u32[]{:S(2)}) collective-permute-start(bf16[1152,128]{1,0:T(8,128)(2,1)S(1)} %get-tuple-element.6), channel_id=1, source_target_pairs={{0,2},{2,4},{4,6},{6,8},{8,10},{10,12},{12,14},{14,0},{1,3},{3,5},... | collective-permute-start | bytes 884744 | tf_op jit(solution)/shard_map/ppermute | solution.py:82
  8.1 3.8 %collective-permute-start.2 = (bf16[1152,128]{1,0:T(8,128)(2,1)S(1)}, bf16[1152,128]{1,0:T(8,128)(2,1)S(1)}, u32[]{:S(2)}, u32[]{:S(2)}) collective-permute-start(bf16[1152,128]{1,0:T(8,128)(2,1)S(1)} %get-tuple-element.6), channel_id=1, source_target_pairs={{0,14},{2,0},{4,2},{6,4},{8,6},{10,8},{12,10},{14,12},{1,15},{3,1}... | collective-permute-start | bytes 884744 | tf_op jit(solution)/shard_map/ppermute | solution.py:85
  12.0 4.7 %collective-permute-start = (bf16[320,1152]{1,0:T(8,128)(2,1)}, bf16[320,1152]{1,0:T(8,128)(2,1)S(1)}, u32[]{:S(2)}, u32[]{:S(2)}) collective-permute-start(bf16[320,1152]{1,0:T(8,128)(2,1)} %param.7), channel_id=1, source_target_pairs={{0,1},{1,0},{2,3},{3,2},{4,5},{5,4},{6,7},{7,6},{8,9},{9,8},{10,11... | collective-permute-start | bytes 2211848 | tf_op jit(solution)/shard_map/ppermute | solution.py:91
  16.8 1.9 %collective-permute-start.3 = (bf16[1152,128]{1,0:T(8,128)(2,1)S(1)}, bf16[1152,128]{1,0:T(8,128)(2,1)S(1)}, u32[]{:S(2)}, u32[]{:S(2)}) collective-permute-start(bf16[1152,128]{1,0:T(8,128)(2,1)S(1)} %collective-permute-done.1), channel_id=1, source_target_pairs={{0,2},{2,4},{4,6},{6,8},{8,10},{10,12},{12,14},{14,0},{1,3},{3,5},... | collective-permute-start | bytes 884744 | tf_op jit(solution)/shard_map/ppermute | solution.py:82
  18.7 4.6 %collective-permute-start.4 = (bf16[1152,128]{1,0:T(8,128)(2,1)S(1)}, bf16[1152,128]{1,0:T(8,128)(2,1)}, u32[]{:S(2)}, u32[]{:S(2)}) collective-permute-start(bf16[1152,128]{1,0:T(8,128)(2,1)S(1)} %collective-permute-done.2), channel_id=1, source_target_pairs={{0,14},{2,0},{4,2},{6,4},{8,6},{10,8},{12,10},{14,12},{1,15},{3,1}... | collective-permute-start | bytes 884744 | tf_op jit(solution)/shard_map/ppermute | solution.py:85
  23.3 0.7 constant_dynamic-update-slice_fusion.3
  24.1 0.7 constant_dynamic-update-slice_fusion.2
  24.8 1.0 collective-permute-done.3
  25.8 1.9 %collective-permute-start.7 = (bf16[1152,128]{1,0:T(8,128)(2,1)S(1)}, bf16[1152,128]{1,0:T(8,128)(2,1)}, u32[]{:S(2)}, u32[]{:S(2)}) collective-permute-start(bf16[1152,128]{1,0:T(8,128)(2,1)S(1)} %collective-permute-done.3), channel_id=1, source_target_pairs={{0,2},{2,4},{4,6},{6,8},{8,10},{10,12},{12,14},{14,0},{1,3},{3,5},... | collective-permute-start | bytes 884744 | tf_op jit(solution)/shard_map/ppermute | solution.py:82
  27.7 4.6 %collective-permute-start.8 = (bf16[1152,128]{1,0:T(8,128)(2,1)}, bf16[1152,128]{1,0:T(8,128)(2,1)}, u32[]{:S(2)}, u32[]{:S(2)}) collective-permute-start(bf16[1152,128]{1,0:T(8,128)(2,1)} %collective-permute-done.4), channel_id=1, source_target_pairs={{0,14},{2,0},{4,2},{6,4},{8,6},{10,8},{12,10},{14,12},{1,15},{3,1}... | collective-permute-start | bytes 884744 | tf_op jit(solution)/shard_map/ppermute | solution.py:85
  32.3 0.7 constant_dynamic-update-slice_fusion.1
  33.0 1.7 constant_dynamic-update-slice_fusion
  34.9 3.0 %gather_fusion.1 = bf16[640,1152]{1,0:T(8,128)(2,1)S(1)} fusion(bf16[640,1152]{1,0:T(8,128)(2,1)S(1)} %pad_maximum_fusion, s32[1024]{0:T(1024)S(1)} %pad_clamp_fusion.3), kind=kCustom, calls=%fused_computation.1 | custom fusion | bytes 2951680 | tf_op jit(solution)/shard_map/jit(_take)/gather | solution.py:129
  37.9 1.9 %collective-permute-start.9 = (bf16[1152,128]{1,0:T(8,128)(2,1)}, bf16[1152,128]{1,0:T(8,128)(2,1)}, u32[]{:S(2)}, u32[]{:S(2)}) collective-permute-start(bf16[1152,128]{1,0:T(8,128)(2,1)} %collective-permute-done.7), channel_id=1, source_target_pairs={{0,2},{2,4},{4,6},{6,8},{8,10},{10,12},{12,14},{14,0},{1,3},{3,5},... | collective-permute-start | bytes 884744 | tf_op jit(solution)/shard_map/ppermute | solution.py:82
  39.9 2.8 %fusion.19 = f32[640,640]{1,0:T(8,128)S(1)} fusion(bf16[1152,640]{1,0:T(8,128)(2,1)} %constant_dynamic-update-slice_fusion, bf16[640,1152]{1,0:T(8,128)(2,1)S(1)} %gather_fusion.1, pred[640]{0:T(1024)(128)(4,1)S(1)} %compare_and_fusion), kind=kOutput, calls=%fused_computation.41 | convolution fusion | flops 944455680 | bytes 4588160 | tf_op jit(solution)/shard_map/dot_general | solution.py:132
  42.8 0.3 copy.18
  43.2 1.2 copy.19
  44.4 7.4 %collective-permute-start.5 = (f32[320,5,128]{2,0,1:T(8,128)}, f32[320,5,128]{2,0,1:T(8,128)S(1)}, u32[]{:S(2)}, u32[]{:S(2)}) collective-permute-start(f32[320,5,128]{2,0,1:T(8,128)} %copy.19), channel_id=1, source_target_pairs={{0,16},{16,0},{1,17},{17,1},{2,18},{18,2},{3,19},{19,3},{4,20},{20... | collective-permute-start | bytes 2457608 | tf_op jit(solution)/shard_map/ppermute | solution.py:59
  51.8 2.2 %fusion.13 = f32[640,384]{1,0:T(8,128)S(1)} fusion(bf16[1152,128]{1,0:T(8,128)(2,1)} %collective-permute-done.9, bf16[1152,128]{1,0:T(8,128)(2,1)} %collective-permute-done.8, bf16[1152,128]{1,0:T(8,128)(2,1)} %collective-permute-done.7, bf16[640,1152]{1,0:T(8,128)(2,1)S(1)} %copy-done.1, pred[640]{0:T(1024)(128)(4,1)S(1)} %compare_and_fusion), kind=kOutput, calls=%fused_computation.32 | convolution fusion | flops 569622528 | bytes 3342976 | tf_op jit(solution)/shard_map/dot_general | solution.py:132
  54.0 0.2 copy.22
  54.3 1.0 copy.23
  55.3 3.7 %collective-permute-start.10 = (f32[320,3,128]{2,0,1:T(8,128)}, f32[320,3,128]{2,0,1:T(8,128)}, u32[]{:S(2)}, u32[]{:S(2)}) collective-permute-start(f32[320,3,128]{2,0,1:T(8,128)} %copy.23), channel_id=1, source_target_pairs={{0,16},{16,0},{1,17},{17,1},{2,18},{18,2},{3,19},{19,3},{4,20},{20... | collective-permute-start | bytes 1474568 | tf_op jit(solution)/shard_map/ppermute | solution.py:59
  59.0 0.2 copy.21
  59.2 0.2 copy.24
  59.4 1.4 collective-permute-done.10
  60.8 1.1 add.395
  61.9 0.7 slice.65
  62.6 1.9 %collective-permute-start.11 = (f32[160,3,128]{2,0,1:T(8,128)}, f32[160,3,128]{2,0,1:T(8,128)S(1)}, u32[]{:S(2)}, u32[]{:S(2)}) collective-permute-start(f32[160,3,128]{2,0,1:T(8,128)} %slice.65), channel_id=1, source_target_pairs={{0,32},{32,0},{1,33},{33,1},{2,34},{34,2},{3,35},{35,3},{4,36},{36... | collective-permute-start | bytes 737288 | tf_op jit(solution)/shard_map/ppermute | solution.py:59
  64.5 0.3 copy.17
  64.8 0.3 copy.20
  65.3 3.4 %collective-permute-start.6 = (f32[160,5,128]{2,0,1:T(8,128)S(1)}, f32[160,5,128]{2,0,1:T(8,128)S(1)}, u32[]{:S(2)}, u32[]{:S(2)}) collective-permute-start(f32[160,5,128]{2,0,1:T(8,128)S(1)} %slice.61), channel_id=1, source_target_pairs={{0,32},{32,0},{1,33},{33,1},{2,34},{34,2},{3,35},{35,3},{4,36},{36... | collective-permute-start | bytes 1228808 | tf_op jit(solution)/shard_map/ppermute | solution.py:59
  68.7 3.1 %collective-permute-done.11 = f32[160,3,128]{2,0,1:T(8,128)S(1)} collective-permute-done((f32[160,3,128]{2,0,1:T(8,128)}, f32[160,3,128]{2,0,1:T(8,128)S(1)}, u32[]{:S(2)}, u32[]{:S(2)}) %collective-permute-start.11) | collective-permute-done | bytes 245792 | tf_op jit(solution)/shard_map/ppermute | solution.py:59
  71.8 8.7 %collective-permute-done.6 = f32[160,5,128]{2,0,1:T(8,128)S(1)} collective-permute-done((f32[160,5,128]{2,0,1:T(8,128)S(1)}, f32[160,5,128]{2,0,1:T(8,128)S(1)}, u32[]{:S(2)}, u32[]{:S(2)}) %collective-permute-start.6) | collective-permute-done | bytes 409632 | tf_op jit(solution)/shard_map/ppermute | solution.py:59
  80.7 0.6 gather_fusion.2
  81.3 0.9 select_bitcast_fusion
  82.2 4.9 %all-to-all-start = ((f32[160,8,128]{2,0,1:T(8,128)}), f32[160,8,128]{2,0,1:T(8,128)S(1)}, u32[]{:S(2)}, u32[]{:S(2)}) async-start(f32[160,8,128]{2,0,1:T(8,128)} %select_bitcast_fusion), calls=%async_computation | async-start | bytes 1310720 | tf_op jit(solution)/shard_map/all_to_all | solution.py:147
  87.3 20.4 %all-to-all-done = f32[160,8,128]{2,0,1:T(8,128)S(1)} async-done(((f32[160,8,128]{2,0,1:T(8,128)}), f32[160,8,128]{2,0,1:T(8,128)S(1)}, u32[]{:S(2)}, u32[]{:S(2)}) %all-to-all-start) | async-done | bytes 655392 | tf_op jit(solution)/shard_map/all_to_all | solution.py:147
  107.8 0.6 gather_fusion.3
  108.5 31.1 %all_to_all.25 = f32[32,40,128]{2,1,0:T(8,128)S(1)} all-to-all(f32[32,40,128]{2,1,0:T(8,128)S(1)} %broadcast_select_fusion.3), channel_id=1, replica_groups=mesh['z'=8,'xl'=2,'c'=2,'y'=8,'xh'=2] {'z','xl','c'}, dimensions={0} | all-to-all | bytes 1310720 | tf_op jit(solution)/shard_map/all_to_all | solution.py:151
  139.6 1.3 multiply_reduce_fusion
  141.5 0.4 fusion.32
  142.0 0.2 fusion.10
  142.2 0.2 fusion
  142.4 0.4 fusion.30
  142.9 0.2 fusion.9
  143.1 0.2 fusion.1
  143.3 0.4 fusion.27
  143.7 0.2 fusion.8
  144.0 0.2 fusion.2
  144.2 0.4 fusion.24
  144.8 0.2 fusion.3
  145.1 0.4 fusion.21
  145.7 0.2 fusion.12
  146.0 15.8 %all_to_all.26 = bf16[8,160,128]{2,1,0:T(8,128)(2,1)S(1)} all-to-all(bf16[8,160,128]{2,1,0:T(8,128)(2,1)S(1)} %broadcast_in_dim.133), channel_id=1, replica_groups=mesh['z'=8,'xl'=2,'c'=2,'y'=8,'xh'=2] {'z'}, dimensions={0} | all-to-all | bytes 655360 | tf_op jit(solution)/shard_map/all_to_all | solution.py:165
  161.8 2.6 %collective-permute-start.12 = (bf16[1280,128]{1,0:T(8,128)(2,1)S(1)}, bf16[1280,128]{1,0:T(8,128)(2,1)S(1)}, u32[]{:S(2)}, u32[]{:S(2)}) collective-permute-start(bf16[1280,128]{1,0:T(8,128)(2,1)S(1)} %bitcast.113), channel_id=1, source_target_pairs={{0,32},{32,0},{1,33},{33,1},{2,34},{34,2},{3,35},{35,3},{4,36},{36... | collective-permute-start | bytes 983048 | tf_op jit(solution)/shard_map/ppermute | solution.py:91
  164.4 7.0 %collective-permute-done.12 = bf16[1280,128]{1,0:T(8,128)(2,1)S(1)} collective-permute-done((bf16[1280,128]{1,0:T(8,128)(2,1)S(1)}, bf16[1280,128]{1,0:T(8,128)(2,1)S(1)}, u32[]{:S(2)}, u32[]{:S(2)}) %collective-permute-start.12) | collective-permute-done | bytes 327712 | tf_op jit(solution)/shard_map/ppermute | solution.py:91
  171.5 4.3 %collective-permute-start.13 = (bf16[2560,128]{1,0:T(8,128)(2,1)S(1)}, bf16[2560,128]{1,0:T(8,128)(2,1)S(1)}, u32[]{:S(2)}, u32[]{:S(2)}) collective-permute-start(bf16[2560,128]{1,0:T(8,128)(2,1)S(1)} %pad_maximum_fusion.3), channel_id=1, source_target_pairs={{0,16},{16,0},{1,17},{17,1},{2,18},{18,2},{3,19},{19,3},{4,20},{20... | collective-permute-start | bytes 1966088 | tf_op jit(solution)/shard_map/ppermute | solution.py:91
  175.8 0.7 gather_fusion
  176.7 0.8 collective-permute-done.13
  177.6 0.8 gather_fusion.4
  178.4 3.4 %bitcast_select_fusion = bf16[5120,128]{1,0:T(8,128)(2,1)} fusion(bf16[32,160,128]{2,1,0:T(8,128)(2,1)S(1)} %gather_fusion.4, pred[5120]{0:T(1024)(128)(4,1)S(1)} %broadcast_in_dim.114), kind=kLoop, calls=%fused_computation.8 | loop fusion | flops 655360 | bytes 2626560 | tf_op jit(solution)/shard_map/jit(take_along_axis)/select_n | solution.py:38
  (51 shorter events, 1.8 us)
Async XLA Ops:
  2.1 32.6 %copy-start.2 = (bf16[320,1152]{1,0:T(8,128)(2,1)S(1)}, bf16[320,1152]{1,0:T(8,128)(2,1)}, u32[]{:S(2)}) copy-start(bf16[320,1152]{1,0:T(8,128)(2,1)} %param.7) | copy-start | bytes 2211844
  4.1 12.7 %collective-permute-start.1 = (bf16[1152,128]{1,0:T(8,128)(2,1)S(1)}, bf16[1152,128]{1,0:T(8,128)(2,1)S(1)}, u32[]{:S(2)}, u32[]{:S(2)}) collective-permute-start(bf16[1152,128]{1,0:T(8,128)(2,1)S(1)} %get-tuple-element.6), channel_id=1, source_target_pairs={{0,2},{2,4},{4,6},{6,8},{8,10},{10,12},{12,14},{14,0},{1,3},{3,5},... | collective-permute-start | bytes 884744 | tf_op jit(solution)/shard_map/ppermute | solution.py:82
  8.1 10.6 %collective-permute-start.2 = (bf16[1152,128]{1,0:T(8,128)(2,1)S(1)}, bf16[1152,128]{1,0:T(8,128)(2,1)S(1)}, u32[]{:S(2)}, u32[]{:S(2)}) collective-permute-start(bf16[1152,128]{1,0:T(8,128)(2,1)S(1)} %get-tuple-element.6), channel_id=1, source_target_pairs={{0,14},{2,0},{4,2},{6,4},{8,6},{10,8},{12,10},{14,12},{1,15},{3,1}... | collective-permute-start | bytes 884744 | tf_op jit(solution)/shard_map/ppermute | solution.py:85
  12.0 22.8 %collective-permute-start = (bf16[320,1152]{1,0:T(8,128)(2,1)}, bf16[320,1152]{1,0:T(8,128)(2,1)S(1)}, u32[]{:S(2)}, u32[]{:S(2)}) collective-permute-start(bf16[320,1152]{1,0:T(8,128)(2,1)} %param.7), channel_id=1, source_target_pairs={{0,1},{1,0},{2,3},{3,2},{4,5},{5,4},{6,7},{7,6},{8,9},{9,8},{10,11... | collective-permute-start | bytes 2211848 | tf_op jit(solution)/shard_map/ppermute | solution.py:91
  16.8 9.0 %collective-permute-start.3 = (bf16[1152,128]{1,0:T(8,128)(2,1)S(1)}, bf16[1152,128]{1,0:T(8,128)(2,1)S(1)}, u32[]{:S(2)}, u32[]{:S(2)}) collective-permute-start(bf16[1152,128]{1,0:T(8,128)(2,1)S(1)} %collective-permute-done.1), channel_id=1, source_target_pairs={{0,2},{2,4},{4,6},{6,8},{8,10},{10,12},{12,14},{14,0},{1,3},{3,5},... | collective-permute-start | bytes 884744 | tf_op jit(solution)/shard_map/ppermute | solution.py:82
  18.7 9.0 %collective-permute-start.4 = (bf16[1152,128]{1,0:T(8,128)(2,1)S(1)}, bf16[1152,128]{1,0:T(8,128)(2,1)}, u32[]{:S(2)}, u32[]{:S(2)}) collective-permute-start(bf16[1152,128]{1,0:T(8,128)(2,1)S(1)} %collective-permute-done.2), channel_id=1, source_target_pairs={{0,14},{2,0},{4,2},{6,4},{8,6},{10,8},{12,10},{14,12},{1,15},{3,1}... | collective-permute-start | bytes 884744 | tf_op jit(solution)/shard_map/ppermute | solution.py:85
  25.8 12.2 %collective-permute-start.7 = (bf16[1152,128]{1,0:T(8,128)(2,1)S(1)}, bf16[1152,128]{1,0:T(8,128)(2,1)}, u32[]{:S(2)}, u32[]{:S(2)}) collective-permute-start(bf16[1152,128]{1,0:T(8,128)(2,1)S(1)} %collective-permute-done.3), channel_id=1, source_target_pairs={{0,2},{2,4},{4,6},{6,8},{8,10},{10,12},{12,14},{14,0},{1,3},{3,5},... | collective-permute-start | bytes 884744 | tf_op jit(solution)/shard_map/ppermute | solution.py:82
  27.7 24.1 %collective-permute-start.8 = (bf16[1152,128]{1,0:T(8,128)(2,1)}, bf16[1152,128]{1,0:T(8,128)(2,1)}, u32[]{:S(2)}, u32[]{:S(2)}) collective-permute-start(bf16[1152,128]{1,0:T(8,128)(2,1)} %collective-permute-done.4), channel_id=1, source_target_pairs={{0,14},{2,0},{4,2},{6,4},{8,6},{10,8},{12,10},{14,12},{1,15},{3,1}... | collective-permute-start | bytes 884744 | tf_op jit(solution)/shard_map/ppermute | solution.py:85
  37.9 2.0 %copy-start = (bf16[640,1152]{1,0:T(8,128)(2,1)}, bf16[640,1152]{1,0:T(8,128)(2,1)S(1)}, u32[]{:S(2)}) copy-start(bf16[640,1152]{1,0:T(8,128)(2,1)S(1)} %gather_fusion.1) | copy-start | bytes 4423684
  37.9 13.9 %collective-permute-start.9 = (bf16[1152,128]{1,0:T(8,128)(2,1)}, bf16[1152,128]{1,0:T(8,128)(2,1)}, u32[]{:S(2)}, u32[]{:S(2)}) collective-permute-start(bf16[1152,128]{1,0:T(8,128)(2,1)} %collective-permute-done.7), channel_id=1, source_target_pairs={{0,2},{2,4},{4,6},{6,8},{8,10},{10,12},{12,14},{14,0},{1,3},{3,5},... | collective-permute-start | bytes 884744 | tf_op jit(solution)/shard_map/ppermute | solution.py:82
  43.2 8.6 %copy-start.1 = (bf16[640,1152]{1,0:T(8,128)(2,1)S(1)}, bf16[640,1152]{1,0:T(8,128)(2,1)}, u32[]{:S(2)}) copy-start(bf16[640,1152]{1,0:T(8,128)(2,1)} %copy-done) | copy-start | bytes 4423684
  44.4 20.8 %collective-permute-start.5 = (f32[320,5,128]{2,0,1:T(8,128)}, f32[320,5,128]{2,0,1:T(8,128)S(1)}, u32[]{:S(2)}, u32[]{:S(2)}) collective-permute-start(f32[320,5,128]{2,0,1:T(8,128)} %copy.19), channel_id=1, source_target_pairs={{0,16},{16,0},{1,17},{17,1},{2,18},{18,2},{3,19},{19,3},{4,20},{20... | collective-permute-start | bytes 2457608 | tf_op jit(solution)/shard_map/ppermute | solution.py:59
  55.3 5.5 %collective-permute-start.10 = (f32[320,3,128]{2,0,1:T(8,128)}, f32[320,3,128]{2,0,1:T(8,128)}, u32[]{:S(2)}, u32[]{:S(2)}) collective-permute-start(f32[320,3,128]{2,0,1:T(8,128)} %copy.23), channel_id=1, source_target_pairs={{0,16},{16,0},{1,17},{17,1},{2,18},{18,2},{3,19},{19,3},{4,20},{20... | collective-permute-start | bytes 1474568 | tf_op jit(solution)/shard_map/ppermute | solution.py:59
  62.6 9.2 %collective-permute-start.11 = (f32[160,3,128]{2,0,1:T(8,128)}, f32[160,3,128]{2,0,1:T(8,128)S(1)}, u32[]{:S(2)}, u32[]{:S(2)}) collective-permute-start(f32[160,3,128]{2,0,1:T(8,128)} %slice.65), channel_id=1, source_target_pairs={{0,32},{32,0},{1,33},{33,1},{2,34},{34,2},{3,35},{35,3},{4,36},{36... | collective-permute-start | bytes 737288 | tf_op jit(solution)/shard_map/ppermute | solution.py:59
  65.3 15.3 %collective-permute-start.6 = (f32[160,5,128]{2,0,1:T(8,128)S(1)}, f32[160,5,128]{2,0,1:T(8,128)S(1)}, u32[]{:S(2)}, u32[]{:S(2)}) collective-permute-start(f32[160,5,128]{2,0,1:T(8,128)S(1)} %slice.61), channel_id=1, source_target_pairs={{0,32},{32,0},{1,33},{33,1},{2,34},{34,2},{3,35},{35,3},{4,36},{36... | collective-permute-start | bytes 1228808 | tf_op jit(solution)/shard_map/ppermute | solution.py:59
  81.3 5.9 %copy-start.4 = (s32[1,32]{1,0:T(1,128)S(1)}, s32[1,32]{1,0:T(1,128)}, u32[]{:S(2)}) copy-start(s32[1,32]{1,0:T(1,128)} %param.12) | copy-start | bytes 388
  82.2 25.5 %all-to-all-start = ((f32[160,8,128]{2,0,1:T(8,128)}), f32[160,8,128]{2,0,1:T(8,128)S(1)}, u32[]{:S(2)}, u32[]{:S(2)}) async-start(f32[160,8,128]{2,0,1:T(8,128)} %select_bitcast_fusion), calls=%async_computation | async-start | bytes 1310720 | tf_op jit(solution)/shard_map/all_to_all | solution.py:147
  108.4 31.2 %copy-start.3 = (f32[160,128]{1,0:T(8,128)S(1)}, f32[160,128]{1,0:T(8,128)}, u32[]{:S(2)}) copy-start(f32[160,128]{1,0:T(8,128)} %param.13) | copy-start | bytes 245764
  161.8 9.7 %collective-permute-start.12 = (bf16[1280,128]{1,0:T(8,128)(2,1)S(1)}, bf16[1280,128]{1,0:T(8,128)(2,1)S(1)}, u32[]{:S(2)}, u32[]{:S(2)}) collective-permute-start(bf16[1280,128]{1,0:T(8,128)(2,1)S(1)} %bitcast.113), channel_id=1, source_target_pairs={{0,32},{32,0},{1,33},{33,1},{2,34},{34,2},{3,35},{35,3},{4,36},{36... | collective-permute-start | bytes 983048 | tf_op jit(solution)/shard_map/ppermute | solution.py:91
  171.5 6.0 %collective-permute-start.13 = (bf16[2560,128]{1,0:T(8,128)(2,1)S(1)}, bf16[2560,128]{1,0:T(8,128)(2,1)S(1)}, u32[]{:S(2)}, u32[]{:S(2)}) collective-permute-start(bf16[2560,128]{1,0:T(8,128)(2,1)S(1)} %pad_maximum_fusion.3), channel_id=1, source_target_pairs={{0,16},{16,0},{1,17},{17,1},{2,18},{18,2},{3,19},{19,3},{4,20},{20... | collective-permute-start | bytes 1966088 | tf_op jit(solution)/shard_map/ppermute | solution.py:91

commit v11 on v10

--- a/solution.py
+++ b/solution.py
@@ -128,16 +128,18 @@
     source_row = shard_slot * feature_rows + (j % sub_blocks) * block_rows + u * quarter_rows + r
     arranged = jnp.take(pair_rows, source_row, axis=0)
 
-    def reduced_heads(pieces):
+    def reduced_heads(rows, pieces):
         partial = jnp.dot(
-            arranged, jnp.concatenate(pieces, axis=1), preferred_element_type=jnp.float32
+            rows, jnp.concatenate(pieces, axis=1), preferred_element_type=jnp.float32
         ).reshape(2 * feature_rows, len(pieces), head_width)
         kept = pair_sum_scatter(partial, "c")
         return pair_sum_scatter(kept, "xl")
 
     early = 2 * 2 + 1
+    kept_early = reduced_heads(arranged, ring_pieces[:early])
+    arranged_late, kept_early = lax.optimization_barrier((arranged, kept_early))
     kept_ring_order = jnp.concatenate(
-        [reduced_heads(ring_pieces[:early]), reduced_heads(ring_pieces[early:])], axis=1
+        [kept_early, reduced_heads(arranged_late, ring_pieces[early:])], axis=1
     )
     head = jnp.arange(y_count, dtype=jnp.int32)
     ahead = (head - y) % y_count

time: 183 us -> 189 us (1.033)
  waiting for transfers between devices: 42.4 us -> 53.2 us
  matrix products: 9.31 us -> 6.65 us
  local copies, waits for them, and re-layouts: 14.7 us -> 12.7 us
    ppermute x4, waiting for transfers between devices: 0.97 us -> 13.6 us  [ring_gather(): from_left = lax.ppermute(from_left, axis, to_right)]
    ppermute x4, waiting for transfers between devices: 13.2 us -> 9.08 us  [pair_sum_scatter(): return blocks[:half] + lax.ppermute(blocks[half:], axis, SWAP)]
    dot_general x2, matrix products: 5 us -> 2.35 us  [reduced_heads(): jnp.dot(rows, jnp.concatenate(pieces, axis=1), preferred_element_type=jnp...]
    slice x12, local copies, waits for them, and re-layouts: 4.78 us -> 2.39 us  [pair_sum_scatter(): return blocks[:half] + lax.ppermute(blocks[half:], axis, SWAP)]
  transfers between devices with their start and end apart: 15 -> 15, of which waited for: 7 -> 11; matrix products, arithmetic and copies ran while one was open for 11% -> 3% of each run, Pallas kernels for 0% -> 0%
where the time goes in v11:
time: 189 us; the launch traced here: 188 us
  starting transfers between devices  56.8 us (30%)
  waiting for transfers between devices  53.2 us (28%)
  blocking collectives  46.3 us (24%)
  local copies, waits for them, and re-layouts  12.7 us (7%)
  other arithmetic  10.3 us (5%)
  matrix products  6.65 us (4%)
  between operations  1.9 us (1%)
    all_to_all x1, blocking collectives, shards(): lax.all_to_all(in_owner_order, DP, split_axis=0, concat_axis=0, tiled=True)  30.5 us
    all_to_all x1, waiting for transfers between devices, shards(): lax.all_to_all(kept, 'y', split_axis=1, concat_axis=0, tiled=True)  20.4 us
    ppermute x4, starting transfers between devices, pair_sum_scatter(): return blocks[:half] + lax.ppermute(blocks[half:], axis, SWAP)  16.4 us
    all_to_all x1, blocking collectives, shards(): lax.all_to_all(jnp.broadcast_to(own_update[None], (z_count,) + own_update...  15.8 us
    ppermute x4, waiting for transfers between devices, ring_gather(): from_left = lax.ppermute(from_left, axis, to_right)  13.6 us
    ppermute x3, starting transfers between devices, ring_gather(): from_right = lax.ppermute(from_right, axis, to_left)  12.9 us
    ppermute x3, starting transfers between devices, pair_gather(): return jnp.concatenate([piece, lax.ppermute(piece, axis, SWAP)], axis=0)  11.5 us
    ppermute x4, starting transfers between devices, ring_gather(): from_left = lax.ppermute(from_left, axis, to_right)  9.76 us
  transfers between devices with their start and end apart: 15, of which 11 were waited for; matrix products, arithmetic and copies ran while one was open for 3% of the time, Pallas kernels for 0%

profile of v11, /device:TPU:1, one launch (start us, length us, event | category | flops | bytes accessed | tf_op | source)
XLA Modules:
  0.0 187.9 jit_solution(9165992013450974554)
XLA Ops:
  0.6 0.8 select_reduce_fusion
  1.4 0.7 multiply_multiply_fusion
  2.1 2.0 %constant_dynamic-update-slice_fusion.4 = (bf16[1152,640]{1,0:T(8,128)(2,1)}, bf16[1152,128]{1,0:T(8,128)(2,1)S(1)}) fusion(f32[1152]{0:T(1024)S(1)} %multiply_multiply_fusion, bf16[1152,128]{1,0:T(8,128)(2,1)} %param.8), kind=kLoop, calls=%fused_computation.74 | loop fusion | flops 442367 | bytes 889344
  4.1 4.0 %collective-permute-start.1 = (bf16[1152,128]{1,0:T(8,128)(2,1)S(1)}, bf16[1152,128]{1,0:T(8,128)(2,1)S(1)}, u32[]{:S(2)}, u32[]{:S(2)}) collective-permute-start(bf16[1152,128]{1,0:T(8,128)(2,1)S(1)} %get-tuple-element.10), channel_id=1, source_target_pairs={{0,2},{2,4},{4,6},{6,8},{8,10},{10,12},{12,14},{14,0},{1,3},{3,5},... | collective-permute-start | bytes 884744 | tf_op jit(solution)/shard_map/ppermute | solution.py:82
  8.2 3.8 %collective-permute-start.2 = (bf16[1152,128]{1,0:T(8,128)(2,1)S(1)}, bf16[1152,128]{1,0:T(8,128)(2,1)S(1)}, u32[]{:S(2)}, u32[]{:S(2)}) collective-permute-start(bf16[1152,128]{1,0:T(8,128)(2,1)S(1)} %get-tuple-element.10), channel_id=1, source_target_pairs={{0,14},{2,0},{4,2},{6,4},{8,6},{10,8},{12,10},{14,12},{1,15},{3,1}... | collective-permute-start | bytes 884744 | tf_op jit(solution)/shard_map/ppermute | solution.py:85
  12.0 4.7 %collective-permute-start = (bf16[320,1152]{1,0:T(8,128)(2,1)}, bf16[320,1152]{1,0:T(8,128)(2,1)S(1)}, u32[]{:S(2)}, u32[]{:S(2)}) collective-permute-start(bf16[320,1152]{1,0:T(8,128)(2,1)} %param.7), channel_id=1, source_target_pairs={{0,1},{1,0},{2,3},{3,2},{4,5},{5,4},{6,7},{7,6},{8,9},{9,8},{10,11... | collective-permute-start | bytes 2211848 | tf_op jit(solution)/shard_map/ppermute | solution.py:91
  16.8 1.9 %collective-permute-start.3 = (bf16[1152,128]{1,0:T(8,128)(2,1)S(1)}, bf16[1152,128]{1,0:T(8,128)(2,1)S(1)}, u32[]{:S(2)}, u32[]{:S(2)}) collective-permute-start(bf16[1152,128]{1,0:T(8,128)(2,1)S(1)} %collective-permute-done.1), channel_id=1, source_target_pairs={{0,2},{2,4},{4,6},{6,8},{8,10},{10,12},{12,14},{14,0},{1,3},{3,5},... | collective-permute-start | bytes 884744 | tf_op jit(solution)/shard_map/ppermute | solution.py:82
  18.7 0.8 constant_dynamic-update-slice_fusion.3
  19.5 4.6 %collective-permute-start.4 = (bf16[1152,128]{1,0:T(8,128)(2,1)S(1)}, bf16[1152,128]{1,0:T(8,128)(2,1)S(1)}, u32[]{:S(2)}, u32[]{:S(2)}) collective-permute-start(bf16[1152,128]{1,0:T(8,128)(2,1)S(1)} %collective-permute-done.2), channel_id=1, source_target_pairs={{0,14},{2,0},{4,2},{6,4},{8,6},{10,8},{12,10},{14,12},{1,15},{3,1}... | collective-permute-start | bytes 884744 | tf_op jit(solution)/shard_map/ppermute | solution.py:85
  24.1 0.7 constant_dynamic-update-slice_fusion.2
  24.8 1.0 collective-permute-done.3
  25.8 0.8 constant_dynamic-update-slice_fusion.1
  26.6 1.1 collective-permute-done.4
  27.7 0.8 constant_dynamic-update-slice_fusion
  28.6 1.2 collective-permute-done
  29.9 3.0 %gather_fusion.1 = bf16[640,1152]{1,0:T(8,128)(2,1)S(1)} fusion(bf16[640,1152]{1,0:T(8,128)(2,1)S(1)} %pad_maximum_fusion, s32[1024]{0:T(1024)S(1)} %pad_clamp_fusion.3), kind=kCustom, calls=%fused_computation.1 | custom fusion | bytes 2951680 | tf_op jit(solution)/shard_map/jit(_take)/gather | solution.py:129
  32.9 0.2 broadcast_select_fusion
  33.2 1.1 copy-done.8
  34.3 1.4 fusion.76
  35.8 0.3 copy.18
  36.1 0.3 copy.19
  36.5 6.7 %collective-permute-start.5 = (f32[320,5,128]{2,0,1:T(8,128)S(1)}, f32[320,5,128]{2,0,1:T(8,128)S(1)}, u32[]{:S(2)}, u32[]{:S(2)}) collective-permute-start(f32[320,5,128]{2,0,1:T(8,128)S(1)} %copy.19), channel_id=1, source_target_pairs={{0,16},{16,0},{1,17},{17,1},{2,18},{18,2},{3,19},{19,3},{4,20},{20... | collective-permute-start | bytes 2457608 | tf_op jit(solution)/shard_map/ppermute | solution.py:59
  43.1 0.3 copy.17
  43.5 0.3 copy.20
  43.8 1.3 collective-permute-done.5
  45.2 3.3 %collective-permute-start.6 = (f32[160,5,128]{2,0,1:T(8,128)S(1)}, f32[160,5,128]{2,0,1:T(8,128)S(1)}, u32[]{:S(2)}, u32[]{:S(2)}) collective-permute-start(f32[160,5,128]{2,0,1:T(8,128)S(1)} %slice.61), channel_id=1, source_target_pairs={{0,32},{32,0},{1,33},{33,1},{2,34},{34,2},{3,35},{35,3},{4,36},{36... | collective-permute-start | bytes 1228808 | tf_op jit(solution)/shard_map/ppermute | solution.py:59
  48.5 1.9 %collective-permute-start.7 = (bf16[1152,128]{1,0:T(8,128)(2,1)S(1)}, bf16[1152,128]{1,0:T(8,128)(2,1)S(1)}, u32[]{:S(2)}, u32[]{:S(2)}) collective-permute-start(bf16[1152,128]{1,0:T(8,128)(2,1)S(1)} %copy-done.6), channel_id=1, source_target_pairs={{0,2},{2,4},{4,6},{6,8},{8,10},{10,12},{12,14},{14,0},{1,3},{3,5},... | collective-permute-start | bytes 884744 | tf_op jit(solution)/shard_map/ppermute | solution.py:82
  50.4 4.6 %collective-permute-start.8 = (bf16[1152,128]{1,0:T(8,128)(2,1)S(1)}, bf16[1152,128]{1,0:T(8,128)(2,1)S(1)}, u32[]{:S(2)}, u32[]{:S(2)}) collective-permute-start(bf16[1152,128]{1,0:T(8,128)(2,1)S(1)} %copy-done.4), channel_id=1, source_target_pairs={{0,14},{2,0},{4,2},{6,4},{8,6},{10,8},{12,10},{14,12},{1,15},{3,1}... | collective-permute-start | bytes 884744 | tf_op jit(solution)/shard_map/ppermute | solution.py:85
  55.0 4.5 %collective-permute-done.7 = bf16[1152,128]{1,0:T(8,128)(2,1)S(1)} collective-permute-done((bf16[1152,128]{1,0:T(8,128)(2,1)S(1)}, bf16[1152,128]{1,0:T(8,128)(2,1)S(1)}, u32[]{:S(2)}, u32[]{:S(2)}) %collective-permute-start.7) | collective-permute-done | bytes 294944 | tf_op jit(solution)/shard_map/ppermute | solution.py:82
  59.5 1.9 %collective-permute-start.9 = (bf16[1152,128]{1,0:T(8,128)(2,1)S(1)}, bf16[1152,128]{1,0:T(8,128)(2,1)S(1)}, u32[]{:S(2)}, u32[]{:S(2)}) collective-permute-start(bf16[1152,128]{1,0:T(8,128)(2,1)S(1)} %collective-permute-done.7), channel_id=1, source_target_pairs={{0,2},{2,4},{4,6},{6,8},{8,10},{10,12},{12,14},{14,0},{1,3},{3,5},... | collective-permute-start | bytes 884744 | tf_op jit(solution)/shard_map/ppermute | solution.py:82
  61.5 8.1 %collective-permute-done.9 = bf16[1152,128]{1,0:T(8,128)(2,1)S(1)} collective-permute-done((bf16[1152,128]{1,0:T(8,128)(2,1)S(1)}, bf16[1152,128]{1,0:T(8,128)(2,1)S(1)}, u32[]{:S(2)}, u32[]{:S(2)}) %collective-permute-start.9) | collective-permute-done | bytes 294944 | tf_op jit(solution)/shard_map/ppermute | solution.py:82
  69.6 1.0 fusion.13
  70.7 0.2 copy.22
  70.9 0.2 copy.23
  71.1 4.3 %collective-permute-start.10 = (f32[320,3,128]{2,0,1:T(8,128)S(1)}, f32[320,3,128]{2,0,1:T(8,128)S(1)}, u32[]{:S(2)}, u32[]{:S(2)}) collective-permute-start(f32[320,3,128]{2,0,1:T(8,128)S(1)} %copy.23), channel_id=1, source_target_pairs={{0,16},{16,0},{1,17},{17,1},{2,18},{18,2},{3,19},{19,3},{4,20},{20... | collective-permute-start | bytes 1474568 | tf_op jit(solution)/shard_map/ppermute | solution.py:59
  75.4 0.2 copy.21
  75.9 1.0 collective-permute-done.10
  76.9 2.2 %collective-permute-start.11 = (f32[160,3,128]{2,0,1:T(8,128)S(1)}, f32[160,3,128]{2,0,1:T(8,128)S(1)}, u32[]{:S(2)}, u32[]{:S(2)}) collective-permute-start(f32[160,3,128]{2,0,1:T(8,128)S(1)} %slice.65), channel_id=1, source_target_pairs={{0,32},{32,0},{1,33},{33,1},{2,34},{34,2},{3,35},{35,3},{4,36},{36... | collective-permute-start | bytes 737288 | tf_op jit(solution)/shard_map/ppermute | solution.py:59
  79.2 6.8 %collective-permute-done.11 = f32[160,3,128]{2,0,1:T(8,128)S(1)} collective-permute-done((f32[160,3,128]{2,0,1:T(8,128)S(1)}, f32[160,3,128]{2,0,1:T(8,128)S(1)}, u32[]{:S(2)}, u32[]{:S(2)}) %collective-permute-start.11) | collective-permute-done | bytes 245792 | tf_op jit(solution)/shard_map/ppermute | solution.py:59
  86.1 0.6 gather_fusion.2
  86.7 0.9 select_bitcast_fusion
  87.6 6.3 %all-to-all-start = ((f32[160,8,128]{2,0,1:T(8,128)}), f32[160,8,128]{2,0,1:T(8,128)S(1)}, u32[]{:S(2)}, u32[]{:S(2)}) async-start(f32[160,8,128]{2,0,1:T(8,128)} %select_bitcast_fusion), calls=%async_computation | async-start | bytes 1310720 | tf_op jit(solution)/shard_map/all_to_all | solution.py:149
  94.1 20.4 %all-to-all-done = f32[160,8,128]{2,0,1:T(8,128)S(1)} async-done(((f32[160,8,128]{2,0,1:T(8,128)}), f32[160,8,128]{2,0,1:T(8,128)S(1)}, u32[]{:S(2)}, u32[]{:S(2)}) %all-to-all-start) | async-done | bytes 655392 | tf_op jit(solution)/shard_map/all_to_all | solution.py:149
  114.5 0.6 gather_fusion.3
  115.3 30.5 %all_to_all.25 = f32[32,40,128]{2,1,0:T(8,128)S(1)} all-to-all(f32[32,40,128]{2,1,0:T(8,128)S(1)} %broadcast_select_fusion.1), channel_id=1, replica_groups=mesh['z'=8,'xl'=2,'c'=2,'y'=8,'xh'=2] {'z','xl','c'}, dimensions={0} | all-to-all | bytes 1310720 | tf_op jit(solution)/shard_map/all_to_all | solution.py:153
  145.8 1.3 multiply_reduce_fusion
  147.7 0.4 fusion.31
  148.4 0.2 fusion
  148.6 0.4 fusion.29
  149.3 0.2 fusion.1
  149.5 0.4 fusion.26
  150.1 0.2 fusion.2
  150.4 0.4 fusion.23
  151.0 0.2 fusion.3
  151.2 0.4 fusion.20
  151.9 0.2 fusion.12
  152.2 15.8 %all_to_all.26 = bf16[8,160,128]{2,1,0:T(8,128)(2,1)S(1)} all-to-all(bf16[8,160,128]{2,1,0:T(8,128)(2,1)S(1)} %broadcast_in_dim.133), channel_id=1, replica_groups=mesh['z'=8,'xl'=2,'c'=2,'y'=8,'xh'=2] {'z'}, dimensions={0} | all-to-all | bytes 655360 | tf_op jit(solution)/shard_map/all_to_all | solution.py:167
  168.0 2.6 %collective-permute-start.12 = (bf16[1280,128]{1,0:T(8,128)(2,1)S(1)}, bf16[1280,128]{1,0:T(8,128)(2,1)S(1)}, u32[]{:S(2)}, u32[]{:S(2)}) collective-permute-start(bf16[1280,128]{1,0:T(8,128)(2,1)S(1)} %bitcast.115), channel_id=1, source_target_pairs={{0,32},{32,0},{1,33},{33,1},{2,34},{34,2},{3,35},{35,3},{4,36},{36... | collective-permute-start | bytes 983048 | tf_op jit(solution)/shard_map/ppermute | solution.py:91
  170.6 7.1 %collective-permute-done.12 = bf16[1280,128]{1,0:T(8,128)(2,1)S(1)} collective-permute-done((bf16[1280,128]{1,0:T(8,128)(2,1)S(1)}, bf16[1280,128]{1,0:T(8,128)(2,1)S(1)}, u32[]{:S(2)}, u32[]{:S(2)}) %collective-permute-start.12) | collective-permute-done | bytes 327712 | tf_op jit(solution)/shard_map/ppermute | solution.py:91
  177.7 4.3 %collective-permute-start.13 = (bf16[2560,128]{1,0:T(8,128)(2,1)S(1)}, bf16[2560,128]{1,0:T(8,128)(2,1)S(1)}, u32[]{:S(2)}, u32[]{:S(2)}) collective-permute-start(bf16[2560,128]{1,0:T(8,128)(2,1)S(1)} %pad_maximum_fusion.3), channel_id=1, source_target_pairs={{0,16},{16,0},{1,17},{17,1},{2,18},{18,2},{3,19},{19,3},{4,20},{20... | collective-permute-start | bytes 1966088 | tf_op jit(solution)/shard_map/ppermute | solution.py:91
  182.0 0.7 gather_fusion
  182.9 0.8 collective-permute-done.13
  183.8 0.8 gather_fusion.4
  184.6 3.4 %bitcast_select_fusion = bf16[5120,128]{1,0:T(8,128)(2,1)} fusion(bf16[32,160,128]{2,1,0:T(8,128)(2,1)S(1)} %gather_fusion.4, pred[5120]{0:T(1024)(128)(4,1)S(1)} %broadcast_in_dim.114), kind=kLoop, calls=%fused_computation.8 | loop fusion | flops 655360 | bytes 2626560 | tf_op jit(solution)/shard_map/jit(take_along_axis)/select_n | solution.py:38
  (62 shorter events, 2.8 us)
Async XLA Ops:
  2.1 27.6 %copy-start.2 = (bf16[320,1152]{1,0:T(8,128)(2,1)S(1)}, bf16[320,1152]{1,0:T(8,128)(2,1)}, u32[]{:S(2)}) copy-start(bf16[320,1152]{1,0:T(8,128)(2,1)} %param.7) | copy-start | bytes 2211844
  4.1 12.7 %collective-permute-start.1 = (bf16[1152,128]{1,0:T(8,128)(2,1)S(1)}, bf16[1152,128]{1,0:T(8,128)(2,1)S(1)}, u32[]{:S(2)}, u32[]{:S(2)}) collective-permute-start(bf16[1152,128]{1,0:T(8,128)(2,1)S(1)} %get-tuple-element.10), channel_id=1, source_target_pairs={{0,2},{2,4},{4,6},{6,8},{8,10},{10,12},{12,14},{14,0},{1,3},{3,5},... | collective-permute-start | bytes 884744 | tf_op jit(solution)/shard_map/ppermute | solution.py:82
  8.2 11.3 %collective-permute-start.2 = (bf16[1152,128]{1,0:T(8,128)(2,1)S(1)}, bf16[1152,128]{1,0:T(8,128)(2,1)S(1)}, u32[]{:S(2)}, u32[]{:S(2)}) collective-permute-start(bf16[1152,128]{1,0:T(8,128)(2,1)S(1)} %get-tuple-element.10), channel_id=1, source_target_pairs={{0,14},{2,0},{4,2},{6,4},{8,6},{10,8},{12,10},{14,12},{1,15},{3,1}... | collective-permute-start | bytes 884744 | tf_op jit(solution)/shard_map/ppermute | solution.py:85
  12.0 17.8 %collective-permute-start = (bf16[320,1152]{1,0:T(8,128)(2,1)}, bf16[320,1152]{1,0:T(8,128)(2,1)S(1)}, u32[]{:S(2)}, u32[]{:S(2)}) collective-permute-start(bf16[320,1152]{1,0:T(8,128)(2,1)} %param.7), channel_id=1, source_target_pairs={{0,1},{1,0},{2,3},{3,2},{4,5},{5,4},{6,7},{7,6},{8,9},{9,8},{10,11... | collective-permute-start | bytes 2211848 | tf_op jit(solution)/shard_map/ppermute | solution.py:91
  16.8 9.0 %collective-permute-start.3 = (bf16[1152,128]{1,0:T(8,128)(2,1)S(1)}, bf16[1152,128]{1,0:T(8,128)(2,1)S(1)}, u32[]{:S(2)}, u32[]{:S(2)}) collective-permute-start(bf16[1152,128]{1,0:T(8,128)(2,1)S(1)} %collective-permute-done.1), channel_id=1, source_target_pairs={{0,2},{2,4},{4,6},{6,8},{8,10},{10,12},{12,14},{14,0},{1,3},{3,5},... | collective-permute-start | bytes 884744 | tf_op jit(solution)/shard_map/ppermute | solution.py:82
  19.5 8.2 %collective-permute-start.4 = (bf16[1152,128]{1,0:T(8,128)(2,1)S(1)}, bf16[1152,128]{1,0:T(8,128)(2,1)S(1)}, u32[]{:S(2)}, u32[]{:S(2)}) collective-permute-start(bf16[1152,128]{1,0:T(8,128)(2,1)S(1)} %collective-permute-done.2), channel_id=1, source_target_pairs={{0,14},{2,0},{4,2},{6,4},{8,6},{10,8},{12,10},{14,12},{1,15},{3,1}... | collective-permute-start | bytes 884744 | tf_op jit(solution)/shard_map/ppermute | solution.py:85
  25.8 2.8 %copy-start.5 = (bf16[1152,128]{1,0:T(8,128)(2,1)}, bf16[1152,128]{1,0:T(8,128)(2,1)S(1)}, u32[]{:S(2)}) copy-start(bf16[1152,128]{1,0:T(8,128)(2,1)S(1)} %collective-permute-done.3) | copy-start | bytes 884740
  27.7 0.9 copy-start.3
  32.9 1.4 copy-start.8
  34.3 1.4 copy-start
  36.5 8.6 %collective-permute-start.5 = (f32[320,5,128]{2,0,1:T(8,128)S(1)}, f32[320,5,128]{2,0,1:T(8,128)S(1)}, u32[]{:S(2)}, u32[]{:S(2)}) collective-permute-start(f32[320,5,128]{2,0,1:T(8,128)S(1)} %copy.19), channel_id=1, source_target_pairs={{0,16},{16,0},{1,17},{17,1},{2,18},{18,2},{3,19},{19,3},{4,20},{20... | collective-permute-start | bytes 2457608 | tf_op jit(solution)/shard_map/ppermute | solution.py:59
  43.8 4.7 %copy-start.6 = (bf16[1152,128]{1,0:T(8,128)(2,1)S(1)}, bf16[1152,128]{1,0:T(8,128)(2,1)}, u32[]{:S(2)}) copy-start(bf16[1152,128]{1,0:T(8,128)(2,1)} %copy-done.5) | copy-start | bytes 884740
  43.8 6.6 %copy-start.4 = (bf16[1152,128]{1,0:T(8,128)(2,1)S(1)}, bf16[1152,128]{1,0:T(8,128)(2,1)}, u32[]{:S(2)}) copy-start(bf16[1152,128]{1,0:T(8,128)(2,1)} %copy-done.3) | copy-start | bytes 884740
  45.1 24.5 %copy-start.1 = (bf16[640,1152]{1,0:T(8,128)(2,1)S(1)}, bf16[640,1152]{1,0:T(8,128)(2,1)}, u32[]{:S(2)}) copy-start(bf16[640,1152]{1,0:T(8,128)(2,1)} %copy-done) | copy-start | bytes 4423684
  45.2 16.2 %collective-permute-start.6 = (f32[160,5,128]{2,0,1:T(8,128)S(1)}, f32[160,5,128]{2,0,1:T(8,128)S(1)}, u32[]{:S(2)}, u32[]{:S(2)}) collective-permute-start(f32[160,5,128]{2,0,1:T(8,128)S(1)} %slice.61), channel_id=1, source_target_pairs={{0,32},{32,0},{1,33},{33,1},{2,34},{34,2},{3,35},{35,3},{4,36},{36... | collective-permute-start | bytes 1228808 | tf_op jit(solution)/shard_map/ppermute | solution.py:59
  48.5 11.0 %collective-permute-start.7 = (bf16[1152,128]{1,0:T(8,128)(2,1)S(1)}, bf16[1152,128]{1,0:T(8,128)(2,1)S(1)}, u32[]{:S(2)}, u32[]{:S(2)}) collective-permute-start(bf16[1152,128]{1,0:T(8,128)(2,1)S(1)} %copy-done.6), channel_id=1, source_target_pairs={{0,2},{2,4},{4,6},{6,8},{8,10},{10,12},{12,14},{14,0},{1,3},{3,5},... | collective-permute-start | bytes 884744 | tf_op jit(solution)/shard_map/ppermute | solution.py:82
  50.4 11.1 %collective-permute-start.8 = (bf16[1152,128]{1,0:T(8,128)(2,1)S(1)}, bf16[1152,128]{1,0:T(8,128)(2,1)S(1)}, u32[]{:S(2)}, u32[]{:S(2)}) collective-permute-start(bf16[1152,128]{1,0:T(8,128)(2,1)S(1)} %copy-done.4), channel_id=1, source_target_pairs={{0,14},{2,0},{4,2},{6,4},{8,6},{10,8},{12,10},{14,12},{1,15},{3,1}... | collective-permute-start | bytes 884744 | tf_op jit(solution)/shard_map/ppermute | solution.py:85
  59.5 10.1 %collective-permute-start.9 = (bf16[1152,128]{1,0:T(8,128)(2,1)S(1)}, bf16[1152,128]{1,0:T(8,128)(2,1)S(1)}, u32[]{:S(2)}, u32[]{:S(2)}) collective-permute-start(bf16[1152,128]{1,0:T(8,128)(2,1)S(1)} %collective-permute-done.7), channel_id=1, source_target_pairs={{0,2},{2,4},{4,6},{6,8},{8,10},{10,12},{12,14},{14,0},{1,3},{3,5},... | collective-permute-start | bytes 884744 | tf_op jit(solution)/shard_map/ppermute | solution.py:82
  71.1 5.8 %collective-permute-start.10 = (f32[320,3,128]{2,0,1:T(8,128)S(1)}, f32[320,3,128]{2,0,1:T(8,128)S(1)}, u32[]{:S(2)}, u32[]{:S(2)}) collective-permute-start(f32[320,3,128]{2,0,1:T(8,128)S(1)} %copy.23), channel_id=1, source_target_pairs={{0,16},{16,0},{1,17},{17,1},{2,18},{18,2},{3,19},{19,3},{4,20},{20... | collective-permute-start | bytes 1474568 | tf_op jit(solution)/shard_map/ppermute | solution.py:59
  76.9 9.0 %collective-permute-start.11 = (f32[160,3,128]{2,0,1:T(8,128)S(1)}, f32[160,3,128]{2,0,1:T(8,128)S(1)}, u32[]{:S(2)}, u32[]{:S(2)}) collective-permute-start(f32[160,3,128]{2,0,1:T(8,128)S(1)} %slice.65), channel_id=1, source_target_pairs={{0,32},{32,0},{1,33},{33,1},{2,34},{34,2},{3,35},{35,3},{4,36},{36... | collective-permute-start | bytes 737288 | tf_op jit(solution)/shard_map/ppermute | solution.py:59
  86.7 7.3 %copy-start.9 = (s32[1,32]{1,0:T(1,128)S(1)}, s32[1,32]{1,0:T(1,128)}, u32[]{:S(2)}) copy-start(s32[1,32]{1,0:T(1,128)} %param.12) | copy-start | bytes 388
  87.6 26.9 %all-to-all-start = ((f32[160,8,128]{2,0,1:T(8,128)}), f32[160,8,128]{2,0,1:T(8,128)S(1)}, u32[]{:S(2)}, u32[]{:S(2)}) async-start(f32[160,8,128]{2,0,1:T(8,128)} %select_bitcast_fusion), calls=%async_computation | async-start | bytes 1310720 | tf_op jit(solution)/shard_map/all_to_all | solution.py:149
  115.1 30.6 %copy-start.7 = (f32[160,128]{1,0:T(8,128)S(1)}, f32[160,128]{1,0:T(8,128)}, u32[]{:S(2)}) copy-start(f32[160,128]{1,0:T(8,128)} %param.13) | copy-start | bytes 245764
  168.0 9.7 %collective-permute-start.12 = (bf16[1280,128]{1,0:T(8,128)(2,1)S(1)}, bf16[1280,128]{1,0:T(8,128)(2,1)S(1)}, u32[]{:S(2)}, u32[]{:S(2)}) collective-permute-start(bf16[1280,128]{1,0:T(8,128)(2,1)S(1)} %bitcast.115), channel_id=1, source_target_pairs={{0,32},{32,0},{1,33},{33,1},{2,34},{34,2},{3,35},{35,3},{4,36},{36... | collective-permute-start | bytes 983048 | tf_op jit(solution)/shard_map/ppermute | solution.py:91
  177.7 6.0 %collective-permute-start.13 = (bf16[2560,128]{1,0:T(8,128)(2,1)S(1)}, bf16[2560,128]{1,0:T(8,128)(2,1)S(1)}, u32[]{:S(2)}, u32[]{:S(2)}) collective-permute-start(bf16[2560,128]{1,0:T(8,128)(2,1)S(1)} %pad_maximum_fusion.3), channel_id=1, source_target_pairs={{0,16},{16,0},{1,17},{17,1},{2,18},{18,2},{3,19},{19,3},{4,20},{20... | collective-permute-start | bytes 1966088 | tf_op jit(solution)/shard_map/ppermute | solution.py:91

commit v12 on v10

--- a/solution.py
+++ b/solution.py
@@ -19,11 +19,14 @@
 SWAP = [(0, 1), (1, 0)]
 
 
-def weigh(cotangents, labels, diff_mask, class_weight, total_tokens):
+def token_factor(labels, diff_mask, class_weight, total_tokens):
     classes = jnp.arange(class_weight.shape[0], dtype=jnp.int32)
     picked = (labels[:, None] == classes[None, :]).astype(jnp.float32)
     token_weight = diff_mask.astype(jnp.float32) * jnp.sum(picked * class_weight[None, :], axis=1)
-    factor = token_weight / math.sqrt(total_tokens)
+    return token_weight / math.sqrt(total_tokens)
+
+
+def weigh(cotangents, factor):
     return (cotangents.astype(jnp.float32) * factor[:, None]).astype(jnp.bfloat16)
 
 
@@ -96,7 +99,7 @@
     z_count = lax.axis_size("z")
     tensor_count = lax.axis_size(TP)
     local_tokens = cotangents.shape[0]
-    scaled = weigh(cotangents, labels, diff_mask, class_weight, local_tokens * dp_count)
+    factor = token_factor(labels, diff_mask, class_weight, local_tokens * dp_count)
     heads_here = owners.shape[0]
     head_width = cotangents.shape[1] // heads_here
     feature_rows = features.shape[0]
@@ -113,7 +116,7 @@
     quarter_rows = block_rows // 4
     pair_rows = pair_gather(features, "xh")
     y = lax.axis_index("y")
-    ring_pieces = ring_gather(scaled, "y")
+    ring_pieces = [weigh(piece, factor) for piece in ring_gather(cotangents, "y")]
     pair_blocks = 2 * sub_blocks
     group_rows = pair_blocks * quarter_rows
     position = jnp.arange(2 * feature_rows, dtype=jnp.int32)

time: 183 us -> 184 us (level)
  other arithmetic: 11.1 us -> 17.3 us
  local copies, waits for them, and re-layouts: 14.7 us -> 10.7 us
    unnamed x1 -> x4, other arithmetic: 1.99 us -> 4.83 us
    unnamed x13 -> x10, local copies, waits for them, and re-layouts: 2.26 us -> 0.02 us
    concatenate x0 -> x1, other arithmetic: none -> 1.92 us  [reduced_heads(): jnp.concatenate(pieces, axis=1)]
  transfers between devices with their start and end apart: 15 -> 15, of which waited for: 7 -> 8; matrix products, arithmetic and copies ran while one was open for 11% -> 13% of each run, Pallas kernels for 0% -> 0%
where the time goes in v12:
time: 184 us; the launch traced here: 183 us
  starting transfers between devices  56 us (30%)
  blocking collectives  46.3 us (25%)
  waiting for transfers between devices  42.3 us (23%)
  other arithmetic  17.3 us (9%)
  local copies, waits for them, and re-layouts  10.7 us (6%)
  matrix products  8.16 us (4%)
  between operations  1.87 us (1%)
    all_to_all x1, blocking collectives, shards(): lax.all_to_all(in_owner_order, DP, split_axis=0, concat_axis=0, tiled=True)  30.5 us
    all_to_all x1, waiting for transfers between devices, shards(): lax.all_to_all(kept, 'y', split_axis=1, concat_axis=0, tiled=True)  20.4 us
    all_to_all x1, blocking collectives, shards(): lax.all_to_all(jnp.broadcast_to(own_update[None], (z_count,) + own_update...  15.8 us
    ppermute x4, starting transfers between devices, pair_sum_scatter(): return blocks[:half] + lax.ppermute(blocks[half:], axis, SWAP)  15.7 us
    ppermute x3, starting transfers between devices, ring_gather(): from_right = lax.ppermute(from_right, axis, to_left)  13.7 us
    ppermute x4, waiting for transfers between devices, pair_sum_scatter(): return blocks[:half] + lax.ppermute(blocks[half:], axis, SWAP)  13.2 us
    ppermute x3, starting transfers between devices, pair_gather(): return jnp.concatenate([piece, lax.ppermute(piece, axis, SWAP)], axis=0)  11.5 us
    ppermute x4, starting transfers between devices, ring_gather(): from_left = lax.ppermute(from_left, axis, to_right)  9.77 us
  transfers between devices with their start and end apart: 15, of which 8 were waited for; matrix products, arithmetic and copies ran while one was open for 13% of the time, Pallas kernels for 0%

profile of v12, /device:TPU:1, one launch (start us, length us, event | category | flops | bytes accessed | tf_op | source)
XLA Modules:
  0.0 182.7 jit_solution(5524682846478524579)
XLA Ops:
  0.6 4.0 %collective-permute-start.1 = (bf16[1152,128]{1,0:T(8,128)(2,1)}, bf16[1152,128]{1,0:T(8,128)(2,1)S(1)}, u32[]{:S(2)}, u32[]{:S(2)}) collective-permute-start(bf16[1152,128]{1,0:T(8,128)(2,1)} %param.8), channel_id=1, source_target_pairs={{0,2},{2,4},{4,6},{6,8},{8,10},{10,12},{12,14},{14,0},{1,3},{3,5},... | collective-permute-start | bytes 884744 | tf_op jit(solution)/shard_map/ppermute | solution.py:85
  4.7 3.8 %collective-permute-start.2 = (bf16[1152,128]{1,0:T(8,128)(2,1)}, bf16[1152,128]{1,0:T(8,128)(2,1)S(1)}, u32[]{:S(2)}, u32[]{:S(2)}) collective-permute-start(bf16[1152,128]{1,0:T(8,128)(2,1)} %param.8), channel_id=1, source_target_pairs={{0,14},{2,0},{4,2},{6,4},{8,6},{10,8},{12,10},{14,12},{1,15},{3,1}... | collective-permute-start | bytes 884744 | tf_op jit(solution)/shard_map/ppermute | solution.py:88
  8.5 4.7 %collective-permute-start = (bf16[320,1152]{1,0:T(8,128)(2,1)}, bf16[320,1152]{1,0:T(8,128)(2,1)S(1)}, u32[]{:S(2)}, u32[]{:S(2)}) collective-permute-start(bf16[320,1152]{1,0:T(8,128)(2,1)} %param.7), channel_id=1, source_target_pairs={{0,1},{1,0},{2,3},{3,2},{4,5},{5,4},{6,7},{7,6},{8,9},{9,8},{10,11... | collective-permute-start | bytes 2211848 | tf_op jit(solution)/shard_map/ppermute | solution.py:94
  13.3 0.8 select_reduce_fusion
  14.1 0.7 multiply_multiply_fusion
  14.8 2.0 %fusion.20 = bf16[1152,640]{1,0:T(8,128)(2,1)} fusion(bf16[1152,128]{1,0:T(8,128)(2,1)} %param.8, f32[1152]{0:T(1024)S(1)} %multiply_multiply_fusion), kind=kLoop, calls=%fused_computation.52 | loop fusion | flops 442367 | bytes 594432
  16.8 1.9 %collective-permute-start.3 = (bf16[1152,128]{1,0:T(8,128)(2,1)S(1)}, bf16[1152,128]{1,0:T(8,128)(2,1)S(1)}, u32[]{:S(2)}, u32[]{:S(2)}) collective-permute-start(bf16[1152,128]{1,0:T(8,128)(2,1)S(1)} %collective-permute-done.1), channel_id=1, source_target_pairs={{0,2},{2,4},{4,6},{6,8},{8,10},{10,12},{12,14},{14,0},{1,3},{3,5},... | collective-permute-start | bytes 884744 | tf_op jit(solution)/shard_map/ppermute | solution.py:85
  18.7 0.9 fusion.21
  19.7 4.6 %collective-permute-start.4 = (bf16[1152,128]{1,0:T(8,128)(2,1)S(1)}, bf16[1152,128]{1,0:T(8,128)(2,1)}, u32[]{:S(2)}, u32[]{:S(2)}) collective-permute-start(bf16[1152,128]{1,0:T(8,128)(2,1)S(1)} %collective-permute-done.2), channel_id=1, source_target_pairs={{0,14},{2,0},{4,2},{6,4},{8,6},{10,8},{12,10},{14,12},{1,15},{3,1}... | collective-permute-start | bytes 884744 | tf_op jit(solution)/shard_map/ppermute | solution.py:88
  24.2 0.9 fusion.22
  25.2 0.6 collective-permute-done.3
  25.8 1.9 %collective-permute-start.7 = (bf16[1152,128]{1,0:T(8,128)(2,1)S(1)}, bf16[1152,128]{1,0:T(8,128)(2,1)}, u32[]{:S(2)}, u32[]{:S(2)}) collective-permute-start(bf16[1152,128]{1,0:T(8,128)(2,1)S(1)} %collective-permute-done.3), channel_id=1, source_target_pairs={{0,2},{2,4},{4,6},{6,8},{8,10},{10,12},{12,14},{14,0},{1,3},{3,5},... | collective-permute-start | bytes 884744 | tf_op jit(solution)/shard_map/ppermute | solution.py:85
  27.9 5.3 %collective-permute-start.8 = (bf16[1152,128]{1,0:T(8,128)(2,1)}, bf16[1152,128]{1,0:T(8,128)(2,1)}, u32[]{:S(2)}, u32[]{:S(2)}) collective-permute-start(bf16[1152,128]{1,0:T(8,128)(2,1)} %collective-permute-done.4), channel_id=1, source_target_pairs={{0,14},{2,0},{4,2},{6,4},{8,6},{10,8},{12,10},{14,12},{1,15},{3,1}... | collective-permute-start | bytes 884744 | tf_op jit(solution)/shard_map/ppermute | solution.py:88
  33.2 0.9 fusion.23
  34.1 1.9 %fusion.24 = bf16[1152,640]{1,0:T(8,128)(2,1)} fusion(bf16[1152,640]{1,0:T(8,128)(2,1)} %fusion.23, bf16[1152,128]{1,0:T(8,128)(2,1)} %collective-permute-done.4, f32[1152]{0:T(1024)S(1)} %multiply_multiply_fusion), kind=kLoop, calls=%fused_computation.56 | loop fusion | flops 442368 | bytes 594432 | tf_op jit(solution)/shard_map/concatenate | solution.py:136
  36.2 3.0 %gather_fusion.1 = bf16[640,1152]{1,0:T(8,128)(2,1)S(1)} fusion(bf16[640,1152]{1,0:T(8,128)(2,1)S(1)} %pad_maximum_fusion, s32[1024]{0:T(1024)S(1)} %pad_clamp_fusion.3), kind=kCustom, calls=%fused_computation.1 | custom fusion | bytes 2951680 | tf_op jit(solution)/shard_map/jit(_take)/gather | solution.py:132
  39.3 1.9 %collective-permute-start.9 = (bf16[1152,128]{1,0:T(8,128)(2,1)}, bf16[1152,128]{1,0:T(8,128)(2,1)}, u32[]{:S(2)}, u32[]{:S(2)}) collective-permute-start(bf16[1152,128]{1,0:T(8,128)(2,1)} %collective-permute-done.7), channel_id=1, source_target_pairs={{0,2},{2,4},{4,6},{6,8},{8,10},{10,12},{12,14},{14,0},{1,3},{3,5},... | collective-permute-start | bytes 884744 | tf_op jit(solution)/shard_map/ppermute | solution.py:85
  41.2 2.8 %fusion.19 = f32[640,640]{1,0:T(8,128)S(1)} fusion(bf16[1152,640]{1,0:T(8,128)(2,1)} %fusion.24, bf16[640,1152]{1,0:T(8,128)(2,1)S(1)} %gather_fusion.1, pred[640]{0:T(1024)(128)(4,1)S(1)} %compare_and_fusion), kind=kOutput, calls=%fused_computation.41 | convolution fusion | flops 944455680 | bytes 4588160 | tf_op jit(solution)/shard_map/dot_general | solution.py:135
  44.1 0.3 copy.18
  44.5 1.2 copy.19
  45.7 6.7 %collective-permute-start.5 = (f32[320,5,128]{2,0,1:T(8,128)}, f32[320,5,128]{2,0,1:T(8,128)S(1)}, u32[]{:S(2)}, u32[]{:S(2)}) collective-permute-start(f32[320,5,128]{2,0,1:T(8,128)} %copy.19), channel_id=1, source_target_pairs={{0,16},{16,0},{1,17},{17,1},{2,18},{18,2},{3,19},{19,3},{4,20},{20... | collective-permute-start | bytes 2457608 | tf_op jit(solution)/shard_map/ppermute | solution.py:62
  52.5 1.4 multiply_convert_fusion.2
  53.9 1.0 fusion.13
  55.0 0.2 copy.22
  55.3 1.0 copy.23
  56.3 3.7 %collective-permute-start.10 = (f32[320,3,128]{2,0,1:T(8,128)}, f32[320,3,128]{2,0,1:T(8,128)}, u32[]{:S(2)}, u32[]{:S(2)}) collective-permute-start(f32[320,3,128]{2,0,1:T(8,128)} %copy.23), channel_id=1, source_target_pairs={{0,16},{16,0},{1,17},{17,1},{2,18},{18,2},{3,19},{19,3},{4,20},{20... | collective-permute-start | bytes 1474568 | tf_op jit(solution)/shard_map/ppermute | solution.py:62
  60.0 0.2 copy.21
  60.2 0.2 copy.24
  60.4 1.4 collective-permute-done.10
  61.8 1.1 add.395
  62.8 0.7 slice.65
  63.6 1.9 %collective-permute-start.11 = (f32[160,3,128]{2,0,1:T(8,128)}, f32[160,3,128]{2,0,1:T(8,128)S(1)}, u32[]{:S(2)}, u32[]{:S(2)}) collective-permute-start(f32[160,3,128]{2,0,1:T(8,128)} %slice.65), channel_id=1, source_target_pairs={{0,32},{32,0},{1,33},{33,1},{2,34},{34,2},{3,35},{35,3},{4,36},{36... | collective-permute-start | bytes 737288 | tf_op jit(solution)/shard_map/ppermute | solution.py:62
  65.5 0.3 copy.17
  65.8 0.3 copy.20
  66.3 3.4 %collective-permute-start.6 = (f32[160,5,128]{2,0,1:T(8,128)S(1)}, f32[160,5,128]{2,0,1:T(8,128)S(1)}, u32[]{:S(2)}, u32[]{:S(2)}) collective-permute-start(f32[160,5,128]{2,0,1:T(8,128)S(1)} %slice.61), channel_id=1, source_target_pairs={{0,32},{32,0},{1,33},{33,1},{2,34},{34,2},{3,35},{35,3},{4,36},{36... | collective-permute-start | bytes 1228808 | tf_op jit(solution)/shard_map/ppermute | solution.py:62
  69.7 3.1 %collective-permute-done.11 = f32[160,3,128]{2,0,1:T(8,128)S(1)} collective-permute-done((f32[160,3,128]{2,0,1:T(8,128)}, f32[160,3,128]{2,0,1:T(8,128)S(1)}, u32[]{:S(2)}, u32[]{:S(2)}) %collective-permute-start.11) | collective-permute-done | bytes 245792 | tf_op jit(solution)/shard_map/ppermute | solution.py:62
  72.8 8.7 %collective-permute-done.6 = f32[160,5,128]{2,0,1:T(8,128)S(1)} collective-permute-done((f32[160,5,128]{2,0,1:T(8,128)S(1)}, f32[160,5,128]{2,0,1:T(8,128)S(1)}, u32[]{:S(2)}, u32[]{:S(2)}) %collective-permute-start.6) | collective-permute-done | bytes 409632 | tf_op jit(solution)/shard_map/ppermute | solution.py:62
  81.7 0.6 gather_fusion.2
  82.3 0.9 select_bitcast_fusion
  83.2 5.4 %all-to-all-start = ((f32[160,8,128]{2,0,1:T(8,128)}), f32[160,8,128]{2,0,1:T(8,128)S(1)}, u32[]{:S(2)}, u32[]{:S(2)}) async-start(f32[160,8,128]{2,0,1:T(8,128)} %select_bitcast_fusion), calls=%async_computation | async-start | bytes 1310720 | tf_op jit(solution)/shard_map/all_to_all | solution.py:150
  88.8 20.4 %all-to-all-done = f32[160,8,128]{2,0,1:T(8,128)S(1)} async-done(((f32[160,8,128]{2,0,1:T(8,128)}), f32[160,8,128]{2,0,1:T(8,128)S(1)}, u32[]{:S(2)}, u32[]{:S(2)}) %all-to-all-start) | async-done | bytes 655392 | tf_op jit(solution)/shard_map/all_to_all | solution.py:150
  109.2 0.6 gather_fusion.3
  110.0 30.5 %all_to_all.25 = f32[32,40,128]{2,1,0:T(8,128)S(1)} all-to-all(f32[32,40,128]{2,1,0:T(8,128)S(1)} %broadcast_select_fusion.3), channel_id=1, replica_groups=mesh['z'=8,'xl'=2,'c'=2,'y'=8,'xh'=2] {'z','xl','c'}, dimensions={0} | all-to-all | bytes 1310720 | tf_op jit(solution)/shard_map/all_to_all | solution.py:154
  140.5 1.3 multiply_reduce_fusion
  142.5 0.4 fusion.37
  143.1 0.2 fusion
  143.3 0.4 fusion.35
  143.8 0.2 fusion.9
  144.0 0.2 fusion.1
  144.2 0.4 fusion.32
  144.7 0.2 fusion.8
  144.9 0.2 fusion.2
  145.1 0.4 fusion.29
  145.7 0.2 fusion.3
  146.0 0.4 fusion.26
  146.6 0.2 fusion.12
  146.9 15.8 %all_to_all.26 = bf16[8,160,128]{2,1,0:T(8,128)(2,1)S(1)} all-to-all(bf16[8,160,128]{2,1,0:T(8,128)(2,1)S(1)} %broadcast_in_dim.140), channel_id=1, replica_groups=mesh['z'=8,'xl'=2,'c'=2,'y'=8,'xh'=2] {'z'}, dimensions={0} | all-to-all | bytes 655360 | tf_op jit(solution)/shard_map/all_to_all | solution.py:168
  162.7 2.6 %collective-permute-start.12 = (bf16[1280,128]{1,0:T(8,128)(2,1)S(1)}, bf16[1280,128]{1,0:T(8,128)(2,1)S(1)}, u32[]{:S(2)}, u32[]{:S(2)}) collective-permute-start(bf16[1280,128]{1,0:T(8,128)(2,1)S(1)} %bitcast.113), channel_id=1, source_target_pairs={{0,32},{32,0},{1,33},{33,1},{2,34},{34,2},{3,35},{35,3},{4,36},{36... | collective-permute-start | bytes 983048 | tf_op jit(solution)/shard_map/ppermute | solution.py:94
  165.3 7.0 %collective-permute-done.12 = bf16[1280,128]{1,0:T(8,128)(2,1)S(1)} collective-permute-done((bf16[1280,128]{1,0:T(8,128)(2,1)S(1)}, bf16[1280,128]{1,0:T(8,128)(2,1)S(1)}, u32[]{:S(2)}, u32[]{:S(2)}) %collective-permute-start.12) | collective-permute-done | bytes 327712 | tf_op jit(solution)/shard_map/ppermute | solution.py:94
  172.4 4.3 %collective-permute-start.13 = (bf16[2560,128]{1,0:T(8,128)(2,1)S(1)}, bf16[2560,128]{1,0:T(8,128)(2,1)S(1)}, u32[]{:S(2)}, u32[]{:S(2)}) collective-permute-start(bf16[2560,128]{1,0:T(8,128)(2,1)S(1)} %pad_maximum_fusion.3), channel_id=1, source_target_pairs={{0,16},{16,0},{1,17},{17,1},{2,18},{18,2},{3,19},{19,3},{4,20},{20... | collective-permute-start | bytes 1966088 | tf_op jit(solution)/shard_map/ppermute | solution.py:94
  176.7 0.7 gather_fusion
  177.6 0.8 collective-permute-done.13
  178.5 0.8 gather_fusion.4
  179.3 3.4 %bitcast_select_fusion = bf16[5120,128]{1,0:T(8,128)(2,1)} fusion(bf16[32,160,128]{2,1,0:T(8,128)(2,1)S(1)} %gather_fusion.4, pred[5120]{0:T(1024)(128)(4,1)S(1)} %broadcast_in_dim.121), kind=kLoop, calls=%fused_computation.8 | loop fusion | flops 655360 | bytes 2626560 | tf_op jit(solution)/shard_map/jit(take_along_axis)/select_n | solution.py:41
  (52 shorter events, 2.2 us)
Async XLA Ops:
  0.6 16.2 %collective-permute-start.1 = (bf16[1152,128]{1,0:T(8,128)(2,1)}, bf16[1152,128]{1,0:T(8,128)(2,1)S(1)}, u32[]{:S(2)}, u32[]{:S(2)}) collective-permute-start(bf16[1152,128]{1,0:T(8,128)(2,1)} %param.8), channel_id=1, source_target_pairs={{0,2},{2,4},{4,6},{6,8},{8,10},{10,12},{12,14},{14,0},{1,3},{3,5},... | collective-permute-start | bytes 884744 | tf_op jit(solution)/shard_map/ppermute | solution.py:85
  4.7 15.0 %collective-permute-start.2 = (bf16[1152,128]{1,0:T(8,128)(2,1)}, bf16[1152,128]{1,0:T(8,128)(2,1)S(1)}, u32[]{:S(2)}, u32[]{:S(2)}) collective-permute-start(bf16[1152,128]{1,0:T(8,128)(2,1)} %param.8), channel_id=1, source_target_pairs={{0,14},{2,0},{4,2},{6,4},{8,6},{10,8},{12,10},{14,12},{1,15},{3,1}... | collective-permute-start | bytes 884744 | tf_op jit(solution)/shard_map/ppermute | solution.py:88
  8.5 27.6 %collective-permute-start = (bf16[320,1152]{1,0:T(8,128)(2,1)}, bf16[320,1152]{1,0:T(8,128)(2,1)S(1)}, u32[]{:S(2)}, u32[]{:S(2)}) collective-permute-start(bf16[320,1152]{1,0:T(8,128)(2,1)} %param.7), channel_id=1, source_target_pairs={{0,1},{1,0},{2,3},{3,2},{4,5},{5,4},{6,7},{7,6},{8,9},{9,8},{10,11... | collective-permute-start | bytes 2211848 | tf_op jit(solution)/shard_map/ppermute | solution.py:94
  14.8 21.3 %copy-start.2 = (bf16[320,1152]{1,0:T(8,128)(2,1)S(1)}, bf16[320,1152]{1,0:T(8,128)(2,1)}, u32[]{:S(2)}) copy-start(bf16[320,1152]{1,0:T(8,128)(2,1)} %param.7) | copy-start | bytes 2211844
  16.8 9.0 %collective-permute-start.3 = (bf16[1152,128]{1,0:T(8,128)(2,1)S(1)}, bf16[1152,128]{1,0:T(8,128)(2,1)S(1)}, u32[]{:S(2)}, u32[]{:S(2)}) collective-permute-start(bf16[1152,128]{1,0:T(8,128)(2,1)S(1)} %collective-permute-done.1), channel_id=1, source_target_pairs={{0,2},{2,4},{4,6},{6,8},{8,10},{10,12},{12,14},{14,0},{1,3},{3,5},... | collective-permute-start | bytes 884744 | tf_op jit(solution)/shard_map/ppermute | solution.py:85
  19.7 8.2 %collective-permute-start.4 = (bf16[1152,128]{1,0:T(8,128)(2,1)S(1)}, bf16[1152,128]{1,0:T(8,128)(2,1)}, u32[]{:S(2)}, u32[]{:S(2)}) collective-permute-start(bf16[1152,128]{1,0:T(8,128)(2,1)S(1)} %collective-permute-done.2), channel_id=1, source_target_pairs={{0,14},{2,0},{4,2},{6,4},{8,6},{10,8},{12,10},{14,12},{1,15},{3,1}... | collective-permute-start | bytes 884744 | tf_op jit(solution)/shard_map/ppermute | solution.py:88
  25.8 13.5 %collective-permute-start.7 = (bf16[1152,128]{1,0:T(8,128)(2,1)S(1)}, bf16[1152,128]{1,0:T(8,128)(2,1)}, u32[]{:S(2)}, u32[]{:S(2)}) collective-permute-start(bf16[1152,128]{1,0:T(8,128)(2,1)S(1)} %collective-permute-done.3), channel_id=1, source_target_pairs={{0,2},{2,4},{4,6},{6,8},{8,10},{10,12},{12,14},{14,0},{1,3},{3,5},... | collective-permute-start | bytes 884744 | tf_op jit(solution)/shard_map/ppermute | solution.py:85
  27.9 24.6 %collective-permute-start.8 = (bf16[1152,128]{1,0:T(8,128)(2,1)}, bf16[1152,128]{1,0:T(8,128)(2,1)}, u32[]{:S(2)}, u32[]{:S(2)}) collective-permute-start(bf16[1152,128]{1,0:T(8,128)(2,1)} %collective-permute-done.4), channel_id=1, source_target_pairs={{0,14},{2,0},{4,2},{6,4},{8,6},{10,8},{12,10},{14,12},{1,15},{3,1}... | collective-permute-start | bytes 884744 | tf_op jit(solution)/shard_map/ppermute | solution.py:88
  39.2 2.0 %copy-start = (bf16[640,1152]{1,0:T(8,128)(2,1)}, bf16[640,1152]{1,0:T(8,128)(2,1)S(1)}, u32[]{:S(2)}) copy-start(bf16[640,1152]{1,0:T(8,128)(2,1)S(1)} %gather_fusion.1) | copy-start | bytes 4423684
  39.3 13.2 %collective-permute-start.9 = (bf16[1152,128]{1,0:T(8,128)(2,1)}, bf16[1152,128]{1,0:T(8,128)(2,1)}, u32[]{:S(2)}, u32[]{:S(2)}) collective-permute-start(bf16[1152,128]{1,0:T(8,128)(2,1)} %collective-permute-done.7), channel_id=1, source_target_pairs={{0,2},{2,4},{4,6},{6,8},{8,10},{10,12},{12,14},{14,0},{1,3},{3,5},... | collective-permute-start | bytes 884744 | tf_op jit(solution)/shard_map/ppermute | solution.py:85
  44.5 9.4 %copy-start.1 = (bf16[640,1152]{1,0:T(8,128)(2,1)S(1)}, bf16[640,1152]{1,0:T(8,128)(2,1)}, u32[]{:S(2)}) copy-start(bf16[640,1152]{1,0:T(8,128)(2,1)} %copy-done) | copy-start | bytes 4423684
  45.7 20.4 %collective-permute-start.5 = (f32[320,5,128]{2,0,1:T(8,128)}, f32[320,5,128]{2,0,1:T(8,128)S(1)}, u32[]{:S(2)}, u32[]{:S(2)}) collective-permute-start(f32[320,5,128]{2,0,1:T(8,128)} %copy.19), channel_id=1, source_target_pairs={{0,16},{16,0},{1,17},{17,1},{2,18},{18,2},{3,19},{19,3},{4,20},{20... | collective-permute-start | bytes 2457608 | tf_op jit(solution)/shard_map/ppermute | solution.py:62
  56.3 5.5 %collective-permute-start.10 = (f32[320,3,128]{2,0,1:T(8,128)}, f32[320,3,128]{2,0,1:T(8,128)}, u32[]{:S(2)}, u32[]{:S(2)}) collective-permute-start(f32[320,3,128]{2,0,1:T(8,128)} %copy.23), channel_id=1, source_target_pairs={{0,16},{16,0},{1,17},{17,1},{2,18},{18,2},{3,19},{19,3},{4,20},{20... | collective-permute-start | bytes 1474568 | tf_op jit(solution)/shard_map/ppermute | solution.py:62
  63.6 9.2 %collective-permute-start.11 = (f32[160,3,128]{2,0,1:T(8,128)}, f32[160,3,128]{2,0,1:T(8,128)S(1)}, u32[]{:S(2)}, u32[]{:S(2)}) collective-permute-start(f32[160,3,128]{2,0,1:T(8,128)} %slice.65), channel_id=1, source_target_pairs={{0,32},{32,0},{1,33},{33,1},{2,34},{34,2},{3,35},{35,3},{4,36},{36... | collective-permute-start | bytes 737288 | tf_op jit(solution)/shard_map/ppermute | solution.py:62
  66.3 15.3 %collective-permute-start.6 = (f32[160,5,128]{2,0,1:T(8,128)S(1)}, f32[160,5,128]{2,0,1:T(8,128)S(1)}, u32[]{:S(2)}, u32[]{:S(2)}) collective-permute-start(f32[160,5,128]{2,0,1:T(8,128)S(1)} %slice.61), channel_id=1, source_target_pairs={{0,32},{32,0},{1,33},{33,1},{2,34},{34,2},{3,35},{35,3},{4,36},{36... | collective-permute-start | bytes 1228808 | tf_op jit(solution)/shard_map/ppermute | solution.py:62
  82.3 6.4 %copy-start.4 = (s32[1,32]{1,0:T(1,128)S(1)}, s32[1,32]{1,0:T(1,128)}, u32[]{:S(2)}) copy-start(s32[1,32]{1,0:T(1,128)} %param.12) | copy-start | bytes 388
  83.2 26.0 %all-to-all-start = ((f32[160,8,128]{2,0,1:T(8,128)}), f32[160,8,128]{2,0,1:T(8,128)S(1)}, u32[]{:S(2)}, u32[]{:S(2)}) async-start(f32[160,8,128]{2,0,1:T(8,128)} %select_bitcast_fusion), calls=%async_computation | async-start | bytes 1310720 | tf_op jit(solution)/shard_map/all_to_all | solution.py:150
  109.8 30.7 %copy-start.3 = (f32[160,128]{1,0:T(8,128)S(1)}, f32[160,128]{1,0:T(8,128)}, u32[]{:S(2)}) copy-start(f32[160,128]{1,0:T(8,128)} %param.13) | copy-start | bytes 245764
  162.7 9.7 %collective-permute-start.12 = (bf16[1280,128]{1,0:T(8,128)(2,1)S(1)}, bf16[1280,128]{1,0:T(8,128)(2,1)S(1)}, u32[]{:S(2)}, u32[]{:S(2)}) collective-permute-start(bf16[1280,128]{1,0:T(8,128)(2,1)S(1)} %bitcast.113), channel_id=1, source_target_pairs={{0,32},{32,0},{1,33},{33,1},{2,34},{34,2},{3,35},{35,3},{4,36},{36... | collective-permute-start | bytes 983048 | tf_op jit(solution)/shard_map/ppermute | solution.py:94
  172.4 6.0 %collective-permute-start.13 = (bf16[2560,128]{1,0:T(8,128)(2,1)S(1)}, bf16[2560,128]{1,0:T(8,128)(2,1)S(1)}, u32[]{:S(2)}, u32[]{:S(2)}) collective-permute-start(bf16[2560,128]{1,0:T(8,128)(2,1)S(1)} %pad_maximum_fusion.3), channel_id=1, source_target_pairs={{0,16},{16,0},{1,17},{17,1},{2,18},{18,2},{3,19},{19,3},{4,20},{20... | collective-permute-start | bytes 1966088 | tf_op jit(solution)/shard_map/ppermute | solution.py:94

commit v13 on v12

--- a/solution.py
+++ b/solution.py
@@ -131,16 +131,21 @@
     source_row = shard_slot * feature_rows + (j % sub_blocks) * block_rows + u * quarter_rows + r
     arranged = jnp.take(pair_rows, source_row, axis=0)
 
-    def reduced_heads(pieces):
+    def core_reduced(rows, pieces):
         partial = jnp.dot(
-            arranged, jnp.concatenate(pieces, axis=1), preferred_element_type=jnp.float32
+            rows, jnp.concatenate(pieces, axis=1), preferred_element_type=jnp.float32
         ).reshape(2 * feature_rows, len(pieces), head_width)
-        kept = pair_sum_scatter(partial, "c")
-        return pair_sum_scatter(kept, "xl")
+        return pair_sum_scatter(partial, "c")
 
     early = 2 * 2 + 1
+    early_core = core_reduced(arranged, ring_pieces[:early])
+    arranged_late, early_core = lax.optimization_barrier((arranged, early_core))
     kept_ring_order = jnp.concatenate(
-        [reduced_heads(ring_pieces[:early]), reduced_heads(ring_pieces[early:])], axis=1
+        [
+            pair_sum_scatter(early_core, "xl"),
+            pair_sum_scatter(core_reduced(arranged_late, ring_pieces[early:]), "xl"),
+        ],
+        axis=1,
     )
     head = jnp.arange(y_count, dtype=jnp.int32)
     ahead = (head - y) % y_count

time: 184 us -> 183 us (level)
  other arithmetic: 17.3 us -> 13.1 us
  starting transfers between devices: 56 us -> 58.5 us
  local copies, waits for them, and re-layouts: 10.7 us -> 12.6 us
    unnamed x10 -> x14, local copies, waits for them, and re-layouts: 0.02 us -> 3.52 us
    ppermute x4, starting transfers between devices: 15.7 us -> 18.8 us  [pair_sum_scatter(): return blocks[:half] + lax.ppermute(blocks[half:], axis, SWAP)]
    unnamed x4, other arithmetic: 4.83 us -> 2.09 us
  transfers between devices with their start and end apart: 15 -> 15, of which waited for: 8 -> 6; matrix products, arithmetic and copies ran while one was open for 13% -> 8% of each run, Pallas kernels for 0% -> 0%
where the time goes in v13:
time: 183 us; the launch traced here: 182 us
  starting transfers between devices  58.5 us (32%)
  blocking collectives  46.2 us (25%)
  waiting for transfers between devices  43 us (23%)
  other arithmetic  13.1 us (7%)
  local copies, waits for them, and re-layouts  12.6 us (7%)
  matrix products  6.66 us (4%)
  between operations  1.96 us (1%)
    all_to_all x1, blocking collectives, shards(): lax.all_to_all(in_owner_order, DP, split_axis=0, concat_axis=0, tiled=True)  30.3 us
    all_to_all x1, waiting for transfers between devices, shards(): lax.all_to_all(kept, 'y', split_axis=1, concat_axis=0, tiled=True)  20.6 us
    ppermute x4, starting transfers between devices, pair_sum_scatter(): return blocks[:half] + lax.ppermute(blocks[half:], axis, SWAP)  18.8 us
    all_to_all x1, blocking collectives, shards(): lax.all_to_all(jnp.broadcast_to(own_update[None], (z_count,) + own_update...  15.9 us
    ppermute x3, starting transfers between devices, ring_gather(): from_right = lax.ppermute(from_right, axis, to_left)  13.2 us
    ppermute x4, waiting for transfers between devices, pair_sum_scatter(): return blocks[:half] + lax.ppermute(blocks[half:], axis, SWAP)  12.4 us
    ppermute x3, starting transfers between devices, pair_gather(): return jnp.concatenate([piece, lax.ppermute(piece, axis, SWAP)], axis=0)  11.3 us
    ppermute x4, starting transfers between devices, ring_gather(): from_left = lax.ppermute(from_left, axis, to_right)  9.78 us
  transfers between devices with their start and end apart: 15, of which 6 were waited for; matrix products, arithmetic and copies ran while one was open for 8% of the time, Pallas kernels for 0%

profile of v13, /device:TPU:1, one launch (start us, length us, event | category | flops | bytes accessed | tf_op | source)
XLA Modules:
  0.0 181.9 jit_solution(14737054996188589883)
XLA Ops:
  0.6 4.0 %collective-permute-start.1 = (bf16[1152,128]{1,0:T(8,128)(2,1)}, bf16[1152,128]{1,0:T(8,128)(2,1)S(1)}, u32[]{:S(2)}, u32[]{:S(2)}) collective-permute-start(bf16[1152,128]{1,0:T(8,128)(2,1)} %param.8), channel_id=1, source_target_pairs={{0,2},{2,4},{4,6},{6,8},{8,10},{10,12},{12,14},{14,0},{1,3},{3,5},... | collective-permute-start | bytes 884744 | tf_op jit(solution)/shard_map/ppermute | solution.py:85
  4.7 3.8 %collective-permute-start.2 = (bf16[1152,128]{1,0:T(8,128)(2,1)}, bf16[1152,128]{1,0:T(8,128)(2,1)S(1)}, u32[]{:S(2)}, u32[]{:S(2)}) collective-permute-start(bf16[1152,128]{1,0:T(8,128)(2,1)} %param.8), channel_id=1, source_target_pairs={{0,14},{2,0},{4,2},{6,4},{8,6},{10,8},{12,10},{14,12},{1,15},{3,1}... | collective-permute-start | bytes 884744 | tf_op jit(solution)/shard_map/ppermute | solution.py:88
  8.5 4.7 %collective-permute-start = (bf16[320,1152]{1,0:T(8,128)(2,1)}, bf16[320,1152]{1,0:T(8,128)(2,1)S(1)}, u32[]{:S(2)}, u32[]{:S(2)}) collective-permute-start(bf16[320,1152]{1,0:T(8,128)(2,1)} %param.7), channel_id=1, source_target_pairs={{0,1},{1,0},{2,3},{3,2},{4,5},{5,4},{6,7},{7,6},{8,9},{9,8},{10,11... | collective-permute-start | bytes 2211848 | tf_op jit(solution)/shard_map/ppermute | solution.py:94
  13.3 0.8 select_reduce_fusion
  14.1 0.7 multiply_multiply_fusion
  14.8 1.2 fusion.19
  16.1 1.9 %collective-permute-start.3 = (bf16[1152,128]{1,0:T(8,128)(2,1)S(1)}, bf16[1152,128]{1,0:T(8,128)(2,1)S(1)}, u32[]{:S(2)}, u32[]{:S(2)}) collective-permute-start(bf16[1152,128]{1,0:T(8,128)(2,1)S(1)} %collective-permute-done.1), channel_id=1, source_target_pairs={{0,2},{2,4},{4,6},{6,8},{8,10},{10,12},{12,14},{14,0},{1,3},{3,5},... | collective-permute-start | bytes 884744 | tf_op jit(solution)/shard_map/ppermute | solution.py:85
  18.0 0.3 fusion.20
  18.3 4.6 %collective-permute-start.4 = (bf16[1152,128]{1,0:T(8,128)(2,1)S(1)}, bf16[1152,128]{1,0:T(8,128)(2,1)}, u32[]{:S(2)}, u32[]{:S(2)}) collective-permute-start(bf16[1152,128]{1,0:T(8,128)(2,1)S(1)} %collective-permute-done.2), channel_id=1, source_target_pairs={{0,14},{2,0},{4,2},{6,4},{8,6},{10,8},{12,10},{14,12},{1,15},{3,1}... | collective-permute-start | bytes 884744 | tf_op jit(solution)/shard_map/ppermute | solution.py:88
  22.9 0.3 fusion.21
  23.2 1.9 %collective-permute-done.3 = bf16[1152,128]{1,0:T(8,128)(2,1)S(1)} collective-permute-done((bf16[1152,128]{1,0:T(8,128)(2,1)S(1)}, bf16[1152,128]{1,0:T(8,128)(2,1)S(1)}, u32[]{:S(2)}, u32[]{:S(2)}) %collective-permute-start.3) | collective-permute-done | bytes 294944 | tf_op jit(solution)/shard_map/ppermute | solution.py:85
  25.0 1.9 %collective-permute-start.7 = (bf16[1152,128]{1,0:T(8,128)(2,1)S(1)}, bf16[1152,128]{1,0:T(8,128)(2,1)}, u32[]{:S(2)}, u32[]{:S(2)}) collective-permute-start(bf16[1152,128]{1,0:T(8,128)(2,1)S(1)} %collective-permute-done.3), channel_id=1, source_target_pairs={{0,2},{2,4},{4,6},{6,8},{8,10},{10,12},{12,14},{14,0},{1,3},{3,5},... | collective-permute-start | bytes 884744 | tf_op jit(solution)/shard_map/ppermute | solution.py:85
  27.0 4.9 %collective-permute-start.8 = (bf16[1152,128]{1,0:T(8,128)(2,1)}, bf16[1152,128]{1,0:T(8,128)(2,1)}, u32[]{:S(2)}, u32[]{:S(2)}) collective-permute-start(bf16[1152,128]{1,0:T(8,128)(2,1)} %collective-permute-done.4), channel_id=1, source_target_pairs={{0,14},{2,0},{4,2},{6,4},{8,6},{10,8},{12,10},{14,12},{1,15},{3,1}... | collective-permute-start | bytes 884744 | tf_op jit(solution)/shard_map/ppermute | solution.py:88
  31.8 0.3 fusion.22
  32.1 1.2 fusion.23
  33.4 1.1 copy-done.4
  34.6 3.0 %gather_fusion.1 = bf16[640,1152]{1,0:T(8,128)(2,1)S(1)} fusion(bf16[640,1152]{1,0:T(8,128)(2,1)S(1)} %pad_maximum_fusion, s32[1024]{0:T(1024)S(1)} %pad_clamp_fusion.3), kind=kCustom, calls=%fused_computation.1 | custom fusion | bytes 2951680 | tf_op jit(solution)/shard_map/jit(_take)/gather | solution.py:132
  37.7 0.2 broadcast_select_fusion
  37.9 1.1 copy-done.5
  39.0 1.4 fusion.81
  40.5 1.9 %collective-permute-start.9 = (bf16[1152,128]{1,0:T(8,128)(2,1)}, bf16[1152,128]{1,0:T(8,128)(2,1)}, u32[]{:S(2)}, u32[]{:S(2)}) collective-permute-start(bf16[1152,128]{1,0:T(8,128)(2,1)} %collective-permute-done.7), channel_id=1, source_target_pairs={{0,2},{2,4},{4,6},{6,8},{8,10},{10,12},{12,14},{14,0},{1,3},{3,5},... | collective-permute-start | bytes 884744 | tf_op jit(solution)/shard_map/ppermute | solution.py:85
  42.5 0.3 copy.18
  42.8 0.3 copy.19
  43.2 6.8 %collective-permute-start.5 = (f32[320,5,128]{2,0,1:T(8,128)S(1)}, f32[320,5,128]{2,0,1:T(8,128)S(1)}, u32[]{:S(2)}, u32[]{:S(2)}) collective-permute-start(f32[320,5,128]{2,0,1:T(8,128)S(1)} %copy.19), channel_id=1, source_target_pairs={{0,16},{16,0},{1,17},{17,1},{2,18},{18,2},{3,19},{19,3},{4,20},{20... | collective-permute-start | bytes 2457608 | tf_op jit(solution)/shard_map/ppermute | solution.py:62
  49.9 0.3 copy.17
  50.2 0.3 copy.20
  50.6 1.4 multiply_convert_fusion.2
  52.1 1.3 copy-done.1
  53.4 1.0 fusion.13
  54.4 0.2 copy.22
  54.7 0.2 copy.23
  54.9 6.8 %collective-permute-start.10 = (f32[320,3,128]{2,0,1:T(8,128)S(1)}, f32[320,3,128]{2,0,1:T(8,128)S(1)}, u32[]{:S(2)}, u32[]{:S(2)}) collective-permute-start(f32[320,3,128]{2,0,1:T(8,128)S(1)} %copy.23), channel_id=1, source_target_pairs={{0,16},{16,0},{1,17},{17,1},{2,18},{18,2},{3,19},{19,3},{4,20},{20... | collective-permute-start | bytes 1474568 | tf_op jit(solution)/shard_map/ppermute | solution.py:62
  61.7 0.8 slice.41
  62.4 1.9 %collective-permute-start.6 = (f32[160,5,128]{2,0,1:T(8,128)}, f32[160,5,128]{2,0,1:T(8,128)S(1)}, u32[]{:S(2)}, u32[]{:S(2)}) collective-permute-start(f32[160,5,128]{2,0,1:T(8,128)} %slice.41), channel_id=1, source_target_pairs={{0,32},{32,0},{1,33},{33,1},{2,34},{34,2},{3,35},{35,3},{4,36},{36... | collective-permute-start | bytes 1228808 | tf_op jit(solution)/shard_map/ppermute | solution.py:62
  64.4 0.2 copy.21
  64.6 0.2 copy.24
  65.0 3.4 %collective-permute-start.11 = (f32[160,3,128]{2,0,1:T(8,128)S(1)}, f32[160,3,128]{2,0,1:T(8,128)S(1)}, u32[]{:S(2)}, u32[]{:S(2)}) collective-permute-start(f32[160,3,128]{2,0,1:T(8,128)S(1)} %slice.63), channel_id=1, source_target_pairs={{0,32},{32,0},{1,33},{33,1},{2,34},{34,2},{3,35},{35,3},{4,36},{36... | collective-permute-start | bytes 737288 | tf_op jit(solution)/shard_map/ppermute | solution.py:62
  68.3 7.2 %collective-permute-done.6 = f32[160,5,128]{2,0,1:T(8,128)S(1)} collective-permute-done((f32[160,5,128]{2,0,1:T(8,128)}, f32[160,5,128]{2,0,1:T(8,128)S(1)}, u32[]{:S(2)}, u32[]{:S(2)}) %collective-permute-start.6) | collective-permute-done | bytes 409632 | tf_op jit(solution)/shard_map/ppermute | solution.py:62
  75.6 5.2 %collective-permute-done.11 = f32[160,3,128]{2,0,1:T(8,128)S(1)} collective-permute-done((f32[160,3,128]{2,0,1:T(8,128)S(1)}, f32[160,3,128]{2,0,1:T(8,128)S(1)}, u32[]{:S(2)}, u32[]{:S(2)}) %collective-permute-start.11) | collective-permute-done | bytes 245792 | tf_op jit(solution)/shard_map/ppermute | solution.py:62
  80.9 0.6 gather_fusion.2
  81.5 0.9 select_bitcast_fusion
  82.5 5.4 %all-to-all-start = ((f32[160,8,128]{2,0,1:T(8,128)}), f32[160,8,128]{2,0,1:T(8,128)S(1)}, u32[]{:S(2)}, u32[]{:S(2)}) async-start(f32[160,8,128]{2,0,1:T(8,128)} %select_bitcast_fusion), calls=%async_computation | async-start | bytes 1310720 | tf_op jit(solution)/shard_map/all_to_all | solution.py:155
  88.0 20.6 %all-to-all-done = f32[160,8,128]{2,0,1:T(8,128)S(1)} async-done(((f32[160,8,128]{2,0,1:T(8,128)}), f32[160,8,128]{2,0,1:T(8,128)S(1)}, u32[]{:S(2)}, u32[]{:S(2)}) %all-to-all-start) | async-done | bytes 655392 | tf_op jit(solution)/shard_map/all_to_all | solution.py:155
  108.6 0.6 gather_fusion.3
  109.3 30.3 %all_to_all.25 = f32[32,40,128]{2,1,0:T(8,128)S(1)} all-to-all(f32[32,40,128]{2,1,0:T(8,128)S(1)} %broadcast_select_fusion.1), channel_id=1, replica_groups=mesh['z'=8,'xl'=2,'c'=2,'y'=8,'xh'=2] {'z','xl','c'}, dimensions={0} | all-to-all | bytes 1310720 | tf_op jit(solution)/shard_map/all_to_all | solution.py:159
  139.7 1.3 multiply_reduce_fusion
  141.7 0.4 fusion.36
  142.3 0.2 fusion
  142.6 0.4 fusion.34
  143.2 0.2 fusion.1
  143.4 0.4 fusion.31
  144.1 0.2 fusion.2
  144.3 0.4 fusion.28
  145.0 0.2 fusion.3
  145.2 0.4 fusion.25
  145.8 0.2 fusion.12
  146.1 15.9 %all_to_all.26 = bf16[8,160,128]{2,1,0:T(8,128)(2,1)S(1)} all-to-all(bf16[8,160,128]{2,1,0:T(8,128)(2,1)S(1)} %broadcast_in_dim.140), channel_id=1, replica_groups=mesh['z'=8,'xl'=2,'c'=2,'y'=8,'xh'=2] {'z'}, dimensions={0} | all-to-all | bytes 655360 | tf_op jit(solution)/shard_map/all_to_all | solution.py:173
  162.0 2.4 %collective-permute-start.12 = (bf16[1280,128]{1,0:T(8,128)(2,1)S(1)}, bf16[1280,128]{1,0:T(8,128)(2,1)S(1)}, u32[]{:S(2)}, u32[]{:S(2)}) collective-permute-start(bf16[1280,128]{1,0:T(8,128)(2,1)S(1)} %bitcast.115), channel_id=1, source_target_pairs={{0,32},{32,0},{1,33},{33,1},{2,34},{34,2},{3,35},{35,3},{4,36},{36... | collective-permute-start | bytes 983048 | tf_op jit(solution)/shard_map/ppermute | solution.py:94
  164.4 7.3 %collective-permute-done.12 = bf16[1280,128]{1,0:T(8,128)(2,1)S(1)} collective-permute-done((bf16[1280,128]{1,0:T(8,128)(2,1)S(1)}, bf16[1280,128]{1,0:T(8,128)(2,1)S(1)}, u32[]{:S(2)}, u32[]{:S(2)}) %collective-permute-start.12) | collective-permute-done | bytes 327712 | tf_op jit(solution)/shard_map/ppermute | solution.py:94
  171.7 4.2 %collective-permute-start.13 = (bf16[2560,128]{1,0:T(8,128)(2,1)S(1)}, bf16[2560,128]{1,0:T(8,128)(2,1)S(1)}, u32[]{:S(2)}, u32[]{:S(2)}) collective-permute-start(bf16[2560,128]{1,0:T(8,128)(2,1)S(1)} %pad_maximum_fusion.3), channel_id=1, source_target_pairs={{0,16},{16,0},{1,17},{17,1},{2,18},{18,2},{3,19},{19,3},{4,20},{20... | collective-permute-start | bytes 1966088 | tf_op jit(solution)/shard_map/ppermute | solution.py:94
  176.0 0.7 gather_fusion
  176.9 0.8 collective-permute-done.13
  177.8 0.8 gather_fusion.4
  178.6 3.4 %bitcast_select_fusion = bf16[5120,128]{1,0:T(8,128)(2,1)} fusion(bf16[32,160,128]{2,1,0:T(8,128)(2,1)S(1)} %gather_fusion.4, pred[5120]{0:T(1024)(128)(4,1)S(1)} %broadcast_in_dim.121), kind=kLoop, calls=%fused_computation.8 | loop fusion | flops 655360 | bytes 2626560 | tf_op jit(solution)/shard_map/jit(take_along_axis)/select_n | solution.py:41
  (57 shorter events, 2.5 us)
Async XLA Ops:
  0.6 15.4 %collective-permute-start.1 = (bf16[1152,128]{1,0:T(8,128)(2,1)}, bf16[1152,128]{1,0:T(8,128)(2,1)S(1)}, u32[]{:S(2)}, u32[]{:S(2)}) collective-permute-start(bf16[1152,128]{1,0:T(8,128)(2,1)} %param.8), channel_id=1, source_target_pairs={{0,2},{2,4},{4,6},{6,8},{8,10},{10,12},{12,14},{14,0},{1,3},{3,5},... | collective-permute-start | bytes 884744 | tf_op jit(solution)/shard_map/ppermute | solution.py:85
  4.7 13.6 %collective-permute-start.2 = (bf16[1152,128]{1,0:T(8,128)(2,1)}, bf16[1152,128]{1,0:T(8,128)(2,1)S(1)}, u32[]{:S(2)}, u32[]{:S(2)}) collective-permute-start(bf16[1152,128]{1,0:T(8,128)(2,1)} %param.8), channel_id=1, source_target_pairs={{0,14},{2,0},{4,2},{6,4},{8,6},{10,8},{12,10},{14,12},{1,15},{3,1}... | collective-permute-start | bytes 884744 | tf_op jit(solution)/shard_map/ppermute | solution.py:88
  8.5 26.0 %collective-permute-start = (bf16[320,1152]{1,0:T(8,128)(2,1)}, bf16[320,1152]{1,0:T(8,128)(2,1)S(1)}, u32[]{:S(2)}, u32[]{:S(2)}) collective-permute-start(bf16[320,1152]{1,0:T(8,128)(2,1)} %param.7), channel_id=1, source_target_pairs={{0,1},{1,0},{2,3},{3,2},{4,5},{5,4},{6,7},{7,6},{8,9},{9,8},{10,11... | collective-permute-start | bytes 2211848 | tf_op jit(solution)/shard_map/ppermute | solution.py:94
  14.8 19.7 %copy-start.2 = (bf16[320,1152]{1,0:T(8,128)(2,1)S(1)}, bf16[320,1152]{1,0:T(8,128)(2,1)}, u32[]{:S(2)}) copy-start(bf16[320,1152]{1,0:T(8,128)(2,1)} %param.7) | copy-start | bytes 2211844
  16.1 9.0 %collective-permute-start.3 = (bf16[1152,128]{1,0:T(8,128)(2,1)S(1)}, bf16[1152,128]{1,0:T(8,128)(2,1)S(1)}, u32[]{:S(2)}, u32[]{:S(2)}) collective-permute-start(bf16[1152,128]{1,0:T(8,128)(2,1)S(1)} %collective-permute-done.1), channel_id=1, source_target_pairs={{0,2},{2,4},{4,6},{6,8},{8,10},{10,12},{12,14},{14,0},{1,3},{3,5},... | collective-permute-start | bytes 884744 | tf_op jit(solution)/shard_map/ppermute | solution.py:85
  18.3 8.7 %collective-permute-start.4 = (bf16[1152,128]{1,0:T(8,128)(2,1)S(1)}, bf16[1152,128]{1,0:T(8,128)(2,1)}, u32[]{:S(2)}, u32[]{:S(2)}) collective-permute-start(bf16[1152,128]{1,0:T(8,128)(2,1)S(1)} %collective-permute-done.2), channel_id=1, source_target_pairs={{0,14},{2,0},{4,2},{6,4},{8,6},{10,8},{12,10},{14,12},{1,15},{3,1}... | collective-permute-start | bytes 884744 | tf_op jit(solution)/shard_map/ppermute | solution.py:88
  25.0 15.4 %collective-permute-start.7 = (bf16[1152,128]{1,0:T(8,128)(2,1)S(1)}, bf16[1152,128]{1,0:T(8,128)(2,1)}, u32[]{:S(2)}, u32[]{:S(2)}) collective-permute-start(bf16[1152,128]{1,0:T(8,128)(2,1)S(1)} %collective-permute-done.3), channel_id=1, source_target_pairs={{0,2},{2,4},{4,6},{6,8},{8,10},{10,12},{12,14},{14,0},{1,3},{3,5},... | collective-permute-start | bytes 884744 | tf_op jit(solution)/shard_map/ppermute | solution.py:85
  27.0 23.6 %collective-permute-start.8 = (bf16[1152,128]{1,0:T(8,128)(2,1)}, bf16[1152,128]{1,0:T(8,128)(2,1)}, u32[]{:S(2)}, u32[]{:S(2)}) collective-permute-start(bf16[1152,128]{1,0:T(8,128)(2,1)} %collective-permute-done.4), channel_id=1, source_target_pairs={{0,14},{2,0},{4,2},{6,4},{8,6},{10,8},{12,10},{14,12},{1,15},{3,1}... | collective-permute-start | bytes 884744 | tf_op jit(solution)/shard_map/ppermute | solution.py:88
  33.4 1.1 copy-start.4
  37.7 1.4 copy-start.5
  39.0 1.4 copy-start
  40.5 10.1 %collective-permute-start.9 = (bf16[1152,128]{1,0:T(8,128)(2,1)}, bf16[1152,128]{1,0:T(8,128)(2,1)}, u32[]{:S(2)}, u32[]{:S(2)}) collective-permute-start(bf16[1152,128]{1,0:T(8,128)(2,1)} %collective-permute-done.7), channel_id=1, source_target_pairs={{0,2},{2,4},{4,6},{6,8},{8,10},{10,12},{12,14},{14,0},{1,3},{3,5},... | collective-permute-start | bytes 884744 | tf_op jit(solution)/shard_map/ppermute | solution.py:85
  43.2 8.9 %collective-permute-start.5 = (f32[320,5,128]{2,0,1:T(8,128)S(1)}, f32[320,5,128]{2,0,1:T(8,128)S(1)}, u32[]{:S(2)}, u32[]{:S(2)}) collective-permute-start(f32[320,5,128]{2,0,1:T(8,128)S(1)} %copy.19), channel_id=1, source_target_pairs={{0,16},{16,0},{1,17},{17,1},{2,18},{18,2},{3,19},{19,3},{4,20},{20... | collective-permute-start | bytes 2457608 | tf_op jit(solution)/shard_map/ppermute | solution.py:62
  52.0 1.4 copy-start.1
  54.9 10.0 %collective-permute-start.10 = (f32[320,3,128]{2,0,1:T(8,128)S(1)}, f32[320,3,128]{2,0,1:T(8,128)S(1)}, u32[]{:S(2)}, u32[]{:S(2)}) collective-permute-start(f32[320,3,128]{2,0,1:T(8,128)S(1)} %copy.23), channel_id=1, source_target_pairs={{0,16},{16,0},{1,17},{17,1},{2,18},{18,2},{3,19},{19,3},{4,20},{20... | collective-permute-start | bytes 1474568 | tf_op jit(solution)/shard_map/ppermute | solution.py:62
  62.4 13.1 %collective-permute-start.6 = (f32[160,5,128]{2,0,1:T(8,128)}, f32[160,5,128]{2,0,1:T(8,128)S(1)}, u32[]{:S(2)}, u32[]{:S(2)}) collective-permute-start(f32[160,5,128]{2,0,1:T(8,128)} %slice.41), channel_id=1, source_target_pairs={{0,32},{32,0},{1,33},{33,1},{2,34},{34,2},{3,35},{35,3},{4,36},{36... | collective-permute-start | bytes 1228808 | tf_op jit(solution)/shard_map/ppermute | solution.py:62
  65.0 15.8 %collective-permute-start.11 = (f32[160,3,128]{2,0,1:T(8,128)S(1)}, f32[160,3,128]{2,0,1:T(8,128)S(1)}, u32[]{:S(2)}, u32[]{:S(2)}) collective-permute-start(f32[160,3,128]{2,0,1:T(8,128)S(1)} %slice.63), channel_id=1, source_target_pairs={{0,32},{32,0},{1,33},{33,1},{2,34},{34,2},{3,35},{35,3},{4,36},{36... | collective-permute-start | bytes 737288 | tf_op jit(solution)/shard_map/ppermute | solution.py:62
  81.5 6.4 %copy-start.6 = (s32[1,32]{1,0:T(1,128)S(1)}, s32[1,32]{1,0:T(1,128)}, u32[]{:S(2)}) copy-start(s32[1,32]{1,0:T(1,128)} %param.12) | copy-start | bytes 388
  82.5 26.2 %all-to-all-start = ((f32[160,8,128]{2,0,1:T(8,128)}), f32[160,8,128]{2,0,1:T(8,128)S(1)}, u32[]{:S(2)}, u32[]{:S(2)}) async-start(f32[160,8,128]{2,0,1:T(8,128)} %select_bitcast_fusion), calls=%async_computation | async-start | bytes 1310720 | tf_op jit(solution)/shard_map/all_to_all | solution.py:155
  109.2 30.5 %copy-start.3 = (f32[160,128]{1,0:T(8,128)S(1)}, f32[160,128]{1,0:T(8,128)}, u32[]{:S(2)}) copy-start(f32[160,128]{1,0:T(8,128)} %param.13) | copy-start | bytes 245764
  162.0 9.7 %collective-permute-start.12 = (bf16[1280,128]{1,0:T(8,128)(2,1)S(1)}, bf16[1280,128]{1,0:T(8,128)(2,1)S(1)}, u32[]{:S(2)}, u32[]{:S(2)}) collective-permute-start(bf16[1280,128]{1,0:T(8,128)(2,1)S(1)} %bitcast.115), channel_id=1, source_target_pairs={{0,32},{32,0},{1,33},{33,1},{2,34},{34,2},{3,35},{35,3},{4,36},{36... | collective-permute-start | bytes 983048 | tf_op jit(solution)/shard_map/ppermute | solution.py:94
  171.7 5.9 %collective-permute-start.13 = (bf16[2560,128]{1,0:T(8,128)(2,1)S(1)}, bf16[2560,128]{1,0:T(8,128)(2,1)S(1)}, u32[]{:S(2)}, u32[]{:S(2)}) collective-permute-start(bf16[2560,128]{1,0:T(8,128)(2,1)S(1)} %pad_maximum_fusion.3), channel_id=1, source_target_pairs={{0,16},{16,0},{1,17},{17,1},{2,18},{18,2},{3,19},{19,3},{4,20},{20... | collective-permute-start | bytes 1966088 | tf_op jit(solution)/shard_map/ppermute | solution.py:94

commit v14 on v13

--- a/solution.py
+++ b/solution.py
@@ -178,14 +178,24 @@
         tiled=True,
     ).reshape(z_count * block_rows, heads_here * head_width)
     gathered = pair_gather(gathered, "xl")
-    gathered = pair_gather(gathered, "c")
+    partner = lax.ppermute(gathered, "c", SWAP)
     d = jnp.arange(dp_count, dtype=jnp.int32)
     update_position = (
         jnp.where(d % 2 == c, 0, half) + jnp.where((d // 2) % 2 == xl, 0, quarter) + d // 4
     )
-    placed = reorder(
-        gathered.reshape(dp_count, block_rows, heads_here, head_width), update_position[owners]
-    )
+    source = update_position[owners[0]]
+    slots = jnp.arange(half, dtype=jnp.int32)[None, :]
+    pick_own = (source[:, None] == slots).astype(jnp.bfloat16)
+    pick_partner = (source[:, None] == slots + half).astype(jnp.bfloat16)
+    block_shape = (half, block_rows, heads_here * head_width)
+    placed = (
+        jnp.einsum(
+            "bk,krc->brc", pick_own, gathered.reshape(block_shape), preferred_element_type=jnp.float32
+        )
+        + jnp.einsum(
+            "bk,krc->brc", pick_partner, partner.reshape(block_shape), preferred_element_type=jnp.float32
+        )
+    ).astype(jnp.bfloat16)
     return (
         placed.reshape(dp_count * block_rows, heads_here * head_width),
         new_momentum.reshape(block_rows, heads_here * head_width),

time: 183 us -> 181 us (0.989)
  other arithmetic: 13.1 us -> 9.6 us
    ppermute x0 -> x1, starting transfers between devices: none -> 4.22 us  [shards(): partner = lax.ppermute(gathered, 'c', SWAP)]
    ppermute x3 -> x2, starting transfers between devices: 11.3 us -> 7.06 us  [pair_gather(): return jnp.concatenate([piece, lax.ppermute(piece, axis, SWAP)], axis=0)]
    select_n x2 -> x1, other arithmetic: 3.38 us -> 0.01 us  [shards(): source = update_position[owners[0]]]
    ppermute x3 -> x2, waiting for transfers between devices: 8.03 us -> 7.29 us  [pair_gather(): return jnp.concatenate([piece, lax.ppermute(piece, axis, SWAP)], axis=0)]
where the time goes in v14:
time: 181 us; the launch traced here: 180 us
  starting transfers between devices  58.5 us (32%)
  blocking collectives  46.2 us (26%)
  waiting for transfers between devices  43.2 us (24%)
  local copies, waits for them, and re-layouts  13.2 us (7%)
  other arithmetic  9.6 us (5%)
  matrix products  7.84 us (4%)
  between operations  1.94 us (1%)
    all_to_all x1, blocking collectives, shards(): lax.all_to_all(in_owner_order, DP, split_axis=0, concat_axis=0, tiled=True)  30.3 us
    all_to_all x1, waiting for transfers between devices, shards(): lax.all_to_all(kept, 'y', split_axis=1, concat_axis=0, tiled=True)  20.6 us
    ppermute x4, starting transfers between devices, pair_sum_scatter(): return blocks[:half] + lax.ppermute(blocks[half:], axis, SWAP)  18.8 us
    all_to_all x1, blocking collectives, shards(): lax.all_to_all(jnp.broadcast_to(own_update[None], (z_count,) + own_update...  15.9 us
    ppermute x3, starting transfers between devices, ring_gather(): from_right = lax.ppermute(from_right, axis, to_left)  13.2 us
    ppermute x4, waiting for transfers between devices, pair_sum_scatter(): return blocks[:half] + lax.ppermute(blocks[half:], axis, SWAP)  12.4 us
    ppermute x4, starting transfers between devices, ring_gather(): from_left = lax.ppermute(from_left, axis, to_right)  9.78 us
    ppermute x2, waiting for transfers between devices, pair_gather(): return jnp.concatenate([piece, lax.ppermute(piece, axis, SWAP)], axis=0)  7.29 us
  transfers between devices with their start and end apart: 15, of which 6 were waited for; matrix products, arithmetic and copies ran while one was open for 8% of the time, Pallas kernels for 0%

profile of v14, /device:TPU:1, one launch (start us, length us, event | category | flops | bytes accessed | tf_op | source)
XLA Modules:
  0.0 180.4 jit_solution(12833926489558612647)
XLA Ops:
  0.6 4.0 %collective-permute-start.1 = (bf16[1152,128]{1,0:T(8,128)(2,1)}, bf16[1152,128]{1,0:T(8,128)(2,1)S(1)}, u32[]{:S(2)}, u32[]{:S(2)}) collective-permute-start(bf16[1152,128]{1,0:T(8,128)(2,1)} %param.8), channel_id=1, source_target_pairs={{0,2},{2,4},{4,6},{6,8},{8,10},{10,12},{12,14},{14,0},{1,3},{3,5},... | collective-permute-start | bytes 884744 | tf_op jit(solution)/shard_map/ppermute | solution.py:85
  4.7 3.8 %collective-permute-start.2 = (bf16[1152,128]{1,0:T(8,128)(2,1)}, bf16[1152,128]{1,0:T(8,128)(2,1)S(1)}, u32[]{:S(2)}, u32[]{:S(2)}) collective-permute-start(bf16[1152,128]{1,0:T(8,128)(2,1)} %param.8), channel_id=1, source_target_pairs={{0,14},{2,0},{4,2},{6,4},{8,6},{10,8},{12,10},{14,12},{1,15},{3,1}... | collective-permute-start | bytes 884744 | tf_op jit(solution)/shard_map/ppermute | solution.py:88
  8.5 4.7 %collective-permute-start = (bf16[320,1152]{1,0:T(8,128)(2,1)}, bf16[320,1152]{1,0:T(8,128)(2,1)S(1)}, u32[]{:S(2)}, u32[]{:S(2)}) collective-permute-start(bf16[320,1152]{1,0:T(8,128)(2,1)} %param.7), channel_id=1, source_target_pairs={{0,1},{1,0},{2,3},{3,2},{4,5},{5,4},{6,7},{7,6},{8,9},{9,8},{10,11... | collective-permute-start | bytes 2211848 | tf_op jit(solution)/shard_map/ppermute | solution.py:94
  13.3 0.8 select_reduce_fusion
  14.1 0.7 multiply_multiply_fusion
  14.8 1.2 fusion.22
  16.1 1.9 %collective-permute-start.3 = (bf16[1152,128]{1,0:T(8,128)(2,1)S(1)}, bf16[1152,128]{1,0:T(8,128)(2,1)S(1)}, u32[]{:S(2)}, u32[]{:S(2)}) collective-permute-start(bf16[1152,128]{1,0:T(8,128)(2,1)S(1)} %collective-permute-done.1), channel_id=1, source_target_pairs={{0,2},{2,4},{4,6},{6,8},{8,10},{10,12},{12,14},{14,0},{1,3},{3,5},... | collective-permute-start | bytes 884744 | tf_op jit(solution)/shard_map/ppermute | solution.py:85
  18.0 0.3 fusion.23
  18.3 4.6 %collective-permute-start.4 = (bf16[1152,128]{1,0:T(8,128)(2,1)S(1)}, bf16[1152,128]{1,0:T(8,128)(2,1)}, u32[]{:S(2)}, u32[]{:S(2)}) collective-permute-start(bf16[1152,128]{1,0:T(8,128)(2,1)S(1)} %collective-permute-done.2), channel_id=1, source_target_pairs={{0,14},{2,0},{4,2},{6,4},{8,6},{10,8},{12,10},{14,12},{1,15},{3,1}... | collective-permute-start | bytes 884744 | tf_op jit(solution)/shard_map/ppermute | solution.py:88
  22.9 0.3 fusion.24
  23.2 1.9 %collective-permute-done.3 = bf16[1152,128]{1,0:T(8,128)(2,1)S(1)} collective-permute-done((bf16[1152,128]{1,0:T(8,128)(2,1)S(1)}, bf16[1152,128]{1,0:T(8,128)(2,1)S(1)}, u32[]{:S(2)}, u32[]{:S(2)}) %collective-permute-start.3) | collective-permute-done | bytes 294944 | tf_op jit(solution)/shard_map/ppermute | solution.py:85
  25.0 1.9 %collective-permute-start.7 = (bf16[1152,128]{1,0:T(8,128)(2,1)S(1)}, bf16[1152,128]{1,0:T(8,128)(2,1)}, u32[]{:S(2)}, u32[]{:S(2)}) collective-permute-start(bf16[1152,128]{1,0:T(8,128)(2,1)S(1)} %collective-permute-done.3), channel_id=1, source_target_pairs={{0,2},{2,4},{4,6},{6,8},{8,10},{10,12},{12,14},{14,0},{1,3},{3,5},... | collective-permute-start | bytes 884744 | tf_op jit(solution)/shard_map/ppermute | solution.py:85
  27.0 4.9 %collective-permute-start.8 = (bf16[1152,128]{1,0:T(8,128)(2,1)}, bf16[1152,128]{1,0:T(8,128)(2,1)}, u32[]{:S(2)}, u32[]{:S(2)}) collective-permute-start(bf16[1152,128]{1,0:T(8,128)(2,1)} %collective-permute-done.4), channel_id=1, source_target_pairs={{0,14},{2,0},{4,2},{6,4},{8,6},{10,8},{12,10},{14,12},{1,15},{3,1}... | collective-permute-start | bytes 884744 | tf_op jit(solution)/shard_map/ppermute | solution.py:88
  31.8 0.3 fusion.25
  32.1 1.2 fusion.26
  33.4 1.1 copy-done.4
  34.6 3.0 %gather_fusion.1 = bf16[640,1152]{1,0:T(8,128)(2,1)S(1)} fusion(bf16[640,1152]{1,0:T(8,128)(2,1)S(1)} %pad_maximum_fusion, s32[1024]{0:T(1024)S(1)} %pad_clamp_fusion.2), kind=kCustom, calls=%fused_computation.1 | custom fusion | bytes 2951680 | tf_op jit(solution)/shard_map/jit(_take)/gather | solution.py:132
  37.7 0.2 broadcast_select_fusion
  37.9 1.1 copy-done.5
  39.0 1.4 fusion.90
  40.5 1.9 %collective-permute-start.9 = (bf16[1152,128]{1,0:T(8,128)(2,1)}, bf16[1152,128]{1,0:T(8,128)(2,1)}, u32[]{:S(2)}, u32[]{:S(2)}) collective-permute-start(bf16[1152,128]{1,0:T(8,128)(2,1)} %collective-permute-done.7), channel_id=1, source_target_pairs={{0,2},{2,4},{4,6},{6,8},{8,10},{10,12},{12,14},{14,0},{1,3},{3,5},... | collective-permute-start | bytes 884744 | tf_op jit(solution)/shard_map/ppermute | solution.py:85
  42.5 0.3 copy.21
  42.8 0.3 copy.22
  43.2 6.8 %collective-permute-start.5 = (f32[320,5,128]{2,0,1:T(8,128)S(1)}, f32[320,5,128]{2,0,1:T(8,128)S(1)}, u32[]{:S(2)}, u32[]{:S(2)}) collective-permute-start(f32[320,5,128]{2,0,1:T(8,128)S(1)} %copy.22), channel_id=1, source_target_pairs={{0,16},{16,0},{1,17},{17,1},{2,18},{18,2},{3,19},{19,3},{4,20},{20... | collective-permute-start | bytes 2457608 | tf_op jit(solution)/shard_map/ppermute | solution.py:62
  49.9 0.3 copy.20
  50.2 0.3 copy.23
  50.6 1.4 multiply_convert_fusion.2
  52.1 1.3 copy-done.1
  53.4 1.0 fusion.13
  54.4 0.2 copy.25
  54.7 0.2 copy.26
  54.9 6.8 %collective-permute-start.10 = (f32[320,3,128]{2,0,1:T(8,128)S(1)}, f32[320,3,128]{2,0,1:T(8,128)S(1)}, u32[]{:S(2)}, u32[]{:S(2)}) collective-permute-start(f32[320,3,128]{2,0,1:T(8,128)S(1)} %copy.26), channel_id=1, source_target_pairs={{0,16},{16,0},{1,17},{17,1},{2,18},{18,2},{3,19},{19,3},{4,20},{20... | collective-permute-start | bytes 1474568 | tf_op jit(solution)/shard_map/ppermute | solution.py:62
  61.7 0.8 slice.41
  62.4 1.9 %collective-permute-start.6 = (f32[160,5,128]{2,0,1:T(8,128)}, f32[160,5,128]{2,0,1:T(8,128)S(1)}, u32[]{:S(2)}, u32[]{:S(2)}) collective-permute-start(f32[160,5,128]{2,0,1:T(8,128)} %slice.41), channel_id=1, source_target_pairs={{0,32},{32,0},{1,33},{33,1},{2,34},{34,2},{3,35},{35,3},{4,36},{36... | collective-permute-start | bytes 1228808 | tf_op jit(solution)/shard_map/ppermute | solution.py:62
  64.4 0.2 copy.24
  65.0 3.4 %collective-permute-start.11 = (f32[160,3,128]{2,0,1:T(8,128)S(1)}, f32[160,3,128]{2,0,1:T(8,128)S(1)}, u32[]{:S(2)}, u32[]{:S(2)}) collective-permute-start(f32[160,3,128]{2,0,1:T(8,128)S(1)} %slice.61), channel_id=1, source_target_pairs={{0,32},{32,0},{1,33},{33,1},{2,34},{34,2},{3,35},{35,3},{4,36},{36... | collective-permute-start | bytes 737288 | tf_op jit(solution)/shard_map/ppermute | solution.py:62
  68.3 7.2 %collective-permute-done.6 = f32[160,5,128]{2,0,1:T(8,128)S(1)} collective-permute-done((f32[160,5,128]{2,0,1:T(8,128)}, f32[160,5,128]{2,0,1:T(8,128)S(1)}, u32[]{:S(2)}, u32[]{:S(2)}) %collective-permute-start.6) | collective-permute-done | bytes 409632 | tf_op jit(solution)/shard_map/ppermute | solution.py:62
  75.6 5.2 %collective-permute-done.11 = f32[160,3,128]{2,0,1:T(8,128)S(1)} collective-permute-done((f32[160,3,128]{2,0,1:T(8,128)S(1)}, f32[160,3,128]{2,0,1:T(8,128)S(1)}, u32[]{:S(2)}, u32[]{:S(2)}) %collective-permute-start.11) | collective-permute-done | bytes 245792 | tf_op jit(solution)/shard_map/ppermute | solution.py:62
  80.9 0.6 gather_fusion.2
  81.5 0.9 select_bitcast_fusion
  82.5 5.4 %all-to-all-start = ((f32[160,8,128]{2,0,1:T(8,128)}), f32[160,8,128]{2,0,1:T(8,128)S(1)}, u32[]{:S(2)}, u32[]{:S(2)}) async-start(f32[160,8,128]{2,0,1:T(8,128)} %select_bitcast_fusion), calls=%async_computation | async-start | bytes 1310720 | tf_op jit(solution)/shard_map/all_to_all | solution.py:155
  88.0 20.6 %all-to-all-done = f32[160,8,128]{2,0,1:T(8,128)S(1)} async-done(((f32[160,8,128]{2,0,1:T(8,128)}), f32[160,8,128]{2,0,1:T(8,128)S(1)}, u32[]{:S(2)}, u32[]{:S(2)}) %all-to-all-start) | async-done | bytes 655392 | tf_op jit(solution)/shard_map/all_to_all | solution.py:155
  108.6 0.6 gather_fusion.3
  109.3 30.3 %all_to_all.25 = f32[32,40,128]{2,1,0:T(8,128)S(1)} all-to-all(f32[32,40,128]{2,1,0:T(8,128)S(1)} %broadcast_select_fusion.1), channel_id=1, replica_groups=mesh['z'=8,'xl'=2,'c'=2,'y'=8,'xh'=2] {'z','xl','c'}, dimensions={0} | all-to-all | bytes 1310720 | tf_op jit(solution)/shard_map/all_to_all | solution.py:159
  139.7 1.3 multiply_reduce_fusion
  141.7 0.4 fusion.39
  142.3 0.2 fusion
  142.6 0.4 fusion.37
  143.2 0.2 fusion.1
  143.4 0.4 fusion.34
  144.1 0.2 fusion.2
  144.3 0.4 fusion.31
  145.0 0.2 fusion.3
  145.2 0.4 fusion.28
  145.8 0.2 fusion.12
  146.1 15.9 %all_to_all.26 = bf16[8,160,128]{2,1,0:T(8,128)(2,1)S(1)} all-to-all(bf16[8,160,128]{2,1,0:T(8,128)(2,1)S(1)} %broadcast_in_dim.125), channel_id=1, replica_groups=mesh['z'=8,'xl'=2,'c'=2,'y'=8,'xh'=2] {'z'}, dimensions={0} | all-to-all | bytes 655360 | tf_op jit(solution)/shard_map/all_to_all | solution.py:173
  162.0 2.4 %collective-permute-start.12 = (bf16[1280,128]{1,0:T(8,128)(2,1)S(1)}, bf16[1280,128]{1,0:T(8,128)(2,1)S(1)}, u32[]{:S(2)}, u32[]{:S(2)}) collective-permute-start(bf16[1280,128]{1,0:T(8,128)(2,1)S(1)} %bitcast.123), channel_id=1, source_target_pairs={{0,32},{32,0},{1,33},{33,1},{2,34},{34,2},{3,35},{35,3},{4,36},{36... | collective-permute-start | bytes 983048 | tf_op jit(solution)/shard_map/ppermute | solution.py:94
  164.4 7.3 %collective-permute-done.12 = bf16[1280,128]{1,0:T(8,128)(2,1)S(1)} collective-permute-done((bf16[1280,128]{1,0:T(8,128)(2,1)S(1)}, bf16[1280,128]{1,0:T(8,128)(2,1)S(1)}, u32[]{:S(2)}, u32[]{:S(2)}) %collective-permute-start.12) | collective-permute-done | bytes 327712 | tf_op jit(solution)/shard_map/ppermute | solution.py:94
  171.7 4.2 %collective-permute-start.13 = (bf16[2560,128]{1,0:T(8,128)(2,1)S(1)}, bf16[2560,128]{1,0:T(8,128)(2,1)S(1)}, u32[]{:S(2)}, u32[]{:S(2)}) collective-permute-start(bf16[2560,128]{1,0:T(8,128)(2,1)S(1)} %pad_maximum_fusion.2), channel_id=1, source_target_pairs={{0,16},{16,0},{1,17},{17,1},{2,18},{18,2},{3,19},{19,3},{4,20},{20... | collective-permute-start | bytes 1966088 | tf_op jit(solution)/shard_map/ppermute | solution.py:181
  176.0 0.7 gather_fusion
  176.7 1.0 collective-permute-done.13
  177.7 0.6 fusion.19
  178.3 0.6 add_convert_fusion
  178.9 1.6 copy.30
  (53 shorter events, 2.4 us)
Async XLA Ops:
  0.6 15.4 %collective-permute-start.1 = (bf16[1152,128]{1,0:T(8,128)(2,1)}, bf16[1152,128]{1,0:T(8,128)(2,1)S(1)}, u32[]{:S(2)}, u32[]{:S(2)}) collective-permute-start(bf16[1152,128]{1,0:T(8,128)(2,1)} %param.8), channel_id=1, source_target_pairs={{0,2},{2,4},{4,6},{6,8},{8,10},{10,12},{12,14},{14,0},{1,3},{3,5},... | collective-permute-start | bytes 884744 | tf_op jit(solution)/shard_map/ppermute | solution.py:85
  4.7 13.6 %collective-permute-start.2 = (bf16[1152,128]{1,0:T(8,128)(2,1)}, bf16[1152,128]{1,0:T(8,128)(2,1)S(1)}, u32[]{:S(2)}, u32[]{:S(2)}) collective-permute-start(bf16[1152,128]{1,0:T(8,128)(2,1)} %param.8), channel_id=1, source_target_pairs={{0,14},{2,0},{4,2},{6,4},{8,6},{10,8},{12,10},{14,12},{1,15},{3,1}... | collective-permute-start | bytes 884744 | tf_op jit(solution)/shard_map/ppermute | solution.py:88
  8.5 26.0 %collective-permute-start = (bf16[320,1152]{1,0:T(8,128)(2,1)}, bf16[320,1152]{1,0:T(8,128)(2,1)S(1)}, u32[]{:S(2)}, u32[]{:S(2)}) collective-permute-start(bf16[320,1152]{1,0:T(8,128)(2,1)} %param.7), channel_id=1, source_target_pairs={{0,1},{1,0},{2,3},{3,2},{4,5},{5,4},{6,7},{7,6},{8,9},{9,8},{10,11... | collective-permute-start | bytes 2211848 | tf_op jit(solution)/shard_map/ppermute | solution.py:94
  14.8 19.7 %copy-start.2 = (bf16[320,1152]{1,0:T(8,128)(2,1)S(1)}, bf16[320,1152]{1,0:T(8,128)(2,1)}, u32[]{:S(2)}) copy-start(bf16[320,1152]{1,0:T(8,128)(2,1)} %param.7) | copy-start | bytes 2211844
  16.1 9.0 %collective-permute-start.3 = (bf16[1152,128]{1,0:T(8,128)(2,1)S(1)}, bf16[1152,128]{1,0:T(8,128)(2,1)S(1)}, u32[]{:S(2)}, u32[]{:S(2)}) collective-permute-start(bf16[1152,128]{1,0:T(8,128)(2,1)S(1)} %collective-permute-done.1), channel_id=1, source_target_pairs={{0,2},{2,4},{4,6},{6,8},{8,10},{10,12},{12,14},{14,0},{1,3},{3,5},... | collective-permute-start | bytes 884744 | tf_op jit(solution)/shard_map/ppermute | solution.py:85
  18.3 8.7 %collective-permute-start.4 = (bf16[1152,128]{1,0:T(8,128)(2,1)S(1)}, bf16[1152,128]{1,0:T(8,128)(2,1)}, u32[]{:S(2)}, u32[]{:S(2)}) collective-permute-start(bf16[1152,128]{1,0:T(8,128)(2,1)S(1)} %collective-permute-done.2), channel_id=1, source_target_pairs={{0,14},{2,0},{4,2},{6,4},{8,6},{10,8},{12,10},{14,12},{1,15},{3,1}... | collective-permute-start | bytes 884744 | tf_op jit(solution)/shard_map/ppermute | solution.py:88
  25.0 15.4 %collective-permute-start.7 = (bf16[1152,128]{1,0:T(8,128)(2,1)S(1)}, bf16[1152,128]{1,0:T(8,128)(2,1)}, u32[]{:S(2)}, u32[]{:S(2)}) collective-permute-start(bf16[1152,128]{1,0:T(8,128)(2,1)S(1)} %collective-permute-done.3), channel_id=1, source_target_pairs={{0,2},{2,4},{4,6},{6,8},{8,10},{10,12},{12,14},{14,0},{1,3},{3,5},... | collective-permute-start | bytes 884744 | tf_op jit(solution)/shard_map/ppermute | solution.py:85
  27.0 23.6 %collective-permute-start.8 = (bf16[1152,128]{1,0:T(8,128)(2,1)}, bf16[1152,128]{1,0:T(8,128)(2,1)}, u32[]{:S(2)}, u32[]{:S(2)}) collective-permute-start(bf16[1152,128]{1,0:T(8,128)(2,1)} %collective-permute-done.4), channel_id=1, source_target_pairs={{0,14},{2,0},{4,2},{6,4},{8,6},{10,8},{12,10},{14,12},{1,15},{3,1}... | collective-permute-start | bytes 884744 | tf_op jit(solution)/shard_map/ppermute | solution.py:88
  33.4 1.1 copy-start.4
  37.7 1.4 copy-start.5
  39.0 1.4 copy-start
  40.5 10.1 %collective-permute-start.9 = (bf16[1152,128]{1,0:T(8,128)(2,1)}, bf16[1152,128]{1,0:T(8,128)(2,1)}, u32[]{:S(2)}, u32[]{:S(2)}) collective-permute-start(bf16[1152,128]{1,0:T(8,128)(2,1)} %collective-permute-done.7), channel_id=1, source_target_pairs={{0,2},{2,4},{4,6},{6,8},{8,10},{10,12},{12,14},{14,0},{1,3},{3,5},... | collective-permute-start | bytes 884744 | tf_op jit(solution)/shard_map/ppermute | solution.py:85
  43.2 8.9 %collective-permute-start.5 = (f32[320,5,128]{2,0,1:T(8,128)S(1)}, f32[320,5,128]{2,0,1:T(8,128)S(1)}, u32[]{:S(2)}, u32[]{:S(2)}) collective-permute-start(f32[320,5,128]{2,0,1:T(8,128)S(1)} %copy.22), channel_id=1, source_target_pairs={{0,16},{16,0},{1,17},{17,1},{2,18},{18,2},{3,19},{19,3},{4,20},{20... | collective-permute-start | bytes 2457608 | tf_op jit(solution)/shard_map/ppermute | solution.py:62
  52.0 1.4 copy-start.1
  54.9 10.0 %collective-permute-start.10 = (f32[320,3,128]{2,0,1:T(8,128)S(1)}, f32[320,3,128]{2,0,1:T(8,128)S(1)}, u32[]{:S(2)}, u32[]{:S(2)}) collective-permute-start(f32[320,3,128]{2,0,1:T(8,128)S(1)} %copy.26), channel_id=1, source_target_pairs={{0,16},{16,0},{1,17},{17,1},{2,18},{18,2},{3,19},{19,3},{4,20},{20... | collective-permute-start | bytes 1474568 | tf_op jit(solution)/shard_map/ppermute | solution.py:62
  62.4 13.1 %collective-permute-start.6 = (f32[160,5,128]{2,0,1:T(8,128)}, f32[160,5,128]{2,0,1:T(8,128)S(1)}, u32[]{:S(2)}, u32[]{:S(2)}) collective-permute-start(f32[160,5,128]{2,0,1:T(8,128)} %slice.41), channel_id=1, source_target_pairs={{0,32},{32,0},{1,33},{33,1},{2,34},{34,2},{3,35},{35,3},{4,36},{36... | collective-permute-start | bytes 1228808 | tf_op jit(solution)/shard_map/ppermute | solution.py:62
  65.0 15.8 %collective-permute-start.11 = (f32[160,3,128]{2,0,1:T(8,128)S(1)}, f32[160,3,128]{2,0,1:T(8,128)S(1)}, u32[]{:S(2)}, u32[]{:S(2)}) collective-permute-start(f32[160,3,128]{2,0,1:T(8,128)S(1)} %slice.61), channel_id=1, source_target_pairs={{0,32},{32,0},{1,33},{33,1},{2,34},{34,2},{3,35},{35,3},{4,36},{36... | collective-permute-start | bytes 737288 | tf_op jit(solution)/shard_map/ppermute | solution.py:62
  81.5 6.4 %copy-start.6 = (s32[1,32]{1,0:T(1,128)S(1)}, s32[1,32]{1,0:T(1,128)}, u32[]{:S(2)}) copy-start(s32[1,32]{1,0:T(1,128)} %param.12) | copy-start | bytes 388
  82.5 26.2 %all-to-all-start = ((f32[160,8,128]{2,0,1:T(8,128)}), f32[160,8,128]{2,0,1:T(8,128)S(1)}, u32[]{:S(2)}, u32[]{:S(2)}) async-start(f32[160,8,128]{2,0,1:T(8,128)} %select_bitcast_fusion), calls=%async_computation | async-start | bytes 1310720 | tf_op jit(solution)/shard_map/all_to_all | solution.py:155
  109.2 30.5 %copy-start.3 = (f32[160,128]{1,0:T(8,128)S(1)}, f32[160,128]{1,0:T(8,128)}, u32[]{:S(2)}) copy-start(f32[160,128]{1,0:T(8,128)} %param.13) | copy-start | bytes 245764
  162.0 9.7 %collective-permute-start.12 = (bf16[1280,128]{1,0:T(8,128)(2,1)S(1)}, bf16[1280,128]{1,0:T(8,128)(2,1)S(1)}, u32[]{:S(2)}, u32[]{:S(2)}) collective-permute-start(bf16[1280,128]{1,0:T(8,128)(2,1)S(1)} %bitcast.123), channel_id=1, source_target_pairs={{0,32},{32,0},{1,33},{33,1},{2,34},{34,2},{3,35},{35,3},{4,36},{36... | collective-permute-start | bytes 983048 | tf_op jit(solution)/shard_map/ppermute | solution.py:94
  171.7 5.9 %collective-permute-start.13 = (bf16[2560,128]{1,0:T(8,128)(2,1)S(1)}, bf16[2560,128]{1,0:T(8,128)(2,1)S(1)}, u32[]{:S(2)}, u32[]{:S(2)}) collective-permute-start(bf16[2560,128]{1,0:T(8,128)(2,1)S(1)} %pad_maximum_fusion.2), channel_id=1, source_target_pairs={{0,16},{16,0},{1,17},{17,1},{2,18},{18,2},{3,19},{19,3},{4,20},{20... | collective-permute-start | bytes 1966088 | tf_op jit(solution)/shard_map/ppermute | solution.py:181

commit v15 on v14

--- a/solution.py
+++ b/solution.py
@@ -140,22 +140,26 @@
     early = 2 * 2 + 1
     early_core = core_reduced(arranged, ring_pieces[:early])
     arranged_late, early_core = lax.optimization_barrier((arranged, early_core))
-    kept_ring_order = jnp.concatenate(
-        [
-            pair_sum_scatter(early_core, "xl"),
-            pair_sum_scatter(core_reduced(arranged_late, ring_pieces[early:]), "xl"),
-        ],
-        axis=1,
-    )
-    head = jnp.arange(y_count, dtype=jnp.int32)
-    ahead = (head - y) % y_count
-    behind = (y - head) % y_count
-    slot = jnp.where(ahead == 0, 0, jnp.where(ahead < behind, 2 * ahead, 2 * behind - 1))
-    kept = jnp.take(kept_ring_order, slot, axis=1)
-    quarters = lax.all_to_all(kept, "y", split_axis=1, concat_axis=0, tiled=True).reshape(
-        dp_count, quarter_rows, head_width
-    )
-    in_owner_order = jnp.take(quarters, inverse[0], axis=0)
+    kept_early = pair_sum_scatter(early_core, "xl")
+    kept_late = pair_sum_scatter(core_reduced(arranged_late, ring_pieces[early:]), "xl")
+    def slot_of(index):
+        return kept_early[:, index] if index < early else kept_late[:, index - early]
+
+    received = [slot_of(0)]
+    shifts = [0]
+    for index in range(1, y_count):
+        distance = (index + 1) // 2
+        shift = -distance if index % 2 == 1 and 2 * distance < y_count else distance
+        perm = [(i, (i + shift) % y_count) for i in range(y_count)]
+        received.append(lax.ppermute(slot_of(index), "y", perm))
+        shifts.append(shift)
+    quarters = jnp.stack(received).reshape(dp_count, quarter_rows, head_width)
+    source_delta = jnp.asarray([-s for s in shifts], dtype=jnp.int32)
+    source_y = (y + source_delta) % y_count
+    source_slot = jnp.zeros(y_count, jnp.int32).at[source_y].set(jnp.arange(y_count, dtype=jnp.int32))
+    block = jnp.arange(dp_count, dtype=jnp.int32)
+    block_at = source_slot[block // pair_blocks] * pair_blocks + block % pair_blocks
+    in_owner_order = jnp.take(quarters, block_at[inverse[0]], axis=0)
     from_all = lax.all_to_all(in_owner_order, DP, split_axis=0, concat_axis=0, tiled=True)
     own_block = jnp.sum(
         from_all.reshape(z_count, dp_count // z_count, quarter_rows, head_width), axis=0

time: 181 us -> 206 us (1.14)
  starting transfers between devices: 58.5 us -> 72.4 us
  other arithmetic: 9.6 us -> 15.7 us
  waiting for transfers between devices: 43.2 us -> 39.1 us
  local copies, waits for them, and re-layouts: 13.2 us -> 16.5 us
  blocking collectives: 46.2 us -> 49.1 us
    ppermute x0 -> x7, starting transfers between devices: none -> 24.6 us  [shards(): received.append(lax.ppermute(slot_of(index), 'y', perm))]
    all_to_all x1 -> x0, waiting for transfers between devices: 20.6 us -> none  [shards(): lax.all_to_all(kept, 'y', split_axis=1, concat_axis=0, tiled=True)]
    ppermute x0 -> x7, waiting for transfers between devices: none -> 8.96 us  [shards(): received.append(lax.ppermute(slot_of(index), 'y', perm))]
    ppermute x4, waiting for transfers between devices: 1.88 us -> 9.99 us  [ring_gather(): from_left = lax.ppermute(from_left, axis, to_right)]
    all_to_all x1 -> x0, starting transfers between devices: 5.39 us -> none  [shards(): lax.all_to_all(kept, 'y', split_axis=1, concat_axis=0, tiled=True)]
    ppermute x4, starting transfers between devices: 18.8 us -> 13.8 us  [pair_sum_scatter(): return blocks[:half] + lax.ppermute(blocks[half:], axis, SWAP)]
    unnamed x4, other arithmetic: 2.09 us -> 5.84 us
    ppermute x0 -> x3, local copies, waits for them, and re-layouts: none -> 2.82 us  [pair_sum_scatter(): return blocks[:half] + lax.ppermute(blocks[half:], axis, SWAP)]
  transfers between devices with their start and end apart: 15 -> 21, of which waited for: 6 -> 9; matrix products, arithmetic and copies ran while one was open for 8% -> 15% of each run, Pallas kernels for 0% -> 0%
where the time goes in v15:
time: 206 us; the launch traced here: 204 us
  starting transfers between devices  72.4 us (35%)
  blocking collectives  49.1 us (24%)
  waiting for transfers between devices  39.1 us (19%)
  local copies, waits for them, and re-layouts  16.5 us (8%)
  other arithmetic  15.7 us (8%)
  matrix products  8.98 us (4%)
  between operations  2.07 us (1%)
    all_to_all x1, blocking collectives, shards(): lax.all_to_all(in_owner_order, DP, split_axis=0, concat_axis=0, tiled=True)  32.9 us
    ppermute x7, starting transfers between devices, shards(): received.append(lax.ppermute(slot_of(index), 'y', perm))  24.6 us
    all_to_all x1, blocking collectives, shards(): lax.all_to_all(jnp.broadcast_to(own_update[None], (z_count,) + own_update...  16.2 us
    ppermute x4, starting transfers between devices, pair_sum_scatter(): return blocks[:half] + lax.ppermute(blocks[half:], axis, SWAP)  13.8 us
    ppermute x3, starting transfers between devices, ring_gather(): from_right = lax.ppermute(from_right, axis, to_left)  13.5 us
    ppermute x4, waiting for transfers between devices, pair_sum_scatter(): return blocks[:half] + lax.ppermute(blocks[half:], axis, SWAP)  11.2 us
    ppermute x4, waiting for transfers between devices, ring_gather(): from_left = lax.ppermute(from_left, axis, to_right)  9.99 us
    ppermute x4, starting transfers between devices, ring_gather(): from_left = lax.ppermute(from_left, axis, to_right)  9.77 us
  transfers between devices with their start and end apart: 21, of which 9 were waited for; matrix products, arithmetic and copies ran while one was open for 15% of the time, Pallas kernels for 0%

profile of v15, /device:TPU:1, one launch (start us, length us, event | category | flops | bytes accessed | tf_op | source)
XLA Modules:
  0.0 204.0 jit_solution(8313805036552449984)
XLA Ops:
  0.6 4.0 %collective-permute-start.1 = (bf16[1152,128]{1,0:T(8,128)(2,1)}, bf16[1152,128]{1,0:T(8,128)(2,1)S(1)}, u32[]{:S(2)}, u32[]{:S(2)}) collective-permute-start(bf16[1152,128]{1,0:T(8,128)(2,1)} %param.9), channel_id=1, source_target_pairs={{0,2},{2,4},{4,6},{6,8},{8,10},{10,12},{12,14},{14,0},{1,3},{3,5},... | collective-permute-start | bytes 884744 | tf_op jit(solution)/shard_map/ppermute | solution.py:85
  4.7 3.8 %collective-permute-start.2 = (bf16[1152,128]{1,0:T(8,128)(2,1)}, bf16[1152,128]{1,0:T(8,128)(2,1)S(1)}, u32[]{:S(2)}, u32[]{:S(2)}) collective-permute-start(bf16[1152,128]{1,0:T(8,128)(2,1)} %param.9), channel_id=1, source_target_pairs={{0,14},{2,0},{4,2},{6,4},{8,6},{10,8},{12,10},{14,12},{1,15},{3,1}... | collective-permute-start | bytes 884744 | tf_op jit(solution)/shard_map/ppermute | solution.py:88
  8.5 4.7 %collective-permute-start = (bf16[320,1152]{1,0:T(8,128)(2,1)}, bf16[320,1152]{1,0:T(8,128)(2,1)S(1)}, u32[]{:S(2)}, u32[]{:S(2)}) collective-permute-start(bf16[320,1152]{1,0:T(8,128)(2,1)} %param.8), channel_id=1, source_target_pairs={{0,1},{1,0},{2,3},{3,2},{4,5},{5,4},{6,7},{7,6},{8,9},{9,8},{10,11... | collective-permute-start | bytes 2211848 | tf_op jit(solution)/shard_map/ppermute | solution.py:94
  13.3 0.8 select_reduce_fusion
  14.1 0.7 multiply_multiply_fusion
  14.8 1.9 fusion.22
  16.7 0.8 select_reduce_fusion.1
  17.5 0.7 compare_select_fusion.14
  18.2 0.6 scatter_custom_fusion
  18.8 0.7 gather_fusion.1
  19.5 0.7 gather_fusion.2
  20.2 0.5 fusion.86
  20.8 1.9 collective-permute-start.3
  22.7 1.0 fusion.23
  23.7 4.6 %collective-permute-start.4 = (bf16[1152,128]{1,0:T(8,128)(2,1)S(1)}, bf16[1152,128]{1,0:T(8,128)(2,1)}, u32[]{:S(2)}, u32[]{:S(2)}) collective-permute-start(bf16[1152,128]{1,0:T(8,128)(2,1)S(1)} %collective-permute-done.2), channel_id=1, source_target_pairs={{0,14},{2,0},{4,2},{6,4},{8,6},{10,8},{12,10},{14,12},{1,15},{3,1}... | collective-permute-start | bytes 884744 | tf_op jit(solution)/shard_map/ppermute | solution.py:88
  28.2 0.9 fusion.24
  29.2 0.5 collective-permute-done.3
  29.7 1.9 collective-permute-start.11
  31.9 5.1 %collective-permute-start.12 = (bf16[1152,128]{1,0:T(8,128)(2,1)}, bf16[1152,128]{1,0:T(8,128)(2,1)S(1)}, u32[]{:S(2)}, u32[]{:S(2)}) collective-permute-start(bf16[1152,128]{1,0:T(8,128)(2,1)} %collective-permute-done.4), channel_id=1, source_target_pairs={{0,14},{2,0},{4,2},{6,4},{8,6},{10,8},{12,10},{14,12},{1,15},{3,1}... | collective-permute-start | bytes 884744 | tf_op jit(solution)/shard_map/ppermute | solution.py:88
  37.0 2.0 fusion.25
  39.0 1.9 fusion.26
  41.1 3.0 %gather_fusion.3 = bf16[640,1152]{1,0:T(8,128)(2,1)S(1)} fusion(bf16[640,1152]{1,0:T(8,128)(2,1)S(1)} %pad_maximum_fusion, s32[1024]{0:T(1024)S(1)} %pad_clamp_fusion.1), kind=kCustom, calls=%fused_computation.3 | custom fusion | bytes 2951680 | tf_op jit(solution)/shard_map/jit(_take)/gather | solution.py:132
  44.4 1.1 copy-done.4
  45.5 1.4 fusion.92
  47.4 1.2 copy.47
  48.6 6.9 %collective-permute-start.5 = (f32[320,5,128]{2,0,1:T(8,128)}, f32[320,5,128]{2,0,1:T(8,128)S(1)}, u32[]{:S(2)}, u32[]{:S(2)}) collective-permute-start(f32[320,5,128]{2,0,1:T(8,128)} %copy.47), channel_id=1, source_target_pairs={{0,16},{16,0},{1,17},{17,1},{2,18},{18,2},{3,19},{19,3},{4,20},{20... | collective-permute-start | bytes 2457608 | tf_op jit(solution)/shard_map/ppermute | solution.py:62
  55.5 1.9 collective-permute-start.13
  57.8 9.4 %collective-permute-done.13 = bf16[1152,128]{1,0:T(8,128)(2,1)} collective-permute-done((bf16[1152,128]{1,0:T(8,128)(2,1)S(1)}, bf16[1152,128]{1,0:T(8,128)(2,1)}, u32[]{:S(2)}, u32[]{:S(2)}) %collective-permute-start.13) | collective-permute-done | bytes 294944 | tf_op jit(solution)/shard_map/ppermute | solution.py:85
  67.3 2.2 %multiply_convert_fusion.2 = (bf16[1152,128]{1,0:T(8,128)(2,1)}, bf16[1152,128]{1,0:T(8,128)(2,1)}, bf16[1152,128]{1,0:T(8,128)(2,1)}) fusion(bf16[1152,128]{1,0:T(8,128)(2,1)S(1)} %collective-permute-done.11, f32[1152]{0:T(1024)S(1)} %multiply_multiply_fusion, bf16[1152,128]{1,0:T(8,128)(2,1)S(1)} %collective-permute-done.12, ...), kind=kLoop, calls=%fused_computation.45 | loop fusion | flops 1327104 | bytes 1774080 | tf_op jit(solution)/shard_map/convert_element_type | solution.py:30
  70.4 1.9 collective-permute-start.6
  72.3 2.1 %fusion.13 = f32[640,384]{1,0:T(8,128)S(1)} fusion(bf16[640,1152]{1,0:T(8,128)(2,1)S(1)} %copy-done.1, bf16[1152,128]{1,0:T(8,128)(2,1)} %get-tuple-element.22, bf16[1152,128]{1,0:T(8,128)(2,1)} %get-tuple-element.21, bf16[1152,128]{1,0:T(8,128)(2,1)} %get-tuple-element.20), kind=kOutput, calls=%fused_computation.32 | convolution fusion | flops 568885248 | bytes 3342336 | tf_op jit(solution)/shard_map/dot_general | solution.py:135
  74.7 1.0 copy.53
  75.7 2.8 %collective-permute-start.14 = (f32[320,3,128]{2,0,1:T(8,128)}, f32[320,3,128]{2,0,1:T(8,128)}, u32[]{:S(2)}, u32[]{:S(2)}) collective-permute-start(f32[320,3,128]{2,0,1:T(8,128)} %copy.53), channel_id=1, source_target_pairs={{0,16},{16,0},{1,17},{17,1},{2,18},{18,2},{3,19},{19,3},{4,20},{20... | collective-permute-start | bytes 1474568 | tf_op jit(solution)/shard_map/ppermute | solution.py:62
  78.8 3.8 %collective-permute-done.6 = f32[160,5,128]{2,0,1:T(8,128)} collective-permute-done((f32[160,5,128]{2,0,1:T(8,128)S(1)}, f32[160,5,128]{2,0,1:T(8,128)}, u32[]{:S(2)}, u32[]{:S(2)}) %collective-permute-start.6) | collective-permute-done | bytes 409632 | tf_op jit(solution)/shard_map/ppermute | solution.py:62
  82.5 1.2 copy.50
  83.9 1.9 collective-permute-start.7
  85.9 3.4 %collective-permute-start.8 = (f32[160,128]{0,1:T(8,128)S(1)}, f32[160,128]{0,1:T(8,128)S(1)}, u32[]{:S(2)}, u32[]{:S(2)}) collective-permute-start(f32[160,128]{0,1:T(8,128)S(1)} %get-tuple-element.15), channel_id=1, source_target_pairs={{0,2},{2,4},{4,6},{6,8},{8,10},{10,12},{12,14},{14,0},{1,3},{3,5},... | collective-permute-start | bytes 245768 | tf_op jit(solution)/shard_map/ppermute | solution.py:154
  89.2 3.0 %collective-permute-start.9 = (f32[160,128]{0,1:T(8,128)S(1)}, f32[160,128]{0,1:T(8,128)S(1)}, u32[]{:S(2)}, u32[]{:S(2)}) collective-permute-start(f32[160,128]{0,1:T(8,128)S(1)} %get-tuple-element.14), channel_id=1, source_target_pairs={{0,12},{2,14},{4,0},{6,2},{8,4},{10,6},{12,8},{14,10},{1,13},{3,15... | collective-permute-start | bytes 245768 | tf_op jit(solution)/shard_map/ppermute | solution.py:154
  92.3 3.1 %collective-permute-start.10 = (f32[160,128]{0,1:T(8,128)S(1)}, f32[160,128]{0,1:T(8,128)S(1)}, u32[]{:S(2)}, u32[]{:S(2)}) collective-permute-start(f32[160,128]{0,1:T(8,128)S(1)} %get-tuple-element.13), channel_id=1, source_target_pairs={{0,4},{2,6},{4,8},{6,10},{8,12},{10,14},{12,0},{14,2},{1,5},{3,7},... | collective-permute-start | bytes 245768 | tf_op jit(solution)/shard_map/ppermute | solution.py:154
  95.4 1.3 copy.54
  96.9 2.2 %collective-permute-start.15 = (f32[160,3,128]{0,2,1:T(8,128)S(1)}, f32[160,3,128]{0,2,1:T(8,128)S(1)}, u32[]{:S(2)}, u32[]{:S(2)}) collective-permute-start(f32[160,3,128]{0,2,1:T(8,128)S(1)} %slice.100), channel_id=1, source_target_pairs={{0,32},{32,0},{1,33},{33,1},{2,34},{34,2},{3,35},{35,3},{4,36},{36... | collective-permute-start | bytes 737288 | tf_op jit(solution)/shard_map/ppermute | solution.py:62
  99.2 7.4 %collective-permute-done.15 = f32[160,3,128]{0,2,1:T(8,128)S(1)} collective-permute-done((f32[160,3,128]{0,2,1:T(8,128)S(1)}, f32[160,3,128]{0,2,1:T(8,128)S(1)}, u32[]{:S(2)}, u32[]{:S(2)}) %collective-permute-start.15) | collective-permute-done | bytes 245792 | tf_op jit(solution)/shard_map/ppermute | solution.py:62
  106.7 5.2 %collective-permute-start.16 = (f32[160,128]{0,1:T(8,128)S(1)}, f32[160,128]{0,1:T(8,128)S(1)}, u32[]{:S(2)}, u32[]{:S(2)}) collective-permute-start(f32[160,128]{0,1:T(8,128)S(1)} %get-tuple-element.19), channel_id=1, source_target_pairs={{0,10},{2,12},{4,14},{6,0},{8,2},{10,4},{12,6},{14,8},{1,11},{3,13... | collective-permute-start | bytes 245768 | tf_op jit(solution)/shard_map/ppermute | solution.py:154
  112.0 3.1 %collective-permute-start.17 = (f32[160,128]{0,1:T(8,128)S(1)}, f32[160,128]{0,1:T(8,128)S(1)}, u32[]{:S(2)}, u32[]{:S(2)}) collective-permute-start(f32[160,128]{0,1:T(8,128)S(1)} %get-tuple-element.18), channel_id=1, source_target_pairs={{0,6},{2,8},{4,10},{6,12},{8,14},{10,0},{12,2},{14,4},{1,7},{3,9},... | collective-permute-start | bytes 245768 | tf_op jit(solution)/shard_map/ppermute | solution.py:154
  115.1 4.8 %collective-permute-start.18 = (f32[160,128]{0,1:T(8,128)S(1)}, f32[160,128]{0,1:T(8,128)S(1)}, u32[]{:S(2)}, u32[]{:S(2)}) collective-permute-start(f32[160,128]{0,1:T(8,128)S(1)} %get-tuple-element.17), channel_id=1, source_target_pairs={{0,8},{2,10},{4,12},{6,14},{8,0},{10,2},{12,4},{14,6},{1,9},{3,11}... | collective-permute-start | bytes 245768 | tf_op jit(solution)/shard_map/ppermute | solution.py:154
  119.9 1.9 collective-permute-done.17
  121.8 7.1 %collective-permute-done.18 = f32[160,128]{0,1:T(8,128)S(1)} collective-permute-done((f32[160,128]{0,1:T(8,128)S(1)}, f32[160,128]{0,1:T(8,128)S(1)}, u32[]{:S(2)}, u32[]{:S(2)}) %collective-permute-start.18) | collective-permute-done | bytes 81952 | tf_op jit(solution)/shard_map/ppermute | solution.py:154
  129.2 0.6 gather_fusion.4
  130.0 32.9 %all_to_all.10 = f32[32,40,128]{2,1,0:T(8,128)S(1)} all-to-all(f32[32,40,128]{2,1,0:T(8,128)S(1)} %broadcast_select_fusion.1), channel_id=1, replica_groups=mesh['z'=8,'xl'=2,'c'=2,'y'=8,'xh'=2] {'z','xl','c'}, dimensions={0} | all-to-all | bytes 1310720 | tf_op jit(solution)/shard_map/all_to_all | solution.py:163
  162.9 1.3 multiply_reduce_fusion
  164.9 0.4 fusion.40
  165.8 0.4 fusion.38
  166.7 0.4 fusion.35
  167.5 0.4 fusion.32
  168.4 0.4 fusion.29
  169.4 16.2 %all_to_all.11 = bf16[8,160,128]{2,1,0:T(8,128)(2,1)S(1)} all-to-all(bf16[8,160,128]{2,1,0:T(8,128)(2,1)S(1)} %broadcast_in_dim.120), channel_id=1, replica_groups=mesh['z'=8,'xl'=2,'c'=2,'y'=8,'xh'=2] {'z'}, dimensions={0} | all-to-all | bytes 655360 | tf_op jit(solution)/shard_map/all_to_all | solution.py:177
  185.6 2.2 %collective-permute-start.19 = (bf16[1280,128]{1,0:T(8,128)(2,1)S(1)}, bf16[1280,128]{1,0:T(8,128)(2,1)S(1)}, u32[]{:S(2)}, u32[]{:S(2)}) collective-permute-start(bf16[1280,128]{1,0:T(8,128)(2,1)S(1)} %bitcast.153), channel_id=1, source_target_pairs={{0,32},{32,0},{1,33},{33,1},{2,34},{34,2},{3,35},{35,3},{4,36},{36... | collective-permute-start | bytes 983048 | tf_op jit(solution)/shard_map/ppermute | solution.py:94
  187.8 7.8 %collective-permute-done.19 = bf16[1280,128]{1,0:T(8,128)(2,1)S(1)} collective-permute-done((bf16[1280,128]{1,0:T(8,128)(2,1)S(1)}, bf16[1280,128]{1,0:T(8,128)(2,1)S(1)}, u32[]{:S(2)}, u32[]{:S(2)}) %collective-permute-start.19) | collective-permute-done | bytes 327712 | tf_op jit(solution)/shard_map/ppermute | solution.py:94
  195.6 3.9 %collective-permute-start.20 = (bf16[2560,128]{1,0:T(8,128)(2,1)S(1)}, bf16[2560,128]{1,0:T(8,128)(2,1)S(1)}, u32[]{:S(2)}, u32[]{:S(2)}) collective-permute-start(bf16[2560,128]{1,0:T(8,128)(2,1)S(1)} %pad_maximum_fusion.1), channel_id=1, source_target_pairs={{0,16},{16,0},{1,17},{17,1},{2,18},{18,2},{3,19},{19,3},{4,20},{20... | collective-permute-start | bytes 1966088 | tf_op jit(solution)/shard_map/ppermute | solution.py:185
  199.6 0.7 gather_fusion
  200.3 1.0 collective-permute-done.20
  201.2 0.6 fusion.19
  201.9 0.6 add_convert_fusion
  202.4 1.6 copy.58
  (85 shorter events, 6.3 us)
Async XLA Ops:
  0.6 20.1 %collective-permute-start.1 = (bf16[1152,128]{1,0:T(8,128)(2,1)}, bf16[1152,128]{1,0:T(8,128)(2,1)S(1)}, u32[]{:S(2)}, u32[]{:S(2)}) collective-permute-start(bf16[1152,128]{1,0:T(8,128)(2,1)} %param.9), channel_id=1, source_target_pairs={{0,2},{2,4},{4,6},{6,8},{8,10},{10,12},{12,14},{14,0},{1,3},{3,5},... | collective-permute-start | bytes 884744 | tf_op jit(solution)/shard_map/ppermute | solution.py:85
  4.7 19.0 %collective-permute-start.2 = (bf16[1152,128]{1,0:T(8,128)(2,1)}, bf16[1152,128]{1,0:T(8,128)(2,1)S(1)}, u32[]{:S(2)}, u32[]{:S(2)}) collective-permute-start(bf16[1152,128]{1,0:T(8,128)(2,1)} %param.9), channel_id=1, source_target_pairs={{0,14},{2,0},{4,2},{6,4},{8,6},{10,8},{12,10},{14,12},{1,15},{3,1}... | collective-permute-start | bytes 884744 | tf_op jit(solution)/shard_map/ppermute | solution.py:88
  8.5 32.5 %collective-permute-start = (bf16[320,1152]{1,0:T(8,128)(2,1)}, bf16[320,1152]{1,0:T(8,128)(2,1)S(1)}, u32[]{:S(2)}, u32[]{:S(2)}) collective-permute-start(bf16[320,1152]{1,0:T(8,128)(2,1)} %param.8), channel_id=1, source_target_pairs={{0,1},{1,0},{2,3},{3,2},{4,5},{5,4},{6,7},{7,6},{8,9},{9,8},{10,11... | collective-permute-start | bytes 2211848 | tf_op jit(solution)/shard_map/ppermute | solution.py:94
  19.5 21.5 %copy-start.2 = (bf16[320,1152]{1,0:T(8,128)(2,1)S(1)}, bf16[320,1152]{1,0:T(8,128)(2,1)}, u32[]{:S(2)}) copy-start(bf16[320,1152]{1,0:T(8,128)(2,1)} %param.8) | copy-start | bytes 2211844
  20.2 9.0 %copy-start.6 = (s32[32]{0:T(128)}, s32[32]{0:T(128)S(1)}, u32[]{:S(2)}) copy-start(s32[32]{0:T(128)S(1)} %gather_fusion.2) | copy-start | bytes 388
  20.8 9.0 %collective-permute-start.3 = (bf16[1152,128]{1,0:T(8,128)(2,1)S(1)}, bf16[1152,128]{1,0:T(8,128)(2,1)}, u32[]{:S(2)}, u32[]{:S(2)}) collective-permute-start(bf16[1152,128]{1,0:T(8,128)(2,1)S(1)} %collective-permute-done.1), channel_id=1, source_target_pairs={{0,2},{2,4},{4,6},{6,8},{8,10},{10,12},{12,14},{14,0},{1,3},{3,5},... | collective-permute-start | bytes 884744 | tf_op jit(solution)/shard_map/ppermute | solution.py:85
  23.7 8.2 %collective-permute-start.4 = (bf16[1152,128]{1,0:T(8,128)(2,1)S(1)}, bf16[1152,128]{1,0:T(8,128)(2,1)}, u32[]{:S(2)}, u32[]{:S(2)}) collective-permute-start(bf16[1152,128]{1,0:T(8,128)(2,1)S(1)} %collective-permute-done.2), channel_id=1, source_target_pairs={{0,14},{2,0},{4,2},{6,4},{8,6},{10,8},{12,10},{14,12},{1,15},{3,1}... | collective-permute-start | bytes 884744 | tf_op jit(solution)/shard_map/ppermute | solution.py:88
  29.7 25.8 %collective-permute-start.11 = (bf16[1152,128]{1,0:T(8,128)(2,1)}, bf16[1152,128]{1,0:T(8,128)(2,1)S(1)}, u32[]{:S(2)}, u32[]{:S(2)}) collective-permute-start(bf16[1152,128]{1,0:T(8,128)(2,1)} %collective-permute-done.3), channel_id=1, source_target_pairs={{0,2},{2,4},{4,6},{6,8},{8,10},{10,12},{12,14},{14,0},{1,3},{3,5},... | collective-permute-start | bytes 884744 | tf_op jit(solution)/shard_map/ppermute | solution.py:85
  31.9 25.9 %collective-permute-start.12 = (bf16[1152,128]{1,0:T(8,128)(2,1)}, bf16[1152,128]{1,0:T(8,128)(2,1)S(1)}, u32[]{:S(2)}, u32[]{:S(2)}) collective-permute-start(bf16[1152,128]{1,0:T(8,128)(2,1)} %collective-permute-done.4), channel_id=1, source_target_pairs={{0,14},{2,0},{4,2},{6,4},{8,6},{10,8},{12,10},{14,12},{1,15},{3,1}... | collective-permute-start | bytes 884744 | tf_op jit(solution)/shard_map/ppermute | solution.py:88
  44.1 1.4 copy-start.4
  45.5 1.4 copy-start
  47.0 10.4 %copy-start.5 = (s32[32]{0:T(128)S(1)}, s32[32]{0:T(128)}, u32[]{:S(2)}) copy-start(s32[32]{0:T(128)} %fusion.86) | copy-start | bytes 388
  47.0 10.5 %copy-start.7 = (s32[32]{0:T(128)S(1)}, s32[32]{0:T(128)}, u32[]{:S(2)}) copy-start(s32[32]{0:T(128)} %copy-done.6) | copy-start | bytes 388
  48.6 20.9 %collective-permute-start.5 = (f32[320,5,128]{2,0,1:T(8,128)}, f32[320,5,128]{2,0,1:T(8,128)S(1)}, u32[]{:S(2)}, u32[]{:S(2)}) collective-permute-start(f32[320,5,128]{2,0,1:T(8,128)} %copy.47), channel_id=1, source_target_pairs={{0,16},{16,0},{1,17},{17,1},{2,18},{18,2},{3,19},{19,3},{4,20},{20... | collective-permute-start | bytes 2457608 | tf_op jit(solution)/shard_map/ppermute | solution.py:62
  55.5 11.8 %collective-permute-start.13 = (bf16[1152,128]{1,0:T(8,128)(2,1)S(1)}, bf16[1152,128]{1,0:T(8,128)(2,1)}, u32[]{:S(2)}, u32[]{:S(2)}) collective-permute-start(bf16[1152,128]{1,0:T(8,128)(2,1)S(1)} %collective-permute-done.11), channel_id=1, source_target_pairs={{0,2},{2,4},{4,6},{6,8},{8,10},{10,12},{12,14},{14,0},{1,3},{3,5},... | collective-permute-start | bytes 884744 | tf_op jit(solution)/shard_map/ppermute | solution.py:85
  69.9 2.4 %copy-start.1 = (bf16[640,1152]{1,0:T(8,128)(2,1)S(1)}, bf16[640,1152]{1,0:T(8,128)(2,1)}, u32[]{:S(2)}) copy-start(bf16[640,1152]{1,0:T(8,128)(2,1)} %copy-done) | copy-start | bytes 4423684
  70.4 12.2 %collective-permute-start.6 = (f32[160,5,128]{2,0,1:T(8,128)S(1)}, f32[160,5,128]{2,0,1:T(8,128)}, u32[]{:S(2)}, u32[]{:S(2)}) collective-permute-start(f32[160,5,128]{2,0,1:T(8,128)S(1)} %copy.49), channel_id=1, source_target_pairs={{0,32},{32,0},{1,33},{33,1},{2,34},{34,2},{3,35},{35,3},{4,36},{36... | collective-permute-start | bytes 1228808 | tf_op jit(solution)/shard_map/ppermute | solution.py:62
  75.7 19.7 %collective-permute-start.14 = (f32[320,3,128]{2,0,1:T(8,128)}, f32[320,3,128]{2,0,1:T(8,128)}, u32[]{:S(2)}, u32[]{:S(2)}) collective-permute-start(f32[320,3,128]{2,0,1:T(8,128)} %copy.53), channel_id=1, source_target_pairs={{0,16},{16,0},{1,17},{17,1},{2,18},{18,2},{3,19},{19,3},{4,20},{20... | collective-permute-start | bytes 1474568 | tf_op jit(solution)/shard_map/ppermute | solution.py:62
  83.9 15.2 %collective-permute-start.7 = (f32[160,128]{0,1:T(8,128)S(1)}, f32[160,128]{0,1:T(8,128)S(1)}, u32[]{:S(2)}, u32[]{:S(2)}) collective-permute-start(f32[160,128]{0,1:T(8,128)S(1)} %get-tuple-element.16), channel_id=1, source_target_pairs={{0,14},{2,0},{4,2},{6,4},{8,6},{10,8},{12,10},{14,12},{1,15},{3,1}... | collective-permute-start | bytes 245768 | tf_op jit(solution)/shard_map/ppermute | solution.py:154
  85.9 13.3 %collective-permute-start.8 = (f32[160,128]{0,1:T(8,128)S(1)}, f32[160,128]{0,1:T(8,128)S(1)}, u32[]{:S(2)}, u32[]{:S(2)}) collective-permute-start(f32[160,128]{0,1:T(8,128)S(1)} %get-tuple-element.15), channel_id=1, source_target_pairs={{0,2},{2,4},{4,6},{6,8},{8,10},{10,12},{12,14},{14,0},{1,3},{3,5},... | collective-permute-start | bytes 245768 | tf_op jit(solution)/shard_map/ppermute | solution.py:154
  89.2 10.0 %collective-permute-start.9 = (f32[160,128]{0,1:T(8,128)S(1)}, f32[160,128]{0,1:T(8,128)S(1)}, u32[]{:S(2)}, u32[]{:S(2)}) collective-permute-start(f32[160,128]{0,1:T(8,128)S(1)} %get-tuple-element.14), channel_id=1, source_target_pairs={{0,12},{2,14},{4,0},{6,2},{8,4},{10,6},{12,8},{14,10},{1,13},{3,15... | collective-permute-start | bytes 245768 | tf_op jit(solution)/shard_map/ppermute | solution.py:154
  92.3 19.7 %collective-permute-start.10 = (f32[160,128]{0,1:T(8,128)S(1)}, f32[160,128]{0,1:T(8,128)S(1)}, u32[]{:S(2)}, u32[]{:S(2)}) collective-permute-start(f32[160,128]{0,1:T(8,128)S(1)} %get-tuple-element.13), channel_id=1, source_target_pairs={{0,4},{2,6},{4,8},{6,10},{8,12},{10,14},{12,0},{14,2},{1,5},{3,7},... | collective-permute-start | bytes 245768 | tf_op jit(solution)/shard_map/ppermute | solution.py:154
  96.9 9.7 %collective-permute-start.15 = (f32[160,3,128]{0,2,1:T(8,128)S(1)}, f32[160,3,128]{0,2,1:T(8,128)S(1)}, u32[]{:S(2)}, u32[]{:S(2)}) collective-permute-start(f32[160,3,128]{0,2,1:T(8,128)S(1)} %slice.100), channel_id=1, source_target_pairs={{0,32},{32,0},{1,33},{33,1},{2,34},{34,2},{3,35},{35,3},{4,36},{36... | collective-permute-start | bytes 737288 | tf_op jit(solution)/shard_map/ppermute | solution.py:62
  106.7 13.2 %collective-permute-start.16 = (f32[160,128]{0,1:T(8,128)S(1)}, f32[160,128]{0,1:T(8,128)S(1)}, u32[]{:S(2)}, u32[]{:S(2)}) collective-permute-start(f32[160,128]{0,1:T(8,128)S(1)} %get-tuple-element.19), channel_id=1, source_target_pairs={{0,10},{2,12},{4,14},{6,0},{8,2},{10,4},{12,6},{14,8},{1,11},{3,13... | collective-permute-start | bytes 245768 | tf_op jit(solution)/shard_map/ppermute | solution.py:154
  112.0 9.8 %collective-permute-start.17 = (f32[160,128]{0,1:T(8,128)S(1)}, f32[160,128]{0,1:T(8,128)S(1)}, u32[]{:S(2)}, u32[]{:S(2)}) collective-permute-start(f32[160,128]{0,1:T(8,128)S(1)} %get-tuple-element.18), channel_id=1, source_target_pairs={{0,6},{2,8},{4,10},{6,12},{8,14},{10,0},{12,2},{14,4},{1,7},{3,9},... | collective-permute-start | bytes 245768 | tf_op jit(solution)/shard_map/ppermute | solution.py:154
  115.1 13.8 %collective-permute-start.18 = (f32[160,128]{0,1:T(8,128)S(1)}, f32[160,128]{0,1:T(8,128)S(1)}, u32[]{:S(2)}, u32[]{:S(2)}) collective-permute-start(f32[160,128]{0,1:T(8,128)S(1)} %get-tuple-element.17), channel_id=1, source_target_pairs={{0,8},{2,10},{4,12},{6,14},{8,0},{10,2},{12,4},{14,6},{1,9},{3,11}... | collective-permute-start | bytes 245768 | tf_op jit(solution)/shard_map/ppermute | solution.py:154
  129.8 33.1 %copy-start.3 = (f32[160,128]{1,0:T(8,128)S(1)}, f32[160,128]{1,0:T(8,128)}, u32[]{:S(2)}) copy-start(f32[160,128]{1,0:T(8,128)} %param.14) | copy-start | bytes 245764
  168.4 31.1 %copy-start.8 = (s32[1,32]{1,0:T(1,128)S(1)}, s32[1,32]{1,0:T(1,128)}, u32[]{:S(2)}) copy-start(s32[1,32]{1,0:T(1,128)} %param.13) | copy-start | bytes 388
  185.6 10.0 %collective-permute-start.19 = (bf16[1280,128]{1,0:T(8,128)(2,1)S(1)}, bf16[1280,128]{1,0:T(8,128)(2,1)S(1)}, u32[]{:S(2)}, u32[]{:S(2)}) collective-permute-start(bf16[1280,128]{1,0:T(8,128)(2,1)S(1)} %bitcast.153), channel_id=1, source_target_pairs={{0,32},{32,0},{1,33},{33,1},{2,34},{34,2},{3,35},{35,3},{4,36},{36... | collective-permute-start | bytes 983048 | tf_op jit(solution)/shard_map/ppermute | solution.py:94
  195.6 5.7 %collective-permute-start.20 = (bf16[2560,128]{1,0:T(8,128)(2,1)S(1)}, bf16[2560,128]{1,0:T(8,128)(2,1)S(1)}, u32[]{:S(2)}, u32[]{:S(2)}) collective-permute-start(bf16[2560,128]{1,0:T(8,128)(2,1)S(1)} %pad_maximum_fusion.1), channel_id=1, source_target_pairs={{0,16},{16,0},{1,17},{17,1},{2,18},{18,2},{3,19},{19,3},{4,20},{20... | collective-permute-start | bytes 1966088 | tf_op jit(solution)/shard_map/ppermute | solution.py:185

commit v16 on v14

--- a/solution.py
+++ b/solution.py
@@ -116,7 +116,7 @@
     quarter_rows = block_rows // 4
     pair_rows = pair_gather(features, "xh")
     y = lax.axis_index("y")
-    ring_pieces = [weigh(piece, factor) for piece in ring_gather(cotangents, "y")]
+    ring_pieces = ring_gather(weigh(cotangents, factor), "y")
     pair_blocks = 2 * sub_blocks
     group_rows = pair_blocks * quarter_rows
     position = jnp.arange(2 * feature_rows, dtype=jnp.int32)

time: 181 us -> 194 us (1.072)
  waiting for transfers between devices: 43.2 us -> 58.2 us
  other arithmetic: 9.6 us -> 6.84 us
  starting transfers between devices: 58.5 us -> 56 us
    ppermute x4, waiting for transfers between devices: 1.88 us -> 14.8 us  [ring_gather(): from_left = lax.ppermute(from_left, axis, to_right)]
    ppermute x4, starting transfers between devices: 18.8 us -> 15.6 us  [pair_sum_scatter(): return blocks[:half] + lax.ppermute(blocks[half:], axis, SWAP)]
  transfers between devices with their start and end apart: 15 -> 15, of which waited for: 6 -> 10; matrix products, arithmetic and copies ran while one was open for 8% -> 3% of each run, Pallas kernels for 0% -> 0%
where the time goes in v16:
time: 194 us; the launch traced here: 193 us
  waiting for transfers between devices  58.2 us (30%)
  starting transfers between devices  56 us (29%)
  blocking collectives  47 us (24%)
  local copies, waits for them, and re-layouts  14 us (7%)
  matrix products  8.98 us (5%)
  other arithmetic  6.84 us (4%)
    all_to_all x1, blocking collectives, shards(): lax.all_to_all(in_owner_order, DP, split_axis=0, concat_axis=0, tiled=True)  31.2 us
    all_to_all x1, waiting for transfers between devices, shards(): lax.all_to_all(kept, 'y', split_axis=1, concat_axis=0, tiled=True)  20.6 us
    all_to_all x1, blocking collectives, shards(): lax.all_to_all(jnp.broadcast_to(own_update[None], (z_count,) + own_update...  15.8 us
    ppermute x4, starting transfers between devices, pair_sum_scatter(): return blocks[:half] + lax.ppermute(blocks[half:], axis, SWAP)  15.6 us
    ppermute x4, waiting for transfers between devices, ring_gather(): from_left = lax.ppermute(from_left, axis, to_right)  14.8 us
    ppermute x3, starting transfers between devices, ring_gather(): from_right = lax.ppermute(from_right, axis, to_left)  12.9 us
    ppermute x4, waiting for transfers between devices, pair_sum_scatter(): return blocks[:half] + lax.ppermute(blocks[half:], axis, SWAP)  12.4 us
    ppermute x4, starting transfers between devices, ring_gather(): from_left = lax.ppermute(from_left, axis, to_right)  9.76 us
  transfers between devices with their start and end apart: 15, of which 10 were waited for; matrix products, arithmetic and copies ran while one was open for 3% of the time, Pallas kernels for 0%

profile of v16, /device:TPU:1, one launch (start us, length us, event | category | flops | bytes accessed | tf_op | source)
XLA Modules:
  0.0 193.0 jit_solution(3550195926320980013)
XLA Ops:
  0.6 0.8 select_reduce_fusion
  1.4 0.7 multiply_multiply_fusion
  2.1 2.0 %constant_dynamic-update-slice_fusion.4 = (bf16[1152,640]{1,0:T(8,128)(2,1)}, bf16[1152,128]{1,0:T(8,128)(2,1)S(1)}) fusion(f32[1152]{0:T(1024)S(1)} %multiply_multiply_fusion, bf16[1152,128]{1,0:T(8,128)(2,1)} %param.8), kind=kLoop, calls=%fused_computation.75 | loop fusion | flops 442367 | bytes 889344
  4.1 4.0 %collective-permute-start.1 = (bf16[1152,128]{1,0:T(8,128)(2,1)S(1)}, bf16[1152,128]{1,0:T(8,128)(2,1)S(1)}, u32[]{:S(2)}, u32[]{:S(2)}) collective-permute-start(bf16[1152,128]{1,0:T(8,128)(2,1)S(1)} %get-tuple-element.10), channel_id=1, source_target_pairs={{0,2},{2,4},{4,6},{6,8},{8,10},{10,12},{12,14},{14,0},{1,3},{3,5},... | collective-permute-start | bytes 884744 | tf_op jit(solution)/shard_map/ppermute | solution.py:85
  8.2 3.8 %collective-permute-start.2 = (bf16[1152,128]{1,0:T(8,128)(2,1)S(1)}, bf16[1152,128]{1,0:T(8,128)(2,1)S(1)}, u32[]{:S(2)}, u32[]{:S(2)}) collective-permute-start(bf16[1152,128]{1,0:T(8,128)(2,1)S(1)} %get-tuple-element.10), channel_id=1, source_target_pairs={{0,14},{2,0},{4,2},{6,4},{8,6},{10,8},{12,10},{14,12},{1,15},{3,1}... | collective-permute-start | bytes 884744 | tf_op jit(solution)/shard_map/ppermute | solution.py:88
  12.0 4.7 %collective-permute-start = (bf16[320,1152]{1,0:T(8,128)(2,1)}, bf16[320,1152]{1,0:T(8,128)(2,1)S(1)}, u32[]{:S(2)}, u32[]{:S(2)}) collective-permute-start(bf16[320,1152]{1,0:T(8,128)(2,1)} %param.7), channel_id=1, source_target_pairs={{0,1},{1,0},{2,3},{3,2},{4,5},{5,4},{6,7},{7,6},{8,9},{9,8},{10,11... | collective-permute-start | bytes 2211848 | tf_op jit(solution)/shard_map/ppermute | solution.py:94
  16.8 1.9 collective-permute-start.3
  18.7 0.8 constant_dynamic-update-slice_fusion.3
  19.5 4.6 %collective-permute-start.4 = (bf16[1152,128]{1,0:T(8,128)(2,1)S(1)}, bf16[1152,128]{1,0:T(8,128)(2,1)S(1)}, u32[]{:S(2)}, u32[]{:S(2)}) collective-permute-start(bf16[1152,128]{1,0:T(8,128)(2,1)S(1)} %collective-permute-done.2), channel_id=1, source_target_pairs={{0,14},{2,0},{4,2},{6,4},{8,6},{10,8},{12,10},{14,12},{1,15},{3,1}... | collective-permute-start | bytes 884744 | tf_op jit(solution)/shard_map/ppermute | solution.py:88
  24.1 0.8 constant_dynamic-update-slice_fusion.2
  24.8 0.9 collective-permute-done.3
  25.8 0.8 constant_dynamic-update-slice_fusion.1
  26.6 1.2 collective-permute-done.4
  27.7 0.8 constant_dynamic-update-slice_fusion
  28.6 1.1 collective-permute-done
  29.9 3.0 %gather_fusion.1 = bf16[640,1152]{1,0:T(8,128)(2,1)S(1)} fusion(bf16[640,1152]{1,0:T(8,128)(2,1)S(1)} %pad_maximum_fusion, s32[1024]{0:T(1024)S(1)} %pad_clamp_fusion.2), kind=kCustom, calls=%fused_computation.1 | custom fusion | bytes 2951680 | tf_op jit(solution)/shard_map/jit(_take)/gather | solution.py:132
  32.9 0.2 broadcast_select_fusion
  33.2 1.1 copy-done.6
  34.3 1.4 fusion.85
  35.8 0.3 copy.21
  36.1 0.3 copy.22
  36.5 6.7 %collective-permute-start.5 = (f32[320,5,128]{2,0,1:T(8,128)S(1)}, f32[320,5,128]{2,0,1:T(8,128)S(1)}, u32[]{:S(2)}, u32[]{:S(2)}) collective-permute-start(f32[320,5,128]{2,0,1:T(8,128)S(1)} %copy.22), channel_id=1, source_target_pairs={{0,16},{16,0},{1,17},{17,1},{2,18},{18,2},{3,19},{19,3},{4,20},{20... | collective-permute-start | bytes 2457608 | tf_op jit(solution)/shard_map/ppermute | solution.py:62
  43.1 1.9 collective-permute-start.7
  45.1 4.6 %collective-permute-start.8 = (bf16[1152,128]{1,0:T(8,128)(2,1)}, bf16[1152,128]{1,0:T(8,128)(2,1)}, u32[]{:S(2)}, u32[]{:S(2)}) collective-permute-start(bf16[1152,128]{1,0:T(8,128)(2,1)} %copy-done.3), channel_id=1, source_target_pairs={{0,14},{2,0},{4,2},{6,4},{8,6},{10,8},{12,10},{14,12},{1,15},{3,1}... | collective-permute-start | bytes 884744 | tf_op jit(solution)/shard_map/ppermute | solution.py:88
  49.6 5.5 %collective-permute-done.7 = bf16[1152,128]{1,0:T(8,128)(2,1)} collective-permute-done((bf16[1152,128]{1,0:T(8,128)(2,1)}, bf16[1152,128]{1,0:T(8,128)(2,1)}, u32[]{:S(2)}, u32[]{:S(2)}) %collective-permute-start.7) | collective-permute-done | bytes 294944 | tf_op jit(solution)/shard_map/ppermute | solution.py:85
  55.1 1.9 collective-permute-start.9
  57.0 0.3 copy.20
  57.3 0.3 copy.23
  57.8 8.4 %collective-permute-done.9 = bf16[1152,128]{1,0:T(8,128)(2,1)} collective-permute-done((bf16[1152,128]{1,0:T(8,128)(2,1)}, bf16[1152,128]{1,0:T(8,128)(2,1)}, u32[]{:S(2)}, u32[]{:S(2)}) %collective-permute-start.9) | collective-permute-done | bytes 294944 | tf_op jit(solution)/shard_map/ppermute | solution.py:85
  66.2 2.1 %fusion.13 = f32[640,384]{1,0:T(8,128)S(1)} fusion(bf16[640,1152]{1,0:T(8,128)(2,1)S(1)} %copy-done.1, bf16[1152,128]{1,0:T(8,128)(2,1)} %collective-permute-done.9, bf16[1152,128]{1,0:T(8,128)(2,1)} %collective-permute-done.8, bf16[1152,128]{1,0:T(8,128)(2,1)} %collective-permute-done.7), kind=kOutput, calls=%fused_computation.30 | convolution fusion | flops 568885248 | bytes 3342336 | tf_op jit(solution)/shard_map/dot_general | solution.py:135
  68.4 0.2 copy.25
  68.8 3.6 %collective-permute-start.10 = (f32[320,3,128]{2,0,1:T(8,128)S(1)}, f32[320,3,128]{2,0,1:T(8,128)S(1)}, u32[]{:S(2)}, u32[]{:S(2)}) collective-permute-start(f32[320,3,128]{2,0,1:T(8,128)S(1)} %copy.26), channel_id=1, source_target_pairs={{0,16},{16,0},{1,17},{17,1},{2,18},{18,2},{3,19},{19,3},{4,20},{20... | collective-permute-start | bytes 1474568 | tf_op jit(solution)/shard_map/ppermute | solution.py:62
  72.5 0.8 slice.41
  73.3 3.1 %collective-permute-start.6 = (f32[160,5,128]{2,0,1:T(8,128)}, f32[160,5,128]{2,0,1:T(8,128)S(1)}, u32[]{:S(2)}, u32[]{:S(2)}) collective-permute-start(f32[160,5,128]{2,0,1:T(8,128)} %slice.41), channel_id=1, source_target_pairs={{0,32},{32,0},{1,33},{33,1},{2,34},{34,2},{3,35},{35,3},{4,36},{36... | collective-permute-start | bytes 1228808 | tf_op jit(solution)/shard_map/ppermute | solution.py:62
  76.4 0.2 copy.24
  77.0 2.2 %collective-permute-start.11 = (f32[160,3,128]{2,0,1:T(8,128)S(1)}, f32[160,3,128]{2,0,1:T(8,128)S(1)}, u32[]{:S(2)}, u32[]{:S(2)}) collective-permute-start(f32[160,3,128]{2,0,1:T(8,128)S(1)} %slice.61), channel_id=1, source_target_pairs={{0,32},{32,0},{1,33},{33,1},{2,34},{34,2},{3,35},{35,3},{4,36},{36... | collective-permute-start | bytes 737288 | tf_op jit(solution)/shard_map/ppermute | solution.py:62
  79.1 7.2 %collective-permute-done.6 = f32[160,5,128]{2,0,1:T(8,128)S(1)} collective-permute-done((f32[160,5,128]{2,0,1:T(8,128)}, f32[160,5,128]{2,0,1:T(8,128)S(1)}, u32[]{:S(2)}, u32[]{:S(2)}) %collective-permute-start.6) | collective-permute-done | bytes 409632 | tf_op jit(solution)/shard_map/ppermute | solution.py:62
  86.4 5.2 %collective-permute-done.11 = f32[160,3,128]{2,0,1:T(8,128)S(1)} collective-permute-done((f32[160,3,128]{2,0,1:T(8,128)S(1)}, f32[160,3,128]{2,0,1:T(8,128)S(1)}, u32[]{:S(2)}, u32[]{:S(2)}) %collective-permute-start.11) | collective-permute-done | bytes 245792 | tf_op jit(solution)/shard_map/ppermute | solution.py:62
  91.7 0.6 gather_fusion.2
  92.3 0.9 select_bitcast_fusion
  93.3 6.3 %all-to-all-start = ((f32[160,8,128]{2,0,1:T(8,128)}), f32[160,8,128]{2,0,1:T(8,128)S(1)}, u32[]{:S(2)}, u32[]{:S(2)}) async-start(f32[160,8,128]{2,0,1:T(8,128)} %select_bitcast_fusion), calls=%async_computation | async-start | bytes 1310720 | tf_op jit(solution)/shard_map/all_to_all | solution.py:155
  99.7 20.6 %all-to-all-done = f32[160,8,128]{2,0,1:T(8,128)S(1)} async-done(((f32[160,8,128]{2,0,1:T(8,128)}), f32[160,8,128]{2,0,1:T(8,128)S(1)}, u32[]{:S(2)}, u32[]{:S(2)}) %all-to-all-start) | async-done | bytes 655392 | tf_op jit(solution)/shard_map/all_to_all | solution.py:155
  120.3 0.6 gather_fusion.3
  121.1 31.2 %all_to_all.25 = f32[32,40,128]{2,1,0:T(8,128)S(1)} all-to-all(f32[32,40,128]{2,1,0:T(8,128)S(1)} %broadcast_select_fusion.1), channel_id=1, replica_groups=mesh['z'=8,'xl'=2,'c'=2,'y'=8,'xh'=2] {'z','xl','c'}, dimensions={0} | all-to-all | bytes 1310720 | tf_op jit(solution)/shard_map/all_to_all | solution.py:159
  152.3 1.3 multiply_reduce_fusion
  154.3 0.4 fusion.34
  154.9 0.2 fusion
  155.2 0.4 fusion.32
  155.8 0.2 fusion.1
  156.0 0.4 fusion.29
  156.7 0.2 fusion.2
  156.9 0.4 fusion.26
  157.6 0.2 fusion.3
  157.8 0.4 fusion.23
  158.5 0.2 fusion.12
  158.7 15.8 %all_to_all.26 = bf16[8,160,128]{2,1,0:T(8,128)(2,1)S(1)} all-to-all(bf16[8,160,128]{2,1,0:T(8,128)(2,1)S(1)} %broadcast_in_dim.118), channel_id=1, replica_groups=mesh['z'=8,'xl'=2,'c'=2,'y'=8,'xh'=2] {'z'}, dimensions={0} | all-to-all | bytes 655360 | tf_op jit(solution)/shard_map/all_to_all | solution.py:173
  174.5 2.5 %collective-permute-start.12 = (bf16[1280,128]{1,0:T(8,128)(2,1)S(1)}, bf16[1280,128]{1,0:T(8,128)(2,1)S(1)}, u32[]{:S(2)}, u32[]{:S(2)}) collective-permute-start(bf16[1280,128]{1,0:T(8,128)(2,1)S(1)} %bitcast.123), channel_id=1, source_target_pairs={{0,32},{32,0},{1,33},{33,1},{2,34},{34,2},{3,35},{35,3},{4,36},{36... | collective-permute-start | bytes 983048 | tf_op jit(solution)/shard_map/ppermute | solution.py:94
  177.0 7.2 %collective-permute-done.12 = bf16[1280,128]{1,0:T(8,128)(2,1)S(1)} collective-permute-done((bf16[1280,128]{1,0:T(8,128)(2,1)S(1)}, bf16[1280,128]{1,0:T(8,128)(2,1)S(1)}, u32[]{:S(2)}, u32[]{:S(2)}) %collective-permute-start.12) | collective-permute-done | bytes 327712 | tf_op jit(solution)/shard_map/ppermute | solution.py:94
  184.2 4.3 %collective-permute-start.13 = (bf16[2560,128]{1,0:T(8,128)(2,1)S(1)}, bf16[2560,128]{1,0:T(8,128)(2,1)S(1)}, u32[]{:S(2)}, u32[]{:S(2)}) collective-permute-start(bf16[2560,128]{1,0:T(8,128)(2,1)S(1)} %pad_maximum_fusion.2), channel_id=1, source_target_pairs={{0,16},{16,0},{1,17},{17,1},{2,18},{18,2},{3,19},{19,3},{4,20},{20... | collective-permute-start | bytes 1966088 | tf_op jit(solution)/shard_map/ppermute | solution.py:181
  188.5 0.7 gather_fusion
  189.2 1.0 collective-permute-done.13
  190.2 0.6 fusion.19
  190.8 0.6 add_convert_fusion
  191.4 1.6 copy.30
  (54 shorter events, 2.7 us)
Async XLA Ops:
  2.1 27.6 %copy-start.2 = (bf16[320,1152]{1,0:T(8,128)(2,1)S(1)}, bf16[320,1152]{1,0:T(8,128)(2,1)}, u32[]{:S(2)}) copy-start(bf16[320,1152]{1,0:T(8,128)(2,1)} %param.7) | copy-start | bytes 2211844
  4.1 12.7 %collective-permute-start.1 = (bf16[1152,128]{1,0:T(8,128)(2,1)S(1)}, bf16[1152,128]{1,0:T(8,128)(2,1)S(1)}, u32[]{:S(2)}, u32[]{:S(2)}) collective-permute-start(bf16[1152,128]{1,0:T(8,128)(2,1)S(1)} %get-tuple-element.10), channel_id=1, source_target_pairs={{0,2},{2,4},{4,6},{6,8},{8,10},{10,12},{12,14},{14,0},{1,3},{3,5},... | collective-permute-start | bytes 884744 | tf_op jit(solution)/shard_map/ppermute | solution.py:85
  8.2 11.4 %collective-permute-start.2 = (bf16[1152,128]{1,0:T(8,128)(2,1)S(1)}, bf16[1152,128]{1,0:T(8,128)(2,1)S(1)}, u32[]{:S(2)}, u32[]{:S(2)}) collective-permute-start(bf16[1152,128]{1,0:T(8,128)(2,1)S(1)} %get-tuple-element.10), channel_id=1, source_target_pairs={{0,14},{2,0},{4,2},{6,4},{8,6},{10,8},{12,10},{14,12},{1,15},{3,1}... | collective-permute-start | bytes 884744 | tf_op jit(solution)/shard_map/ppermute | solution.py:88
  12.0 17.8 %collective-permute-start = (bf16[320,1152]{1,0:T(8,128)(2,1)}, bf16[320,1152]{1,0:T(8,128)(2,1)S(1)}, u32[]{:S(2)}, u32[]{:S(2)}) collective-permute-start(bf16[320,1152]{1,0:T(8,128)(2,1)} %param.7), channel_id=1, source_target_pairs={{0,1},{1,0},{2,3},{3,2},{4,5},{5,4},{6,7},{7,6},{8,9},{9,8},{10,11... | collective-permute-start | bytes 2211848 | tf_op jit(solution)/shard_map/ppermute | solution.py:94
  16.8 9.0 %collective-permute-start.3 = (bf16[1152,128]{1,0:T(8,128)(2,1)S(1)}, bf16[1152,128]{1,0:T(8,128)(2,1)S(1)}, u32[]{:S(2)}, u32[]{:S(2)}) collective-permute-start(bf16[1152,128]{1,0:T(8,128)(2,1)S(1)} %collective-permute-done.1), channel_id=1, source_target_pairs={{0,2},{2,4},{4,6},{6,8},{8,10},{10,12},{12,14},{14,0},{1,3},{3,5},... | collective-permute-start | bytes 884744 | tf_op jit(solution)/shard_map/ppermute | solution.py:85
  19.5 8.2 %collective-permute-start.4 = (bf16[1152,128]{1,0:T(8,128)(2,1)S(1)}, bf16[1152,128]{1,0:T(8,128)(2,1)S(1)}, u32[]{:S(2)}, u32[]{:S(2)}) collective-permute-start(bf16[1152,128]{1,0:T(8,128)(2,1)S(1)} %collective-permute-done.2), channel_id=1, source_target_pairs={{0,14},{2,0},{4,2},{6,4},{8,6},{10,8},{12,10},{14,12},{1,15},{3,1}... | collective-permute-start | bytes 884744 | tf_op jit(solution)/shard_map/ppermute | solution.py:88
  25.8 2.8 %copy-start.4 = (bf16[1152,128]{1,0:T(8,128)(2,1)}, bf16[1152,128]{1,0:T(8,128)(2,1)S(1)}, u32[]{:S(2)}) copy-start(bf16[1152,128]{1,0:T(8,128)(2,1)S(1)} %collective-permute-done.3) | copy-start | bytes 884740
  27.7 0.9 copy-start.3
  32.9 1.4 copy-start.6
  34.3 1.4 copy-start
  36.5 21.2 %collective-permute-start.5 = (f32[320,5,128]{2,0,1:T(8,128)S(1)}, f32[320,5,128]{2,0,1:T(8,128)S(1)}, u32[]{:S(2)}, u32[]{:S(2)}) collective-permute-start(f32[320,5,128]{2,0,1:T(8,128)S(1)} %copy.22), channel_id=1, source_target_pairs={{0,16},{16,0},{1,17},{17,1},{2,18},{18,2},{3,19},{19,3},{4,20},{20... | collective-permute-start | bytes 2457608 | tf_op jit(solution)/shard_map/ppermute | solution.py:62
  43.1 12.0 %collective-permute-start.7 = (bf16[1152,128]{1,0:T(8,128)(2,1)}, bf16[1152,128]{1,0:T(8,128)(2,1)}, u32[]{:S(2)}, u32[]{:S(2)}) collective-permute-start(bf16[1152,128]{1,0:T(8,128)(2,1)} %copy-done.4), channel_id=1, source_target_pairs={{0,2},{2,4},{4,6},{6,8},{8,10},{10,12},{12,14},{14,0},{1,3},{3,5},... | collective-permute-start | bytes 884744 | tf_op jit(solution)/shard_map/ppermute | solution.py:85
  45.1 12.7 %collective-permute-start.8 = (bf16[1152,128]{1,0:T(8,128)(2,1)}, bf16[1152,128]{1,0:T(8,128)(2,1)}, u32[]{:S(2)}, u32[]{:S(2)}) collective-permute-start(bf16[1152,128]{1,0:T(8,128)(2,1)} %copy-done.3), channel_id=1, source_target_pairs={{0,14},{2,0},{4,2},{6,4},{8,6},{10,8},{12,10},{14,12},{1,15},{3,1}... | collective-permute-start | bytes 884744 | tf_op jit(solution)/shard_map/ppermute | solution.py:88
  55.1 11.1 %collective-permute-start.9 = (bf16[1152,128]{1,0:T(8,128)(2,1)}, bf16[1152,128]{1,0:T(8,128)(2,1)}, u32[]{:S(2)}, u32[]{:S(2)}) collective-permute-start(bf16[1152,128]{1,0:T(8,128)(2,1)} %collective-permute-done.7), channel_id=1, source_target_pairs={{0,2},{2,4},{4,6},{6,8},{8,10},{10,12},{12,14},{14,0},{1,3},{3,5},... | collective-permute-start | bytes 884744 | tf_op jit(solution)/shard_map/ppermute | solution.py:85
  57.7 8.5 %copy-start.1 = (bf16[640,1152]{1,0:T(8,128)(2,1)S(1)}, bf16[640,1152]{1,0:T(8,128)(2,1)}, u32[]{:S(2)}) copy-start(bf16[640,1152]{1,0:T(8,128)(2,1)} %copy-done) | copy-start | bytes 4423684
  68.8 8.1 %collective-permute-start.10 = (f32[320,3,128]{2,0,1:T(8,128)S(1)}, f32[320,3,128]{2,0,1:T(8,128)S(1)}, u32[]{:S(2)}, u32[]{:S(2)}) collective-permute-start(f32[320,3,128]{2,0,1:T(8,128)S(1)} %copy.26), channel_id=1, source_target_pairs={{0,16},{16,0},{1,17},{17,1},{2,18},{18,2},{3,19},{19,3},{4,20},{20... | collective-permute-start | bytes 1474568 | tf_op jit(solution)/shard_map/ppermute | solution.py:62
  73.3 13.1 %collective-permute-start.6 = (f32[160,5,128]{2,0,1:T(8,128)}, f32[160,5,128]{2,0,1:T(8,128)S(1)}, u32[]{:S(2)}, u32[]{:S(2)}) collective-permute-start(f32[160,5,128]{2,0,1:T(8,128)} %slice.41), channel_id=1, source_target_pairs={{0,32},{32,0},{1,33},{33,1},{2,34},{34,2},{3,35},{35,3},{4,36},{36... | collective-permute-start | bytes 1228808 | tf_op jit(solution)/shard_map/ppermute | solution.py:62
  77.0 14.6 %collective-permute-start.11 = (f32[160,3,128]{2,0,1:T(8,128)S(1)}, f32[160,3,128]{2,0,1:T(8,128)S(1)}, u32[]{:S(2)}, u32[]{:S(2)}) collective-permute-start(f32[160,3,128]{2,0,1:T(8,128)S(1)} %slice.61), channel_id=1, source_target_pairs={{0,32},{32,0},{1,33},{33,1},{2,34},{34,2},{3,35},{35,3},{4,36},{36... | collective-permute-start | bytes 737288 | tf_op jit(solution)/shard_map/ppermute | solution.py:62
  92.3 7.3 %copy-start.7 = (s32[1,32]{1,0:T(1,128)S(1)}, s32[1,32]{1,0:T(1,128)}, u32[]{:S(2)}) copy-start(s32[1,32]{1,0:T(1,128)} %param.12) | copy-start | bytes 388
  93.3 27.1 %all-to-all-start = ((f32[160,8,128]{2,0,1:T(8,128)}), f32[160,8,128]{2,0,1:T(8,128)S(1)}, u32[]{:S(2)}, u32[]{:S(2)}) async-start(f32[160,8,128]{2,0,1:T(8,128)} %select_bitcast_fusion), calls=%async_computation | async-start | bytes 1310720 | tf_op jit(solution)/shard_map/all_to_all | solution.py:155
  120.9 31.4 %copy-start.5 = (f32[160,128]{1,0:T(8,128)S(1)}, f32[160,128]{1,0:T(8,128)}, u32[]{:S(2)}) copy-start(f32[160,128]{1,0:T(8,128)} %param.13) | copy-start | bytes 245764
  174.5 9.6 %collective-permute-start.12 = (bf16[1280,128]{1,0:T(8,128)(2,1)S(1)}, bf16[1280,128]{1,0:T(8,128)(2,1)S(1)}, u32[]{:S(2)}, u32[]{:S(2)}) collective-permute-start(bf16[1280,128]{1,0:T(8,128)(2,1)S(1)} %bitcast.123), channel_id=1, source_target_pairs={{0,32},{32,0},{1,33},{33,1},{2,34},{34,2},{3,35},{35,3},{4,36},{36... | collective-permute-start | bytes 983048 | tf_op jit(solution)/shard_map/ppermute | solution.py:94
  184.2 6.0 %collective-permute-start.13 = (bf16[2560,128]{1,0:T(8,128)(2,1)S(1)}, bf16[2560,128]{1,0:T(8,128)(2,1)S(1)}, u32[]{:S(2)}, u32[]{:S(2)}) collective-permute-start(bf16[2560,128]{1,0:T(8,128)(2,1)S(1)} %pad_maximum_fusion.2), channel_id=1, source_target_pairs={{0,16},{16,0},{1,17},{17,1},{2,18},{18,2},{3,19},{19,3},{4,20},{20... | collective-permute-start | bytes 1966088 | tf_op jit(solution)/shard_map/ppermute | solution.py:181

commit v17 on v13

--- a/solution.py
+++ b/solution.py
@@ -177,15 +177,22 @@
         concat_axis=0,
         tiled=True,
     ).reshape(z_count * block_rows, heads_here * head_width)
-    gathered = pair_gather(gathered, "xl")
-    gathered = pair_gather(gathered, "c")
-    d = jnp.arange(dp_count, dtype=jnp.int32)
-    update_position = (
-        jnp.where(d % 2 == c, 0, half) + jnp.where((d // 2) % 2 == xl, 0, quarter) + d // 4
-    )
-    placed = reorder(
-        gathered.reshape(dp_count, block_rows, heads_here, head_width), update_position[owners]
-    )
+    from_xl = lax.ppermute(gathered, "xl", SWAP)
+    from_c = lax.ppermute(gathered, "c", SWAP)
+    from_both = lax.ppermute(from_xl, "c", SWAP)
+    source = owners[0]
+    part = jnp.where((source // 2) % 2 == xl, 0, 1) + jnp.where(source % 2 == c, 0, 2)
+    slots = jnp.arange(z_count, dtype=jnp.int32)[None, :]
+    block_shape = (z_count, block_rows, heads_here * head_width)
+    placed = sum(
+        jnp.einsum(
+            "bk,krc->brc",
+            ((part[:, None] == index) & (source[:, None] // 4 == slots)).astype(jnp.bfloat16),
+            blocks.reshape(block_shape),
+            preferred_element_type=jnp.float32,
+        )
+        for index, blocks in enumerate((gathered, from_xl, from_c, from_both))
+    ).astype(jnp.bfloat16)
     return (
         placed.reshape(dp_count * block_rows, heads_here * head_width),
         new_momentum.reshape(block_rows, heads_here * head_width),

time: 183 us -> 182 us (level)
  blocking collectives: 46.2 us -> 30.3 us
  waiting for transfers between devices: 43 us -> 55.6 us
  other arithmetic: 13.1 us -> 9.57 us
  starting transfers between devices: 58.5 us -> 61.6 us
  matrix products: 6.66 us -> 8.97 us
    all_to_all x1 -> x0, blocking collectives: 15.9 us -> none  [shards(): lax.all_to_all(jnp.broadcast_to(own_update[None], (z_count,) + own_update...]
    all_to_all x0 -> x1, waiting for transfers between devices: none -> 11.3 us  [shards(): lax.all_to_all(jnp.broadcast_to(own_update[None], (z_count,) + own_update...]
    ppermute x0 -> x3, starting transfers between devices: none -> 10.9 us  [the longest x1 4.74 us: shards(): from_c = lax.ppermute(gathered, 'c', SWAP)]
    ppermute x3 -> x1, waiting for transfers between devices: 8.03 us -> 0.01 us  [pair_gather(): return jnp.concatenate([piece, lax.ppermute(piece, axis, SWAP)], axis=0)]
    ppermute x0 -> x3, waiting for transfers between devices: none -> 7.6 us  [the longest x1 7.49 us: shards(): from_xl = lax.ppermute(gathered, 'xl', SWAP)]
    ppermute x3 -> x1, starting transfers between devices: 11.3 us -> 4.65 us  [pair_gather(): return jnp.concatenate([piece, lax.ppermute(piece, axis, SWAP)], axis=0)]
    ppermute x4, starting transfers between devices: 18.8 us -> 15.3 us  [pair_sum_scatter(): return blocks[:half] + lax.ppermute(blocks[half:], axis, SWAP)]
    all_to_all x0 -> x1, starting transfers between devices: none -> 3.43 us  [shards(): lax.all_to_all(jnp.broadcast_to(own_update[None], (z_count,) + own_update...]
  transfers between devices with their start and end apart: 15 -> 17, of which waited for: 6 -> 8; matrix products, arithmetic and copies ran while one was open for 8% -> 9% of each run, Pallas kernels for 0% -> 0%
where the time goes in v17:
time: 182 us; the launch traced here: 181 us
  starting transfers between devices  61.6 us (34%)
  waiting for transfers between devices  55.6 us (31%)
  blocking collectives  30.3 us (17%)
  local copies, waits for them, and re-layouts  13.2 us (7%)
  other arithmetic  9.57 us (5%)
  matrix products  8.97 us (5%)
  between operations  1.95 us (1%)
    all_to_all x1, blocking collectives, shards(): lax.all_to_all(in_owner_order, DP, split_axis=0, concat_axis=0, tiled=True)  30.3 us
    all_to_all x1, waiting for transfers between devices, shards(): lax.all_to_all(kept, 'y', split_axis=1, concat_axis=0, tiled=True)  20.6 us
    ppermute x3, starting transfers between devices, ring_gather(): from_right = lax.ppermute(from_right, axis, to_left)  15.9 us
    ppermute x4, starting transfers between devices, pair_sum_scatter(): return blocks[:half] + lax.ppermute(blocks[half:], axis, SWAP)  15.3 us
    ppermute x4, waiting for transfers between devices, pair_sum_scatter(): return blocks[:half] + lax.ppermute(blocks[half:], axis, SWAP)  12.4 us
    all_to_all x1, waiting for transfers between devices, shards(): lax.all_to_all(jnp.broadcast_to(own_update[None], (z_count,) + own_update...  11.3 us
    ppermute x4, starting transfers between devices, ring_gather(): from_left = lax.ppermute(from_left, axis, to_right)  7.69 us
    ppermute x1, waiting for transfers between devices, shards(): from_xl = lax.ppermute(gathered, 'xl', SWAP)  7.49 us
  transfers between devices with their start and end apart: 17, of which 8 were waited for; matrix products, arithmetic and copies ran while one was open for 9% of the time, Pallas kernels for 0%

profile of v17, /device:TPU:1, one launch (start us, length us, event | category | flops | bytes accessed | tf_op | source)
XLA Modules:
  0.0 181.3 jit_solution(16779051819339982255)
XLA Ops:
  0.6 5.9 %collective-permute-start.2 = (bf16[1152,128]{1,0:T(8,128)(2,1)}, bf16[1152,128]{1,0:T(8,128)(2,1)S(1)}, u32[]{:S(2)}, u32[]{:S(2)}) collective-permute-start(bf16[1152,128]{1,0:T(8,128)(2,1)} %param.8), channel_id=1, source_target_pairs={{0,14},{2,0},{4,2},{6,4},{8,6},{10,8},{12,10},{14,12},{1,15},{3,1}... | collective-permute-start | bytes 884744 | tf_op jit(solution)/shard_map/ppermute | solution.py:88
  6.6 1.9 %collective-permute-start.1 = (bf16[1152,128]{1,0:T(8,128)(2,1)}, bf16[1152,128]{1,0:T(8,128)(2,1)S(1)}, u32[]{:S(2)}, u32[]{:S(2)}) collective-permute-start(bf16[1152,128]{1,0:T(8,128)(2,1)} %param.8), channel_id=1, source_target_pairs={{0,2},{2,4},{4,6},{6,8},{8,10},{10,12},{12,14},{14,0},{1,3},{3,5},... | collective-permute-start | bytes 884744 | tf_op jit(solution)/shard_map/ppermute | solution.py:85
  8.5 4.7 %collective-permute-start = (bf16[320,1152]{1,0:T(8,128)(2,1)}, bf16[320,1152]{1,0:T(8,128)(2,1)S(1)}, u32[]{:S(2)}, u32[]{:S(2)}) collective-permute-start(bf16[320,1152]{1,0:T(8,128)(2,1)} %param.7), channel_id=1, source_target_pairs={{0,1},{1,0},{2,3},{3,2},{4,5},{5,4},{6,7},{7,6},{8,9},{9,8},{10,11... | collective-permute-start | bytes 2211848 | tf_op jit(solution)/shard_map/ppermute | solution.py:94
  13.3 0.8 select_reduce_fusion
  14.1 0.7 multiply_multiply_fusion
  14.8 1.2 fusion.26
  16.1 4.6 %collective-permute-start.4 = (bf16[1152,128]{1,0:T(8,128)(2,1)S(1)}, bf16[1152,128]{1,0:T(8,128)(2,1)}, u32[]{:S(2)}, u32[]{:S(2)}) collective-permute-start(bf16[1152,128]{1,0:T(8,128)(2,1)S(1)} %collective-permute-done.2), channel_id=1, source_target_pairs={{0,14},{2,0},{4,2},{6,4},{8,6},{10,8},{12,10},{14,12},{1,15},{3,1}... | collective-permute-start | bytes 884744 | tf_op jit(solution)/shard_map/ppermute | solution.py:88
  20.7 1.9 %collective-permute-start.3 = (bf16[1152,128]{1,0:T(8,128)(2,1)S(1)}, bf16[1152,128]{1,0:T(8,128)(2,1)S(1)}, u32[]{:S(2)}, u32[]{:S(2)}) collective-permute-start(bf16[1152,128]{1,0:T(8,128)(2,1)S(1)} %collective-permute-done.1), channel_id=1, source_target_pairs={{0,2},{2,4},{4,6},{6,8},{8,10},{10,12},{12,14},{14,0},{1,3},{3,5},... | collective-permute-start | bytes 884744 | tf_op jit(solution)/shard_map/ppermute | solution.py:85
  22.6 0.3 fusion.27
  22.9 0.3 fusion.28
  23.2 2.3 %collective-permute-done.4 = bf16[1152,128]{1,0:T(8,128)(2,1)} collective-permute-done((bf16[1152,128]{1,0:T(8,128)(2,1)S(1)}, bf16[1152,128]{1,0:T(8,128)(2,1)}, u32[]{:S(2)}, u32[]{:S(2)}) %collective-permute-start.4) | collective-permute-done | bytes 294944 | tf_op jit(solution)/shard_map/ppermute | solution.py:88
  25.5 5.4 %collective-permute-start.8 = (bf16[1152,128]{1,0:T(8,128)(2,1)}, bf16[1152,128]{1,0:T(8,128)(2,1)}, u32[]{:S(2)}, u32[]{:S(2)}) collective-permute-start(bf16[1152,128]{1,0:T(8,128)(2,1)} %collective-permute-done.4), channel_id=1, source_target_pairs={{0,14},{2,0},{4,2},{6,4},{8,6},{10,8},{12,10},{14,12},{1,15},{3,1}... | collective-permute-start | bytes 884744 | tf_op jit(solution)/shard_map/ppermute | solution.py:88
  30.9 1.9 %collective-permute-start.7 = (bf16[1152,128]{1,0:T(8,128)(2,1)S(1)}, bf16[1152,128]{1,0:T(8,128)(2,1)}, u32[]{:S(2)}, u32[]{:S(2)}) collective-permute-start(bf16[1152,128]{1,0:T(8,128)(2,1)S(1)} %collective-permute-done.3), channel_id=1, source_target_pairs={{0,2},{2,4},{4,6},{6,8},{8,10},{10,12},{12,14},{14,0},{1,3},{3,5},... | collective-permute-start | bytes 884744 | tf_op jit(solution)/shard_map/ppermute | solution.py:85
  32.8 0.3 fusion.29
  33.1 1.2 fusion.30
  34.4 1.1 copy-done.4
  35.6 3.0 %gather_fusion = bf16[640,1152]{1,0:T(8,128)(2,1)S(1)} fusion(bf16[640,1152]{1,0:T(8,128)(2,1)S(1)} %pad_maximum_fusion, s32[1024]{0:T(1024)S(1)} %pad_clamp_fusion.2), kind=kCustom, calls=%fused_computation | custom fusion | bytes 2951680 | tf_op jit(solution)/shard_map/jit(_take)/gather | solution.py:132
  38.7 0.2 broadcast_select_fusion
  38.9 1.1 copy-done.5
  40.0 1.4 fusion.106
  41.5 1.9 %collective-permute-start.9 = (bf16[1152,128]{1,0:T(8,128)(2,1)}, bf16[1152,128]{1,0:T(8,128)(2,1)}, u32[]{:S(2)}, u32[]{:S(2)}) collective-permute-start(bf16[1152,128]{1,0:T(8,128)(2,1)} %collective-permute-done.7), channel_id=1, source_target_pairs={{0,2},{2,4},{4,6},{6,8},{8,10},{10,12},{12,14},{14,0},{1,3},{3,5},... | collective-permute-start | bytes 884744 | tf_op jit(solution)/shard_map/ppermute | solution.py:85
  43.5 0.3 copy.36
  43.8 0.3 copy.37
  44.2 4.6 %collective-permute-start.5 = (f32[320,5,128]{2,0,1:T(8,128)S(1)}, f32[320,5,128]{2,0,1:T(8,128)S(1)}, u32[]{:S(2)}, u32[]{:S(2)}) collective-permute-start(f32[320,5,128]{2,0,1:T(8,128)S(1)} %copy.37), channel_id=1, source_target_pairs={{0,16},{16,0},{1,17},{17,1},{2,18},{18,2},{3,19},{19,3},{4,20},{20... | collective-permute-start | bytes 2457608 | tf_op jit(solution)/shard_map/ppermute | solution.py:62
  48.7 0.3 copy.35
  49.1 0.3 copy.38
  49.4 1.4 collective-permute-done.9
  50.8 1.4 multiply_convert_fusion.2
  52.3 1.3 copy-done.1
  53.6 1.0 fusion.13
  54.6 0.2 copy.40
  55.1 5.4 %collective-permute-start.10 = (f32[320,3,128]{2,0,1:T(8,128)S(1)}, f32[320,3,128]{2,0,1:T(8,128)S(1)}, u32[]{:S(2)}, u32[]{:S(2)}) collective-permute-start(f32[320,3,128]{2,0,1:T(8,128)S(1)} %copy.41), channel_id=1, source_target_pairs={{0,16},{16,0},{1,17},{17,1},{2,18},{18,2},{3,19},{19,3},{4,20},{20... | collective-permute-start | bytes 1474568 | tf_op jit(solution)/shard_map/ppermute | solution.py:62
  60.5 0.8 slice.41
  61.3 2.2 %collective-permute-start.6 = (f32[160,5,128]{2,0,1:T(8,128)}, f32[160,5,128]{2,0,1:T(8,128)S(1)}, u32[]{:S(2)}, u32[]{:S(2)}) collective-permute-start(f32[160,5,128]{2,0,1:T(8,128)} %slice.41), channel_id=1, source_target_pairs={{0,32},{32,0},{1,33},{33,1},{2,34},{34,2},{3,35},{35,3},{4,36},{36... | collective-permute-start | bytes 1228808 | tf_op jit(solution)/shard_map/ppermute | solution.py:62
  63.6 0.2 copy.39
  64.1 3.1 %collective-permute-start.11 = (f32[160,3,128]{2,0,1:T(8,128)S(1)}, f32[160,3,128]{2,0,1:T(8,128)S(1)}, u32[]{:S(2)}, u32[]{:S(2)}) collective-permute-start(f32[160,3,128]{2,0,1:T(8,128)S(1)} %slice.59), channel_id=1, source_target_pairs={{0,32},{32,0},{1,33},{33,1},{2,34},{34,2},{3,35},{35,3},{4,36},{36... | collective-permute-start | bytes 737288 | tf_op jit(solution)/shard_map/ppermute | solution.py:62
  67.2 7.2 %collective-permute-done.6 = f32[160,5,128]{2,0,1:T(8,128)S(1)} collective-permute-done((f32[160,5,128]{2,0,1:T(8,128)}, f32[160,5,128]{2,0,1:T(8,128)S(1)}, u32[]{:S(2)}, u32[]{:S(2)}) %collective-permute-start.6) | collective-permute-done | bytes 409632 | tf_op jit(solution)/shard_map/ppermute | solution.py:62
  74.4 5.2 %collective-permute-done.11 = f32[160,3,128]{2,0,1:T(8,128)S(1)} collective-permute-done((f32[160,3,128]{2,0,1:T(8,128)S(1)}, f32[160,3,128]{2,0,1:T(8,128)S(1)}, u32[]{:S(2)}, u32[]{:S(2)}) %collective-permute-start.11) | collective-permute-done | bytes 245792 | tf_op jit(solution)/shard_map/ppermute | solution.py:62
  79.7 0.6 gather_fusion.1
  80.4 0.9 select_bitcast_fusion
  81.3 3.8 %all-to-all-start = ((f32[160,8,128]{2,0,1:T(8,128)}), f32[160,8,128]{2,0,1:T(8,128)S(1)}, u32[]{:S(2)}, u32[]{:S(2)}) async-start(f32[160,8,128]{2,0,1:T(8,128)} %select_bitcast_fusion), calls=%async_computation | async-start | bytes 1310720 | tf_op jit(solution)/shard_map/all_to_all | solution.py:155
  85.3 20.6 %all-to-all-done = f32[160,8,128]{2,0,1:T(8,128)S(1)} async-done(((f32[160,8,128]{2,0,1:T(8,128)}), f32[160,8,128]{2,0,1:T(8,128)S(1)}, u32[]{:S(2)}, u32[]{:S(2)}) %all-to-all-start) | async-done | bytes 655392 | tf_op jit(solution)/shard_map/all_to_all | solution.py:155
  105.9 0.6 gather_fusion.2
  106.6 30.3 %all_to_all.25 = f32[32,40,128]{2,1,0:T(8,128)S(1)} all-to-all(f32[32,40,128]{2,1,0:T(8,128)S(1)} %broadcast_select_fusion.1), channel_id=1, replica_groups=mesh['z'=8,'xl'=2,'c'=2,'y'=8,'xh'=2] {'z','xl','c'}, dimensions={0} | all-to-all | bytes 1310720 | tf_op jit(solution)/shard_map/all_to_all | solution.py:159
  137.0 1.3 multiply_reduce_fusion
  138.9 0.4 fusion.43
  139.8 0.4 fusion.41
  140.5 0.2 fusion.1
  140.7 0.4 fusion.38
  141.6 0.4 fusion.35
  142.4 0.4 fusion.32
  143.1 0.2 fusion.12
  143.3 0.8 broadcast_in_dim.120
  144.1 3.4 %all-to-all-start.2 = ((bf16[8,160,128]{2,1,0:T(8,128)(2,1)}), bf16[8,160,128]{2,1,0:T(8,128)(2,1)S(1)}, u32[]{:S(2)}, u32[]{:S(2)}) async-start(bf16[8,160,128]{2,1,0:T(8,128)(2,1)} %broadcast_in_dim.120), calls=%async_computation.2 | async-start | bytes 655360 | tf_op jit(solution)/shard_map/all_to_all | solution.py:173
  147.6 11.3 %all-to-all-done.2 = bf16[8,160,128]{2,1,0:T(8,128)(2,1)S(1)} async-done(((bf16[8,160,128]{2,1,0:T(8,128)(2,1)}), bf16[8,160,128]{2,1,0:T(8,128)(2,1)S(1)}, u32[]{:S(2)}, u32[]{:S(2)}) %all-to-all-start.2) | async-done | bytes 327712 | tf_op jit(solution)/shard_map/all_to_all | solution.py:173
  158.8 4.7 %collective-permute-start.13 = (bf16[1280,128]{1,0:T(8,128)(2,1)S(1)}, bf16[1280,128]{1,0:T(8,128)(2,1)S(1)}, u32[]{:S(2)}, u32[]{:S(2)}) collective-permute-start(bf16[1280,128]{1,0:T(8,128)(2,1)S(1)} %bitcast.129), channel_id=1, source_target_pairs={{0,16},{16,0},{1,17},{17,1},{2,18},{18,2},{3,19},{19,3},{4,20},{20... | collective-permute-start | bytes 983048 | tf_op jit(solution)/shard_map/ppermute | solution.py:181
  163.6 3.7 %collective-permute-start.12 = (bf16[1280,128]{1,0:T(8,128)(2,1)S(1)}, bf16[1280,128]{1,0:T(8,128)(2,1)S(1)}, u32[]{:S(2)}, u32[]{:S(2)}) collective-permute-start(bf16[1280,128]{1,0:T(8,128)(2,1)S(1)} %bitcast.130), channel_id=1, source_target_pairs={{0,32},{32,0},{1,33},{33,1},{2,34},{34,2},{3,35},{35,3},{4,36},{36... | collective-permute-start | bytes 983048 | tf_op jit(solution)/shard_map/ppermute | solution.py:180
  167.3 0.5 fusion.24
  167.9 7.5 %collective-permute-done.12 = bf16[1280,128]{1,0:T(8,128)(2,1)S(1)} collective-permute-done((bf16[1280,128]{1,0:T(8,128)(2,1)S(1)}, bf16[1280,128]{1,0:T(8,128)(2,1)S(1)}, u32[]{:S(2)}, u32[]{:S(2)}) %collective-permute-start.12) | collective-permute-done | bytes 327712 | tf_op jit(solution)/shard_map/ppermute | solution.py:180
  175.3 2.5 %collective-permute-start.14 = (bf16[1280,128]{1,0:T(8,128)(2,1)S(1)}, bf16[1280,128]{1,0:T(8,128)(2,1)S(1)}, u32[]{:S(2)}, u32[]{:S(2)}) collective-permute-start(bf16[1280,128]{1,0:T(8,128)(2,1)S(1)} %collective-permute-done.12), channel_id=1, source_target_pairs={{0,16},{16,0},{1,17},{17,1},{2,18},{18,2},{3,19},{19,3},{4,20},{20... | collective-permute-start | bytes 983048 | tf_op jit(solution)/shard_map/ppermute | solution.py:182
  177.9 0.6 fusion.20
  178.4 0.5 fusion.22
  179.1 0.7 add_convert_fusion
  179.8 1.6 copy.47
  (55 shorter events, 3.3 us)
Async XLA Ops:
  0.6 15.4 %collective-permute-start.2 = (bf16[1152,128]{1,0:T(8,128)(2,1)}, bf16[1152,128]{1,0:T(8,128)(2,1)S(1)}, u32[]{:S(2)}, u32[]{:S(2)}) collective-permute-start(bf16[1152,128]{1,0:T(8,128)(2,1)} %param.8), channel_id=1, source_target_pairs={{0,14},{2,0},{4,2},{6,4},{8,6},{10,8},{12,10},{14,12},{1,15},{3,1}... | collective-permute-start | bytes 884744 | tf_op jit(solution)/shard_map/ppermute | solution.py:88
  6.6 14.1 %collective-permute-start.1 = (bf16[1152,128]{1,0:T(8,128)(2,1)}, bf16[1152,128]{1,0:T(8,128)(2,1)S(1)}, u32[]{:S(2)}, u32[]{:S(2)}) collective-permute-start(bf16[1152,128]{1,0:T(8,128)(2,1)} %param.8), channel_id=1, source_target_pairs={{0,2},{2,4},{4,6},{6,8},{8,10},{10,12},{12,14},{14,0},{1,3},{3,5},... | collective-permute-start | bytes 884744 | tf_op jit(solution)/shard_map/ppermute | solution.py:85
  8.5 27.0 %collective-permute-start = (bf16[320,1152]{1,0:T(8,128)(2,1)}, bf16[320,1152]{1,0:T(8,128)(2,1)S(1)}, u32[]{:S(2)}, u32[]{:S(2)}) collective-permute-start(bf16[320,1152]{1,0:T(8,128)(2,1)} %param.7), channel_id=1, source_target_pairs={{0,1},{1,0},{2,3},{3,2},{4,5},{5,4},{6,7},{7,6},{8,9},{9,8},{10,11... | collective-permute-start | bytes 2211848 | tf_op jit(solution)/shard_map/ppermute | solution.py:94
  14.8 20.7 %copy-start.2 = (bf16[320,1152]{1,0:T(8,128)(2,1)S(1)}, bf16[320,1152]{1,0:T(8,128)(2,1)}, u32[]{:S(2)}) copy-start(bf16[320,1152]{1,0:T(8,128)(2,1)} %param.7) | copy-start | bytes 2211844
  16.1 9.4 %collective-permute-start.4 = (bf16[1152,128]{1,0:T(8,128)(2,1)S(1)}, bf16[1152,128]{1,0:T(8,128)(2,1)}, u32[]{:S(2)}, u32[]{:S(2)}) collective-permute-start(bf16[1152,128]{1,0:T(8,128)(2,1)S(1)} %collective-permute-done.2), channel_id=1, source_target_pairs={{0,14},{2,0},{4,2},{6,4},{8,6},{10,8},{12,10},{14,12},{1,15},{3,1}... | collective-permute-start | bytes 884744 | tf_op jit(solution)/shard_map/ppermute | solution.py:88
  20.7 10.2 %collective-permute-start.3 = (bf16[1152,128]{1,0:T(8,128)(2,1)S(1)}, bf16[1152,128]{1,0:T(8,128)(2,1)S(1)}, u32[]{:S(2)}, u32[]{:S(2)}) collective-permute-start(bf16[1152,128]{1,0:T(8,128)(2,1)S(1)} %collective-permute-done.1), channel_id=1, source_target_pairs={{0,2},{2,4},{4,6},{6,8},{8,10},{10,12},{12,14},{14,0},{1,3},{3,5},... | collective-permute-start | bytes 884744 | tf_op jit(solution)/shard_map/ppermute | solution.py:85
  25.5 23.9 %collective-permute-start.8 = (bf16[1152,128]{1,0:T(8,128)(2,1)}, bf16[1152,128]{1,0:T(8,128)(2,1)}, u32[]{:S(2)}, u32[]{:S(2)}) collective-permute-start(bf16[1152,128]{1,0:T(8,128)(2,1)} %collective-permute-done.4), channel_id=1, source_target_pairs={{0,14},{2,0},{4,2},{6,4},{8,6},{10,8},{12,10},{14,12},{1,15},{3,1}... | collective-permute-start | bytes 884744 | tf_op jit(solution)/shard_map/ppermute | solution.py:88
  30.9 10.5 %collective-permute-start.7 = (bf16[1152,128]{1,0:T(8,128)(2,1)S(1)}, bf16[1152,128]{1,0:T(8,128)(2,1)}, u32[]{:S(2)}, u32[]{:S(2)}) collective-permute-start(bf16[1152,128]{1,0:T(8,128)(2,1)S(1)} %collective-permute-done.3), channel_id=1, source_target_pairs={{0,2},{2,4},{4,6},{6,8},{8,10},{10,12},{12,14},{14,0},{1,3},{3,5},... | collective-permute-start | bytes 884744 | tf_op jit(solution)/shard_map/ppermute | solution.py:85
  34.4 1.1 copy-start.4
  38.7 1.4 copy-start.5
  40.0 1.4 copy-start
  41.5 9.3 %collective-permute-start.9 = (bf16[1152,128]{1,0:T(8,128)(2,1)}, bf16[1152,128]{1,0:T(8,128)(2,1)}, u32[]{:S(2)}, u32[]{:S(2)}) collective-permute-start(bf16[1152,128]{1,0:T(8,128)(2,1)} %collective-permute-done.7), channel_id=1, source_target_pairs={{0,2},{2,4},{4,6},{6,8},{8,10},{10,12},{12,14},{14,0},{1,3},{3,5},... | collective-permute-start | bytes 884744 | tf_op jit(solution)/shard_map/ppermute | solution.py:85
  44.2 8.1 %collective-permute-start.5 = (f32[320,5,128]{2,0,1:T(8,128)S(1)}, f32[320,5,128]{2,0,1:T(8,128)S(1)}, u32[]{:S(2)}, u32[]{:S(2)}) collective-permute-start(f32[320,5,128]{2,0,1:T(8,128)S(1)} %copy.37), channel_id=1, source_target_pairs={{0,16},{16,0},{1,17},{17,1},{2,18},{18,2},{3,19},{19,3},{4,20},{20... | collective-permute-start | bytes 2457608 | tf_op jit(solution)/shard_map/ppermute | solution.py:62
  52.2 1.4 copy-start.1
  55.1 8.9 %collective-permute-start.10 = (f32[320,3,128]{2,0,1:T(8,128)S(1)}, f32[320,3,128]{2,0,1:T(8,128)S(1)}, u32[]{:S(2)}, u32[]{:S(2)}) collective-permute-start(f32[320,3,128]{2,0,1:T(8,128)S(1)} %copy.41), channel_id=1, source_target_pairs={{0,16},{16,0},{1,17},{17,1},{2,18},{18,2},{3,19},{19,3},{4,20},{20... | collective-permute-start | bytes 1474568 | tf_op jit(solution)/shard_map/ppermute | solution.py:62
  61.3 13.1 %collective-permute-start.6 = (f32[160,5,128]{2,0,1:T(8,128)}, f32[160,5,128]{2,0,1:T(8,128)S(1)}, u32[]{:S(2)}, u32[]{:S(2)}) collective-permute-start(f32[160,5,128]{2,0,1:T(8,128)} %slice.41), channel_id=1, source_target_pairs={{0,32},{32,0},{1,33},{33,1},{2,34},{34,2},{3,35},{35,3},{4,36},{36... | collective-permute-start | bytes 1228808 | tf_op jit(solution)/shard_map/ppermute | solution.py:62
  64.1 15.5 %collective-permute-start.11 = (f32[160,3,128]{2,0,1:T(8,128)S(1)}, f32[160,3,128]{2,0,1:T(8,128)S(1)}, u32[]{:S(2)}, u32[]{:S(2)}) collective-permute-start(f32[160,3,128]{2,0,1:T(8,128)S(1)} %slice.59), channel_id=1, source_target_pairs={{0,32},{32,0},{1,33},{33,1},{2,34},{34,2},{3,35},{35,3},{4,36},{36... | collective-permute-start | bytes 737288 | tf_op jit(solution)/shard_map/ppermute | solution.py:62
  80.3 4.8 %copy-start.6 = (s32[1,32]{1,0:T(1,128)S(1)}, s32[1,32]{1,0:T(1,128)}, u32[]{:S(2)}) copy-start(s32[1,32]{1,0:T(1,128)} %param.12) | copy-start | bytes 388
  81.3 24.6 %all-to-all-start = ((f32[160,8,128]{2,0,1:T(8,128)}), f32[160,8,128]{2,0,1:T(8,128)S(1)}, u32[]{:S(2)}, u32[]{:S(2)}) async-start(f32[160,8,128]{2,0,1:T(8,128)} %select_bitcast_fusion), calls=%async_computation | async-start | bytes 1310720 | tf_op jit(solution)/shard_map/all_to_all | solution.py:155
  106.5 30.5 %copy-start.3 = (f32[160,128]{1,0:T(8,128)S(1)}, f32[160,128]{1,0:T(8,128)}, u32[]{:S(2)}) copy-start(f32[160,128]{1,0:T(8,128)} %param.13) | copy-start | bytes 245764
  144.1 14.7 %all-to-all-start.2 = ((bf16[8,160,128]{2,1,0:T(8,128)(2,1)}), bf16[8,160,128]{2,1,0:T(8,128)(2,1)S(1)}, u32[]{:S(2)}, u32[]{:S(2)}) async-start(bf16[8,160,128]{2,1,0:T(8,128)(2,1)} %broadcast_in_dim.120), calls=%async_computation.2 | async-start | bytes 655360 | tf_op jit(solution)/shard_map/all_to_all | solution.py:173
  158.8 19.0 %collective-permute-start.13 = (bf16[1280,128]{1,0:T(8,128)(2,1)S(1)}, bf16[1280,128]{1,0:T(8,128)(2,1)S(1)}, u32[]{:S(2)}, u32[]{:S(2)}) collective-permute-start(bf16[1280,128]{1,0:T(8,128)(2,1)S(1)} %bitcast.129), channel_id=1, source_target_pairs={{0,16},{16,0},{1,17},{17,1},{2,18},{18,2},{3,19},{19,3},{4,20},{20... | collective-permute-start | bytes 983048 | tf_op jit(solution)/shard_map/ppermute | solution.py:181
  163.6 11.7 %collective-permute-start.12 = (bf16[1280,128]{1,0:T(8,128)(2,1)S(1)}, bf16[1280,128]{1,0:T(8,128)(2,1)S(1)}, u32[]{:S(2)}, u32[]{:S(2)}) collective-permute-start(bf16[1280,128]{1,0:T(8,128)(2,1)S(1)} %bitcast.130), channel_id=1, source_target_pairs={{0,32},{32,0},{1,33},{33,1},{2,34},{34,2},{3,35},{35,3},{4,36},{36... | collective-permute-start | bytes 983048 | tf_op jit(solution)/shard_map/ppermute | solution.py:180
  175.3 3.7 %collective-permute-start.14 = (bf16[1280,128]{1,0:T(8,128)(2,1)S(1)}, bf16[1280,128]{1,0:T(8,128)(2,1)S(1)}, u32[]{:S(2)}, u32[]{:S(2)}) collective-permute-start(bf16[1280,128]{1,0:T(8,128)(2,1)S(1)} %collective-permute-done.12), channel_id=1, source_target_pairs={{0,16},{16,0},{1,17},{17,1},{2,18},{18,2},{3,19},{19,3},{4,20},{20... | collective-permute-start | bytes 983048 | tf_op jit(solution)/shard_map/ppermute | solution.py:182
